TPU v7x, 32 devices: a whole 2x2x4 slice. The times are simulated.
32 devices in a mesh: group: 2 (over y), seq: 8 (over z, x), head: 2 (over core).
Axes of the slice: x: 2, y: 2, z: 4, core: 2. Of those that a mesh axis runs over, the one named last changes fastest.
Arguments:
- x_in: bfloat16 [4096, 4096], P(('group', 'seq'), 'head'), parts along dimension 0, may hold values from -6 to 6
- step_size: float32 [64, 4096], P('head', ('group', 'seq')), parts along dimension 1, may hold values from 0.002 to 0.128
- a_log: float32 [64], P('head'), may hold values from -8.5 to 0.9
- d_skip: float32 [64], P('head'), may hold values from 0.1 to 1.9
- b_in: bfloat16 [4096, 128], P(('group', 'seq')), parts along dimension 0, may hold values from -6 to 6
- c_in: bfloat16 [4096, 128], P(('group', 'seq')), parts along dimension 0, may hold values from -0.52734375 to 0.52734375
- queries: bfloat16 [4096, 2048], P(('group', 'seq'), 'head'), parts along dimension 0, may hold values from -4.5 to 4.5
- key_rows: bfloat16 [4096, 512], P(('group', 'seq'), 'head'), parts along dimension 0, may hold values from -4.5 to 4.5
- values: bfloat16 [4096, 512], P(('group', 'seq'), 'head'), parts along dimension 0, may hold values from -6 to 6
Outputs:
- mamba_out: bfloat16 [4096, 4096], P(('group', 'seq'), 'head'), parts along dimension 0
- attn_out: bfloat16 [4096, 2048], P(('group', 'seq'), 'head'), parts along dimension 0
There are 2 independent parts, one for each index of `group`. A program takes and returns all parts, laid end to end along the dimension named above; an argument that names none is the same for every part. Nothing has to cross between parts.
All inputs are finite; a program needn't handle non-finite values.
Results may differ from a plain program's by a relative error of at most 0.009.
Values may be sent and summed in bfloat16 or wider, within the bound.
No kernel may reach another device: no remote copies, remote signals or barrier semaphores. Data moves between devices by JAX's collectives and lax.ppermute only.
A program may use at most 320 MiB of HBM per device.

v0:
```python
import jax
import jax.numpy as jnp
from jax import lax
from jax.sharding import PartitionSpec as P

BLOCK = 128
HEADDIM = 64
STATE = 128
QHEADS = 16
KVHEADS = 4
HD = 128


NEG = -1e30


def carried_in(value, axis, combine, identity):
    count, mine = (lax.axis_size(axis), lax.axis_index(axis))
    everything = jax.tree.map(
        lambda part, kind: lax.all_gather(part.astype(kind), axis),
        value,
        (jnp.bfloat16, jnp.bfloat16),
    )
    start = jax.tree.map(
        lambda part, zero: jnp.broadcast_to(jnp.asarray(zero, part.dtype), part.shape),
        value,
        identity,
    )

    def turn(k, before):
        reached = k < mine
        new = combine(
            before, jax.tree.map(lambda part, own: part[k].astype(own.dtype), everything, value)
        )
        return jax.tree.map(lambda a, b: jnp.where(reached, a, b), new, before)

    return lax.fori_loop(0, count, turn, start)


def broadcast(value, axis, source):
    kept = jnp.where(lax.axis_index(axis) == source, value, 0).astype(value.dtype)
    return lax.psum(kept, axis)


def ssd_local(x_blocks, steps, rate, b_blocks, c_blocks):
    cum = jnp.cumsum(steps * rate[None, :, None], axis=2)
    causal = jnp.arange(BLOCK)[:, None] >= jnp.arange(BLOCK)[None, :]
    log_gap = jnp.where(causal, cum[:, :, :, None] - cum[:, :, None, :], -jnp.inf)
    inner = jnp.einsum("cin,cjn->cij", c_blocks, b_blocks, preferred_element_type=jnp.float32)
    mixing = (inner[:, None] * jnp.exp(log_gap) * steps[:, :, None, :]).astype(jnp.bfloat16)
    intra = jnp.einsum("chij,cjhp->cihp", mixing, x_blocks, preferred_element_type=jnp.float32)
    log_total = cum[:, :, -1]
    factor = (jnp.exp(log_total[:, :, None] - cum) * steps).transpose(0, 2, 1)[..., None]
    scaled = (factor * x_blocks.astype(jnp.float32)).astype(jnp.bfloat16)
    block_state = jnp.einsum("cjhp,cjn->chpn", scaled, b_blocks, preferred_element_type=jnp.float32)
    return (intra, block_state, log_total, cum)


def ssd_finish(intra, cum, c_blocks, incoming, d_skip, x_blocks):
    carried = jnp.einsum(
        "cin,chpn->cihp", c_blocks.astype(jnp.float32), incoming, precision=lax.Precision.HIGHEST
    )
    carried = carried * jnp.exp(cum).transpose(0, 2, 1)[..., None]
    return (intra + carried + d_skip[None, None, :, None] * x_blocks.astype(jnp.float32)).astype(
        jnp.bfloat16
    )


def chain(earlier, later):
    return (earlier[0] * later[0], later[0][..., None, None] * earlier[1] + later[1])


def local(x_in, step_size, a_log, d_skip, b_in, c_in, queries, key_rows, values):
    my_index = lax.axis_index("seq")
    seq_count = lax.axis_size("seq")
    tok_rows = x_in.shape[0]
    slots = tok_rows // BLOCK
    mamba_local = step_size.shape[0]
    rate = -jnp.exp(a_log)
    x_blocks = x_in.reshape(slots, BLOCK, mamba_local, HEADDIM)
    steps = step_size.reshape(mamba_local, slots, BLOCK).transpose(1, 0, 2)
    b_blocks = b_in.reshape(slots, BLOCK, STATE)
    c_blocks = c_in.reshape(slots, BLOCK, STATE)
    intra, block_state, log_total, cum = ssd_local(x_blocks, steps, rate, b_blocks, c_blocks)
    decay = jnp.exp(log_total)
    identity = (jnp.ones_like(decay), jnp.zeros_like(block_state))
    prefix = carried_in((decay, block_state), "seq", chain, identity)
    inclusive = chain(prefix, (decay, block_state))
    total_decay, total_state = (
        broadcast(inclusive[0].astype(jnp.bfloat16), "seq", lax.axis_size("seq") - 1).astype(
            jnp.float32
        ),
        broadcast(inclusive[1].astype(jnp.bfloat16), "seq", lax.axis_size("seq") - 1).astype(
            jnp.float32
        ),
    )
    carry_state = jnp.zeros_like(block_state[0])
    entering = []
    for slot in range(slots):
        entering.append(prefix[0][slot][:, None, None] * carry_state + prefix[1][slot])
        carry_state = total_decay[slot][:, None, None] * carry_state + total_state[slot]
    incoming = jnp.stack(entering, axis=0)
    mamba_out = ssd_finish(intra, cum, c_blocks, incoming, d_skip, x_blocks).reshape(
        tok_rows, mamba_local * HEADDIM
    )
    per_kv = QHEADS // KVHEADS
    kv_local = key_rows.shape[1] // HD
    score_scale = 1.0 / HD**0.5
    stride = seq_count * BLOCK
    q_flat = queries.reshape(slots, BLOCK, kv_local, per_kv, HD).transpose(2, 0, 3, 1, 4)
    q_flat = q_flat.reshape(kv_local, slots * per_kv * BLOCK, HD)
    q_slot = jnp.arange(slots)[:, None, None]
    q_row = jnp.arange(BLOCK)[None, None, :]
    query_pos = (
        q_slot * stride + my_index * BLOCK + q_row + jnp.zeros((slots, per_kv, BLOCK), jnp.int32)
    ).reshape(-1)
    k_slots = key_rows.reshape(slots, BLOCK, kv_local * HD)
    v_slots = values.reshape(slots, BLOCK, kv_local * HD)
    q_total = slots * per_kv * BLOCK
    start_state = (
        jnp.full((kv_local, q_total), NEG, jnp.float32),
        jnp.zeros((kv_local, q_total), jnp.float32),
        jnp.zeros((kv_local, q_total, HD), jnp.float32),
    )
    running = start_state
    k_piece = lax.all_gather(k_slots, "seq", axis=1, tiled=True)
    v_piece = lax.all_gather(v_slots, "seq", axis=1, tiled=True)
    rows = k_piece.shape[1]
    block_rows = 512
    count = rows // block_rows
    k_blocks = k_piece.reshape(slots, count, block_rows, kv_local, HD).transpose(1, 0, 2, 3, 4)
    v_blocks = v_piece.reshape(slots, count, block_rows, kv_local, HD).transpose(1, 0, 2, 3, 4)
    k_slot = jnp.arange(slots)[:, None]
    k_row = jnp.arange(block_rows)[None, :]

    def per_block(state, inputs):
        k_block, v_block, number = inputs
        run_max, run_sum, run_acc = state
        k_flat = k_block.reshape(slots * block_rows, kv_local, HD)
        v_flat = v_block.reshape(slots * block_rows, kv_local, HD)
        key_pos = (k_slot * stride + number * block_rows + k_row).reshape(-1)
        visible = key_pos[None, None, :] <= query_pos[None, :, None]
        scores = (
            jnp.einsum("gqd,kgd->gqk", q_flat, k_flat, preferred_element_type=jnp.float32)
            * score_scale
        )
        scores = jnp.where(visible, scores, NEG)
        new_max = jnp.maximum(run_max, jnp.max(scores, axis=-1))
        rescale = jnp.exp(run_max - new_max)
        weights = jnp.where(visible, jnp.exp(scores - new_max[..., None]), 0.0)
        new_sum = run_sum * rescale + jnp.sum(weights, axis=-1)
        update = jnp.einsum(
            "gqk,kgd->gqd", weights.astype(jnp.bfloat16), v_flat, preferred_element_type=jnp.float32
        )
        return ((new_max, new_sum, run_acc * rescale[..., None] + update), None)

    numbers = jnp.arange(count)
    running, unused = lax.scan(per_block, running, (k_blocks, v_blocks, numbers))
    run_max, run_sum, run_acc = running
    attended = (run_acc / run_sum[..., None]).astype(jnp.bfloat16)
    attn_out = (
        attended.reshape(kv_local, slots, per_kv, BLOCK, HD)
        .transpose(1, 3, 0, 2, 4)
        .reshape(tok_rows, kv_local * per_kv * HD)
    )
    return (mamba_out, attn_out)


def solution(mesh):
    in_specs = (
        P(("group", "seq"), "head"),
        P("head", ("group", "seq")),
        P("head"),
        P("head"),
        P(("group", "seq"), None),
        P(("group", "seq"), None),
        P(("group", "seq"), "head"),
        P(("group", "seq"), "head"),
        P(("group", "seq"), "head"),
    )
    out_specs = (P(("group", "seq"), "head"), P(("group", "seq"), "head"))
    return jax.shard_map(local, mesh=mesh, in_specs=in_specs, out_specs=out_specs, check_vma=False)
```

profile of v0, /device:TPU:0, one launch (start us, length us, event | category | flops | bytes accessed | tf_op | source)
XLA Modules:
  0.0 329.5 jit_solution(400362677163292108)
XLA Ops:
  10.9 3.3 %reshape.215 = bf16[2,128,32,64]{3,2,1,0:T(8,128)(2,1)S(1)} reshape(bf16[256,2048]{1,0:T(8,128)(2,1)} %param.13) | data formatting | bytes 2097152 | tf_op jit(solution)/shard_map/reshape | solution.py:80
  14.3 2.2 copy.44
  16.6 2.1 fusion.48
  18.9 22.4 %all-gather = bf16[16,32,1]{1,2,0:T(2,128)(2,1)S(1)} all-gather(bf16[2,32,1]{1,2,0:T(2,128)(2,1)S(1)} %copy.46), channel_id=2, replica_groups=mesh['group'=2,'seq'=8,'head'=2] {'seq'}, dimensions={0}, use_global_device_ids=true | all-gather | bytes 1152 | tf_op jit(solution)/shard_map/all_gather | solution.py:20
  41.4 2.2 reshape.198
  43.6 2.0 copy.50
  45.8 3.4 %fusion.24 = f32[2,32,128,64]{2,3,1,0:T(8,128)} fusion(bf16[2,128,32,64]{1,3,2,0:T(8,128)(2,1)S(1)} %copy.44, f32[2,32,128]{2,1,0:T(8,128)S(1)} %bitcast_bitcast_fusion.1, f32[2,32,128]{2,1,0:T(8,128)S(1)} %reduce_window_sum.11, f32[2,128,128]{2,1,0:T(8,128)S(1)} %fusion.49, pred[128,128]{1,0:T(8,128)(4,1)S(1)} %iota_compare_fusion), kind=kOutput, calls=%fused_computation.35 | convolution fusion | flops 139460608 | bytes 3358720 | tf_op jit(solution)/shard_map/chij,cjhp->cihp/dot_general | solution.py:51
  49.2 4.0 %all-gather.6.cloned.1.call-done = bf16[2,1024,256]{2,1,0:T(8,128)(2,1)} async-done(((bf16[2,128,256]{2,1,0:T(8,128)(2,1)}), bf16[2,1024,256]{2,1,0:T(8,128)(2,1)}) %all-gather.6.cloned.1.call-update) | async-done | bytes 1048592 | tf_op jit(solution)/shard_map/all_gather | solution.py:126
  53.1 2.2 reshape.197
  55.4 39.0 %all-gather.8.cloned.1.call-done = bf16[2,1024,256]{2,1,0:T(8,128)(2,1)} async-done(((bf16[2,128,256]{2,1,0:T(8,128)(2,1)}), bf16[2,1024,256]{2,1,0:T(8,128)(2,1)}) %all-gather.8.cloned.1.call-update) | async-done | bytes 1048592 | tf_op jit(solution)/shard_map/all_gather | solution.py:127
  94.3 2.1 reshape.201
  96.4 123.7 %all-gather.10.cloned.1.call-done = bf16[16,32,64,128]{3,2,1,0:T(8,128)(2,1)} async-done(((bf16[2,32,64,128]{3,2,1,0:T(8,128)(2,1)}), bf16[16,32,64,128]{3,2,1,0:T(8,128)(2,1)}) %all-gather.10.cloned.1.call-update) | async-done | bytes 8388624 | tf_op jit(solution)/shard_map/all_gather | solution.py:20
  220.2 14.6 %while.31 = (s32[]{:T(128)}, f32[2,32]{1,0:T(2,128)S(1)}, f32[2,32,64,128]{3,2,1,0:T(8,128)S(1)}, s32[]{:T(128)}, bf16[8,2,32]{2,1,0:T(2,128)(2,1)S(1)}, /*index...) while((s32[]{:T(128)}, f32[2,32]{1,0:T(2,128)S(1)}, f32[2,32,64,128]{3,2,1,0:T(8,128)S(1)}, ...), condition=%wide.region_2.3_spmd.clone, body=%wide.region_1.2_spmd.clone.sunk | while | flops 2621764 | bytes 5244279 | solution.py:37
  222.0 1.8 fusion.73
  223.8 1.8 fusion.73
  225.6 1.8 fusion.73
  227.5 1.8 fusion.73
  229.3 1.8 fusion.73
  234.8 3.0 fusion.41
  237.7 41.9 %while.32 = (s32[]{:T(128)}, f32[2,1024]{1,0:T(2,128)S(1)}, f32[2,1024]{1,0:T(2,128)S(1)}, f32[2,1024,128]{2,1,0:T(8,128)}, s32[2]{0:T(128)S(1)}, /*index=5*/bf1...) while((s32[]{:T(128)}, f32[2,1024]{1,0:T(2,128)S(1)}, ...), condition=%wide.region_8.9_spmd.clone, body=%wide.region_5.8_spmd.clone.sunk | while | flops 1102851072 | bytes 83518768 | solution.py:158
  239.7 2.7 constant_dynamic-slice_fusion.3
  242.6 5.0 %fusion.80 = (f32[2,1024]{1,0:T(2,128)S(1)}, f32[2,1024,1024]{2,1,0:T(8,128)}) fusion(pred[1024,1024]{0,1:T(8,128)(4,1)S(1)} %broadcast_compare_fusion.2, bf16[1024,2,128]{2,0,1:T(8,128)(2,1)S(1)} %bitcast.142, bf16[2,1024,128]{2,1,0:T(8,128)(2,1)S(1)} %copy-done.8), kind=kOutput, calls=%fused_computation.9.clone.1 | convolution fusion | flops 543160320 | bytes 10493952 | tf_op jit(solution)/shard_map/while/body/eval_jaxpr/gqd,kgd->gqk/dot_general | solution.py:144
  247.6 4.8 %fusion.82 = f32[2,1024]{1,0:T(2,128)S(1)} fusion(f32[2,1024,1024]{2,1,0:T(8,128)} %get-tuple-element.407, f32[2,1024]{1,0:T(2,128)S(1)} %fusion.81, pred[1024,1024]{0,1:T(8,128)(4,1)S(1)} %broadcast_compare_fusion.2), kind=kLoop, calls=%fused_computation.11.clone.1 | loop fusion | flops 10483712 | bytes 9453568 | tf_op jit(solution)/shard_map/while/body/eval_jaxpr/reduce_sum | solution.py:151
  254.0 3.7 %fusion.84 = f32[2,1024,128]{2,1,0:T(8,128)S(1)} fusion(bf16[1024,2,128]{2,0,1:T(8,128)(2,1)S(1)} %bitcast.141, f32[2,1024,1024]{2,1,0:T(8,128)S(1)} %copy-done.1, f32[2,1024]{1,0:T(2,128)S(1)} %fusion.81, pred[1024,1024]{0,1:T(8,128)(4,1)S(1)} %broadcast_compare_fusion.2, f32[2,1024,128]{2,1,0:T(8,128)S(1)} %copy-done.6, ...), kind=kOutput, calls=%fused_computation.15.clone.1 | convolution fusion | flops 548143104 | bytes 12075009 | tf_op jit(solution)/shard_map/while/body/eval_jaxpr/gqk,kgd->gqd/dot_general | solution.py:152
  260.7 2.8 constant_dynamic-slice_fusion.3
  263.6 5.0 %fusion.80 = (f32[2,1024]{1,0:T(2,128)S(1)}, f32[2,1024,1024]{2,1,0:T(8,128)}) fusion(pred[1024,1024]{0,1:T(8,128)(4,1)S(1)} %broadcast_compare_fusion.2, bf16[1024,2,128]{2,0,1:T(8,128)(2,1)S(1)} %bitcast.142, bf16[2,1024,128]{2,1,0:T(8,128)(2,1)S(1)} %copy-done.8), kind=kOutput, calls=%fused_computation.9.clone.1 | convolution fusion | flops 543160320 | bytes 10493952 | tf_op jit(solution)/shard_map/while/body/eval_jaxpr/gqd,kgd->gqk/dot_general | solution.py:144
  268.6 4.8 %fusion.82 = f32[2,1024]{1,0:T(2,128)S(1)} fusion(f32[2,1024,1024]{2,1,0:T(8,128)} %get-tuple-element.407, f32[2,1024]{1,0:T(2,128)S(1)} %fusion.81, pred[1024,1024]{0,1:T(8,128)(4,1)S(1)} %broadcast_compare_fusion.2), kind=kLoop, calls=%fused_computation.11.clone.1 | loop fusion | flops 10483712 | bytes 9453568 | tf_op jit(solution)/shard_map/while/body/eval_jaxpr/reduce_sum | solution.py:151
  274.9 3.7 %fusion.84 = f32[2,1024,128]{2,1,0:T(8,128)S(1)} fusion(bf16[1024,2,128]{2,0,1:T(8,128)(2,1)S(1)} %bitcast.141, f32[2,1024,1024]{2,1,0:T(8,128)S(1)} %copy-done.1, f32[2,1024]{1,0:T(2,128)S(1)} %fusion.81, pred[1024,1024]{0,1:T(8,128)(4,1)S(1)} %broadcast_compare_fusion.2, f32[2,1024,128]{2,1,0:T(8,128)S(1)} %copy-done.6, ...), kind=kOutput, calls=%fused_computation.15.clone.1 | convolution fusion | flops 548143104 | bytes 12075009 | tf_op jit(solution)/shard_map/while/body/eval_jaxpr/gqk,kgd->gqd/dot_general | solution.py:152
  282.9 18.6 %psum.14 = bf16[2,32]{1,0:T(2,128)(2,1)S(1)} all-reduce(bf16[2,32]{1,0:T(2,128)(2,1)S(1)} %broadcast_select_fusion.1), channel_id=1, replica_groups=mesh['group'=2,'seq'=8,'head'=2] {'seq'}, use_global_device_ids=true, to_apply=%region_3.4 | all-reduce | flops 64 | bytes 256 | tf_op jit(solution)/shard_map/psum | solution.py:42
  301.5 12.5 %all-reduce.2.cloned.1.call-done = bf16[2,32,64,128]{3,2,1,0:T(8,128)(2,1)} async-done(((bf16[2,32,64,128]{3,2,1,0:T(8,128)(2,1)}), bf16[2,32,64,128]{3,2,1,0:T(8,128)(2,1)}) %all-reduce.2.cloned.1.call-update) | async-done | bytes 1048592 | tf_op jit(solution)/shard_map/psum | solution.py:42
  317.6 3.0 copy.58
  320.6 2.4 reshape.214
  (113 shorter events, 24.3 us)
Async XLA Ops:
  7.2 9.5 %copy-start = (bf16[256,128]{1,0:T(8,128)(2,1)S(1)}, bf16[256,128]{1,0:T(8,128)(2,1)}, u32[]{:S(2)}) copy-start(bf16[256,128]{1,0:T(8,128)(2,1)} %param.17) | copy-start | bytes 196612
  7.2 46.0 %all-gather.6.cloned.1.call-start = ((), (), s32[]{:S(2)}) async-start(), calls=%async_computation.1 | async-start | bytes 1179648 | tf_op jit(solution)/shard_map/all_gather | solution.py:126
  7.9 86.4 %all-gather.8.cloned.1.call-start = ((), (), s32[]{:S(2)}) async-start(), calls=%async_computation.2 | async-start | bytes 1179648 | tf_op jit(solution)/shard_map/all_gather | solution.py:127
  8.7 211.5 %all-gather.10.cloned.1.call-start = ((), (), s32[]{:S(2)}) async-start(), calls=%async_computation.3 | async-start | bytes 9437184 | tf_op jit(solution)/shard_map/all_gather | solution.py:20
  14.3 2.2 copy-start.9
  16.5 29.3 %copy-start.3 = (bf16[2,128,32,64]{1,3,2,0:T(8,128)(2,1)}, bf16[2,128,32,64]{1,3,2,0:T(8,128)(2,1)S(1)}, u32[]{:S(2)}) copy-start(bf16[2,128,32,64]{1,3,2,0:T(8,128)(2,1)S(1)} %copy.44) | copy-start | bytes 3145732
  18.8 26.9 %copy-start.10 = (bf16[256,128]{1,0:T(8,128)(2,1)S(1)}, bf16[256,128]{1,0:T(8,128)(2,1)}, u32[]{:S(2)}) copy-start(bf16[256,128]{1,0:T(8,128)(2,1)} %param.18) | copy-start | bytes 196612
  18.8 295.2 %all-reduce.2.cloned.1.call-start = ((), (), s32[]{:S(2)}) async-start(), calls=%async_computation | async-start | bytes 2097152 | tf_op jit(solution)/shard_map/psum | solution.py:42
  239.1 3.5 %copy-start.8 = (bf16[2,1024,128]{2,1,0:T(8,128)(2,1)S(1)}, bf16[2,1024,128]{2,1,0:T(8,128)(2,1)}, u32[]{:S(2)}) copy-start(bf16[2,1024,128]{2,1,0:T(8,128)(2,1)} %get-tuple-element.465) | copy-start | bytes 1572868 | tf_op jit(solution)/shard_map/while
  247.6 4.9 %copy-start.2 = (bf16[1,2,512,2,128]{4,3,2,0,1:T(2,128)(2,1)S(1)}, bf16[1,2,512,2,128]{4,3,2,0,1:T(2,128)(2,1)}, u32[]{:S(2)}) copy-start(bf16[1,2,512,2,128]{4,3,2,0,1:T(2,128)(2,1)} %get-tuple-element.409) | copy-start | bytes 1572868 | tf_op jit(solution)/shard_map/while
  247.6 6.2 %copy-start.1 = (f32[2,1024,1024]{2,1,0:T(8,128)S(1)}, f32[2,1024,1024]{2,1,0:T(8,128)}, u32[]{:S(2)}) copy-start(f32[2,1024,1024]{2,1,0:T(8,128)} %get-tuple-element.407) | copy-start | bytes 25165828 | tf_op jit(solution)/shard_map/while
  247.6 6.4 %copy-start.6 = (f32[2,1024,128]{2,1,0:T(8,128)S(1)}, f32[2,1024,128]{2,1,0:T(8,128)}, u32[]{:S(2)}) copy-start(f32[2,1024,128]{2,1,0:T(8,128)} %get-tuple-element.450) | copy-start | bytes 3145732 | tf_op jit(solution)/shard_map/while
  257.7 1.0 copy-start.7
  260.0 3.5 %copy-start.8 = (bf16[2,1024,128]{2,1,0:T(8,128)(2,1)S(1)}, bf16[2,1024,128]{2,1,0:T(8,128)(2,1)}, u32[]{:S(2)}) copy-start(bf16[2,1024,128]{2,1,0:T(8,128)(2,1)} %get-tuple-element.465) | copy-start | bytes 1572868 | tf_op jit(solution)/shard_map/while
  268.6 4.9 %copy-start.2 = (bf16[1,2,512,2,128]{4,3,2,0,1:T(2,128)(2,1)S(1)}, bf16[1,2,512,2,128]{4,3,2,0,1:T(2,128)(2,1)}, u32[]{:S(2)}) copy-start(bf16[1,2,512,2,128]{4,3,2,0,1:T(2,128)(2,1)} %get-tuple-element.409) | copy-start | bytes 1572868 | tf_op jit(solution)/shard_map/while
  268.6 6.1 %copy-start.1 = (f32[2,1024,1024]{2,1,0:T(8,128)S(1)}, f32[2,1024,1024]{2,1,0:T(8,128)}, u32[]{:S(2)}) copy-start(f32[2,1024,1024]{2,1,0:T(8,128)} %get-tuple-element.407) | copy-start | bytes 25165828 | tf_op jit(solution)/shard_map/while
  268.6 6.3 %copy-start.6 = (f32[2,1024,128]{2,1,0:T(8,128)S(1)}, f32[2,1024,128]{2,1,0:T(8,128)}, u32[]{:S(2)}) copy-start(f32[2,1024,128]{2,1,0:T(8,128)} %get-tuple-element.450) | copy-start | bytes 3145732 | tf_op jit(solution)/shard_map/while
  278.7 1.0 copy-start.7
  314.0 1.5 copy-start.4
  314.0 2.1 copy-start.5
  314.0 2.1 copy-start.11
Sparse Core Ops, SparseCore 0:
  10.2 42.9 all-gather.5
  55.3 38.9 all-gather.7
  96.4 123.6 all-gather.9
  237.8 76.1 all-reduce.1
where the time goes:
time: 330 us
  waiting for transfers between devices  181 us (55%)
  blocking collectives  41.1 us (12%)
  other arithmetic  33.8 us (10%)
  local copies, waits for them, and re-layouts  33.6 us (10%)
  matrix products  24.6 us (7%)
  between operations  14 us (4%)
    all_gather x1, waiting for transfers between devices, carried_in(): lax.all_gather(part.astype(kind), axis)  124 us
    all_gather x1, waiting for transfers between devices, local(): v_piece = lax.all_gather(v_slots, 'seq', axis=1, tiled=True)  39 us
    all_gather x1, blocking collectives, carried_in(): lax.all_gather(part.astype(kind), axis)  22.4 us
    psum x1, blocking collectives, broadcast(): return lax.psum(kept, axis)  18.6 us
    select_n x16, other arithmetic, turn(): return jax.tree.map(lambda a, b: jnp.where(reached, a, b), new, before)  14.3 us
    psum x1, waiting for transfers between devices, broadcast(): return lax.psum(kept, axis)  12.5 us
    dot_general x2, matrix products, per_block(): jnp.einsum('gqd,kgd->gqk', q_flat, k_flat, preferred_element_type=jnp.flo...  10 us
    reduce_sum x2, other arithmetic, per_block(): new_sum = run_sum * rescale + jnp.sum(weights, axis=-1)  9.6 us
  transfers between devices with their start and end apart: 4, of which 4 were waited for; matrix products, arithmetic and copies ran while one was open for 18% of the time, Pallas kernels for 0%

commit v1 on v0

--- a/solution.py
+++ b/solution.py
@@ -14,32 +14,51 @@
 NEG = -1e30
 
 
-def carried_in(value, axis, combine, identity):
-    count, mine = (lax.axis_size(axis), lax.axis_index(axis))
-    everything = jax.tree.map(
-        lambda part, kind: lax.all_gather(part.astype(kind), axis),
-        value,
-        (jnp.bfloat16, jnp.bfloat16),
-    )
-    start = jax.tree.map(
-        lambda part, zero: jnp.broadcast_to(jnp.asarray(zero, part.dtype), part.shape),
-        value,
-        identity,
-    )
-
-    def turn(k, before):
-        reached = k < mine
-        new = combine(
-            before, jax.tree.map(lambda part, own: part[k].astype(own.dtype), everything, value)
-        )
-        return jax.tree.map(lambda a, b: jnp.where(reached, a, b), new, before)
-
-    return lax.fori_loop(0, count, turn, start)
+def combine_if(lower, earlier, later):
+    a_e, s_e = earlier
+    a_l, s_l = later
+    joined_a = a_e * a_l
+    joined_s = a_l[..., None, None] * s_e + s_l
+    return (jnp.where(lower, joined_a, a_l), jnp.where(lower, joined_s, s_l))
 
 
-def broadcast(value, axis, source):
-    kept = jnp.where(lax.axis_index(axis) == source, value, 0).astype(value.dtype)
-    return lax.psum(kept, axis)
+def exchange(value, axis, pairs):
+    decay, state = value
+    got_decay = lax.ppermute(decay, axis, pairs)
+    got_state = lax.ppermute(state.astype(jnp.bfloat16), axis, pairs).astype(jnp.float32)
+    return (got_decay, got_state)
+
+
+def entering_states(decay, block_state, count, mine):
+    slots = decay.shape[0]
+    excl = (jnp.ones_like(decay), jnp.zeros_like(block_state))
+    total = (decay, block_state)
+    span = 1
+    while span < count:
+        lower = (mine // span) % 2 == 1
+        last = span * 2 >= count
+        pairs = [(i, i ^ span) for i in range(count)]
+        if last and slots > 1:
+            head = exchange(jax.tree.map(lambda v: v[:-1], total), "seq", pairs)
+            up_pairs = [(i, i ^ span) for i in range(count) if (i // span) % 2 == 0]
+            tail = exchange(jax.tree.map(lambda v: v[-1:], total), "seq", up_pairs)
+            got = jax.tree.map(lambda a, b: jnp.concatenate([a, b], axis=0), head, tail)
+        else:
+            got = exchange(total, "seq", pairs)
+        excl = combine_if(lower, got, excl)
+        joined_low = combine_if(lower, got, total)
+        joined_high = (total[0] * got[0], got[0][..., None, None] * total[1] + got[1])
+        total = (
+            jnp.where(lower, joined_low[0], joined_high[0]),
+            jnp.where(lower, joined_low[1], joined_high[1]),
+        )
+        span *= 2
+    carry = jnp.zeros_like(block_state[0])
+    entering = []
+    for slot in range(slots):
+        entering.append(excl[0][slot][:, None, None] * carry + excl[1][slot])
+        carry = total[0][slot][:, None, None] * carry + total[1][slot]
+    return jnp.stack(entering, axis=0)
 
 
 def ssd_local(x_blocks, steps, rate, b_blocks, c_blocks):
@@ -66,10 +85,6 @@
     )
 
 
-def chain(earlier, later):
-    return (earlier[0] * later[0], later[0][..., None, None] * earlier[1] + later[1])
-
-
 def local(x_in, step_size, a_log, d_skip, b_in, c_in, queries, key_rows, values):
     my_index = lax.axis_index("seq")
     seq_count = lax.axis_size("seq")
@@ -83,23 +98,7 @@
     c_blocks = c_in.reshape(slots, BLOCK, STATE)
     intra, block_state, log_total, cum = ssd_local(x_blocks, steps, rate, b_blocks, c_blocks)
     decay = jnp.exp(log_total)
-    identity = (jnp.ones_like(decay), jnp.zeros_like(block_state))
-    prefix = carried_in((decay, block_state), "seq", chain, identity)
-    inclusive = chain(prefix, (decay, block_state))
-    total_decay, total_state = (
-        broadcast(inclusive[0].astype(jnp.bfloat16), "seq", lax.axis_size("seq") - 1).astype(
-            jnp.float32
-        ),
-        broadcast(inclusive[1].astype(jnp.bfloat16), "seq", lax.axis_size("seq") - 1).astype(
-            jnp.float32
-        ),
-    )
-    carry_state = jnp.zeros_like(block_state[0])
-    entering = []
-    for slot in range(slots):
-        entering.append(prefix[0][slot][:, None, None] * carry_state + prefix[1][slot])
-        carry_state = total_decay[slot][:, None, None] * carry_state + total_state[slot]
-    incoming = jnp.stack(entering, axis=0)
+    incoming = entering_states(decay, block_state, seq_count, my_index)
     mamba_out = ssd_finish(intra, cum, c_blocks, incoming, d_skip, x_blocks).reshape(
         tok_rows, mamba_local * HEADDIM
     )
@@ -123,8 +122,9 @@
         jnp.zeros((kv_local, q_total, HD), jnp.float32),
     )
     running = start_state
-    k_piece = lax.all_gather(k_slots, "seq", axis=1, tiled=True)
-    v_piece = lax.all_gather(v_slots, "seq", axis=1, tiled=True)
+    kv_piece = lax.all_gather(jnp.concatenate([k_slots, v_slots], axis=2), "seq", axis=1, tiled=True)
+    k_piece = kv_piece[..., : kv_local * HD]
+    v_piece = kv_piece[..., kv_local * HD :]
     rows = k_piece.shape[1]
     block_rows = 512
     count = rows // block_rows

time: 330 us -> 189 us (0.57)
  the two profiles are of different devices: /device:TPU:0 before, /device:TPU:29 now
where the time goes in v1:
time: 189 us
  waiting for transfers between devices  99.7 us (53%)
  local copies, waits for them, and re-layouts  25.3 us (13%)
  other arithmetic  20.6 us (11%)
  matrix products  18.5 us (10%)
  between operations  14.4 us (8%)
  starting transfers between devices  8.7 us (5%)
    ppermute x4, waiting for transfers between devices, exchange(): got_decay = lax.ppermute(decay, axis, pairs)  99.7 us
    dot_general x2, matrix products, per_block(): jnp.einsum('gqk,kgd->gqd', weights.astype(jnp.bfloat16), v_flat, preferre...  7.51 us
    unnamed x18, local copies, waits for them, and re-layouts  7.43 us
    ppermute x4, starting transfers between devices, exchange(): got_decay = lax.ppermute(decay, axis, pairs)  5.89 us
    reshape x2, local copies, waits for them, and re-layouts, local(): x_blocks = x_in.reshape(slots, BLOCK, mamba_local, HEADDIM)  5.54 us
    reduce_sum x2, other arithmetic, per_block(): new_sum = run_sum * rescale + jnp.sum(weights, axis=-1)  4.51 us
  transfers between devices with their start and end apart: 9, of which 3 were waited for; matrix products, arithmetic and copies ran while one was open for 14% of the time, Pallas kernels for 0%

profile of v1, /device:TPU:29, one launch (start us, length us, event | category | flops | bytes accessed | tf_op | source)
XLA Modules:
  0.0 188.7 jit_solution(4055690801852620943)
XLA Ops:
  10.3 3.3 %reshape.190 = bf16[2,128,32,64]{3,2,1,0:T(8,128)(2,1)S(1)} reshape(bf16[256,2048]{1,0:T(8,128)(2,1)} %param.11) | data formatting | bytes 2097152 | tf_op jit(solution)/shard_map/reshape | solution.py:95
  13.7 2.2 %copy.30 = bf16[2,128,32,64]{1,3,2,0:T(8,128)(2,1)S(1)} copy(bf16[2,128,32,64]{3,2,1,0:T(8,128)(2,1)S(1)} %reshape.190) | data formatting | bytes 2097152 | tf_op jit(solution)/shard_map/reshape | solution.py:95
  15.9 1.4 fusion.58
  17.3 1.2 collective-permute-start.4
  19.7 24.8 %collective-permute-done = f32[2,32]{1,0:T(2,128)S(1)} collective-permute-done((f32[2,32]{1,0:T(2,128)S(1)}, f32[2,32]{1,0:T(2,128)S(1)}, u32[]{:S(2)}, u32[]{:S(2)}) %collective-permute-start) | collective-permute-done | bytes 288 | tf_op jit(solution)/shard_map/ppermute | solution.py:27
  44.5 2.9 %fusion.49 = bf16[2,32,64,128]{3,2,1,0:T(8,128)(2,1)} fusion(f32[2,32,64,128]{3,2,1,0:T(8,128)S(1)} %get-tuple-element.166, f32[2,32]{1,0:T(2,128)S(1)} %collective-permute-done, bf16[2,32,64,128]{3,2,1,0:T(8,128)(2,1)} %collective-permute-done.4, f32[2,32]{1,0:T(2,128)S(1)} %exp.35, pred[]{:T(512)S(6)} %eq.15), kind=kLoop, calls=%fused_computation.69 | loop fusion | flops 4194304 | bytes 4194817 | tf_op jit(solution)/shard_map/convert_element_type | solution.py:28
  47.9 3.3 %fusion.23 = f32[2,32,128,64]{2,3,1,0:T(8,128)} fusion(bf16[2,128,32,64]{1,3,2,0:T(8,128)(2,1)S(1)} %copy.30, f32[2,32,128]{2,1,0:T(8,128)S(1)} %bitcast_bitcast_fusion.1, f32[2,32,128]{2,1,0:T(8,128)S(1)} %reduce_window_sum.11, f32[2,128,128]{2,1,0:T(8,128)S(1)} %fusion.59, pred[128,128]{1,0:T(8,128)(4,1)S(1)} %iota_compare_fusion), kind=kOutput, calls=%fused_computation.41 | convolution fusion | flops 139460608 | bytes 3358720 | tf_op jit(solution)/shard_map/chij,cjhp->cihp/dot_general | solution.py:70
  51.2 1.3 collective-permute-start.1
  52.5 2.2 %reshape.180 = bf16[2,128,2,4,128]{4,3,2,1,0:T(4,128)(2,1)} reshape(bf16[256,1024]{1,0:T(8,128)(2,1)} %param.17) | data formatting | bytes 1048576 | tf_op jit(solution)/shard_map/reshape | solution.py:109
  54.6 33.6 %collective-permute-done.1 = f32[2,32]{1,0:T(2,128)S(1)} collective-permute-done((f32[2,32]{1,0:T(2,128)S(1)}, f32[2,32]{1,0:T(2,128)S(1)}, u32[]{:S(2)}, u32[]{:S(2)}) %collective-permute-start.1) | collective-permute-done | bytes 288 | tf_op jit(solution)/shard_map/ppermute | solution.py:27
  88.3 3.3 %fusion.53 = (bf16[2,32,64,128]{3,2,1,0:T(8,128)(2,1)S(1)}, f32[2,32,64,128]{3,2,1,0:T(8,128)S(1)}) fusion(f32[2,32]{1,0:T(2,128)S(1)} %collective-permute-done.1, f32[2,32,64,128]{3,2,1,0:T(8,128)S(1)} %get-tuple-element.166, f32[2,32]{1,0:T(2,128)S(1)} %collective-permute-done, bf16[2,32,64,128]{3,2,1,0:T(8,128)(2,1)} %collective-permute-done.4, ...), kind=kLoop, calls=%fused_computation.94 | loop fusion | flops 7864320 | bytes 7341058 | tf_op jit(solution)/shard_map/convert.2
  91.8 1.3 collective-permute-start.7
  93.1 1.3 collective-permute-start.3
  94.4 3.1 %collective-permute-start.2 = (f32[1,32]{1,0:T(1,128)S(1)}, f32[1,32]{1,0:T(1,128)S(1)}, u32[]{:S(2)}, u32[]{:S(2)}) collective-permute-start(f32[1,32]{1,0:T(1,128)S(1)} %get-tuple-element.163), channel_id=1, source_target_pairs={{0,8},{2,10},{4,12},{6,14},{8,0},{10,2},{12,4},{14,6},{1,9},{3,11}... | collective-permute-start | bytes 392 | tf_op jit(solution)/shard_map/ppermute | solution.py:27
  98.4 41.2 %collective-permute-done.3 = f32[1,32]{1,0:T(1,128)S(1)} collective-permute-done((f32[1,32]{1,0:T(1,128)S(1)}, f32[1,32]{1,0:T(1,128)S(1)}, u32[]{:S(2)}, u32[]{:S(2)}) %collective-permute-start.3) | collective-permute-done | bytes 160 | tf_op jit(solution)/shard_map/ppermute | solution.py:27
  139.8 2.3 %add_select_fusion = f32[2,32,64,128]{3,2,1,0:T(8,128)S(1)} fusion(bf16[2,32,64,128]{3,2,1,0:T(8,128)(2,1)} %collective-permute-done.4, bf16[2,32,64,128]{3,2,1,0:T(8,128)(2,1)} %collective-permute-done.5, f32[2,32]{1,0:T(2,128)S(1)} %get-tuple-element.162, f32[2,32]{1,0:T(2,128)S(1)} %get-tuple-element.161, pred[]{:T(512)S(6)} %eq.15, pred[]{:T(512)S(6)} %eq.14, ...), kind=kLoop, calls=%fused_computation.29 | loop fusion | flops 5767168 | bytes 5243395 | tf_op jit(solution)/shard_map/jit(_where)/select_n | solution.py:22
  142.6 1.0 copy-done.1
  143.7 2.5 %fusion.26 = bf16[2,128,32,64]{1,3,2,0:T(8,128)(2,1)} fusion(bf16[2,128,32,64]{1,3,2,0:T(8,128)(2,1)S(1)} %copy.30, f32[2,32,128,64]{2,3,1,0:T(8,128)S(1)} %copy-done.1, bf16[2,128,128,1]{2,1,3,0:T(8,128)(2,1)S(1)} %bitcast.131, f32[1,32,64,128]{3,2,1,0:T(8,128)S(1)} %get-tuple-element.153, f32[1,32,64,128]{3,2,1,0:T(8,128)S(1)} %get-tuple-element.152, ...), kind=kOutput, calls=%fused_computation.44 | convolution fusion | flops 808976384 | bytes 6389888 | tf_op jit(solution)/shard_map/cin,chpn->cihp/dot_general | solution.py:79
  146.1 3.9 %copy.42 = bf16[2,128,32,64]{3,2,1,0:T(8,128)(2,1)S(1)} copy(bf16[2,128,32,64]{1,3,2,0:T(8,128)(2,1)} %fusion.26) | data formatting | bytes 2097152
  150.0 2.5 %reshape.189 = bf16[256,2048]{1,0:T(8,128)(2,1)} reshape(bf16[2,128,32,64]{3,2,1,0:T(8,128)(2,1)S(1)} %copy.42) | data formatting | bytes 2097152
  152.5 1.7 fusion.55
  154.8 23.9 %while.15 = (s32[]{:T(128)}, f32[2,1024]{1,0:T(2,128)S(1)}, f32[2,1024]{1,0:T(2,128)S(1)}, f32[2,1024,128]{2,1,0:T(8,128)}, s32[2]{0:T(128)S(1)}, /*index=5*/bf1...) while((s32[]{:T(128)}, f32[2,1024]{1,0:T(2,128)S(1)}, ...), condition=%wide.region_4.5_spmd.clone, body=%wide.region_1.4_spmd.clone.sunk | while | flops 1102851072 | bytes 47867144 | solution.py:158
  157.8 1.8 fusion.88
  159.7 2.3 %fusion.90 = f32[2,1024]{1,0:T(2,128)S(1)} fusion(f32[2,1024,1024]{2,1,0:T(8,128)S(1)} %get-tuple-element.231, f32[2,1024]{1,0:T(2,128)S(1)} %fusion.89, pred[1024,1024]{0,1:T(8,128)(4,1)S(1)} %broadcast_compare_fusion.2), kind=kLoop, calls=%fused_computation.7.clone.1 | loop fusion | flops 10483712 | bytes 9453568 | tf_op jit(solution)/shard_map/while/body/eval_jaxpr/reduce_sum | solution.py:151
  162.0 3.8 %fusion.92 = f32[2,1024,128]{2,1,0:T(8,128)S(1)} fusion(bf16[1024,2,128]{2,0,1:T(8,128)(2,1)S(1)} %bitcast.121, f32[2,1024,1024]{2,1,0:T(8,128)S(1)} %get-tuple-element.231, f32[2,1024]{1,0:T(2,128)S(1)} %fusion.89, pred[1024,1024]{0,1:T(8,128)(4,1)S(1)} %broadcast_compare_fusion.2, f32[2,1024,128]{2,1,0:T(8,128)S(1)} %copy-done.3, ...), kind=kOutput, calls=%fused_computation.11.clone.1 | convolution fusion | flops 548143104 | bytes 12075009 | tf_op jit(solution)/shard_map/while/body/eval_jaxpr/gqk,kgd->gqd/dot_general | solution.py:152
  165.8 1.0 copy-done.4
  169.7 1.8 fusion.88
  171.6 2.3 %fusion.90 = f32[2,1024]{1,0:T(2,128)S(1)} fusion(f32[2,1024,1024]{2,1,0:T(8,128)S(1)} %get-tuple-element.231, f32[2,1024]{1,0:T(2,128)S(1)} %fusion.89, pred[1024,1024]{0,1:T(8,128)(4,1)S(1)} %broadcast_compare_fusion.2), kind=kLoop, calls=%fused_computation.7.clone.1 | loop fusion | flops 10483712 | bytes 9453568 | tf_op jit(solution)/shard_map/while/body/eval_jaxpr/reduce_sum | solution.py:151
  173.9 3.8 %fusion.92 = f32[2,1024,128]{2,1,0:T(8,128)S(1)} fusion(bf16[1024,2,128]{2,0,1:T(8,128)(2,1)S(1)} %bitcast.121, f32[2,1024,1024]{2,1,0:T(8,128)S(1)} %get-tuple-element.231, f32[2,1024]{1,0:T(2,128)S(1)} %fusion.89, pred[1024,1024]{0,1:T(8,128)(4,1)S(1)} %broadcast_compare_fusion.2, f32[2,1024,128]{2,1,0:T(8,128)S(1)} %copy-done.3, ...), kind=kOutput, calls=%fused_computation.11.clone.1 | convolution fusion | flops 548143104 | bytes 12075009 | tf_op jit(solution)/shard_map/while/body/eval_jaxpr/gqk,kgd->gqd/dot_general | solution.py:152
  177.7 1.0 copy-done.4
  178.7 1.6 divide_convert_fusion
  180.6 1.2 reshape.184
  (90 shorter events, 12.1 us)
Async XLA Ops:
  7.2 8.7 %copy-start = (bf16[256,128]{1,0:T(8,128)(2,1)S(1)}, bf16[256,128]{1,0:T(8,128)(2,1)}, u32[]{:S(2)}) copy-start(bf16[256,128]{1,0:T(8,128)(2,1)} %param.15) | copy-start | bytes 196612
  7.2 145.3 %all-gather.2.cloned.1.call-start = ((), (), s32[]{:S(2)}) async-start(), calls=%async_computation | async-start | bytes 2359296 | tf_op jit(solution)/shard_map/all_gather | solution.py:125
  15.9 2.9 %copy-start.8 = (bf16[256,256]{1,0:T(8,128)(2,1)S(1)}, bf16[256,256]{1,0:T(8,128)(2,1)}, u32[]{:S(2)}) copy-start(bf16[256,256]{1,0:T(8,128)(2,1)} %param.19) | copy-start | bytes 393220
  15.9 2.9 %copy-start.9 = (bf16[256,256]{1,0:T(8,128)(2,1)S(1)}, bf16[256,256]{1,0:T(8,128)(2,1)}, u32[]{:S(2)}) copy-start(bf16[256,256]{1,0:T(8,128)(2,1)} %param.18) | copy-start | bytes 393220
  15.9 3.7 %copy-start.6 = (f32[32,256]{1,0:T(8,128)S(1)}, f32[32,256]{1,0:T(8,128)}, u32[]{:S(2)}) copy-start(f32[32,256]{1,0:T(8,128)} %param.12) | copy-start | bytes 98308
  17.3 27.2 %collective-permute-start.4 = (bf16[2,32,64,128]{3,2,1,0:T(8,128)(2,1)}, bf16[2,32,64,128]{3,2,1,0:T(8,128)(2,1)}, u32[]{:S(2)}, u32[]{:S(2)}) collective-permute-start(bf16[2,32,64,128]{3,2,1,0:T(8,128)(2,1)} %get-tuple-element.165), channel_id=1, source_target_pairs={{0,2},{2,0},{4,6},{6,4},{8,10},{10,8},{12,14},{14,12},{1,3},{3,1},... | collective-permute-start | bytes 3145736 | tf_op jit(solution)/shard_map/ppermute | solution.py:28
  18.5 25.9 %collective-permute-start = (f32[2,32]{1,0:T(2,128)S(1)}, f32[2,32]{1,0:T(2,128)S(1)}, u32[]{:S(2)}, u32[]{:S(2)}) collective-permute-start(f32[2,32]{1,0:T(2,128)S(1)} %exp.35), channel_id=1, source_target_pairs={{0,2},{2,0},{4,6},{6,4},{8,10},{10,8},{12,14},{14,12},{1,3},{3,1},... | collective-permute-start | bytes 776 | tf_op jit(solution)/shard_map/ppermute | solution.py:27
  44.5 3.2 %copy-start.7 = (bf16[256,128]{1,0:T(8,128)(2,1)S(1)}, bf16[256,128]{1,0:T(8,128)(2,1)}, u32[]{:S(2)}) copy-start(bf16[256,128]{1,0:T(8,128)(2,1)} %param.16) | copy-start | bytes 196612
  47.4 40.9 %collective-permute-start.5 = (bf16[2,32,64,128]{3,2,1,0:T(8,128)(2,1)}, bf16[2,32,64,128]{3,2,1,0:T(8,128)(2,1)}, u32[]{:S(2)}, u32[]{:S(2)}) collective-permute-start(bf16[2,32,64,128]{3,2,1,0:T(8,128)(2,1)} %fusion.49), channel_id=1, source_target_pairs={{0,4},{2,6},{4,0},{6,2},{8,12},{10,14},{12,8},{14,10},{1,5},{3,7},... | collective-permute-start | bytes 3145736 | tf_op jit(solution)/shard_map/ppermute | solution.py:28
  51.2 37.1 %collective-permute-start.1 = (f32[2,32]{1,0:T(2,128)S(1)}, f32[2,32]{1,0:T(2,128)S(1)}, u32[]{:S(2)}, u32[]{:S(2)}) collective-permute-start(f32[2,32]{1,0:T(2,128)S(1)} %select_select_fusion.2), channel_id=1, source_target_pairs={{0,4},{2,6},{4,0},{6,2},{8,12},{10,14},{12,8},{14,10},{1,5},{3,7},... | collective-permute-start | bytes 776 | tf_op jit(solution)/shard_map/ppermute | solution.py:27
  91.6 5.9 %copy-start.2 = (bf16[2,128,2,4,128]{4,3,2,1,0:T(4,128)(2,1)S(1)}, bf16[2,128,2,4,128]{4,3,2,1,0:T(4,128)(2,1)}, u32[]{:S(2)}) copy-start(bf16[2,128,2,4,128]{4,3,2,1,0:T(4,128)(2,1)} %reshape.180) | copy-start | bytes 1572868
  91.7 47.9 %collective-permute-start.6 = (bf16[1,32,64,128]{3,2,1,0:T(8,128)(2,1)S(1)}, bf16[1,32,64,128]{3,2,1,0:T(8,128)(2,1)S(1)}, u32[]{:S(2)}, u32[]{:S(2)}) collective-permute-start(bf16[1,32,64,128]{3,2,1,0:T(8,128)(2,1)S(1)} %get-tuple-element.154), channel_id=1, source_target_pairs={{0,8},{2,10},{4,12},{6,14},{8,0},{10,2},{12,4},{14,6},{1,9},{3,11}... | collective-permute-start | bytes 1572872 | tf_op jit(solution)/shard_map/ppermute | solution.py:28
  91.8 47.8 %collective-permute-start.7 = (bf16[1,32,64,128]{3,2,1,0:T(8,128)(2,1)S(1)}, bf16[1,32,64,128]{3,2,1,0:T(8,128)(2,1)S(1)}, u32[]{:S(2)}, u32[]{:S(2)}) collective-permute-start(bf16[1,32,64,128]{3,2,1,0:T(8,128)(2,1)S(1)} %get-tuple-element.155), channel_id=1, source_target_pairs={{0,8},{2,10},{4,12},{6,14},{1,9},{3,11},{5,13},{7,15},{16,24},{18,... | collective-permute-start | bytes 1572872 | tf_op jit(solution)/shard_map/ppermute | solution.py:28
  93.1 46.5 %collective-permute-start.3 = (f32[1,32]{1,0:T(1,128)S(1)}, f32[1,32]{1,0:T(1,128)S(1)}, u32[]{:S(2)}, u32[]{:S(2)}) collective-permute-start(f32[1,32]{1,0:T(1,128)S(1)} %get-tuple-element.164), channel_id=1, source_target_pairs={{0,8},{2,10},{4,12},{6,14},{1,9},{3,11},{5,13},{7,15},{16,24},{18,... | collective-permute-start | bytes 392 | tf_op jit(solution)/shard_map/ppermute | solution.py:27
  94.4 45.2 %collective-permute-start.2 = (f32[1,32]{1,0:T(1,128)S(1)}, f32[1,32]{1,0:T(1,128)S(1)}, u32[]{:S(2)}, u32[]{:S(2)}) collective-permute-start(f32[1,32]{1,0:T(1,128)S(1)} %get-tuple-element.163), channel_id=1, source_target_pairs={{0,8},{2,10},{4,12},{6,14},{8,0},{10,2},{12,4},{14,6},{1,9},{3,11}... | collective-permute-start | bytes 392 | tf_op jit(solution)/shard_map/ppermute | solution.py:27
  142.1 1.6 copy-start.1
  142.1 1.6 copy-start.10
  156.8 1.0 copy-start.5
  159.7 2.3 %copy-start.3 = (f32[2,1024,128]{2,1,0:T(8,128)S(1)}, f32[2,1024,128]{2,1,0:T(8,128)}, u32[]{:S(2)}) copy-start(f32[2,1024,128]{2,1,0:T(8,128)} %get-tuple-element.250) | copy-start | bytes 3145732 | tf_op jit(solution)/shard_map/while
  165.7 1.0 copy-start.4
  168.7 1.0 copy-start.5
  171.6 2.3 %copy-start.3 = (f32[2,1024,128]{2,1,0:T(8,128)S(1)}, f32[2,1024,128]{2,1,0:T(8,128)}, u32[]{:S(2)}) copy-start(f32[2,1024,128]{2,1,0:T(8,128)} %get-tuple-element.250) | copy-start | bytes 3145732 | tf_op jit(solution)/shard_map/while
  177.7 1.0 copy-start.4
Sparse Core Ops, SparseCore 0:
  19.7 64.8 all-gather.1

commit v2 on v1

--- a/solution.py
+++ b/solution.py
@@ -29,7 +29,7 @@
     return (got_decay, got_state)
 
 
-def entering_states(decay, block_state, count, mine):
+def entering_states(decay, block_state, count, mine, inside, inside_args):
     slots = decay.shape[0]
     excl = (jnp.ones_like(decay), jnp.zeros_like(block_state))
     total = (decay, block_state)
@@ -38,13 +38,12 @@
         lower = (mine // span) % 2 == 1
         last = span * 2 >= count
         pairs = [(i, i ^ span) for i in range(count)]
-        if last and slots > 1:
-            head = exchange(jax.tree.map(lambda v: v[:-1], total), "seq", pairs)
-            up_pairs = [(i, i ^ span) for i in range(count) if (i // span) % 2 == 0]
-            tail = exchange(jax.tree.map(lambda v: v[-1:], total), "seq", up_pairs)
-            got = jax.tree.map(lambda a, b: jnp.concatenate([a, b], axis=0), head, tail)
-        else:
-            got = exchange(total, "seq", pairs)
+        if last:
+            total, inside_args = lax.optimization_barrier((total, inside_args))
+        got = exchange(total, "seq", pairs)
+        if last:
+            covered = inside(*inside_args)
+            got, covered = lax.optimization_barrier((got, covered))
         excl = combine_if(lower, got, excl)
         joined_low = combine_if(lower, got, total)
         joined_high = (total[0] * got[0], got[0][..., None, None] * total[1] + got[1])
@@ -58,7 +57,7 @@
     for slot in range(slots):
         entering.append(excl[0][slot][:, None, None] * carry + excl[1][slot])
         carry = total[0][slot][:, None, None] * carry + total[1][slot]
-    return jnp.stack(entering, axis=0)
+    return (jnp.stack(entering, axis=0), covered)
 
 
 def ssd_local(x_blocks, steps, rate, b_blocks, c_blocks):
@@ -85,25 +84,12 @@
     )
 
 
-def local(x_in, step_size, a_log, d_skip, b_in, c_in, queries, key_rows, values):
-    my_index = lax.axis_index("seq")
+def attention(queries, kv_piece, my_index):
     seq_count = lax.axis_size("seq")
-    tok_rows = x_in.shape[0]
+    tok_rows = queries.shape[0]
     slots = tok_rows // BLOCK
-    mamba_local = step_size.shape[0]
-    rate = -jnp.exp(a_log)
-    x_blocks = x_in.reshape(slots, BLOCK, mamba_local, HEADDIM)
-    steps = step_size.reshape(mamba_local, slots, BLOCK).transpose(1, 0, 2)
-    b_blocks = b_in.reshape(slots, BLOCK, STATE)
-    c_blocks = c_in.reshape(slots, BLOCK, STATE)
-    intra, block_state, log_total, cum = ssd_local(x_blocks, steps, rate, b_blocks, c_blocks)
-    decay = jnp.exp(log_total)
-    incoming = entering_states(decay, block_state, seq_count, my_index)
-    mamba_out = ssd_finish(intra, cum, c_blocks, incoming, d_skip, x_blocks).reshape(
-        tok_rows, mamba_local * HEADDIM
-    )
+    kv_local = kv_piece.shape[2] // (2 * HD)
     per_kv = QHEADS // KVHEADS
-    kv_local = key_rows.shape[1] // HD
     score_scale = 1.0 / HD**0.5
     stride = seq_count * BLOCK
     q_flat = queries.reshape(slots, BLOCK, kv_local, per_kv, HD).transpose(2, 0, 3, 1, 4)
@@ -113,8 +99,6 @@
     query_pos = (
         q_slot * stride + my_index * BLOCK + q_row + jnp.zeros((slots, per_kv, BLOCK), jnp.int32)
     ).reshape(-1)
-    k_slots = key_rows.reshape(slots, BLOCK, kv_local * HD)
-    v_slots = values.reshape(slots, BLOCK, kv_local * HD)
     q_total = slots * per_kv * BLOCK
     start_state = (
         jnp.full((kv_local, q_total), NEG, jnp.float32),
@@ -122,7 +106,6 @@
         jnp.zeros((kv_local, q_total, HD), jnp.float32),
     )
     running = start_state
-    kv_piece = lax.all_gather(jnp.concatenate([k_slots, v_slots], axis=2), "seq", axis=1, tiled=True)
     k_piece = kv_piece[..., : kv_local * HD]
     v_piece = kv_piece[..., kv_local * HD :]
     rows = k_piece.shape[1]
@@ -155,13 +138,42 @@
         return ((new_max, new_sum, run_acc * rescale[..., None] + update), None)
 
     numbers = jnp.arange(count)
-    running, unused = lax.scan(per_block, running, (k_blocks, v_blocks, numbers))
+    running, unused = lax.scan(per_block, running, (k_blocks, v_blocks, numbers), unroll=True)
     run_max, run_sum, run_acc = running
     attended = (run_acc / run_sum[..., None]).astype(jnp.bfloat16)
     attn_out = (
         attended.reshape(kv_local, slots, per_kv, BLOCK, HD)
         .transpose(1, 3, 0, 2, 4)
         .reshape(tok_rows, kv_local * per_kv * HD)
+    )
+    return attn_out
+
+
+def local(x_in, step_size, a_log, d_skip, b_in, c_in, queries, key_rows, values):
+    my_index = lax.axis_index("seq")
+    seq_count = lax.axis_size("seq")
+    slots_kv = key_rows.shape[0] // BLOCK
+    width_kv = key_rows.shape[1]
+    kv_cat = jnp.concatenate(
+        [key_rows.reshape(slots_kv, BLOCK, width_kv), values.reshape(slots_kv, BLOCK, width_kv)], axis=2
+    )
+    kv_cat, x_in, step_size = lax.optimization_barrier((kv_cat, x_in, step_size))
+    kv_piece = lax.all_gather(kv_cat, "seq", axis=1, tiled=True)
+    tok_rows = x_in.shape[0]
+    slots = tok_rows // BLOCK
+    mamba_local = step_size.shape[0]
+    rate = -jnp.exp(a_log)
+    x_blocks = x_in.reshape(slots, BLOCK, mamba_local, HEADDIM)
+    steps = step_size.reshape(mamba_local, slots, BLOCK).transpose(1, 0, 2)
+    b_blocks = b_in.reshape(slots, BLOCK, STATE)
+    c_blocks = c_in.reshape(slots, BLOCK, STATE)
+    intra, block_state, log_total, cum = ssd_local(x_blocks, steps, rate, b_blocks, c_blocks)
+    decay = jnp.exp(log_total)
+    incoming, attn_out = entering_states(
+        decay, block_state, seq_count, my_index, attention, (queries, kv_piece, my_index)
+    )
+    mamba_out = ssd_finish(intra, cum, c_blocks, incoming, d_skip, x_blocks).reshape(
+        tok_rows, mamba_local * HEADDIM
     )
     return (mamba_out, attn_out)
 

time: 189 us -> 175 us (0.926)
  the two profiles are of different devices: /device:TPU:29 before, /device:TPU:0 now
where the time goes in v2:
time: 175 us
  waiting for transfers between devices  77.5 us (44%)
  local copies, waits for them, and re-layouts  30.8 us (18%)
  other arithmetic  23.2 us (13%)
  matrix products  19.6 us (11%)
  between operations  15.7 us (9%)
  starting transfers between devices  7.99 us (5%)
    ppermute x3, waiting for transfers between devices, exchange(): got_decay = lax.ppermute(decay, axis, pairs)  54.6 us
    ppermute x3, waiting for transfers between devices, exchange(): lax.ppermute(state.astype(jnp.bfloat16), axis, pairs).astype(jnp.float32)  22.9 us
    dot_general x2, matrix products, per_block(): jnp.einsum('gqk,kgd->gqd', weights.astype(jnp.bfloat16), v_flat, preferre...  8.55 us
    ppermute x3, starting transfers between devices, exchange(): lax.ppermute(state.astype(jnp.bfloat16), axis, pairs).astype(jnp.float32)  7.42 us
    unnamed x28, local copies, waits for them, and re-layouts  7.41 us
    slice x7, local copies, waits for them, and re-layouts, attention(): lax.scan(per_block, running, (k_blocks, v_blocks, numbers), unroll=True)  6.9 us
    reshape x2, local copies, waits for them, and re-layouts, local(): x_blocks = x_in.reshape(slots, BLOCK, mamba_local, HEADDIM)  5.55 us
    select_n x1, other arithmetic, entering_states(): jnp.where(lower, joined_low[1], joined_high[1])  4.84 us
  transfers between devices with their start and end apart: 7, of which 3 were waited for; matrix products, arithmetic and copies ran while one was open for 25% of the time, Pallas kernels for 0%

profile of v2, /device:TPU:0, one launch (start us, length us, event | category | flops | bytes accessed | tf_op | source)
XLA Modules:
  0.0 174.8 jit_solution(11486839142064670101)
XLA Ops:
  7.2 1.7 pad_maximum_fusion
  11.2 3.3 %reshape.254 = bf16[2,128,32,64]{3,2,1,0:T(8,128)(2,1)S(1)} reshape(bf16[256,2048]{1,0:T(8,128)(2,1)} %param.9) | data formatting | bytes 2097152 | tf_op jit(solution)/shard_map/reshape | solution.py:166
  14.5 2.2 %copy.33 = bf16[2,128,32,64]{1,3,2,0:T(8,128)(2,1)S(1)} copy(bf16[2,128,32,64]{3,2,1,0:T(8,128)(2,1)S(1)} %reshape.254) | data formatting | bytes 2097152 | tf_op jit(solution)/shard_map/reshape | solution.py:166
  16.9 1.4 fusion.67
  18.3 2.9 %collective-permute-start.2 = (bf16[2,32,64,128]{3,2,1,0:T(8,128)(2,1)}, bf16[2,32,64,128]{3,2,1,0:T(8,128)(2,1)}, u32[]{:S(2)}, u32[]{:S(2)}) collective-permute-start(bf16[2,32,64,128]{3,2,1,0:T(8,128)(2,1)} %get-tuple-element.51), channel_id=1, source_target_pairs={{0,2},{2,0},{4,6},{6,4},{8,10},{10,8},{12,14},{14,12},{1,3},{3,1},... | collective-permute-start | bytes 3145736 | tf_op jit(solution)/shard_map/ppermute | solution.py:28
  23.3 28.1 %collective-permute-done = f32[2,32]{1,0:T(2,128)S(1)} collective-permute-done((f32[2,32]{1,0:T(2,128)S(1)}, f32[2,32]{1,0:T(2,128)S(1)}, u32[]{:S(2)}, u32[]{:S(2)}) %collective-permute-start) | collective-permute-done | bytes 288 | tf_op jit(solution)/shard_map/ppermute | solution.py:27
  51.4 2.9 %fusion.49 = bf16[2,32,64,128]{3,2,1,0:T(8,128)(2,1)} fusion(f32[2,32,64,128]{3,2,1,0:T(8,128)S(1)} %get-tuple-element.52, f32[2,32]{1,0:T(2,128)S(1)} %collective-permute-done, bf16[2,32,64,128]{3,2,1,0:T(8,128)(2,1)} %collective-permute-done.2, f32[2,32]{1,0:T(2,128)S(1)} %exp.55, pred[]{:T(512)S(6)} %eq.15), kind=kLoop, calls=%fused_computation.59 | loop fusion | flops 4194304 | bytes 4194817 | tf_op jit(solution)/shard_map/convert_element_type | solution.py:28
  54.3 2.1 %collective-permute-start.3 = (bf16[2,32,64,128]{3,2,1,0:T(8,128)(2,1)}, bf16[2,32,64,128]{3,2,1,0:T(8,128)(2,1)}, u32[]{:S(2)}, u32[]{:S(2)}) collective-permute-start(bf16[2,32,64,128]{3,2,1,0:T(8,128)(2,1)} %fusion.49), channel_id=1, source_target_pairs={{0,4},{2,6},{4,0},{6,2},{8,12},{10,14},{12,8},{14,10},{1,5},{3,7},... | collective-permute-start | bytes 3145736 | tf_op jit(solution)/shard_map/ppermute | solution.py:28
  56.6 3.3 %fusion.12 = f32[2,32,64,128]{3,2,1,0:T(8,128)} fusion(bf16[2,128,32,64]{1,3,2,0:T(8,128)(2,1)S(1)} %copy.33, f32[2,32,128]{2,1,0:T(8,128)S(1)} %bitcast_bitcast_fusion.1, f32[2,32,128]{2,1,0:T(8,128)S(1)} %reduce_window_sum.11, f32[2,128,128]{2,1,0:T(8,128)S(1)} %fusion.68, pred[128,128]{1,0:T(8,128)(4,1)S(1)} %iota_compare_fusion), kind=kOutput, calls=%fused_computation.27 | convolution fusion | flops 139460608 | bytes 3358720 | tf_op jit(solution)/shard_map/chij,cjhp->cihp/dot_general | solution.py:69
  59.9 26.5 %collective-permute-done.1 = f32[2,32]{1,0:T(2,128)S(1)} collective-permute-done((f32[2,32]{1,0:T(2,128)S(1)}, f32[2,32]{1,0:T(2,128)S(1)}, u32[]{:S(2)}, u32[]{:S(2)}) %collective-permute-start.1) | collective-permute-done | bytes 288 | tf_op jit(solution)/shard_map/ppermute | solution.py:27
  86.5 4.8 %fusion.17 = f32[2,32,64,128]{3,2,1,0:T(8,128)} fusion(bf16[2,32,64,128]{3,2,1,0:T(8,128)(2,1)} %collective-permute-done.3, f32[2,32]{1,0:T(2,128)S(1)} %collective-permute-done.1, f32[2,32]{1,0:T(2,128)S(1)} %select_select_fusion.2, pred[]{:T(512)S(6)} %eq.14, f32[2,32,64,128]{3,2,1,0:T(8,128)S(1)} %get-tuple-element.52, ...), kind=kLoop, calls=%fused_computation.32 | loop fusion | flops 7340032 | bytes 6292482 | tf_op jit(solution)/shard_map/jit(_where)/select_n | solution.py:52
  91.3 2.6 %fusion.63 = (bf16[2,1024,256]{2,1,0:T(8,128)(2,1)}, bf16[2,1024,256]{2,1,0:T(8,128)(2,1)S(1)}) fusion(bf16[2,1024,512]{2,1,0:T(8,128)(2,1)} %all-gather.2.cloned.1.call-done), kind=kLoop, calls=%fused_computation.98 | loop fusion | bytes 4194304 | tf_op jit(solution)/shard_map/slice | solution.py:109
  94.0 1.3 reshape.246
  95.3 1.5 fusion.65
  97.8 1.4 reshape.244
  102.1 2.1 %fusion.64 = (bf16[1,2,512,2,128]{4,3,2,0,1:T(2,128)(2,1)S(1)}, bf16[1,2,512,2,128]{4,3,2,0,1:T(2,128)(2,1)S(1)}) fusion(bf16[2,2,512,2,128]{4,3,2,0,1:T(2,128)(2,1)} %bitcast.88), kind=kLoop, calls=%fused_computation.99 | loop fusion | bytes 2097152 | tf_op jit(solution)/shard_map/slice | solution.py:141
  105.0 1.2 convert_element_type.48
  106.2 2.4 %collective-permute-start.5 = (bf16[2,32,64,128]{3,2,1,0:T(8,128)(2,1)}, bf16[2,32,64,128]{3,2,1,0:T(8,128)(2,1)}, u32[]{:S(2)}, u32[]{:S(2)}) collective-permute-start(bf16[2,32,64,128]{3,2,1,0:T(8,128)(2,1)} %convert_element_type.48), channel_id=1, source_target_pairs={{0,8},{2,10},{4,12},{6,14},{8,0},{10,2},{12,4},{14,6},{1,9},{3,11}... | collective-permute-start | bytes 3145736 | tf_op jit(solution)/shard_map/ppermute | solution.py:28
  109.1 1.5 broadcast_compare_fusion.1
  110.6 1.8 %fusion = (f32[2,1024]{1,0:T(2,128)S(1)}, f32[2,1024,1024]{1,2,0:T(8,128)S(1)}) fusion(pred[1024,1024]{0,1:T(8,128)(4,1)S(1)} %get-tuple-element.44, bf16[2,1024,128]{2,1,0:T(8,128)(2,1)S(1)} %bitcast.91, bf16[1024,2,128]{2,0,1:T(8,128)(2,1)S(1)} %bitcast.90), kind=kOutput, calls=%fused_computation.4 | convolution fusion | flops 543160320 | bytes 10493952 | tf_op jit(solution)/shard_map/eval_jaxpr/gqd,kgd->gqk/dot_general | solution.py:127
  112.5 1.8 %fusion.1 = (f32[2,1024]{1,0:T(2,128)S(1)}, f32[2,1024,1024]{1,2,0:T(8,128)S(1)}) fusion(pred[1024,1024]{0,1:T(8,128)(4,1)S(1)} %get-tuple-element.45, bf16[2,1024,128]{2,1,0:T(8,128)(2,1)S(1)} %bitcast.92, bf16[1024,2,128]{2,0,1:T(8,128)(2,1)S(1)} %bitcast.93), kind=kOutput, calls=%fused_computation.5 | convolution fusion | flops 543160320 | bytes 10493952 | tf_op jit(solution)/shard_map/eval_jaxpr/gqd,kgd->gqk/dot_general | solution.py:127
  114.4 4.3 %fusion.6 = f32[2,1024,128]{2,1,0:T(8,128)} fusion(bf16[1024,2,128]{2,0,1:T(8,128)(2,1)S(1)} %bitcast.94, f32[2,1024,1024]{1,2,0:T(8,128)S(1)} %get-tuple-element.56, f32[2,1024]{1,0:T(2,128)S(1)} %get-tuple-element.42, pred[1024,1024]{0,1:T(8,128)(4,1)S(1)} %get-tuple-element.45), kind=kOutput, calls=%fused_computation.11 | convolution fusion | flops 547356672 | bytes 11018240 | tf_op jit(solution)/shard_map/eval_jaxpr/gqk,kgd->gqd/dot_general | solution.py:135
  118.6 4.4 %fusion.2 = (f32[2,1024]{1,0:T(2,128)S(1)}, f32[2,1024]{1,0:T(2,128)S(1)}) fusion(f32[2,1024,1024]{1,2,0:T(8,128)S(1)} %get-tuple-element.54, f32[2,1024]{1,0:T(2,128)S(1)} %get-tuple-element.43, pred[1024,1024]{0,1:T(8,128)(4,1)S(1)} %get-tuple-element.44, f32[2,1024]{1,0:T(2,128)S(1)} %get-tuple-element.42, f32[2,1024,1024]{1,2,0:T(8,128)S(1)} %get-tuple-element.56, ...), kind=kLoop, calls=%fused_computation.6 | loop fusion | flops 20967424 | bytes 18907136 | tf_op jit(solution)/shard_map/eval_jaxpr/reduce_sum | solution.py:134
  123.2 4.3 %divide_convert_fusion = bf16[2,1024,128]{2,1,0:T(8,128)(2,1)S(1)} fusion(f32[2,1024,128]{2,1,0:T(8,128)S(1)} %copy-done.11, bf16[1024,2,128]{2,0,1:T(8,128)(2,1)S(1)} %bitcast.95, f32[2,1024,1024]{1,2,0:T(8,128)S(1)} %get-tuple-element.54, f32[2,1024]{1,0:T(2,128)S(1)} %get-tuple-element.43, pred[1024,1024]{0,1:T(8,128)(4,1)S(1)} %get-tuple-element.44, ...), kind=kOutput, calls=%fused_computation.57 | convolution fusion | flops 548667392 | bytes 11567104 | tf_op jit(solution)/shard_map/eval_jaxpr/gqk,kgd->gqd/dot_general | solution.py:135
  127.5 1.2 copy.43
  128.7 2.2 %reshape.249 = bf16[256,1024]{1,0:T(8,128)(2,1)} reshape(bf16[2,128,2,4,128]{4,3,2,1,0:T(4,128)(2,1)} %copy.43) | data formatting | bytes 1048576 | tf_op jit(solution)/shard_map/reshape | solution.py:147
  130.9 22.9 %collective-permute-done.5 = bf16[2,32,64,128]{3,2,1,0:T(8,128)(2,1)} collective-permute-done((bf16[2,32,64,128]{3,2,1,0:T(8,128)(2,1)}, bf16[2,32,64,128]{3,2,1,0:T(8,128)(2,1)}, u32[]{:S(2)}, u32[]{:S(2)}) %collective-permute-start.5) | collective-permute-done | bytes 1048608 | tf_op jit(solution)/shard_map/ppermute | solution.py:28
  153.7 1.5 convert_element_type.49
  155.3 2.2 %add_select_fusion = f32[2,32,64,128]{3,2,1,0:T(8,128)S(1)} fusion(bf16[2,32,64,128]{3,2,1,0:T(8,128)(2,1)} %collective-permute-done.2, bf16[2,32,64,128]{3,2,1,0:T(8,128)(2,1)} %collective-permute-done.3, f32[2,32,64,128]{3,2,1,0:T(8,128)S(1)} %convert_element_type.49, f32[2,32]{1,0:T(2,128)S(1)} %get-tuple-element.30, f32[2,32]{1,0:T(2,128)S(1)} %get-tuple-element.29, ...), kind=kLoop, calls=%fused_computation.15 | loop fusion | flops 4718592 | bytes 6291971 | tf_op jit(solution)/shard_map/jit(_where)/select_n | solution.py:22
  159.1 2.5 %fusion.15 = bf16[2,128,32,64]{1,3,2,0:T(8,128)(2,1)} fusion(bf16[2,128,32,64]{1,3,2,0:T(8,128)(2,1)S(1)} %copy.33, f32[2,32,64,128]{3,2,1,0:T(8,128)S(1)} %copy-done.2, bf16[2,128,128,1]{2,1,3,0:T(8,128)(2,1)S(1)} %bitcast.98, f32[1,32,64,128]{3,2,1,0:T(8,128)S(1)} %get-tuple-element.34, f32[1,32,64,128]{3,2,1,0:T(8,128)S(1)} %get-tuple-element.33, ...), kind=kOutput, calls=%fused_computation.30 | convolution fusion | flops 808976384 | bytes 6389888 | tf_op jit(solution)/shard_map/cin,chpn->cihp/dot_general | solution.py:78
  161.6 3.9 %copy.50 = bf16[2,128,32,64]{3,2,1,0:T(8,128)(2,1)S(1)} copy(bf16[2,128,32,64]{1,3,2,0:T(8,128)(2,1)} %fusion.15) | data formatting | bytes 2097152
  165.5 2.4 %reshape.253 = bf16[256,2048]{1,0:T(8,128)(2,1)} reshape(bf16[2,128,32,64]{3,2,1,0:T(8,128)(2,1)S(1)} %copy.50) | data formatting | bytes 2097152
  (70 shorter events, 10.3 us)
Async XLA Ops:
  7.2 9.7 %copy-start = (bf16[256,128]{1,0:T(8,128)(2,1)S(1)}, bf16[256,128]{1,0:T(8,128)(2,1)}, u32[]{:S(2)}) copy-start(bf16[256,128]{1,0:T(8,128)(2,1)} %param.13) | copy-start | bytes 196612
  7.2 84.1 %all-gather.2.cloned.1.call-start = ((), (), s32[]{:S(2)}) async-start(), calls=%async_computation | async-start | bytes 2359296 | tf_op jit(solution)/shard_map/all_gather | solution.py:161
  14.5 2.2 %copy-start.8 = (f32[32,256]{1,0:T(8,128)S(1)}, f32[32,256]{1,0:T(8,128)}, u32[]{:S(2)}) copy-start(f32[32,256]{1,0:T(8,128)} %param.10) | copy-start | bytes 98308
  18.3 33.1 %collective-permute-start.2 = (bf16[2,32,64,128]{3,2,1,0:T(8,128)(2,1)}, bf16[2,32,64,128]{3,2,1,0:T(8,128)(2,1)}, u32[]{:S(2)}, u32[]{:S(2)}) collective-permute-start(bf16[2,32,64,128]{3,2,1,0:T(8,128)(2,1)} %get-tuple-element.51), channel_id=1, source_target_pairs={{0,2},{2,0},{4,6},{6,4},{8,10},{10,8},{12,14},{14,12},{1,3},{3,1},... | collective-permute-start | bytes 3145736 | tf_op jit(solution)/shard_map/ppermute | solution.py:28
  21.2 30.2 %collective-permute-start = (f32[2,32]{1,0:T(2,128)S(1)}, f32[2,32]{1,0:T(2,128)S(1)}, u32[]{:S(2)}, u32[]{:S(2)}) collective-permute-start(f32[2,32]{1,0:T(2,128)S(1)} %exp.55), channel_id=1, source_target_pairs={{0,2},{2,0},{4,6},{6,4},{8,10},{10,8},{12,14},{14,12},{1,3},{3,1},... | collective-permute-start | bytes 776 | tf_op jit(solution)/shard_map/ppermute | solution.py:27
  51.4 5.0 %copy-start.9 = (bf16[256,128]{1,0:T(8,128)(2,1)S(1)}, bf16[256,128]{1,0:T(8,128)(2,1)}, u32[]{:S(2)}) copy-start(bf16[256,128]{1,0:T(8,128)(2,1)} %param.14) | copy-start | bytes 196612
  54.3 32.2 %collective-permute-start.3 = (bf16[2,32,64,128]{3,2,1,0:T(8,128)(2,1)}, bf16[2,32,64,128]{3,2,1,0:T(8,128)(2,1)}, u32[]{:S(2)}, u32[]{:S(2)}) collective-permute-start(bf16[2,32,64,128]{3,2,1,0:T(8,128)(2,1)} %fusion.49), channel_id=1, source_target_pairs={{0,4},{2,6},{4,0},{6,2},{8,12},{10,14},{12,8},{14,10},{1,5},{3,7},... | collective-permute-start | bytes 3145736 | tf_op jit(solution)/shard_map/ppermute | solution.py:28
  59.9 26.6 %collective-permute-start.1 = (f32[2,32]{1,0:T(2,128)S(1)}, f32[2,32]{1,0:T(2,128)S(1)}, u32[]{:S(2)}, u32[]{:S(2)}) collective-permute-start(f32[2,32]{1,0:T(2,128)S(1)} %select_select_fusion.2), channel_id=1, source_target_pairs={{0,4},{2,6},{4,0},{6,2},{8,12},{10,14},{12,8},{14,10},{1,5},{3,7},... | collective-permute-start | bytes 776 | tf_op jit(solution)/shard_map/ppermute | solution.py:27
  96.8 3.3 %copy-start.3 = (bf16[1,2,512,2,128]{4,3,2,0,1:T(2,128)(2,1)S(1)}, bf16[1,2,512,2,128]{4,3,2,0,1:T(2,128)(2,1)}, u32[]{:S(2)}) copy-start(bf16[1,2,512,2,128]{4,3,2,0,1:T(2,128)(2,1)} %get-tuple-element.40) | copy-start | bytes 1572868
  102.1 2.9 %copy-start.1 = (f32[2,32,64,128]{3,2,1,0:T(8,128)S(1)}, f32[2,32,64,128]{3,2,1,0:T(8,128)}, u32[]{:S(2)}) copy-start(f32[2,32,64,128]{3,2,1,0:T(8,128)} %fusion.17) | copy-start | bytes 6291460
  105.0 5.6 %copy-start.4 = (bf16[1,2,512,2,128]{4,2,1,3,0:T(8,128)(2,1)S(1)}, bf16[1,2,512,2,128]{4,2,1,3,0:T(8,128)(2,1)}, u32[]{:S(2)}) copy-start(bf16[1,2,512,2,128]{4,2,1,3,0:T(8,128)(2,1)} %copy.37) | copy-start | bytes 1572868
  105.0 5.6 %copy-start.5 = (bf16[2,2,4,128,128]{4,3,2,1,0:T(8,128)(2,1)S(1)}, bf16[2,2,4,128,128]{4,3,2,1,0:T(8,128)(2,1)}, u32[]{:S(2)}) copy-start(bf16[2,2,4,128,128]{4,3,2,1,0:T(8,128)(2,1)} %copy.36) | copy-start | bytes 1572868
  106.2 47.5 %collective-permute-start.5 = (bf16[2,32,64,128]{3,2,1,0:T(8,128)(2,1)}, bf16[2,32,64,128]{3,2,1,0:T(8,128)(2,1)}, u32[]{:S(2)}, u32[]{:S(2)}) collective-permute-start(bf16[2,32,64,128]{3,2,1,0:T(8,128)(2,1)} %convert_element_type.48), channel_id=1, source_target_pairs={{0,8},{2,10},{4,12},{6,14},{8,0},{10,2},{12,4},{14,6},{1,9},{3,11}... | collective-permute-start | bytes 3145736 | tf_op jit(solution)/shard_map/ppermute | solution.py:28
  108.6 46.6 %collective-permute-start.4 = (f32[2,32]{1,0:T(2,128)S(1)}, f32[2,32]{1,0:T(2,128)S(1)}, u32[]{:S(2)}, u32[]{:S(2)}) collective-permute-start(f32[2,32]{1,0:T(2,128)S(1)} %select_select_fusion.1), channel_id=1, source_target_pairs={{0,8},{2,10},{4,12},{6,14},{8,0},{10,2},{12,4},{14,6},{1,9},{3,11}... | collective-permute-start | bytes 776 | tf_op jit(solution)/shard_map/ppermute | solution.py:27
  110.6 1.8 %copy-start.6 = (bf16[1,2,512,2,128]{4,2,1,3,0:T(8,128)(2,1)S(1)}, bf16[1,2,512,2,128]{4,2,1,3,0:T(8,128)(2,1)}, u32[]{:S(2)}) copy-start(bf16[1,2,512,2,128]{4,2,1,3,0:T(8,128)(2,1)} %copy.40) | copy-start | bytes 1572868
  112.5 1.9 %copy-start.7 = (bf16[1,2,512,2,128]{4,2,1,3,0:T(8,128)(2,1)S(1)}, bf16[1,2,512,2,128]{4,2,1,3,0:T(8,128)(2,1)}, u32[]{:S(2)}) copy-start(bf16[1,2,512,2,128]{4,2,1,3,0:T(8,128)(2,1)} %copy.41) | copy-start | bytes 1572868
  118.6 4.6 %copy-start.11 = (f32[2,1024,128]{2,1,0:T(8,128)S(1)}, f32[2,1024,128]{2,1,0:T(8,128)}, u32[]{:S(2)}) copy-start(f32[2,1024,128]{2,1,0:T(8,128)} %fusion.6) | copy-start | bytes 3145732
  157.5 1.6 copy-start.2
  157.5 1.6 copy-start.10
Sparse Core Ops, SparseCore 0:
  10.8 60.1 all-gather.1

commit v3 on v2

v3 whole, which is shorter than its diff:
```python
import jax
import jax.numpy as jnp
from jax import lax
from jax.experimental import pallas as pl
from jax.experimental.pallas import tpu as pltpu
from jax.sharding import PartitionSpec as P

BLOCK = 128
HEADDIM = 64
STATE = 128
QHEADS = 16
KVHEADS = 4
HD = 128


NEG = -1e30


def spread(a):
    return jnp.repeat(a, HEADDIM, axis=-1)


def combine_if(lower, earlier, later):
    a_e, s_e = earlier
    a_l, s_l = later
    joined_a = a_e * a_l
    joined_s = spread(a_l)[:, None, :] * s_e + s_l
    return (jnp.where(lower, joined_a, a_l), jnp.where(lower, joined_s, s_l))


def exchange(value, axis, pairs):
    decay, state = value
    spread_decay = spread(decay)[:, None, :]
    high = spread_decay.astype(jnp.bfloat16)
    low = (spread_decay - high.astype(jnp.float32)).astype(jnp.bfloat16)
    pad = jnp.zeros((state.shape[0], 6, state.shape[2]), jnp.bfloat16)
    sent = jnp.concatenate([state.astype(jnp.bfloat16), high, low, pad], axis=1)
    got = lax.ppermute(sent, axis, pairs)
    rows = state.shape[1]
    got_decay = got[:, rows, ::HEADDIM].astype(jnp.float32) + got[:, rows + 1, ::HEADDIM].astype(jnp.float32)
    return (got_decay, got[:, :rows].astype(jnp.float32))


def entering_states(decay, block_state, count, mine, hooks):
    slots = decay.shape[0]
    excl = (jnp.ones_like(decay), jnp.zeros_like(block_state))
    total = (decay, block_state)
    results = {}
    span, step = 1, 0
    while span < count:
        lower = (mine // span) % 2 == 1
        pairs = [(i, i ^ span) for i in range(count)]
        hook = hooks.get(step if span * 2 < count else -1)
        if hook is not None:
            total, args = lax.optimization_barrier((total, hook[1]))
        got = exchange(total, "seq", pairs)
        if hook is not None:
            done = hook[0](*args)
            got, done = lax.optimization_barrier((got, done))
            results[hook[0].__name__] = done
        excl = combine_if(lower, got, excl)
        joined_low = combine_if(lower, got, total)
        joined_high = (total[0] * got[0], spread(got[0])[:, None, :] * total[1] + got[1])
        total = (
            jnp.where(lower, joined_low[0], joined_high[0]),
            jnp.where(lower, joined_low[1], joined_high[1]),
        )
        span, step = span * 2, step + 1
    carry = jnp.zeros_like(block_state[0])
    entering = []
    for slot in range(slots):
        entering.append(spread(excl[0][slot])[None, :] * carry + excl[1][slot])
        carry = spread(total[0][slot])[None, :] * carry + total[1][slot]
    return (jnp.stack(entering, axis=0), results)


def mamba_base(x_in, steps, cum, b_blocks, c_blocks, d_skip):
    slots, heads = steps.shape[:2]
    x_blocks = x_in.reshape(slots, BLOCK, heads, HEADDIM)
    causal = jnp.arange(BLOCK)[:, None] >= jnp.arange(BLOCK)[None, :]
    log_gap = jnp.where(causal, cum[:, :, :, None] - cum[:, :, None, :], -jnp.inf)
    inner = jnp.einsum("cin,cjn->cij", c_blocks, b_blocks, preferred_element_type=jnp.float32)
    mixing = (inner[:, None] * jnp.exp(log_gap) * steps[:, :, None, :]).astype(jnp.bfloat16)
    intra = jnp.einsum("chij,cjhp->cihp", mixing, x_blocks, preferred_element_type=jnp.float32)
    base = intra + d_skip[None, None, :, None] * x_blocks.astype(jnp.float32)
    return base.reshape(slots, BLOCK, heads * HEADDIM)


KEY_CHUNK = 256


def attention_prep(queries, kv_piece, my_index):
    tok_rows = queries.shape[0]
    slots = tok_rows // BLOCK
    kv_local = kv_piece.shape[2] // (2 * HD)
    per_kv = QHEADS // KVHEADS
    q_flat = queries.reshape(slots, BLOCK, kv_local, per_kv, HD).transpose(2, 0, 3, 1, 4)
    q_flat = q_flat.reshape(kv_local, slots * per_kv * BLOCK, HD)
    rows = kv_piece.shape[0] * kv_piece.shape[1]
    k_all = kv_piece[..., : kv_local * HD].reshape(rows, kv_local, HD).transpose(1, 0, 2)
    v_all = kv_piece[..., kv_local * HD :].reshape(rows, kv_local, HD).transpose(1, 0, 2)
    return (q_flat, k_all, v_all)


def attention_kernel(q_ref, k_ref, v_ref, o_ref):
    seq_count = lax.axis_size("seq")
    me = lax.axis_index("seq")
    slot = pl.program_id(1)
    rows = q_ref.shape[1]
    first = (slot * seq_count + me) * BLOCK
    chunks = (first + BLOCK + KEY_CHUNK - 1) // KEY_CHUNK
    q = q_ref[0]
    query_pos = first + lax.broadcasted_iota(jnp.int32, (rows, KEY_CHUNK), 0) % BLOCK
    key_col = lax.broadcasted_iota(jnp.int32, (rows, KEY_CHUNK), 1)
    score_scale = 1.0 / HD**0.5

    def scores(c):
        start = pl.multiple_of(c * KEY_CHUNK, KEY_CHUNK)
        k = k_ref[0, pl.ds(start, KEY_CHUNK), :]
        s = lax.dot_general(q, k, (((1,), (1,)), ((), ())), preferred_element_type=jnp.float32)
        visible = start + key_col <= query_pos
        return s * score_scale, visible, start

    def top_of(c, top):
        s, visible, unused = scores(c)
        return jnp.maximum(top, jnp.max(jnp.where(visible, s, NEG), axis=1, keepdims=True))

    top = lax.fori_loop(0, chunks, top_of, jnp.full((rows, 1), NEG, jnp.float32))

    def add_of(c, carry):
        total, acc = carry
        s, visible, start = scores(c)
        probs = jnp.where(visible, jnp.exp(s - top), 0.0)
        v = v_ref[0, pl.ds(start, KEY_CHUNK), :]
        acc = acc + jnp.dot(probs.astype(jnp.bfloat16), v, preferred_element_type=jnp.float32)
        return (total + jnp.sum(probs, axis=1, keepdims=True), acc)

    start_carry = (jnp.zeros((rows, 1), jnp.float32), jnp.zeros((rows, HD), jnp.float32))
    total, acc = lax.fori_loop(0, chunks, add_of, start_carry)
    o_ref[0] = (acc / total).astype(o_ref.dtype)


def attention_core(q_flat, k_all, v_all):
    groups, q_total, unused = q_flat.shape
    keys = k_all.shape[1]
    slots = q_total // ((QHEADS // KVHEADS) * BLOCK)
    block_q = q_total // slots
    cost = pl.CostEstimate(
        flops=4 * groups * q_total * keys * HD,
        transcendentals=groups * q_total * keys,
        bytes_accessed=2 * (2 * q_flat.size + k_all.size + v_all.size),
    )
    attended = pl.pallas_call(
        attention_kernel,
        out_shape=jax.ShapeDtypeStruct(q_flat.shape, jnp.bfloat16),
        grid=(groups, slots),
        in_specs=[
            pl.BlockSpec((1, block_q, HD), lambda g, s: (g, s, 0)),
            pl.BlockSpec((1, keys, HD), lambda g, s: (g, 0, 0)),
            pl.BlockSpec((1, keys, HD), lambda g, s: (g, 0, 0)),
        ],
        out_specs=pl.BlockSpec((1, block_q, HD), lambda g, s: (g, s, 0)),
        cost_estimate=cost,
    )(q_flat, k_all, v_all)
    per_kv = QHEADS // KVHEADS
    return (
        attended.reshape(groups, slots, per_kv, BLOCK, HD)
        .transpose(1, 3, 0, 2, 4)
        .reshape(slots * BLOCK, groups * per_kv * HD)
    )


def local(x_in, step_size, a_log, d_skip, b_in, c_in, queries, key_rows, values):
    my_index = lax.axis_index("seq")
    seq_count = lax.axis_size("seq")
    tok_rows, width = x_in.shape
    slots = tok_rows // BLOCK
    heads = step_size.shape[0]
    kv_cat = jnp.concatenate(
        [key_rows.reshape(slots, BLOCK, -1), values.reshape(slots, BLOCK, -1)], axis=2
    )
    kv_cat, x_in, step_size = lax.optimization_barrier((kv_cat, x_in, step_size))
    kv_piece = lax.all_gather(kv_cat, "seq", axis=1, tiled=True)
    rate = -jnp.exp(a_log)
    steps = step_size.reshape(heads, slots, BLOCK).transpose(1, 0, 2)
    cum = jnp.cumsum(steps * rate[None, :, None], axis=2)
    log_total = cum[:, :, -1]
    factor = (jnp.exp(log_total[:, :, None] - cum) * steps).transpose(0, 2, 1)
    x3 = x_in.reshape(slots, BLOCK, width)
    scaled = (spread(factor) * x3.astype(jnp.float32)).astype(jnp.bfloat16)
    b_blocks = b_in.reshape(slots, BLOCK, STATE)
    c_blocks = c_in.reshape(slots, BLOCK, STATE)
    block_state = jnp.einsum("ctn,ctk->cnk", b_blocks, scaled, preferred_element_type=jnp.float32)
    decay = jnp.exp(log_total)
    prepared = attention_prep(queries, kv_piece, my_index)
    hooks = {
        0: (mamba_base, (x_in, steps, cum, b_blocks, c_blocks, d_skip)),
        -1: (attention_core, prepared),
    }
    incoming, results = entering_states(decay, block_state, seq_count, my_index, hooks)
    carried = jnp.einsum(
        "ctn,cnk->ctk", c_blocks.astype(jnp.float32), incoming, precision=lax.Precision.HIGHEST
    )
    carried = carried * spread(jnp.exp(cum).transpose(0, 2, 1))
    mamba_out = (results["mamba_base"] + carried).astype(jnp.bfloat16).reshape(tok_rows, width)
    return (mamba_out, results["attention_core"])


def solution(mesh):
    in_specs = (
        P(("group", "seq"), "head"),
        P("head", ("group", "seq")),
        P("head"),
        P("head"),
        P(("group", "seq"), None),
        P(("group", "seq"), None),
        P(("group", "seq"), "head"),
        P(("group", "seq"), "head"),
        P(("group", "seq"), "head"),
    )
    out_specs = (P(("group", "seq"), "head"), P(("group", "seq"), "head"))
    return jax.shard_map(local, mesh=mesh, in_specs=in_specs, out_specs=out_specs, check_vma=False)
```

time: 175 us -> 205 us (1.17)
  local copies, waits for them, and re-layouts: 30.8 us -> 63.2 us
  matrix products: 19.6 us -> 6.42 us
  Pallas kernels: 0 us -> 12 us
  waiting for transfers between devices: 77.5 us -> 72 us
  other arithmetic: 23.2 us -> 28.6 us
    dot_general x8 -> x4, matrix products: 19.6 us -> 6.42 us  [the longest x1 3.35 us: mamba_base(): jnp.einsum('chij,cjhp->cihp', mixing, x_blocks, preferred_element_type=jn...]
    pallas_call x0 -> x1, Pallas kernels: none -> 12 us  [attention_core(): pl.pallas_call(attention_kernel, out_shape=jax.ShapeDtypeStruct(q_flat.sh...]
    concatenate x0 -> x4, local copies, waits for them, and re-layouts: none -> 9.94 us  [exchange(): sent = jnp.concatenate([state.astype(jnp.bfloat16), high, low, pad], axis=1)]
    convert_element_type x0 -> x7, local copies, waits for them, and re-layouts: none -> 8.03 us  [the longest x3 4.15 us: exchange(): low = (spread_decay - high.astype(jnp.float32)).astype(jnp.bfloat16)]
    ppermute x6 -> x3, waiting for transfers between devices: 77.5 us -> 72 us  [exchange(): got = lax.ppermute(sent, axis, pairs)]
    concatenate x1 -> x4, other arithmetic: 1.69 us -> 6.69 us  [the longest x3 5 us: exchange(): sent = jnp.concatenate([state.astype(jnp.bfloat16), high, low, pad], axis=1)]
    slice x11 -> x14, local copies, waits for them, and re-layouts: 9.7 us -> 14.5 us  [the longest x3 5.91 us: exchange(): return (got_decay, got[:, :rows].astype(jnp.float32))]
    reduce_sum x1 -> x0, other arithmetic: 4.42 us -> none  [per_block(): new_sum = run_sum * rescale + jnp.sum(weights, axis=-1)]
  transfers between devices with their start and end apart: 7 -> 4, of which waited for: 3 -> 3; matrix products, arithmetic and copies ran while one was open for 25% -> 24% of each run, Pallas kernels for 0% -> 6%
where the time goes in v3:
time: 205 us; the launch traced here: 204 us
  waiting for transfers between devices  72 us (35%)
  local copies, waits for them, and re-layouts  63.2 us (31%)
  other arithmetic  28.6 us (14%)
  between operations  14.5 us (7%)
  Pallas kernels  12 us (6%)
  starting transfers between devices  7.22 us (4%)
  matrix products  6.42 us (3%)
    ppermute x3, waiting for transfers between devices, exchange(): got = lax.ppermute(sent, axis, pairs)  72 us
    pallas_call x1, Pallas kernels, attention_core(): pl.pallas_call(attention_kernel, out_shape=jax.ShapeDtypeStruct(q_flat.sh...  12 us
    concatenate x4, local copies, waits for them, and re-layouts, exchange(): sent = jnp.concatenate([state.astype(jnp.bfloat16), high, low, pad], axis=1)  9.94 us
    unnamed x37, local copies, waits for them, and re-layouts  7.41 us
    ppermute x3, starting transfers between devices, exchange(): got = lax.ppermute(sent, axis, pairs)  7.18 us
    reshape x2, local copies, waits for them, and re-layouts, mamba_base(): x_blocks = x_in.reshape(slots, BLOCK, heads, HEADDIM)  6.5 us
    select_n x1, other arithmetic, entering_states(): jnp.where(lower, joined_low[1], joined_high[1])  5.92 us
    slice x3, local copies, waits for them, and re-layouts, exchange(): return (got_decay, got[:, :rows].astype(jnp.float32))  5.91 us
  transfers between devices with their start and end apart: 4, of which 3 were waited for; matrix products, arithmetic and copies ran while one was open for 24% of the time, Pallas kernels for 6%

profile of v3, /device:TPU:0, one launch (start us, length us, event | category | flops | bytes accessed | tf_op | source)
XLA Modules:
  0.0 204.0 jit_solution(4517787194299243428)
XLA Ops:
  7.2 1.7 pad_maximum_fusion
  12.8 1.5 copy.65
  18.2 2.1 %maximum_maximum_fusion = bf16[2,136,2048]{1,2,0:T(8,128)(2,1)} fusion(bf16[2,1,2048]{1,2,0:T(8,128)(2,1)S(1)} %copy-done.9, bf16[2,1,2048]{1,2,0:T(8,128)(2,1)S(1)} %copy.66, bf16[2,128,2048]{1,2,0:T(8,128)(2,1)S(1)} %convert_element_type.175, bf16[136]{0:T(256)(128)(2,1)S(1)} %pad.13.clone), kind=kLoop, calls=%fused_computation.16 | loop fusion | flops 4456448 | bytes 2179344 | tf_op jit(solution)/shard_map/concatenate | solution.py:37
  20.3 3.8 %copy.68 = bf16[2,136,2048]{2,1,0:T(8,128)(2,1)} copy(bf16[2,136,2048]{1,2,0:T(8,128)(2,1)} %maximum_maximum_fusion) | data formatting | bytes 2228224 | tf_op jit(solution)/shard_map/concatenate | solution.py:37
  24.0 2.9 %collective-permute-start = (bf16[2,136,2048]{2,1,0:T(8,128)(2,1)}, bf16[2,136,2048]{2,1,0:T(8,128)(2,1)}, u32[]{:S(2)}, u32[]{:S(2)}) collective-permute-start(bf16[2,136,2048]{2,1,0:T(8,128)(2,1)} %copy.68), channel_id=1, source_target_pairs={{0,2},{2,0},{4,6},{6,4},{8,10},{10,8},{12,14},{14,12},{1,3},{3,1},... | collective-permute-start | bytes 3342344 | tf_op jit(solution)/shard_map/ppermute | solution.py:38
  27.1 3.2 %reshape.230 = bf16[2,128,32,64]{3,2,1,0:T(8,128)(2,1)} reshape(bf16[256,2048]{1,0:T(8,128)(2,1)S(1)} %copy-done.8) | data formatting | bytes 2097152 | tf_op jit(solution)/shard_map/reshape | solution.py:79
  30.3 3.3 %copy.71 = bf16[2,128,32,64]{1,3,2,0:T(8,128)(2,1)S(1)} copy(bf16[2,128,32,64]{3,2,1,0:T(8,128)(2,1)} %reshape.230) | data formatting | bytes 2097152 | tf_op jit(solution)/shard_map/reshape | solution.py:79
  33.8 3.3 %bitcast_add_fusion = f32[2,128,32,64]{1,3,2,0:T(8,128)} fusion(bf16[2,128,32,64]{1,3,2,0:T(8,128)(2,1)S(1)} %copy.71, f32[2,32,128]{2,1,0:T(8,128)S(1)} %bitcast_bitcast_fusion.1, f32[2,32,128]{2,1,0:T(8,128)S(1)} %reduce_window_sum.11, f32[2,128,128]{2,1,0:T(8,128)S(1)} %fusion.25, pred[128,128]{1,0:T(8,128)(4,1)S(1)} %iota_compare_fusion, ...), kind=kOutput, calls=%fused_computation.22 | convolution fusion | flops 141033472 | bytes 3358848 | tf_op jit(solution)/shard_map/chij,cjhp->cihp/dot_general | solution.py:84
  37.2 17.5 %collective-permute-done = bf16[2,136,2048]{2,1,0:T(8,128)(2,1)} collective-permute-done((bf16[2,136,2048]{2,1,0:T(8,128)(2,1)}, bf16[2,136,2048]{2,1,0:T(8,128)(2,1)}, u32[]{:S(2)}, u32[]{:S(2)}) %collective-permute-start) | collective-permute-done | bytes 1114144 | tf_op jit(solution)/shard_map/ppermute | solution.py:38
  54.6 2.3 %slice.73 = bf16[2,128,2048]{2,1,0:T(8,128)(2,1)} slice(bf16[2,136,2048]{2,1,0:T(8,128)(2,1)} %collective-permute-done), slice={[0:2], [0:128], [0:2048]} | slice | bytes 2097152 | tf_op jit(solution)/shard_map/slice | solution.py:41
  56.9 1.6 copy.91
  58.6 1.5 convert_element_type.181
  64.2 3.2 %fusion.20 = bf16[2,128,2048]{1,2,0:T(8,128)(2,1)S(1)} fusion(f32[2,128,2048]{1,2,0:T(8,128)} %convert_element_type.181, f32[2,128,2048]{1,2,0:T(8,128)S(1)} %convolution_bitcast_fusion, f32[2,2048]{1,0:T(2,128)S(1)} %mul.196, f32[2,2048]{1,0:T(2,128)S(1)} %mul.193, pred[]{:T(512)S(6)} %eq.15), kind=kLoop, calls=%fused_computation.39 | loop fusion | flops 3670016 | bytes 5275649 | tf_op jit(solution)/shard_map/convert_element_type | solution.py:37
  67.5 2.1 %maximum_maximum_fusion.1 = bf16[2,136,2048]{1,2,0:T(8,128)(2,1)} fusion(bf16[2,1,2048]{1,2,0:T(8,128)(2,1)S(1)} %copy-done.12, bf16[2,1,2048]{1,2,0:T(8,128)(2,1)S(1)} %copy.73, bf16[2,128,2048]{1,2,0:T(8,128)(2,1)S(1)} %fusion.20, bf16[136]{0:T(256)(128)(2,1)S(1)} %pad.13.clone), kind=kLoop, calls=%fused_computation.17 | loop fusion | flops 4456448 | bytes 2179344 | tf_op jit(solution)/shard_map/concatenate | solution.py:37
  69.6 3.7 %copy.75 = bf16[2,136,2048]{2,1,0:T(8,128)(2,1)} copy(bf16[2,136,2048]{1,2,0:T(8,128)(2,1)} %maximum_maximum_fusion.1) | data formatting | bytes 2228224 | tf_op jit(solution)/shard_map/concatenate | solution.py:37
  73.3 1.8 collective-permute-start.1
  76.5 25.7 %collective-permute-done.1 = bf16[2,136,2048]{2,1,0:T(8,128)(2,1)} collective-permute-done((bf16[2,136,2048]{2,1,0:T(8,128)(2,1)}, bf16[2,136,2048]{2,1,0:T(8,128)(2,1)}, u32[]{:S(2)}, u32[]{:S(2)}) %collective-permute-start.1) | collective-permute-done | bytes 1114144 | tf_op jit(solution)/shard_map/ppermute | solution.py:38
  104.2 2.3 %slice.74 = bf16[2,128,2048]{2,1,0:T(8,128)(2,1)} slice(bf16[2,136,2048]{2,1,0:T(8,128)(2,1)} %collective-permute-done.1), slice={[0:2], [0:128], [0:2048]} | slice | bytes 2097152 | tf_op jit(solution)/shard_map/slice | solution.py:41
  106.6 1.6 copy.92
  108.2 5.9 %fusion.5 = f32[2,128,2048]{1,2,0:T(8,128)} fusion(bf16[2,128,2048]{1,2,0:T(8,128)(2,1)S(1)} %copy.92, f32[2,2048]{1,0:T(2,128)S(1)} %mul.204, f32[2,2048]{1,0:T(2,128)S(1)} %mul.201, pred[]{:T(512)S(6)} %eq.14, f32[2,128,2048]{1,2,0:T(8,128)} %convert_element_type.181, f32[2,128,2048]{1,2,0:T(8,128)S(1)} %convolution_bitcast_fusion, ...), kind=kLoop, calls=%fused_computation.15 | loop fusion | flops 6815744 | bytes 7405570 | tf_op jit(solution)/shard_map/jit(_where)/select_n | solution.py:66
  114.1 2.6 %fusion.24 = (bf16[2,1024,256]{2,1,0:T(8,128)(2,1)S(1)}, bf16[2,1024,256]{2,1,0:T(8,128)(2,1)}) fusion(bf16[2,1024,512]{2,1,0:T(8,128)(2,1)} %all-gather.2.cloned.1.call-done), kind=kLoop, calls=%fused_computation.66 | loop fusion | bytes 4194304 | tf_op jit(solution)/shard_map/slice | solution.py:101
  119.2 2.8 %copy_bitcast_fusion = (bf16[2,2048,128]{2,1,0:T(8,128)(2,1)}, bf16[2,2048,128]{2,1,0:T(8,128)(2,1)}) fusion(bf16[2048,2,128]{2,1,0:T(2,128)(2,1)} %reshape.224, bf16[2048,2,128]{2,1,0:T(2,128)(2,1)S(1)} %reshape.223), kind=kLoop, calls=%fused_computation.37 | loop fusion | bytes 4194304 | tf_op jit(solution)/shard_map/transpose | solution.py:101
  127.3 2.4 %copy.82 = bf16[2,136,2048]{2,1,0:T(8,128)(2,1)} copy(bf16[2,136,2048]{1,2,0:T(8,128)(2,1)S(1)} %maximum_maximum_fusion.2) | data formatting | bytes 2228224 | tf_op jit(solution)/shard_map/concatenate | solution.py:37
  129.7 2.4 %collective-permute-start.2 = (bf16[2,136,2048]{2,1,0:T(8,128)(2,1)}, bf16[2,136,2048]{2,1,0:T(8,128)(2,1)}, u32[]{:S(2)}, u32[]{:S(2)}) collective-permute-start(bf16[2,136,2048]{2,1,0:T(8,128)(2,1)} %copy.82), channel_id=1, source_target_pairs={{0,8},{2,10},{4,12},{6,14},{8,0},{10,2},{12,4},{14,6},{1,9},{3,11}... | collective-permute-start | bytes 3342344 | tf_op jit(solution)/shard_map/ppermute | solution.py:38
  132.3 1.9 copy.86
  134.2 3.0 %copy.87 = f32[2,128,2048]{2,1,0:T(8,128)} copy(f32[2,128,2048]{1,2,0:T(8,128)} %bitcast.80) | data formatting | bytes 4194304 | tf_op jit(solution)/shard_map/optimization_barrier | solution.py:59
  137.2 12.0 %shard_map.104 = bf16[2,1024,128]{2,1,0:T(8,128)(2,1)} custom-call(bf16[2,1024,128]{2,1,0:T(8,128)(2,1)} %bitcast.82, bf16[2,2048,128]{2,1,0:T(8,128)(2,1)} %get-tuple-element.41.k_ref, bf16[2,2048,128]{2,1,0:T(8,128)(2,1)} %get-tuple-element.42.v_ref), custom_call_target="tpu_custom_call" | custom-call | flops 2147483648 | bytes 3145728 | tf_op jit(solution)/shard_map/pallas_call | solution.py:153
  151.9 28.9 %collective-permute-done.2 = bf16[2,136,2048]{2,1,0:T(8,128)(2,1)} collective-permute-done((bf16[2,136,2048]{2,1,0:T(8,128)(2,1)}, bf16[2,136,2048]{2,1,0:T(8,128)(2,1)}, u32[]{:S(2)}, u32[]{:S(2)}) %collective-permute-start.2) | collective-permute-done | bytes 1114144 | tf_op jit(solution)/shard_map/ppermute | solution.py:38
  183.3 2.8 %convert_element_type.197 = f32[2,128,2048]{1,2,0:T(8,128)} convert(bf16[2,128,2048]{1,2,0:T(8,128)(2,1)} %copy.93) | non-fusion elementwise | flops 524288 | bytes 3145728 | tf_op jit(solution)/shard_map/convert_element_type | solution.py:41
  189.1 3.3 %add_select_fusion = f32[2,128,2048]{1,2,0:T(8,128)S(1)} fusion(bf16[2,128,2048]{1,2,0:T(8,128)(2,1)S(1)} %copy.92, f32[2,128,2048]{1,2,0:T(8,128)S(1)} %copy-done.2, f32[2,128,2048]{1,2,0:T(8,128)} %convert_element_type.197, f32[2,2048]{1,0:T(2,128)S(1)} %mul.216, f32[2,2048]{1,0:T(2,128)S(1)} %mul.213, pred[]{:T(512)S(6)} %eq.13, pred[]{:T(512)S(6)} %eq.14, ...), kind=kLoop, calls=%fused_computation.1 | loop fusion | flops 4194304 | bytes 7372803 | tf_op jit(solution)/shard_map/jit(_where)/select_n | solution.py:28
  192.5 1.7 slice_add_fusion
  194.7 2.5 %fusion.2 = bf16[2,128,2048]{2,1,0:T(8,128)(2,1)} fusion(f32[2,128,2048]{2,1,0:T(8,128)S(1)} %copy-done.7, f32[2,128,2048]{2,1,0:T(8,128)S(1)} %copy-done.6, bf16[2,128,128]{2,1,0:T(8,128)(2,1)S(1)} %bitcast.85, f32[1,128,2048]{1,2,0:T(8,128)S(1)} %get-tuple-element.56, f32[1,128,2048]{1,2,0:T(8,128)S(1)} %get-tuple-element.55), kind=kOutput, calls=%fused_computation.12 | convolution fusion | flops 807403520 | bytes 7405568 | tf_op jit(solution)/shard_map/ctn,cnk->ctk/dot_general | solution.py:201
  (114 shorter events, 32.1 us)
Async XLA Ops:
  7.2 7.3 %copy-start = (bf16[256,128]{1,0:T(8,128)(2,1)S(1)}, bf16[256,128]{1,0:T(8,128)(2,1)}, u32[]{:S(2)}) copy-start(bf16[256,128]{1,0:T(8,128)(2,1)} %param.13) | copy-start | bytes 196612
  7.2 106.9 %all-gather.2.cloned.1.call-start = ((), (), s32[]{:S(2)}) async-start(), calls=%async_computation | async-start | bytes 2359296 | tf_op jit(solution)/shard_map/all_gather | solution.py:183
  16.9 1.2 copy-start.9
  20.3 6.8 %copy-start.8 = (bf16[256,2048]{1,0:T(8,128)(2,1)S(1)}, bf16[256,2048]{1,0:T(8,128)(2,1)}, u32[]{:S(2)}) copy-start(bf16[256,2048]{1,0:T(8,128)(2,1)} %param.9) | copy-start | bytes 3145732
  24.0 30.6 %collective-permute-start = (bf16[2,136,2048]{2,1,0:T(8,128)(2,1)}, bf16[2,136,2048]{2,1,0:T(8,128)(2,1)}, u32[]{:S(2)}, u32[]{:S(2)}) collective-permute-start(bf16[2,136,2048]{2,1,0:T(8,128)(2,1)} %copy.68), channel_id=1, source_target_pairs={{0,2},{2,0},{4,6},{6,4},{8,10},{10,8},{12,14},{14,12},{1,3},{3,1},... | collective-permute-start | bytes 3342344 | tf_op jit(solution)/shard_map/ppermute | solution.py:38
  30.3 3.4 %copy-start.14 = (bf16[256,128]{1,0:T(8,128)(2,1)S(1)}, bf16[256,128]{1,0:T(8,128)(2,1)}, u32[]{:S(2)}) copy-start(bf16[256,128]{1,0:T(8,128)(2,1)} %param.14) | copy-start | bytes 196612
  30.3 3.5 %copy-start.16 = (f32[32]{0:T(128)S(1)}, f32[32]{0:T(128)}, u32[]{:S(2)}) copy-start(f32[32]{0:T(128)} %param.12) | copy-start | bytes 388
  64.2 3.2 %copy-start.12 = (bf16[2,1,2048]{1,2,0:T(8,128)(2,1)S(1)}, bf16[2,1,2048]{1,2,0:T(8,128)(2,1)}, u32[]{:S(2)}) copy-start(bf16[2,1,2048]{1,2,0:T(8,128)(2,1)} %copy.74) | copy-start | bytes 24580
  69.6 5.6 %copy-start.13 = (bf16[256,1024]{1,0:T(8,128)(2,1)S(1)}, bf16[256,1024]{1,0:T(8,128)(2,1)}, u32[]{:S(2)}) copy-start(bf16[256,1024]{1,0:T(8,128)(2,1)} %param.15) | copy-start | bytes 1572868
  73.3 28.8 %collective-permute-start.1 = (bf16[2,136,2048]{2,1,0:T(8,128)(2,1)}, bf16[2,136,2048]{2,1,0:T(8,128)(2,1)}, u32[]{:S(2)}, u32[]{:S(2)}) collective-permute-start(bf16[2,136,2048]{2,1,0:T(8,128)(2,1)} %copy.75), channel_id=1, source_target_pairs={{0,4},{2,6},{4,0},{6,2},{8,12},{10,14},{12,8},{14,10},{1,5},{3,7},... | collective-permute-start | bytes 3342344 | tf_op jit(solution)/shard_map/ppermute | solution.py:38
  122.0 3.0 %copy-start.3 = (f32[2,128,2048]{1,2,0:T(8,128)S(1)}, f32[2,128,2048]{1,2,0:T(8,128)}, u32[]{:S(2)}) copy-start(f32[2,128,2048]{1,2,0:T(8,128)} %fusion.5) | copy-start | bytes 6291460
  125.0 1.2 copy-start.10
  125.0 1.5 copy-start.11
  129.7 51.0 %collective-permute-start.2 = (bf16[2,136,2048]{2,1,0:T(8,128)(2,1)}, bf16[2,136,2048]{2,1,0:T(8,128)(2,1)}, u32[]{:S(2)}, u32[]{:S(2)}) collective-permute-start(bf16[2,136,2048]{2,1,0:T(8,128)(2,1)} %copy.82), channel_id=1, source_target_pairs={{0,8},{2,10},{4,12},{6,14},{8,0},{10,2},{12,4},{14,6},{1,9},{3,11}... | collective-permute-start | bytes 3342344 | tf_op jit(solution)/shard_map/ppermute | solution.py:38
  137.2 14.6 %copy-start.15 = (f32[2,2048]{1,0:T(2,128)}, f32[2,2048]{1,0:T(2,128)S(1)}, u32[]{:S(2)}) copy-start(f32[2,2048]{1,0:T(2,128)S(1)} %mul.226) | copy-start | bytes 49156
  183.3 5.8 %copy-start.2 = (f32[2,128,2048]{1,2,0:T(8,128)S(1)}, f32[2,128,2048]{1,2,0:T(8,128)}, u32[]{:S(2)}) copy-start(f32[2,128,2048]{1,2,0:T(8,128)} %convert_element_type.181) | copy-start | bytes 6291460
  189.1 3.3 %copy-start.4 = (f32[2,128,2048]{1,2,0:T(8,128)S(1)}, f32[2,128,2048]{1,2,0:T(8,128)}, u32[]{:S(2)}) copy-start(f32[2,128,2048]{1,2,0:T(8,128)} %fusion.5) | copy-start | bytes 6291460
  189.1 3.3 %copy-start.5 = (f32[2,128,2048]{1,2,0:T(8,128)S(1)}, f32[2,128,2048]{1,2,0:T(8,128)}, u32[]{:S(2)}) copy-start(f32[2,128,2048]{1,2,0:T(8,128)} %convert_element_type.197) | copy-start | bytes 6291460
  189.1 3.3 %slice-start = ((f32[2,2048]{1,0:T(2,128)}), f32[1,2048]{1,0:T(1,128)S(1)}, s32[]{:S(2)}) async-start(f32[2,2048]{1,0:T(2,128)} %copy-done.15), calls=%async_computation.1 | async-start | bytes 16384 | tf_op jit(solution)/shard_map/slice | solution.py:73
  192.4 1.8 copy-start.6
  192.4 2.2 %copy-start.7 = (f32[2,128,2048]{2,1,0:T(8,128)S(1)}, f32[2,128,2048]{2,1,0:T(8,128)}, u32[]{:S(2)}) copy-start(f32[2,128,2048]{2,1,0:T(8,128)} %copy.87) | copy-start | bytes 6291460
  194.2 3.0 %copy-start.1 = (bf16[256,128]{1,0:T(8,128)(2,1)S(1)}, bf16[256,128]{1,0:T(8,128)(2,1)}, u32[]{:S(2)}) copy-start(bf16[256,128]{1,0:T(8,128)(2,1)} %param.13) | copy-start | bytes 196612
Sparse Core Ops, SparseCore 0:
  27.1 52.9 all-gather.1

commit v4 on v3

--- a/solution.py
+++ b/solution.py
@@ -20,57 +20,49 @@
     return jnp.repeat(a, HEADDIM, axis=-1)
 
 
-def combine_if(lower, earlier, later):
-    a_e, s_e = earlier
-    a_l, s_l = later
-    joined_a = a_e * a_l
-    joined_s = spread(a_l)[:, None, :] * s_e + s_l
-    return (jnp.where(lower, joined_a, a_l), jnp.where(lower, joined_s, s_l))
-
-
-def exchange(value, axis, pairs):
-    decay, state = value
-    spread_decay = spread(decay)[:, None, :]
-    high = spread_decay.astype(jnp.bfloat16)
-    low = (spread_decay - high.astype(jnp.float32)).astype(jnp.bfloat16)
-    pad = jnp.zeros((state.shape[0], 6, state.shape[2]), jnp.bfloat16)
-    sent = jnp.concatenate([state.astype(jnp.bfloat16), high, low, pad], axis=1)
-    got = lax.ppermute(sent, axis, pairs)
-    rows = state.shape[1]
-    got_decay = got[:, rows, ::HEADDIM].astype(jnp.float32) + got[:, rows + 1, ::HEADDIM].astype(jnp.float32)
-    return (got_decay, got[:, :rows].astype(jnp.float32))
-
-
-def entering_states(decay, block_state, count, mine, hooks):
-    slots = decay.shape[0]
-    excl = (jnp.ones_like(decay), jnp.zeros_like(block_state))
-    total = (decay, block_state)
-    results = {}
-    span, step = 1, 0
+def decay_scan(decay, count, mine):
+    excl = jnp.ones_like(decay)
+    total = decay
+    steps = []
+    span = 1
     while span < count:
         lower = (mine // span) % 2 == 1
+        got = lax.ppermute(total, "seq", [(i, i ^ span) for i in range(count)])
+        steps.append((lower, excl, total, got))
+        excl = jnp.where(lower, got * excl, excl)
+        total = total * got
+        span *= 2
+    return steps, excl, total
+
+
+def entering_states(decay, block_state, count, mine, hooks):
+    steps, excl_decay, total_decay = decay_scan(decay, count, mine)
+    excl = jnp.zeros_like(block_state)
+    total = block_state
+    results = {}
+    span = 1
+    for step, (lower, excl_a, own_a, got_a) in enumerate(steps):
         pairs = [(i, i ^ span) for i in range(count)]
-        hook = hooks.get(step if span * 2 < count else -1)
+        hook = hooks.get(step if step + 1 < len(steps) else -1)
         if hook is not None:
             total, args = lax.optimization_barrier((total, hook[1]))
-        got = exchange(total, "seq", pairs)
+        got = lax.ppermute(total.astype(jnp.bfloat16), "seq", pairs).astype(jnp.float32)
         if hook is not None:
             done = hook[0](*args)
             got, done = lax.optimization_barrier((got, done))
             results[hook[0].__name__] = done
-        excl = combine_if(lower, got, excl)
-        joined_low = combine_if(lower, got, total)
-        joined_high = (total[0] * got[0], spread(got[0])[:, None, :] * total[1] + got[1])
-        total = (
-            jnp.where(lower, joined_low[0], joined_high[0]),
-            jnp.where(lower, joined_low[1], joined_high[1]),
+        excl = jnp.where(lower, spread(excl_a)[:, None, :] * got + excl, excl)
+        total = jnp.where(
+            lower,
+            spread(own_a)[:, None, :] * got + total,
+            spread(got_a)[:, None, :] * total + got,
         )
-        span, step = span * 2, step + 1
+        span *= 2
     carry = jnp.zeros_like(block_state[0])
     entering = []
-    for slot in range(slots):
-        entering.append(spread(excl[0][slot])[None, :] * carry + excl[1][slot])
-        carry = spread(total[0][slot])[None, :] * carry + total[1][slot]
+    for slot in range(decay.shape[0]):
+        entering.append(spread(excl_decay[slot])[None, :] * carry + excl[slot])
+        carry = spread(total_decay[slot])[None, :] * carry + total[slot]
     return (jnp.stack(entering, axis=0), results)
 
 

time: 205 us -> 185 us (0.902)
  the two profiles are of different devices: /device:TPU:0 before, /device:TPU:31 now
where the time goes in v4:
time: 185 us
  waiting for transfers between devices  86.2 us (47%)
  local copies, waits for them, and re-layouts  29.3 us (16%)
  other arithmetic  22.9 us (12%)
  Pallas kernels  21.1 us (11%)
  between operations  14.4 us (8%)
  starting transfers between devices  5.4 us (3%)
  matrix products  5.32 us (3%)
    ppermute x3, waiting for transfers between devices, decay_scan(): got = lax.ppermute(total, 'seq', [(i, i ^ span) for i in range(count)])  86.2 us
    pallas_call x1, Pallas kernels, attention_core(): pl.pallas_call(attention_kernel, out_shape=jax.ShapeDtypeStruct(q_flat.sh...  21.1 us
    reshape x2, local copies, waits for them, and re-layouts, mamba_base(): x_blocks = x_in.reshape(slots, BLOCK, heads, HEADDIM)  6.45 us
    select_n x1, other arithmetic, entering_states(): jnp.where(lower, spread(own_a)[:, None, :] * got + total, spread(got_a)[:...  6.18 us
    ppermute x3, starting transfers between devices, decay_scan(): got = lax.ppermute(total, 'seq', [(i, i ^ span) for i in range(count)])  4.99 us
    convert_element_type x3, other arithmetic, entering_states(): total.astype(jnp.bfloat16)  4.81 us
    reshape x2, local copies, waits for them, and re-layouts, attention_prep(): queries.reshape(slots, BLOCK, kv_local, per_kv, HD).transpose(2, 0, 3, 1, 4)  4.13 us
  transfers between devices with their start and end apart: 7, of which 3 were waited for; matrix products, arithmetic and copies ran while one was open for 23% of the time, Pallas kernels for 11%

profile of v4, /device:TPU:31, one launch (start us, length us, event | category | flops | bytes accessed | tf_op | source)
XLA Modules:
  0.0 184.6 jit_solution(8766273747073761554)
XLA Ops:
  7.2 1.7 pad_maximum_fusion
  9.6 0.8 broadcast_multiply_fusion
  11.2 0.9 fusion.15
  12.8 1.5 copy.33
  14.9 1.1 convert_element_type.40
  16.3 1.2 collective-permute-start.1
  17.5 3.1 %reshape.113 = bf16[2,128,32,64]{3,2,1,0:T(8,128)(2,1)} reshape(bf16[256,2048]{1,0:T(8,128)(2,1)S(1)} %copy-done.7) | data formatting | bytes 2097152 | tf_op jit(solution)/shard_map/reshape | solution.py:71
  20.6 3.3 %copy.35 = bf16[2,128,32,64]{1,3,2,0:T(8,128)(2,1)S(1)} copy(bf16[2,128,32,64]{3,2,1,0:T(8,128)(2,1)} %reshape.113) | data formatting | bytes 2097152 | tf_op jit(solution)/shard_map/reshape | solution.py:71
  24.1 3.4 %bitcast_add_fusion = f32[2,128,32,64]{1,3,2,0:T(8,128)} fusion(bf16[2,128,32,64]{1,3,2,0:T(8,128)(2,1)S(1)} %copy.35, f32[2,32,128]{2,1,0:T(8,128)S(1)} %bitcast_bitcast_fusion.1, f32[2,32,128]{2,1,0:T(8,128)S(1)} %reduce_window_sum.11, f32[2,128,128]{2,1,0:T(8,128)S(1)} %fusion.19, pred[128,128]{1,0:T(8,128)(4,1)S(1)} %iota_compare_fusion, ...), kind=kOutput, calls=%fused_computation.15 | convolution fusion | flops 141033472 | bytes 3358848 | tf_op jit(solution)/shard_map/chij,cjhp->cihp/dot_general | solution.py:76
  27.7 16.6 %collective-permute-done.1 = f32[2,32]{1,0:T(2,128)S(1)} collective-permute-done((f32[2,32]{1,0:T(2,128)S(1)}, f32[2,32]{1,0:T(2,128)S(1)}, u32[]{:S(2)}, u32[]{:S(2)}) %collective-permute-start.1) | collective-permute-done | bytes 288 | tf_op jit(solution)/shard_map/ppermute | solution.py:30
  44.5 1.4 convert_element_type.41
  45.9 2.6 %fusion.14 = bf16[2,128,2048]{1,2,0:T(8,128)(2,1)} fusion(f32[2,128,2048]{1,2,0:T(8,128)S(1)} %convert_element_type.41, f32[2,128,2048]{1,2,0:T(8,128)S(1)} %convolution_bitcast_fusion, f32[2,2048]{1,0:T(2,128)S(1)} %mul.205, f32[2,2048]{1,0:T(2,128)S(1)} %mul.202, pred[]{:T(512)S(6)} %eq.15), kind=kLoop, calls=%fused_computation.30 | loop fusion | flops 3145728 | bytes 5275649 | tf_op jit(solution)/shard_map/convert_element_type | solution.py:49
  48.6 1.4 collective-permute-start.2
  49.9 2.2 %reshape.104 = bf16[2,128,2,4,128]{4,3,2,1,0:T(4,128)(2,1)} reshape(bf16[256,1024]{1,0:T(8,128)(2,1)} %param.15) | data formatting | bytes 1048576 | tf_op jit(solution)/shard_map/reshape | solution.py:89
  52.1 1.9 %copy.37 = bf16[2,128,2,4,128]{4,1,3,0,2:T(8,128)(2,1)} copy(bf16[2,128,2,4,128]{4,3,2,1,0:T(4,128)(2,1)} %reshape.104) | data formatting | bytes 1048576 | tf_op jit(solution)/shard_map/reshape | solution.py:89
  54.2 26.3 %collective-permute-done.2 = f32[2,32]{1,0:T(2,128)S(1)} collective-permute-done((f32[2,32]{1,0:T(2,128)S(1)}, f32[2,32]{1,0:T(2,128)S(1)}, u32[]{:S(2)}, u32[]{:S(2)}) %collective-permute-start.2) | collective-permute-done | bytes 288 | tf_op jit(solution)/shard_map/ppermute | solution.py:30
  80.8 6.2 %fusion.3 = f32[2,128,2048]{1,2,0:T(8,128)} fusion(bf16[2,128,2048]{1,2,0:T(8,128)(2,1)S(1)} %collective-permute-done.4, f32[2,2048]{1,0:T(2,128)S(1)} %mul.209, f32[2,2048]{1,0:T(2,128)S(1)} %mul.200, pred[]{:T(512)S(6)} %eq.14, f32[2,128,2048]{1,2,0:T(8,128)} %copy-done.1, f32[2,128,2048]{1,2,0:T(8,128)S(1)} %convolution_bitcast_fusion, ...), kind=kLoop, calls=%fused_computation.11 | loop fusion | flops 5767168 | bytes 7405570 | tf_op jit(solution)/shard_map/jit(_where)/select_n | solution.py:55
  86.9 1.7 fusion.18
  89.2 1.6 copy_bitcast_fusion
  91.6 1.1 convert_element_type.46
  92.7 2.4 %collective-permute-start.3 = (f32[2,32]{1,0:T(2,128)S(1)}, f32[2,32]{1,0:T(2,128)S(1)}, u32[]{:S(2)}, u32[]{:S(2)}) collective-permute-start(f32[2,32]{1,0:T(2,128)S(1)} %mul.191), channel_id=1, source_target_pairs={{0,8},{2,10},{4,12},{6,14},{8,0},{10,2},{12,4},{14,6},{1,9},{3,11}... | collective-permute-start | bytes 776 | tf_op jit(solution)/shard_map/ppermute | solution.py:30
  95.3 1.9 %copy.42 = f32[2,128,2048]{2,1,0:T(8,128)} copy(f32[2,128,2048]{1,2,0:T(8,128)S(1)} %bitcast.71) | data formatting | bytes 4194304 | tf_op jit(solution)/shard_map/reshape | solution.py:20
  97.3 43.2 %collective-permute-done.3 = f32[2,32]{1,0:T(2,128)S(1)} collective-permute-done((f32[2,32]{1,0:T(2,128)S(1)}, f32[2,32]{1,0:T(2,128)S(1)}, u32[]{:S(2)}, u32[]{:S(2)}) %collective-permute-start.3) | collective-permute-done | bytes 288 | tf_op jit(solution)/shard_map/ppermute | solution.py:30
  141.5 3.0 %copy.43 = f32[2,128,2048]{2,1,0:T(8,128)} copy(f32[2,128,2048]{1,2,0:T(8,128)} %bitcast.73) | data formatting | bytes 4194304 | tf_op jit(solution)/shard_map/optimization_barrier | solution.py:52
  144.5 21.1 %shard_map.104 = bf16[2,1024,128]{2,1,0:T(8,128)(2,1)} custom-call(bf16[2,1024,128]{2,1,0:T(8,128)(2,1)} %bitcast.75, bf16[2,2048,128]{2,1,0:T(8,128)(2,1)} %get-tuple-element.34.k_ref, bf16[2,2048,128]{2,1,0:T(8,128)(2,1)} %get-tuple-element.35.v_ref), custom_call_target="tpu_custom_call" | custom-call | flops 2147483648 | bytes 3145728 | tf_op jit(solution)/shard_map/pallas_call | solution.py:145
  165.6 2.2 %copy.40 = bf16[2,128,2,4,128]{4,3,2,1,0:T(4,128)(2,1)} copy(bf16[2,128,2,4,128]{4,1,3,0,2:T(8,128)(2,1)} %bitcast.76) | data formatting | bytes 1048576 | tf_op jit(solution)/shard_map/transpose | solution.py:160
  167.8 2.3 %reshape.109 = bf16[256,1024]{1,0:T(8,128)(2,1)} reshape(bf16[2,128,2,4,128]{4,3,2,1,0:T(4,128)(2,1)} %copy.40) | data formatting | bytes 1048576 | tf_op jit(solution)/shard_map/reshape | solution.py:161
  170.2 1.4 convert_element_type.47
  171.6 1.4 add_select_fusion
  173.2 1.7 slice_add_fusion.1
  174.9 1.3 fusion
  176.5 1.2 add_convert_fusion
  (80 shorter events, 7.0 us)
Async XLA Ops:
  7.2 7.3 %copy-start = (bf16[256,128]{1,0:T(8,128)(2,1)S(1)}, bf16[256,128]{1,0:T(8,128)(2,1)}, u32[]{:S(2)}) copy-start(bf16[256,128]{1,0:T(8,128)(2,1)} %param.13) | copy-start | bytes 196612
  7.2 79.8 %all-gather.2.cloned.1.call-start = ((), (), s32[]{:S(2)}) async-start(), calls=%async_computation | async-start | bytes 2359296 | tf_op jit(solution)/shard_map/all_gather | solution.py:175
  14.9 2.6 %copy-start.7 = (bf16[256,2048]{1,0:T(8,128)(2,1)S(1)}, bf16[256,2048]{1,0:T(8,128)(2,1)}, u32[]{:S(2)}) copy-start(bf16[256,2048]{1,0:T(8,128)(2,1)} %param.9) | copy-start | bytes 3145732
  16.0 28.5 %collective-permute-start = (bf16[2,128,2048]{1,2,0:T(8,128)(2,1)}, bf16[2,128,2048]{1,2,0:T(8,128)(2,1)}, u32[]{:S(2)}, u32[]{:S(2)}) collective-permute-start(bf16[2,128,2048]{1,2,0:T(8,128)(2,1)} %convert_element_type.40), channel_id=1, source_target_pairs={{0,2},{2,0},{4,6},{6,4},{8,10},{10,8},{12,14},{14,12},{1,3},{3,1},... | collective-permute-start | bytes 3145736 | tf_op jit(solution)/shard_map/ppermute | solution.py:49
  16.3 28.1 %collective-permute-start.1 = (f32[2,32]{1,0:T(2,128)S(1)}, f32[2,32]{1,0:T(2,128)S(1)}, u32[]{:S(2)}, u32[]{:S(2)}) collective-permute-start(f32[2,32]{1,0:T(2,128)S(1)} %exp.27), channel_id=1, source_target_pairs={{0,2},{2,0},{4,6},{6,4},{8,10},{10,8},{12,14},{14,12},{1,3},{3,1},... | collective-permute-start | bytes 776 | tf_op jit(solution)/shard_map/ppermute | solution.py:30
  20.6 3.4 %copy-start.10 = (bf16[256,128]{1,0:T(8,128)(2,1)S(1)}, bf16[256,128]{1,0:T(8,128)(2,1)}, u32[]{:S(2)}) copy-start(bf16[256,128]{1,0:T(8,128)(2,1)} %param.14) | copy-start | bytes 196612
  20.6 3.5 %copy-start.13 = (f32[32]{0:T(128)S(1)}, f32[32]{0:T(128)}, u32[]{:S(2)}) copy-start(f32[32]{0:T(128)} %param.12) | copy-start | bytes 388
  45.9 2.6 %copy-start.1 = (f32[2,128,2048]{1,2,0:T(8,128)}, f32[2,128,2048]{1,2,0:T(8,128)S(1)}, u32[]{:S(2)}) copy-start(f32[2,128,2048]{1,2,0:T(8,128)S(1)} %convert_element_type.41) | copy-start | bytes 6291460
  48.5 32.3 %collective-permute-start.4 = (bf16[2,128,2048]{1,2,0:T(8,128)(2,1)}, bf16[2,128,2048]{1,2,0:T(8,128)(2,1)S(1)}, u32[]{:S(2)}, u32[]{:S(2)}) collective-permute-start(bf16[2,128,2048]{1,2,0:T(8,128)(2,1)} %fusion.14), channel_id=1, source_target_pairs={{0,4},{2,6},{4,0},{6,2},{8,12},{10,14},{12,8},{14,10},{1,5},{3,7},... | collective-permute-start | bytes 3145736 | tf_op jit(solution)/shard_map/ppermute | solution.py:49
  48.6 32.0 %collective-permute-start.2 = (f32[2,32]{1,0:T(2,128)S(1)}, f32[2,32]{1,0:T(2,128)S(1)}, u32[]{:S(2)}, u32[]{:S(2)}) collective-permute-start(f32[2,32]{1,0:T(2,128)S(1)} %exponential_multiply_fusion), channel_id=1, source_target_pairs={{0,4},{2,6},{4,0},{6,2},{8,12},{10,14},{12,8},{14,10},{1,5},{3,7},... | collective-permute-start | bytes 776 | tf_op jit(solution)/shard_map/ppermute | solution.py:30
  80.7 6.2 %copy-start.8 = (bf16[2,128,2048]{1,2,0:T(8,128)(2,1)}, bf16[2,128,2048]{1,2,0:T(8,128)(2,1)S(1)}, u32[]{:S(2)}) copy-start(bf16[2,128,2048]{1,2,0:T(8,128)(2,1)S(1)} %collective-permute-done.4) | copy-start | bytes 3145732
  89.2 2.3 %copy-start.3 = (f32[2,128,2048]{1,2,0:T(8,128)S(1)}, f32[2,128,2048]{1,2,0:T(8,128)}, u32[]{:S(2)}) copy-start(f32[2,128,2048]{1,2,0:T(8,128)} %fusion.3) | copy-start | bytes 6291460
  92.7 77.5 %collective-permute-start.5 = (bf16[2,128,2048]{1,2,0:T(8,128)(2,1)}, bf16[2,128,2048]{1,2,0:T(8,128)(2,1)}, u32[]{:S(2)}, u32[]{:S(2)}) collective-permute-start(bf16[2,128,2048]{1,2,0:T(8,128)(2,1)} %convert_element_type.46), channel_id=1, source_target_pairs={{0,8},{2,10},{4,12},{6,14},{8,0},{10,2},{12,4},{14,6},{1,9},{3,11}... | collective-permute-start | bytes 3145736 | tf_op jit(solution)/shard_map/ppermute | solution.py:49
  92.7 47.8 %collective-permute-start.3 = (f32[2,32]{1,0:T(2,128)S(1)}, f32[2,32]{1,0:T(2,128)S(1)}, u32[]{:S(2)}, u32[]{:S(2)}) collective-permute-start(f32[2,32]{1,0:T(2,128)S(1)} %mul.191), channel_id=1, source_target_pairs={{0,8},{2,10},{4,12},{6,14},{8,0},{10,2},{12,4},{14,6},{1,9},{3,11}... | collective-permute-start | bytes 776 | tf_op jit(solution)/shard_map/ppermute | solution.py:30
  97.3 47.2 %copy-start.11 = (f32[2,2048]{1,0:T(2,128)}, f32[2,2048]{1,0:T(2,128)S(1)}, u32[]{:S(2)}) copy-start(f32[2,2048]{1,0:T(2,128)S(1)} %mul.223) | copy-start | bytes 49156
  141.5 3.0 %copy-start.12 = (f32[2,2048]{1,0:T(2,128)}, f32[2,2048]{1,0:T(2,128)S(1)}, u32[]{:S(2)}) copy-start(f32[2,2048]{1,0:T(2,128)S(1)} %mul.226) | copy-start | bytes 49156
  167.8 3.7 %copy-start.2 = (f32[2,128,2048]{1,2,0:T(8,128)S(1)}, f32[2,128,2048]{1,2,0:T(8,128)}, u32[]{:S(2)}) copy-start(f32[2,128,2048]{1,2,0:T(8,128)} %copy-done.1) | copy-start | bytes 6291460
  167.8 3.7 %copy-start.9 = (bf16[2,128,2048]{1,2,0:T(8,128)(2,1)S(1)}, bf16[2,128,2048]{1,2,0:T(8,128)(2,1)}, u32[]{:S(2)}) copy-start(bf16[2,128,2048]{1,2,0:T(8,128)(2,1)} %copy-done.8) | copy-start | bytes 3145732
  171.6 1.6 copy-start.4
  171.6 1.6 slice-start
  171.6 1.6 slice-start.1
  173.2 1.7 copy-start.5
  174.9 1.6 copy-start.6
Sparse Core Ops, SparseCore 0:
  10.2 57.3 all-gather.1

commit v5 on v4

--- a/solution.py
+++ b/solution.py
@@ -37,8 +37,10 @@
 
 def entering_states(decay, block_state, count, mine, hooks):
     steps, excl_decay, total_decay = decay_scan(decay, count, mine)
+    total, steps, excl_decay, total_decay = lax.optimization_barrier(
+        (block_state, steps, excl_decay, total_decay)
+    )
     excl = jnp.zeros_like(block_state)
-    total = block_state
     results = {}
     span = 1
     for step, (lower, excl_a, own_a, got_a) in enumerate(steps):

time: 185 us -> 159 us (0.86)
  the two profiles are of different devices: /device:TPU:31 before, /device:TPU:0 now
where the time goes in v5:
time: 159 us
  waiting for transfers between devices  63 us (40%)
  local copies, waits for them, and re-layouts  29.3 us (18%)
  other arithmetic  23.4 us (15%)
  between operations  14.5 us (9%)
  Pallas kernels  12 us (8%)
  starting transfers between devices  11.1 us (7%)
  matrix products  5.34 us (3%)
    ppermute x3, waiting for transfers between devices, entering_states(): lax.ppermute(total.astype(jnp.bfloat16), 'seq', pairs).astype(jnp.float32)  59.1 us
    pallas_call x1, Pallas kernels, attention_core(): pl.pallas_call(attention_kernel, out_shape=jax.ShapeDtypeStruct(q_flat.sh...  12 us
    ppermute x3, starting transfers between devices, decay_scan(): got = lax.ppermute(total, 'seq', [(i, i ^ span) for i in range(count)])  7.23 us
    reshape x2, local copies, waits for them, and re-layouts, mamba_base(): x_blocks = x_in.reshape(slots, BLOCK, heads, HEADDIM)  6.47 us
    select_n x1, other arithmetic, entering_states(): jnp.where(lower, spread(own_a)[:, None, :] * got + total, spread(got_a)[:...  6.12 us
    convert_element_type x3, other arithmetic, entering_states(): total.astype(jnp.bfloat16)  4.81 us
    reshape x2, local copies, waits for them, and re-layouts, attention_prep(): queries.reshape(slots, BLOCK, kv_local, per_kv, HD).transpose(2, 0, 3, 1, 4)  4.13 us
    ppermute x3, waiting for transfers between devices, decay_scan(): got = lax.ppermute(total, 'seq', [(i, i ^ span) for i in range(count)])  3.88 us
  transfers between devices with their start and end apart: 7, of which 5 were waited for; matrix products, arithmetic and copies ran while one was open for 26% of the time, Pallas kernels for 8%

profile of v5, /device:TPU:0, one launch (start us, length us, event | category | flops | bytes accessed | tf_op | source)
XLA Modules:
  0.0 158.6 jit_solution(17376142170751218878)
XLA Ops:
  7.2 1.7 %pad_maximum_fusion = bf16[2,128,512]{2,1,0:T(8,128)(2,1)} fusion(bf16[2,128,256]{2,1,0:T(8,128)(2,1)} %bitcast.79, bf16[2,128,256]{2,1,0:T(8,128)(2,1)} %bitcast.80), kind=kLoop, calls=%fused_computation.31 | loop fusion | flops 524288 | bytes 524288 | tf_op jit(solution)/shard_map/concatenate | solution.py:173
  11.2 3.0 %collective-permute-start = (f32[2,32]{1,0:T(2,128)S(1)}, f32[2,32]{1,0:T(2,128)S(1)}, u32[]{:S(2)}, u32[]{:S(2)}) collective-permute-start(f32[2,32]{1,0:T(2,128)S(1)} %exp.26), channel_id=1, source_target_pairs={{0,2},{2,0},{4,6},{6,4},{8,10},{10,8},{12,14},{14,12},{1,3},{3,1},... | collective-permute-start | bytes 776 | tf_op jit(solution)/shard_map/ppermute | solution.py:30
  15.8 1.5 copy.33
  18.0 1.6 %collective-permute-start.1 = (f32[2,32]{1,0:T(2,128)S(1)}, f32[2,32]{1,0:T(2,128)S(1)}, u32[]{:S(2)}, u32[]{:S(2)}) collective-permute-start(f32[2,32]{1,0:T(2,128)S(1)} %exponential_multiply_fusion), channel_id=1, source_target_pairs={{0,4},{2,6},{4,0},{6,2},{8,12},{10,14},{12,8},{14,10},{1,5},{3,7},... | collective-permute-start | bytes 776 | tf_op jit(solution)/shard_map/ppermute | solution.py:30
  19.6 2.0 %collective-permute-done.1 = f32[2,32]{1,0:T(2,128)S(1)} collective-permute-done((f32[2,32]{1,0:T(2,128)S(1)}, f32[2,32]{1,0:T(2,128)S(1)}, u32[]{:S(2)}, u32[]{:S(2)}) %collective-permute-start.1) | collective-permute-done | bytes 288 | tf_op jit(solution)/shard_map/ppermute | solution.py:30
  21.6 2.6 %collective-permute-start.2 = (f32[2,32]{1,0:T(2,128)S(1)}, f32[2,32]{1,0:T(2,128)S(1)}, u32[]{:S(2)}, u32[]{:S(2)}) collective-permute-start(f32[2,32]{1,0:T(2,128)S(1)} %mul.196), channel_id=1, source_target_pairs={{0,8},{2,10},{4,12},{6,14},{8,0},{10,2},{12,4},{14,6},{1,9},{3,11}... | collective-permute-start | bytes 776 | tf_op jit(solution)/shard_map/ppermute | solution.py:30
  24.2 1.9 %collective-permute-done.2 = f32[2,32]{1,0:T(2,128)S(1)} collective-permute-done((f32[2,32]{1,0:T(2,128)S(1)}, f32[2,32]{1,0:T(2,128)S(1)}, u32[]{:S(2)}, u32[]{:S(2)}) %collective-permute-start.2) | collective-permute-done | bytes 288 | tf_op jit(solution)/shard_map/ppermute | solution.py:30
  27.4 3.1 %reshape.114 = bf16[2,128,32,64]{3,2,1,0:T(8,128)(2,1)} reshape(bf16[256,2048]{1,0:T(8,128)(2,1)S(1)} %copy-done.7) | data formatting | bytes 2097152 | tf_op jit(solution)/shard_map/reshape | solution.py:73
  30.6 3.3 %copy.35 = bf16[2,128,32,64]{1,3,2,0:T(8,128)(2,1)S(1)} copy(bf16[2,128,32,64]{3,2,1,0:T(8,128)(2,1)} %reshape.114) | data formatting | bytes 2097152 | tf_op jit(solution)/shard_map/reshape | solution.py:73
  34.4 3.4 %bitcast_add_fusion = f32[2,128,32,64]{1,3,2,0:T(8,128)} fusion(bf16[2,128,32,64]{1,3,2,0:T(8,128)(2,1)S(1)} %copy.35, f32[2,32,128]{2,1,0:T(8,128)S(1)} %bitcast_bitcast_fusion.1, f32[2,32,128]{2,1,0:T(8,128)S(1)} %reduce_window_sum.11, f32[2,128,128]{2,1,0:T(8,128)S(1)} %fusion.19, pred[128,128]{1,0:T(8,128)(4,1)S(1)} %iota_compare_fusion, ...), kind=kOutput, calls=%fused_computation.15 | convolution fusion | flops 141033472 | bytes 3358848 | tf_op jit(solution)/shard_map/chij,cjhp->cihp/dot_general | solution.py:78
  37.8 22.7 %collective-permute-done.3 = bf16[2,128,2048]{1,2,0:T(8,128)(2,1)} collective-permute-done((bf16[2,128,2048]{1,2,0:T(8,128)(2,1)}, bf16[2,128,2048]{1,2,0:T(8,128)(2,1)}, u32[]{:S(2)}, u32[]{:S(2)}) %collective-permute-start.3) | collective-permute-done | bytes 1048608 | tf_op jit(solution)/shard_map/ppermute | solution.py:51
  60.6 1.4 convert_element_type.41
  61.9 2.6 %fusion.14 = bf16[2,128,2048]{1,2,0:T(8,128)(2,1)} fusion(f32[2,128,2048]{1,2,0:T(8,128)S(1)} %convert_element_type.41, f32[2,128,2048]{1,2,0:T(8,128)S(1)} %convolution_bitcast_fusion, f32[2,2048]{1,0:T(2,128)S(1)} %mul.216, f32[2,2048]{1,0:T(2,128)S(1)} %mul.213, pred[]{:T(512)S(6)} %eq.13), kind=kLoop, calls=%fused_computation.30 | loop fusion | flops 3145728 | bytes 5275649 | tf_op jit(solution)/shard_map/convert_element_type | solution.py:51
  64.5 1.6 collective-permute-start.4
  66.1 2.2 %reshape.105 = bf16[2,128,2,4,128]{4,3,2,1,0:T(4,128)(2,1)} reshape(bf16[256,1024]{1,0:T(8,128)(2,1)} %param.15) | data formatting | bytes 1048576 | tf_op jit(solution)/shard_map/reshape | solution.py:91
  68.3 1.9 %copy.37 = bf16[2,128,2,4,128]{4,1,3,0,2:T(8,128)(2,1)} copy(bf16[2,128,2,4,128]{4,3,2,1,0:T(4,128)(2,1)} %reshape.105) | data formatting | bytes 1048576 | tf_op jit(solution)/shard_map/reshape | solution.py:91
  70.6 17.6 %collective-permute-done.4 = bf16[2,128,2048]{1,2,0:T(8,128)(2,1)S(1)} collective-permute-done((bf16[2,128,2048]{1,2,0:T(8,128)(2,1)}, bf16[2,128,2048]{1,2,0:T(8,128)(2,1)S(1)}, u32[]{:S(2)}, u32[]{:S(2)}) %collective-permute-start.4) | collective-permute-done | bytes 1048608 | tf_op jit(solution)/shard_map/ppermute | solution.py:51
  88.2 6.1 %fusion.3 = f32[2,128,2048]{1,2,0:T(8,128)} fusion(bf16[2,128,2048]{1,2,0:T(8,128)(2,1)S(1)} %collective-permute-done.4, f32[2,2048]{1,0:T(2,128)S(1)} %mul.220, f32[2,2048]{1,0:T(2,128)S(1)} %mul.211, pred[]{:T(512)S(6)} %eq.14, f32[2,128,2048]{1,2,0:T(8,128)} %copy-done.1, f32[2,128,2048]{1,2,0:T(8,128)S(1)} %convolution_bitcast_fusion, ...), kind=kLoop, calls=%fused_computation.11 | loop fusion | flops 5767168 | bytes 7405570 | tf_op jit(solution)/shard_map/jit(_where)/select_n | solution.py:57
  94.3 1.7 %fusion.18 = (bf16[2,1024,256]{2,1,0:T(8,128)(2,1)S(1)}, bf16[2,1024,256]{2,1,0:T(8,128)(2,1)S(1)}) fusion(bf16[2,1024,512]{2,1,0:T(8,128)(2,1)} %all-gather.2.cloned.1.call-done), kind=kLoop, calls=%fused_computation.49 | loop fusion | bytes 4194304 | tf_op jit(solution)/shard_map/slice | solution.py:95
  96.6 1.6 copy_bitcast_fusion
  100.1 2.0 %collective-permute-start.5 = (bf16[2,128,2048]{1,2,0:T(8,128)(2,1)}, bf16[2,128,2048]{1,2,0:T(8,128)(2,1)}, u32[]{:S(2)}, u32[]{:S(2)}) collective-permute-start(bf16[2,128,2048]{1,2,0:T(8,128)(2,1)} %convert_element_type.46), channel_id=1, source_target_pairs={{0,8},{2,10},{4,12},{6,14},{8,0},{10,2},{12,4},{14,6},{1,9},{3,11}... | collective-permute-start | bytes 3145736 | tf_op jit(solution)/shard_map/ppermute | solution.py:51
  102.3 1.9 %copy.42 = f32[2,128,2048]{2,1,0:T(8,128)} copy(f32[2,128,2048]{1,2,0:T(8,128)S(1)} %bitcast.71) | data formatting | bytes 4194304 | tf_op jit(solution)/shard_map/reshape | solution.py:20
  105.4 3.0 %copy.43 = f32[2,128,2048]{2,1,0:T(8,128)} copy(f32[2,128,2048]{1,2,0:T(8,128)} %bitcast.73) | data formatting | bytes 4194304 | tf_op jit(solution)/shard_map/optimization_barrier | solution.py:54
  108.4 12.0 %shard_map.104 = bf16[2,1024,128]{2,1,0:T(8,128)(2,1)} custom-call(bf16[2,1024,128]{2,1,0:T(8,128)(2,1)} %bitcast.75, bf16[2,2048,128]{2,1,0:T(8,128)(2,1)} %get-tuple-element.59.k_ref, bf16[2,2048,128]{2,1,0:T(8,128)(2,1)} %get-tuple-element.60.v_ref), custom_call_target="tpu_custom_call" | custom-call | flops 2147483648 | bytes 3145728 | tf_op jit(solution)/shard_map/pallas_call | solution.py:147
  120.4 2.2 %copy.40 = bf16[2,128,2,4,128]{4,3,2,1,0:T(4,128)(2,1)} copy(bf16[2,128,2,4,128]{4,1,3,0,2:T(8,128)(2,1)} %bitcast.76) | data formatting | bytes 1048576 | tf_op jit(solution)/shard_map/transpose | solution.py:162
  122.7 2.3 %reshape.110 = bf16[256,1024]{1,0:T(8,128)(2,1)} reshape(bf16[2,128,2,4,128]{4,3,2,1,0:T(4,128)(2,1)} %copy.40) | data formatting | bytes 1048576 | tf_op jit(solution)/shard_map/reshape | solution.py:163
  125.0 18.7 %collective-permute-done.5 = bf16[2,128,2048]{1,2,0:T(8,128)(2,1)} collective-permute-done((bf16[2,128,2048]{1,2,0:T(8,128)(2,1)}, bf16[2,128,2048]{1,2,0:T(8,128)(2,1)}, u32[]{:S(2)}, u32[]{:S(2)}) %collective-permute-start.5) | collective-permute-done | bytes 1048608 | tf_op jit(solution)/shard_map/ppermute | solution.py:51
  143.7 1.4 convert_element_type.47
  145.1 1.9 %add_select_fusion = f32[2,128,2048]{1,2,0:T(8,128)S(1)} fusion(bf16[2,128,2048]{1,2,0:T(8,128)(2,1)S(1)} %copy-done.9, f32[2,128,2048]{1,2,0:T(8,128)S(1)} %copy-done.2, f32[2,128,2048]{1,2,0:T(8,128)S(1)} %convert_element_type.47, f32[2,2048]{1,0:T(2,128)S(1)} %mul.227, f32[2,2048]{1,0:T(2,128)S(1)} %mul.224, f32[2,2048]{1,0:T(2,128)S(1)} %mul.209, ...), kind=kLoop, calls=%fused_computation.1 | loop fusion | flops 4718592 | bytes 7389187 | tf_op jit(solution)/shard_map/jit(_where)/select_n | solution.py:56
  147.1 1.7 %slice_add_fusion.1 = (f32[1,128,2048]{1,2,0:T(8,128)S(1)}, f32[1,128,2048]{1,2,0:T(8,128)S(1)}) fusion(f32[2,128,2048]{1,2,0:T(8,128)S(1)} %add_select_fusion, f32[2048]{0:T(1024)S(1)} %mul.207, f32[1,2048]{1,0:T(1,128)S(1)} %slice-done.1, f32[2,128,2048]{1,2,0:T(8,128)S(1)} %copy-done.4, f32[2,128,2048]{1,2,0:T(8,128)S(1)} %convert_element_type.47, ...), kind=kLoop, calls=%fused_computation.27 | loop fusion | flops 2359296 | bytes 6332417 | tf_op jit(solution)/shard_map/add | solution.py:66
  148.9 1.3 fusion
  150.5 1.2 add_convert_fusion
  (83 shorter events, 10.8 us)
Async XLA Ops:
  7.2 10.3 %copy-start = (bf16[256,128]{1,0:T(8,128)(2,1)S(1)}, bf16[256,128]{1,0:T(8,128)(2,1)}, u32[]{:S(2)}) copy-start(bf16[256,128]{1,0:T(8,128)(2,1)} %param.13) | copy-start | bytes 196612
  7.2 87.1 %all-gather.2.cloned.1.call-start = ((), (), s32[]{:S(2)}) async-start(), calls=%async_computation | async-start | bytes 2359296 | tf_op jit(solution)/shard_map/all_gather | solution.py:177
  11.2 6.8 %collective-permute-start = (f32[2,32]{1,0:T(2,128)S(1)}, f32[2,32]{1,0:T(2,128)S(1)}, u32[]{:S(2)}, u32[]{:S(2)}) collective-permute-start(f32[2,32]{1,0:T(2,128)S(1)} %exp.26), channel_id=1, source_target_pairs={{0,2},{2,0},{4,6},{6,4},{8,10},{10,8},{12,14},{14,12},{1,3},{3,1},... | collective-permute-start | bytes 776 | tf_op jit(solution)/shard_map/ppermute | solution.py:30
  17.9 9.5 %copy-start.7 = (bf16[256,2048]{1,0:T(8,128)(2,1)S(1)}, bf16[256,2048]{1,0:T(8,128)(2,1)}, u32[]{:S(2)}) copy-start(bf16[256,2048]{1,0:T(8,128)(2,1)} %param.9) | copy-start | bytes 3145732
  18.0 3.6 %collective-permute-start.1 = (f32[2,32]{1,0:T(2,128)S(1)}, f32[2,32]{1,0:T(2,128)S(1)}, u32[]{:S(2)}, u32[]{:S(2)}) collective-permute-start(f32[2,32]{1,0:T(2,128)S(1)} %exponential_multiply_fusion), channel_id=1, source_target_pairs={{0,4},{2,6},{4,0},{6,2},{8,12},{10,14},{12,8},{14,10},{1,5},{3,7},... | collective-permute-start | bytes 776 | tf_op jit(solution)/shard_map/ppermute | solution.py:30
  21.6 4.5 %collective-permute-start.2 = (f32[2,32]{1,0:T(2,128)S(1)}, f32[2,32]{1,0:T(2,128)S(1)}, u32[]{:S(2)}, u32[]{:S(2)}) collective-permute-start(f32[2,32]{1,0:T(2,128)S(1)} %mul.196), channel_id=1, source_target_pairs={{0,8},{2,10},{4,12},{6,14},{8,0},{10,2},{12,4},{14,6},{1,9},{3,11}... | collective-permute-start | bytes 776 | tf_op jit(solution)/shard_map/ppermute | solution.py:30
  27.2 33.4 %collective-permute-start.3 = (bf16[2,128,2048]{1,2,0:T(8,128)(2,1)}, bf16[2,128,2048]{1,2,0:T(8,128)(2,1)}, u32[]{:S(2)}, u32[]{:S(2)}) collective-permute-start(bf16[2,128,2048]{1,2,0:T(8,128)(2,1)} %convert_element_type.40), channel_id=1, source_target_pairs={{0,2},{2,0},{4,6},{6,4},{8,10},{10,8},{12,14},{14,12},{1,3},{3,1},... | collective-permute-start | bytes 3145736 | tf_op jit(solution)/shard_map/ppermute | solution.py:51
  30.6 3.7 %copy-start.10 = (bf16[256,128]{1,0:T(8,128)(2,1)S(1)}, bf16[256,128]{1,0:T(8,128)(2,1)}, u32[]{:S(2)}) copy-start(bf16[256,128]{1,0:T(8,128)(2,1)} %param.14) | copy-start | bytes 196612
  30.6 3.8 %copy-start.13 = (f32[32]{0:T(128)S(1)}, f32[32]{0:T(128)}, u32[]{:S(2)}) copy-start(f32[32]{0:T(128)} %param.12) | copy-start | bytes 388
  61.9 2.6 %copy-start.1 = (f32[2,128,2048]{1,2,0:T(8,128)}, f32[2,128,2048]{1,2,0:T(8,128)S(1)}, u32[]{:S(2)}) copy-start(f32[2,128,2048]{1,2,0:T(8,128)S(1)} %convert_element_type.41) | copy-start | bytes 6291460
  64.5 23.7 %collective-permute-start.4 = (bf16[2,128,2048]{1,2,0:T(8,128)(2,1)}, bf16[2,128,2048]{1,2,0:T(8,128)(2,1)S(1)}, u32[]{:S(2)}, u32[]{:S(2)}) collective-permute-start(bf16[2,128,2048]{1,2,0:T(8,128)(2,1)} %fusion.14), channel_id=1, source_target_pairs={{0,4},{2,6},{4,0},{6,2},{8,12},{10,14},{12,8},{14,10},{1,5},{3,7},... | collective-permute-start | bytes 3145736 | tf_op jit(solution)/shard_map/ppermute | solution.py:51
  88.2 6.1 %copy-start.8 = (bf16[2,128,2048]{1,2,0:T(8,128)(2,1)}, bf16[2,128,2048]{1,2,0:T(8,128)(2,1)S(1)}, u32[]{:S(2)}) copy-start(bf16[2,128,2048]{1,2,0:T(8,128)(2,1)S(1)} %collective-permute-done.4) | copy-start | bytes 3145732
  96.6 2.3 %copy-start.3 = (f32[2,128,2048]{1,2,0:T(8,128)S(1)}, f32[2,128,2048]{1,2,0:T(8,128)}, u32[]{:S(2)}) copy-start(f32[2,128,2048]{1,2,0:T(8,128)} %fusion.3) | copy-start | bytes 6291460
  100.1 43.7 %collective-permute-start.5 = (bf16[2,128,2048]{1,2,0:T(8,128)(2,1)}, bf16[2,128,2048]{1,2,0:T(8,128)(2,1)}, u32[]{:S(2)}, u32[]{:S(2)}) collective-permute-start(bf16[2,128,2048]{1,2,0:T(8,128)(2,1)} %convert_element_type.46), channel_id=1, source_target_pairs={{0,8},{2,10},{4,12},{6,14},{8,0},{10,2},{12,4},{14,6},{1,9},{3,11}... | collective-permute-start | bytes 3145736 | tf_op jit(solution)/shard_map/ppermute | solution.py:51
  105.2 3.2 %copy-start.11 = (f32[2,2048]{1,0:T(2,128)}, f32[2,2048]{1,0:T(2,128)S(1)}, u32[]{:S(2)}) copy-start(f32[2,2048]{1,0:T(2,128)S(1)} %mul.236) | copy-start | bytes 49156
  105.4 3.0 %copy-start.12 = (f32[2,2048]{1,0:T(2,128)}, f32[2,2048]{1,0:T(2,128)S(1)}, u32[]{:S(2)}) copy-start(f32[2,2048]{1,0:T(2,128)S(1)} %mul.239) | copy-start | bytes 49156
  122.7 22.4 %copy-start.2 = (f32[2,128,2048]{1,2,0:T(8,128)S(1)}, f32[2,128,2048]{1,2,0:T(8,128)}, u32[]{:S(2)}) copy-start(f32[2,128,2048]{1,2,0:T(8,128)} %copy-done.1) | copy-start | bytes 6291460
  122.7 22.4 %copy-start.9 = (bf16[2,128,2048]{1,2,0:T(8,128)(2,1)S(1)}, bf16[2,128,2048]{1,2,0:T(8,128)(2,1)}, u32[]{:S(2)}) copy-start(bf16[2,128,2048]{1,2,0:T(8,128)(2,1)} %copy-done.8) | copy-start | bytes 3145732
  145.1 2.0 %copy-start.4 = (f32[2,128,2048]{1,2,0:T(8,128)S(1)}, f32[2,128,2048]{1,2,0:T(8,128)}, u32[]{:S(2)}) copy-start(f32[2,128,2048]{1,2,0:T(8,128)} %fusion.3) | copy-start | bytes 6291460
  145.1 2.0 %slice-start = ((f32[2,2048]{1,0:T(2,128)}), f32[1,2048]{1,0:T(1,128)S(1)}, s32[]{:S(2)}) async-start(f32[2,2048]{1,0:T(2,128)} %copy-done.11), calls=%async_computation.1 | async-start | bytes 16384 | tf_op jit(solution)/shard_map/slice | solution.py:67
  145.1 2.0 %slice-start.1 = ((f32[2,2048]{1,0:T(2,128)}), f32[1,2048]{1,0:T(1,128)S(1)}, s32[]{:S(2)}) async-start(f32[2,2048]{1,0:T(2,128)} %copy-done.12), calls=%async_computation.2 | async-start | bytes 16384 | tf_op jit(solution)/shard_map/slice | solution.py:67
  147.1 1.8 %copy-start.5 = (f32[2,128,2048]{2,1,0:T(8,128)S(1)}, f32[2,128,2048]{2,1,0:T(8,128)}, u32[]{:S(2)}) copy-start(f32[2,128,2048]{2,1,0:T(8,128)} %copy.42) | copy-start | bytes 6291460
  148.9 1.6 %copy-start.6 = (f32[2,128,2048]{2,1,0:T(8,128)S(1)}, f32[2,128,2048]{2,1,0:T(8,128)}, u32[]{:S(2)}) copy-start(f32[2,128,2048]{2,1,0:T(8,128)} %copy.43) | copy-start | bytes 6291460
Sparse Core Ops, SparseCore 0:
  14.3 58.9 all-gather.1

commit v6 on v4

--- a/solution.py
+++ b/solution.py
@@ -37,15 +37,15 @@
 
 def entering_states(decay, block_state, count, mine, hooks):
     steps, excl_decay, total_decay = decay_scan(decay, count, mine)
+    total = block_state
     excl = jnp.zeros_like(block_state)
-    total = block_state
     results = {}
     span = 1
-    for step, (lower, excl_a, own_a, got_a) in enumerate(steps):
+    for step, known in enumerate(steps):
         pairs = [(i, i ^ span) for i in range(count)]
         hook = hooks.get(step if step + 1 < len(steps) else -1)
-        if hook is not None:
-            total, args = lax.optimization_barrier((total, hook[1]))
+        total, known, args = lax.optimization_barrier((total, known, hook[1] if hook else ()))
+        lower, excl_a, own_a, got_a = known
         got = lax.ppermute(total.astype(jnp.bfloat16), "seq", pairs).astype(jnp.float32)
         if hook is not None:
             done = hook[0](*args)
@@ -81,85 +81,75 @@
 KEY_CHUNK = 256
 
 
-def attention_prep(queries, kv_piece, my_index):
-    tok_rows = queries.shape[0]
-    slots = tok_rows // BLOCK
-    kv_local = kv_piece.shape[2] // (2 * HD)
-    per_kv = QHEADS // KVHEADS
-    q_flat = queries.reshape(slots, BLOCK, kv_local, per_kv, HD).transpose(2, 0, 3, 1, 4)
-    q_flat = q_flat.reshape(kv_local, slots * per_kv * BLOCK, HD)
-    rows = kv_piece.shape[0] * kv_piece.shape[1]
-    k_all = kv_piece[..., : kv_local * HD].reshape(rows, kv_local, HD).transpose(1, 0, 2)
-    v_all = kv_piece[..., kv_local * HD :].reshape(rows, kv_local, HD).transpose(1, 0, 2)
-    return (q_flat, k_all, v_all)
-
-
 def attention_kernel(q_ref, k_ref, v_ref, o_ref):
     seq_count = lax.axis_size("seq")
     me = lax.axis_index("seq")
     slot = pl.program_id(1)
-    rows = q_ref.shape[1]
+    per_kv = q_ref.shape[1] // HD
+    rows = per_kv * BLOCK
+    held = k_ref.shape[1]
     first = (slot * seq_count + me) * BLOCK
     chunks = (first + BLOCK + KEY_CHUNK - 1) // KEY_CHUNK
-    q = q_ref[0]
+    q = jnp.concatenate([q_ref[:, j * HD : (j + 1) * HD] for j in range(per_kv)], axis=0)
     query_pos = first + lax.broadcasted_iota(jnp.int32, (rows, KEY_CHUNK), 0) % BLOCK
     key_col = lax.broadcasted_iota(jnp.int32, (rows, KEY_CHUNK), 1)
     score_scale = 1.0 / HD**0.5
 
+    def place(c):
+        start = c * KEY_CHUNK
+        return start, start // held, pl.multiple_of(start % held, KEY_CHUNK)
+
     def scores(c):
-        start = pl.multiple_of(c * KEY_CHUNK, KEY_CHUNK)
-        k = k_ref[0, pl.ds(start, KEY_CHUNK), :]
+        start, at_slot, at_row = place(c)
+        k = k_ref[at_slot, pl.ds(at_row, KEY_CHUNK), :]
         s = lax.dot_general(q, k, (((1,), (1,)), ((), ())), preferred_element_type=jnp.float32)
-        visible = start + key_col <= query_pos
-        return s * score_scale, visible, start
+        return s * score_scale, start + key_col <= query_pos
 
     def top_of(c, top):
-        s, visible, unused = scores(c)
+        s, visible = scores(c)
         return jnp.maximum(top, jnp.max(jnp.where(visible, s, NEG), axis=1, keepdims=True))
 
     top = lax.fori_loop(0, chunks, top_of, jnp.full((rows, 1), NEG, jnp.float32))
 
     def add_of(c, carry):
         total, acc = carry
-        s, visible, start = scores(c)
+        s, visible = scores(c)
         probs = jnp.where(visible, jnp.exp(s - top), 0.0)
-        v = v_ref[0, pl.ds(start, KEY_CHUNK), :]
+        unused, at_slot, at_row = place(c)
+        v = v_ref[at_slot, pl.ds(at_row, KEY_CHUNK), :]
         acc = acc + jnp.dot(probs.astype(jnp.bfloat16), v, preferred_element_type=jnp.float32)
         return (total + jnp.sum(probs, axis=1, keepdims=True), acc)
 
     start_carry = (jnp.zeros((rows, 1), jnp.float32), jnp.zeros((rows, HD), jnp.float32))
     total, acc = lax.fori_loop(0, chunks, add_of, start_carry)
-    o_ref[0] = (acc / total).astype(o_ref.dtype)
-
-
-def attention_core(q_flat, k_all, v_all):
-    groups, q_total, unused = q_flat.shape
-    keys = k_all.shape[1]
-    slots = q_total // ((QHEADS // KVHEADS) * BLOCK)
-    block_q = q_total // slots
+    out = (acc / total).astype(o_ref.dtype)
+    for j in range(per_kv):
+        o_ref[:, j * HD : (j + 1) * HD] = out[j * BLOCK : (j + 1) * BLOCK]
+
+
+def attention_core(queries, kv_piece):
+    tok_rows, width = queries.shape
+    slots, held, unused = kv_piece.shape
+    kv_local = kv_piece.shape[2] // (2 * HD)
+    group_width = width // kv_local
+    keys = slots * held
     cost = pl.CostEstimate(
-        flops=4 * groups * q_total * keys * HD,
-        transcendentals=groups * q_total * keys,
-        bytes_accessed=2 * (2 * q_flat.size + k_all.size + v_all.size),
-    )
-    attended = pl.pallas_call(
+        flops=4 * tok_rows * width * keys,
+        transcendentals=tok_rows * width * keys // HD,
+        bytes_accessed=2 * (2 * queries.size + kv_piece.size),
+    )
+    return pl.pallas_call(
         attention_kernel,
-        out_shape=jax.ShapeDtypeStruct(q_flat.shape, jnp.bfloat16),
-        grid=(groups, slots),
+        out_shape=jax.ShapeDtypeStruct(queries.shape, jnp.bfloat16),
+        grid=(kv_local, slots),
         in_specs=[
-            pl.BlockSpec((1, block_q, HD), lambda g, s: (g, s, 0)),
-            pl.BlockSpec((1, keys, HD), lambda g, s: (g, 0, 0)),
-            pl.BlockSpec((1, keys, HD), lambda g, s: (g, 0, 0)),
+            pl.BlockSpec((BLOCK, group_width), lambda g, s: (s, g)),
+            pl.BlockSpec((slots, held, HD), lambda g, s: (0, 0, g)),
+            pl.BlockSpec((slots, held, HD), lambda g, s: (0, 0, kv_local + g)),
         ],
-        out_specs=pl.BlockSpec((1, block_q, HD), lambda g, s: (g, s, 0)),
+        out_specs=pl.BlockSpec((BLOCK, group_width), lambda g, s: (s, g)),
         cost_estimate=cost,
-    )(q_flat, k_all, v_all)
-    per_kv = QHEADS // KVHEADS
-    return (
-        attended.reshape(groups, slots, per_kv, BLOCK, HD)
-        .transpose(1, 3, 0, 2, 4)
-        .reshape(slots * BLOCK, groups * per_kv * HD)
-    )
+    )(queries, kv_piece, kv_piece)
 
 
 def local(x_in, step_size, a_log, d_skip, b_in, c_in, queries, key_rows, values):
@@ -184,10 +174,9 @@
     c_blocks = c_in.reshape(slots, BLOCK, STATE)
     block_state = jnp.einsum("ctn,ctk->cnk", b_blocks, scaled, preferred_element_type=jnp.float32)
     decay = jnp.exp(log_total)
-    prepared = attention_prep(queries, kv_piece, my_index)
     hooks = {
         0: (mamba_base, (x_in, steps, cum, b_blocks, c_blocks, d_skip)),
-        -1: (attention_core, prepared),
+        -1: (attention_core, (queries, kv_piece)),
     }
     incoming, results = entering_states(decay, block_state, seq_count, my_index, hooks)
     carried = jnp.einsum(

time: 185 us -> 152 us (0.82)
  the two profiles are of different devices: /device:TPU:31 before, /device:TPU:0 now
where the time goes in v6:
time: 152 us; the launch traced here: 151 us
  waiting for transfers between devices  68.4 us (45%)
  local copies, waits for them, and re-layouts  20.2 us (13%)
  other arithmetic  19.2 us (13%)
  between operations  14.4 us (9%)
  Pallas kernels  12 us (8%)
  starting transfers between devices  11.8 us (8%)
  matrix products  5.26 us (3%)
    ppermute x3, waiting for transfers between devices, entering_states(): lax.ppermute(total.astype(jnp.bfloat16), 'seq', pairs).astype(jnp.float32)  66.8 us
    pallas_call x1, Pallas kernels, attention_core(): pl.pallas_call(attention_kernel, out_shape=jax.ShapeDtypeStruct(queries.s...  12 us
    ppermute x3, starting transfers between devices, decay_scan(): got = lax.ppermute(total, 'seq', [(i, i ^ span) for i in range(count)])  7.47 us
    reshape x2, local copies, waits for them, and re-layouts, mamba_base(): x_blocks = x_in.reshape(slots, BLOCK, heads, HEADDIM)  6.52 us
    select_n x2, other arithmetic, entering_states(): jnp.where(lower, spread(own_a)[:, None, :] * got + total, spread(got_a)[:...  4.38 us
    ppermute x3, starting transfers between devices, entering_states(): lax.ppermute(total.astype(jnp.bfloat16), 'seq', pairs).astype(jnp.float32)  4.26 us
    dot_general x1, matrix products, mamba_base(): jnp.einsum('chij,cjhp->cihp', mixing, x_blocks, preferred_element_type=jn...  3.35 us
  transfers between devices with their start and end apart: 7, of which 4 were waited for; matrix products, arithmetic and copies ran while one was open for 20% of the time, Pallas kernels for 8%

profile of v6, /device:TPU:0, one launch (start us, length us, event | category | flops | bytes accessed | tf_op | source)
XLA Modules:
  0.0 151.2 jit_solution(16284203643699658109)
XLA Ops:
  7.2 1.7 %pad_maximum_fusion = bf16[2,128,512]{2,1,0:T(8,128)(2,1)} fusion(bf16[2,128,256]{2,1,0:T(8,128)(2,1)} %bitcast.67, bf16[2,128,256]{2,1,0:T(8,128)(2,1)} %bitcast.68), kind=kLoop, calls=%fused_computation.28 | loop fusion | flops 524288 | bytes 524288 | tf_op jit(solution)/shard_map/concatenate | solution.py:161
  9.6 0.8 broadcast_multiply_fusion
  11.2 3.0 %collective-permute-start = (f32[2,32]{1,0:T(2,128)S(1)}, f32[2,32]{1,0:T(2,128)S(1)}, u32[]{:S(2)}, u32[]{:S(2)}) collective-permute-start(f32[2,32]{1,0:T(2,128)S(1)} %exp.26), channel_id=1, source_target_pairs={{0,2},{2,0},{4,6},{6,4},{8,10},{10,8},{12,14},{14,12},{1,3},{3,1},... | collective-permute-start | bytes 776 | tf_op jit(solution)/shard_map/ppermute | solution.py:30
  14.2 0.8 fusion.14
  15.0 0.8 bitcast_bitcast_fusion.1
  15.8 1.5 copy.27
  17.9 1.1 convert_element_type.40
  19.4 3.1 %reshape.90 = bf16[2,128,32,64]{3,2,1,0:T(8,128)(2,1)} reshape(bf16[256,2048]{1,0:T(8,128)(2,1)S(1)} %copy-done.6) | data formatting | bytes 2097152 | tf_op jit(solution)/shard_map/reshape | solution.py:71
  22.6 3.4 %copy.29 = bf16[2,128,32,64]{1,3,2,0:T(8,128)(2,1)S(1)} copy(bf16[2,128,32,64]{3,2,1,0:T(8,128)(2,1)} %reshape.90) | data formatting | bytes 2097152 | tf_op jit(solution)/shard_map/reshape | solution.py:71
  26.0 1.9 %collective-permute-start.2 = (f32[2,32]{1,0:T(2,128)S(1)}, f32[2,32]{1,0:T(2,128)S(1)}, u32[]{:S(2)}, u32[]{:S(2)}) collective-permute-start(f32[2,32]{1,0:T(2,128)S(1)} %exponential_multiply_fusion), channel_id=1, source_target_pairs={{0,4},{2,6},{4,0},{6,2},{8,12},{10,14},{12,8},{14,10},{1,5},{3,7},... | collective-permute-start | bytes 776 | tf_op jit(solution)/shard_map/ppermute | solution.py:30
  28.0 3.3 %bitcast_add_fusion = f32[2,128,32,64]{1,3,2,0:T(8,128)} fusion(bf16[2,128,32,64]{1,3,2,0:T(8,128)(2,1)S(1)} %copy.29, f32[2,32,128]{2,1,0:T(8,128)S(1)} %bitcast_bitcast_fusion.1, f32[2,32,128]{2,1,0:T(8,128)S(1)} %reduce_window_sum.11, f32[2,128,128]{2,1,0:T(8,128)S(1)} %fusion.17, pred[128,128]{1,0:T(8,128)(4,1)S(1)} %iota_compare_fusion, ...), kind=kOutput, calls=%fused_computation.15 | convolution fusion | flops 141033472 | bytes 3358848 | tf_op jit(solution)/shard_map/chij,cjhp->cihp/dot_general | solution.py:76
  31.4 2.6 %collective-permute-start.3 = (f32[2,32]{1,0:T(2,128)S(1)}, f32[2,32]{1,0:T(2,128)S(1)}, u32[]{:S(2)}, u32[]{:S(2)}) collective-permute-start(f32[2,32]{1,0:T(2,128)S(1)} %mul.201), channel_id=1, source_target_pairs={{0,8},{2,10},{4,12},{6,14},{8,0},{10,2},{12,4},{14,6},{1,9},{3,11}... | collective-permute-start | bytes 776 | tf_op jit(solution)/shard_map/ppermute | solution.py:30
  34.3 1.6 %collective-permute-done.3 = f32[2,32]{1,0:T(2,128)S(1)} collective-permute-done((f32[2,32]{1,0:T(2,128)S(1)}, f32[2,32]{1,0:T(2,128)S(1)}, u32[]{:S(2)}, u32[]{:S(2)}) %collective-permute-start.3) | collective-permute-done | bytes 288 | tf_op jit(solution)/shard_map/ppermute | solution.py:30
  35.9 12.2 %collective-permute-done.1 = bf16[2,128,2048]{1,2,0:T(8,128)(2,1)} collective-permute-done((bf16[2,128,2048]{1,2,0:T(8,128)(2,1)}, bf16[2,128,2048]{1,2,0:T(8,128)(2,1)}, u32[]{:S(2)}, u32[]{:S(2)}) %collective-permute-start.1) | collective-permute-done | bytes 1048608 | tf_op jit(solution)/shard_map/ppermute | solution.py:49
  48.1 1.4 convert_element_type.41
  49.5 1.3 add_select_fusion.2
  50.8 1.3 copy-done.1
  52.3 1.8 %collective-permute-start.4 = (bf16[2,128,2048]{1,2,0:T(8,128)(2,1)S(1)}, bf16[2,128,2048]{1,2,0:T(8,128)(2,1)S(1)}, u32[]{:S(2)}, u32[]{:S(2)}) collective-permute-start(bf16[2,128,2048]{1,2,0:T(8,128)(2,1)S(1)} %convert_element_type.44), channel_id=1, source_target_pairs={{0,4},{2,6},{4,0},{6,2},{8,12},{10,14},{12,8},{14,10},{1,5},{3,7},... | collective-permute-start | bytes 3145736 | tf_op jit(solution)/shard_map/ppermute | solution.py:49
  54.4 30.8 %collective-permute-done.4 = bf16[2,128,2048]{1,2,0:T(8,128)(2,1)S(1)} collective-permute-done((bf16[2,128,2048]{1,2,0:T(8,128)(2,1)S(1)}, bf16[2,128,2048]{1,2,0:T(8,128)(2,1)S(1)}, u32[]{:S(2)}, u32[]{:S(2)}) %collective-permute-start.4) | collective-permute-done | bytes 1048608 | tf_op jit(solution)/shard_map/ppermute | solution.py:49
  85.3 3.1 %fusion.3 = f32[2,128,2048]{1,2,0:T(8,128)S(1)} fusion(f32[2,128,2048]{1,2,0:T(8,128)} %copy-done.1, bf16[2,128,2048]{1,2,0:T(8,128)(2,1)S(1)} %collective-permute-done.4, f32[2,2048]{1,0:T(2,128)S(1)} %mul.217, f32[2,2048]{1,0:T(2,128)S(1)} %mul.214, pred[]{:T(512)S(6)} %eq.15), kind=kLoop, calls=%fused_computation.11 | loop fusion | flops 3145728 | bytes 5275649 | tf_op jit(solution)/shard_map/jit(_where)/select_n | solution.py:55
  88.4 1.1 convert_element_type.46
  89.5 2.4 %collective-permute-start.5 = (bf16[2,128,2048]{1,2,0:T(8,128)(2,1)}, bf16[2,128,2048]{1,2,0:T(8,128)(2,1)}, u32[]{:S(2)}, u32[]{:S(2)}) collective-permute-start(bf16[2,128,2048]{1,2,0:T(8,128)(2,1)} %convert_element_type.46), channel_id=1, source_target_pairs={{0,8},{2,10},{4,12},{6,14},{8,0},{10,2},{12,4},{14,6},{1,9},{3,11}... | collective-permute-start | bytes 3145736 | tf_op jit(solution)/shard_map/ppermute | solution.py:49
  92.0 1.5 %broadcast_in_dim.85 = f32[2,128,32,64]{1,3,2,0:T(8,128)} broadcast(f32[2,128,32]{1,2,0:T(8,128)S(1)} %exponential_bitcast_fusion), dimensions={0,1,2} | broadcast | bytes 2129920 | tf_op jit(solution)/shard_map/broadcast_in_dim | solution.py:20
  93.5 2.9 %copy.32 = f32[2,128,2048]{2,1,0:T(8,128)} copy(f32[2,128,2048]{1,2,0:T(8,128)} %bitcast.61) | data formatting | bytes 4194304 | tf_op jit(solution)/shard_map/reshape | solution.py:20
  97.2 3.0 %copy.33 = f32[2,128,2048]{2,1,0:T(8,128)} copy(f32[2,128,2048]{1,2,0:T(8,128)} %bitcast.63) | data formatting | bytes 4194304 | tf_op jit(solution)/shard_map/optimization_barrier | solution.py:52
  100.7 12.0 %shard_map.104 = bf16[256,1024]{1,0:T(8,128)(2,1)} custom-call(bf16[256,1024]{1,0:T(8,128)(2,1)} %q_ref, bf16[2,1024,512]{2,1,0:T(8,128)(2,1)} %all-gather.2.cloned.1.call-done.k_ref.v_ref, bf16[2,1024,512]{2,1,0:T(8,128)(2,1)} %all-gather.2.cloned.1.call-done.k_ref.v_ref), custom_call_target="tpu_custom_call" | custom-call | flops 2147483648 | bytes 3145728 | tf_op jit(solution)/shard_map/pallas_call | solution.py:141
  112.7 23.8 %collective-permute-done.5 = bf16[2,128,2048]{1,2,0:T(8,128)(2,1)} collective-permute-done((bf16[2,128,2048]{1,2,0:T(8,128)(2,1)}, bf16[2,128,2048]{1,2,0:T(8,128)(2,1)}, u32[]{:S(2)}, u32[]{:S(2)}) %collective-permute-start.5) | collective-permute-done | bytes 1048608 | tf_op jit(solution)/shard_map/ppermute | solution.py:49
  136.4 1.4 convert_element_type.47
  137.8 1.9 %add_select_fusion = f32[2,128,2048]{1,2,0:T(8,128)S(1)} fusion(bf16[2,128,2048]{1,2,0:T(8,128)(2,1)S(1)} %collective-permute-done.4, f32[2,128,2048]{1,2,0:T(8,128)S(1)} %copy-done.3, f32[2,128,2048]{1,2,0:T(8,128)S(1)} %convert_element_type.47, f32[2,2048]{1,0:T(2,128)S(1)} %mul.226, f32[2,2048]{1,0:T(2,128)S(1)} %mul.223, f32[2,2048]{1,0:T(2,128)S(1)} %mul.220, ...), kind=kLoop, calls=%fused_computation.1 | loop fusion | flops 4718592 | bytes 7389187 | tf_op jit(solution)/shard_map/jit(_where)/select_n | solution.py:54
  139.8 1.7 %slice_add_fusion.1 = (f32[1,128,2048]{1,2,0:T(8,128)S(1)}, f32[1,128,2048]{1,2,0:T(8,128)S(1)}) fusion(f32[2,128,2048]{1,2,0:T(8,128)S(1)} %add_select_fusion, f32[2048]{0:T(1024)S(1)} %mul.206, f32[1,2048]{1,0:T(1,128)S(1)} %slice-done.1, f32[2,128,2048]{1,2,0:T(8,128)S(1)} %fusion.3, f32[2,128,2048]{1,2,0:T(8,128)S(1)} %convert_element_type.47, ...), kind=kLoop, calls=%fused_computation.27 | loop fusion | flops 2359296 | bytes 6332417 | tf_op jit(solution)/shard_map/add | solution.py:64
  141.6 1.3 fusion
  143.2 1.2 add_convert_fusion
  (70 shorter events, 4.9 us)
Async XLA Ops:
  7.2 10.3 %copy-start = (bf16[256,128]{1,0:T(8,128)(2,1)S(1)}, bf16[256,128]{1,0:T(8,128)(2,1)}, u32[]{:S(2)}) copy-start(bf16[256,128]{1,0:T(8,128)(2,1)} %param.13) | copy-start | bytes 196612
  7.2 81.2 %all-gather.2.cloned.1.call-start = ((), (), s32[]{:S(2)}) async-start(), calls=%async_computation | async-start | bytes 2359296 | tf_op jit(solution)/shard_map/all_gather | solution.py:165
  11.2 6.8 %collective-permute-start = (f32[2,32]{1,0:T(2,128)S(1)}, f32[2,32]{1,0:T(2,128)S(1)}, u32[]{:S(2)}, u32[]{:S(2)}) collective-permute-start(f32[2,32]{1,0:T(2,128)S(1)} %exp.26), channel_id=1, source_target_pairs={{0,2},{2,0},{4,6},{6,4},{8,10},{10,8},{12,14},{14,12},{1,3},{3,1},... | collective-permute-start | bytes 776 | tf_op jit(solution)/shard_map/ppermute | solution.py:30
  17.9 1.6 %copy-start.6 = (bf16[256,2048]{1,0:T(8,128)(2,1)S(1)}, bf16[256,2048]{1,0:T(8,128)(2,1)}, u32[]{:S(2)}) copy-start(bf16[256,2048]{1,0:T(8,128)(2,1)} %param.9) | copy-start | bytes 3145732
  19.0 29.1 %collective-permute-start.1 = (bf16[2,128,2048]{1,2,0:T(8,128)(2,1)}, bf16[2,128,2048]{1,2,0:T(8,128)(2,1)}, u32[]{:S(2)}, u32[]{:S(2)}) collective-permute-start(bf16[2,128,2048]{1,2,0:T(8,128)(2,1)} %convert_element_type.40), channel_id=1, source_target_pairs={{0,2},{2,0},{4,6},{6,4},{8,10},{10,8},{12,14},{14,12},{1,3},{3,1},... | collective-permute-start | bytes 3145736 | tf_op jit(solution)/shard_map/ppermute | solution.py:49
  22.6 5.3 %copy-start.7 = (bf16[256,128]{1,0:T(8,128)(2,1)S(1)}, bf16[256,128]{1,0:T(8,128)(2,1)}, u32[]{:S(2)}) copy-start(bf16[256,128]{1,0:T(8,128)(2,1)} %param.14) | copy-start | bytes 196612
  22.6 5.4 %copy-start.10 = (f32[32]{0:T(128)S(1)}, f32[32]{0:T(128)}, u32[]{:S(2)}) copy-start(f32[32]{0:T(128)} %param.12) | copy-start | bytes 388
  26.0 5.4 %collective-permute-start.2 = (f32[2,32]{1,0:T(2,128)S(1)}, f32[2,32]{1,0:T(2,128)S(1)}, u32[]{:S(2)}, u32[]{:S(2)}) collective-permute-start(f32[2,32]{1,0:T(2,128)S(1)} %exponential_multiply_fusion), channel_id=1, source_target_pairs={{0,4},{2,6},{4,0},{6,2},{8,12},{10,14},{12,8},{14,10},{1,5},{3,7},... | collective-permute-start | bytes 776 | tf_op jit(solution)/shard_map/ppermute | solution.py:30
  31.4 4.5 %collective-permute-start.3 = (f32[2,32]{1,0:T(2,128)S(1)}, f32[2,32]{1,0:T(2,128)S(1)}, u32[]{:S(2)}, u32[]{:S(2)}) collective-permute-start(f32[2,32]{1,0:T(2,128)S(1)} %mul.201), channel_id=1, source_target_pairs={{0,8},{2,10},{4,12},{6,14},{8,0},{10,2},{12,4},{14,6},{1,9},{3,11}... | collective-permute-start | bytes 776 | tf_op jit(solution)/shard_map/ppermute | solution.py:30
  49.5 1.3 copy-start.2
  50.8 1.3 copy-start.1
  52.3 33.0 %collective-permute-start.4 = (bf16[2,128,2048]{1,2,0:T(8,128)(2,1)S(1)}, bf16[2,128,2048]{1,2,0:T(8,128)(2,1)S(1)}, u32[]{:S(2)}, u32[]{:S(2)}) collective-permute-start(bf16[2,128,2048]{1,2,0:T(8,128)(2,1)S(1)} %convert_element_type.44), channel_id=1, source_target_pairs={{0,4},{2,6},{4,0},{6,2},{8,12},{10,14},{12,8},{14,10},{1,5},{3,7},... | collective-permute-start | bytes 3145736 | tf_op jit(solution)/shard_map/ppermute | solution.py:49
  89.5 46.9 %collective-permute-start.5 = (bf16[2,128,2048]{1,2,0:T(8,128)(2,1)}, bf16[2,128,2048]{1,2,0:T(8,128)(2,1)}, u32[]{:S(2)}, u32[]{:S(2)}) collective-permute-start(bf16[2,128,2048]{1,2,0:T(8,128)(2,1)} %convert_element_type.46), channel_id=1, source_target_pairs={{0,8},{2,10},{4,12},{6,14},{8,0},{10,2},{12,4},{14,6},{1,9},{3,11}... | collective-permute-start | bytes 3145736 | tf_op jit(solution)/shard_map/ppermute | solution.py:49
  100.5 12.2 %copy-start.8 = (f32[2,2048]{1,0:T(2,128)}, f32[2,2048]{1,0:T(2,128)S(1)}, u32[]{:S(2)}) copy-start(f32[2,2048]{1,0:T(2,128)S(1)} %mul.236) | copy-start | bytes 49156
  100.6 12.0 %copy-start.9 = (f32[2,2048]{1,0:T(2,128)}, f32[2,2048]{1,0:T(2,128)S(1)}, u32[]{:S(2)}) copy-start(f32[2,2048]{1,0:T(2,128)S(1)} %mul.239) | copy-start | bytes 49156
  112.7 25.1 %copy-start.3 = (f32[2,128,2048]{1,2,0:T(8,128)S(1)}, f32[2,128,2048]{1,2,0:T(8,128)}, u32[]{:S(2)}) copy-start(f32[2,128,2048]{1,2,0:T(8,128)} %copy-done.2) | copy-start | bytes 6291460
  137.8 2.0 %slice-start = ((f32[2,2048]{1,0:T(2,128)}), f32[1,2048]{1,0:T(1,128)S(1)}, s32[]{:S(2)}) async-start(f32[2,2048]{1,0:T(2,128)} %copy-done.8), calls=%async_computation.1 | async-start | bytes 16384 | tf_op jit(solution)/shard_map/slice | solution.py:65
  137.8 2.0 %slice-start.1 = ((f32[2,2048]{1,0:T(2,128)}), f32[1,2048]{1,0:T(1,128)S(1)}, s32[]{:S(2)}) async-start(f32[2,2048]{1,0:T(2,128)} %copy-done.9), calls=%async_computation.2 | async-start | bytes 16384 | tf_op jit(solution)/shard_map/slice | solution.py:65
  139.8 1.8 %copy-start.4 = (f32[2,128,2048]{2,1,0:T(8,128)S(1)}, f32[2,128,2048]{2,1,0:T(8,128)}, u32[]{:S(2)}) copy-start(f32[2,128,2048]{2,1,0:T(8,128)} %copy.32) | copy-start | bytes 6291460
  141.6 1.6 %copy-start.5 = (f32[2,128,2048]{2,1,0:T(8,128)S(1)}, f32[2,128,2048]{2,1,0:T(8,128)}, u32[]{:S(2)}) copy-start(f32[2,128,2048]{2,1,0:T(8,128)} %copy.33) | copy-start | bytes 6291460
Sparse Core Ops, SparseCore 0:
  14.3 55.9 all-gather.1

commit v7 on v6

--- a/solution.py
+++ b/solution.py
@@ -35,35 +35,49 @@
     return steps, excl, total
 
 
-def entering_states(decay, block_state, count, mine, hooks):
+def entering_states(decay, block_state, count, mine, hooks, parts):
     steps, excl_decay, total_decay = decay_scan(decay, count, mine)
-    total = block_state
-    excl = jnp.zeros_like(block_state)
+    heads, width = decay.shape[1], block_state.shape[2]
+    head_cut, width_cut = heads // parts, width // parts
+    totals = [block_state[:, :, j * width_cut : (j + 1) * width_cut] for j in range(parts)]
+    excls = [jnp.zeros_like(t) for t in totals]
     results = {}
     span = 1
-    for step, known in enumerate(steps):
+    for step, known_all in enumerate(steps):
         pairs = [(i, i ^ span) for i in range(count)]
-        hook = hooks.get(step if step + 1 < len(steps) else -1)
-        total, known, args = lax.optimization_barrier((total, known, hook[1] if hook else ()))
-        lower, excl_a, own_a, got_a = known
-        got = lax.ppermute(total.astype(jnp.bfloat16), "seq", pairs).astype(jnp.float32)
-        if hook is not None:
-            done = hook[0](*args)
-            got, done = lax.optimization_barrier((got, done))
-            results[hook[0].__name__] = done
-        excl = jnp.where(lower, spread(excl_a)[:, None, :] * got + excl, excl)
-        total = jnp.where(
-            lower,
-            spread(own_a)[:, None, :] * got + total,
-            spread(got_a)[:, None, :] * total + got,
-        )
+        before = ()
+        for j in range(parts):
+            hook = hooks.get((j, step if step + 1 < len(steps) else -1))
+            totals[j], known, args, unused = lax.optimization_barrier(
+                (totals[j], known_all, hook[1] if hook else (), before)
+            )
+            lower, excl_a, own_a, got_a = [
+                v if v.ndim == 0 else v[:, j * head_cut : (j + 1) * head_cut] for v in known
+            ]
+            got = lax.ppermute(totals[j].astype(jnp.bfloat16), "seq", pairs).astype(jnp.float32)
+            if hook is not None:
+                done = hook[0](*args)
+                got, done = lax.optimization_barrier((got, done))
+                results[hook[0].__name__] = done
+            excls[j] = jnp.where(lower, spread(excl_a)[:, None, :] * got + excls[j], excls[j])
+            totals[j] = jnp.where(
+                lower,
+                spread(own_a)[:, None, :] * got + totals[j],
+                spread(got_a)[:, None, :] * totals[j] + got,
+            )
+            before = got
         span *= 2
-    carry = jnp.zeros_like(block_state[0])
     entering = []
-    for slot in range(decay.shape[0]):
-        entering.append(spread(excl_decay[slot])[None, :] * carry + excl[slot])
-        carry = spread(total_decay[slot])[None, :] * carry + total[slot]
-    return (jnp.stack(entering, axis=0), results)
+    for j in range(parts):
+        carry = jnp.zeros_like(totals[j][0])
+        rows = []
+        for slot in range(decay.shape[0]):
+            a_excl = excl_decay[slot, j * head_cut : (j + 1) * head_cut]
+            a_total = total_decay[slot, j * head_cut : (j + 1) * head_cut]
+            rows.append(spread(a_excl)[None, :] * carry + excls[j][slot])
+            carry = spread(a_total)[None, :] * carry + totals[j][slot]
+        entering.append(jnp.stack(rows, axis=0))
+    return (entering, results)
 
 
 def mamba_base(x_in, steps, cum, b_blocks, c_blocks, d_skip):
@@ -174,13 +188,19 @@
     c_blocks = c_in.reshape(slots, BLOCK, STATE)
     block_state = jnp.einsum("ctn,ctk->cnk", b_blocks, scaled, preferred_element_type=jnp.float32)
     decay = jnp.exp(log_total)
+    parts = 2 if heads % 2 == 0 else 1
     hooks = {
-        0: (mamba_base, (x_in, steps, cum, b_blocks, c_blocks, d_skip)),
-        -1: (attention_core, (queries, kv_piece)),
+        (0, 0): (mamba_base, (x_in, steps, cum, b_blocks, c_blocks, d_skip)),
+        (0, -1): (attention_core, (queries, kv_piece)),
     }
-    incoming, results = entering_states(decay, block_state, seq_count, my_index, hooks)
-    carried = jnp.einsum(
-        "ctn,cnk->ctk", c_blocks.astype(jnp.float32), incoming, precision=lax.Precision.HIGHEST
+    incoming, results = entering_states(decay, block_state, seq_count, my_index, hooks, parts)
+    c_wide = c_blocks.astype(jnp.float32)
+    carried = jnp.concatenate(
+        [
+            jnp.einsum("ctn,cnk->ctk", c_wide, part, precision=lax.Precision.HIGHEST)
+            for part in incoming
+        ],
+        axis=2,
     )
     carried = carried * spread(jnp.exp(cum).transpose(0, 2, 1))
     mamba_out = (results["mamba_base"] + carried).astype(jnp.bfloat16).reshape(tok_rows, width)

time: 152 us -> 147 us (0.967)
  waiting for transfers between devices: 68.4 us -> 52 us
  other arithmetic: 19.2 us -> 27.9 us
  starting transfers between devices: 11.8 us -> 19.3 us
  local copies, waits for them, and re-layouts: 20.2 us -> 15.4 us
    ppermute x3 -> x6, waiting for transfers between devices: 66.8 us -> 51.4 us  [entering_states(): lax.ppermute(totals[j].astype(jnp.bfloat16), 'seq', pairs)]
    ppermute x3 -> x6, starting transfers between devices: 4.26 us -> 11.5 us  [entering_states(): lax.ppermute(totals[j].astype(jnp.bfloat16), 'seq', pairs)]
    select_n x3 -> x6, other arithmetic: 6.33 us -> 11.9 us  [the longest x4 7.81 us: entering_states(): jnp.where(lower, spread(own_a)[:, None, :] * got + totals[j], spread(got_...]
    convert_element_type x5 -> x9, other arithmetic: 5.08 us -> 9.84 us  [the longest x6 6.42 us: entering_states(): totals[j].astype(jnp.bfloat16)]
    optimization_barrier x1 -> x0, local copies, waits for them, and re-layouts: 2.96 us -> none  [entering_states(): got, done = lax.optimization_barrier((got, done))]
    reshape x1 -> x0, local copies, waits for them, and re-layouts: 2.91 us -> none  [spread(): return jnp.repeat(a, HEADDIM, axis=-1)]
    ppermute x3, waiting for transfers between devices: 1.58 us -> 0.01 us  [decay_scan(): got = lax.ppermute(total, 'seq', [(i, i ^ span) for i in range(count)])]
  transfers between devices with their start and end apart: 7 -> 10, of which waited for: 4 -> 5; matrix products, arithmetic and copies ran while one was open for 20% -> 25% of each run, Pallas kernels for 8% -> 8%
where the time goes in v7:
time: 147 us; the launch traced here: 146 us
  waiting for transfers between devices  52 us (35%)
  other arithmetic  27.9 us (19%)
  starting transfers between devices  19.3 us (13%)
  local copies, waits for them, and re-layouts  15.4 us (10%)
  between operations  14.5 us (10%)
  Pallas kernels  12 us (8%)
  matrix products  5.14 us (3%)
    ppermute x6, waiting for transfers between devices, entering_states(): lax.ppermute(totals[j].astype(jnp.bfloat16), 'seq', pairs)  51.4 us
    pallas_call x1, Pallas kernels, attention_core(): pl.pallas_call(attention_kernel, out_shape=jax.ShapeDtypeStruct(queries.s...  12 us
    ppermute x6, starting transfers between devices, entering_states(): lax.ppermute(totals[j].astype(jnp.bfloat16), 'seq', pairs)  11.5 us
    select_n x4, other arithmetic, entering_states(): jnp.where(lower, spread(own_a)[:, None, :] * got + totals[j], spread(got_...  7.81 us
    ppermute x3, starting transfers between devices, decay_scan(): got = lax.ppermute(total, 'seq', [(i, i ^ span) for i in range(count)])  7.7 us
    reshape x2, local copies, waits for them, and re-layouts, mamba_base(): x_blocks = x_in.reshape(slots, BLOCK, heads, HEADDIM)  6.49 us
    convert_element_type x6, other arithmetic, entering_states(): totals[j].astype(jnp.bfloat16)  6.42 us
    select_n x2, other arithmetic, entering_states(): jnp.where(lower, spread(excl_a)[:, None, :] * got + excls[j], excls[j])  4.08 us
  transfers between devices with their start and end apart: 10, of which 5 were waited for; matrix products, arithmetic and copies ran while one was open for 25% of the time, Pallas kernels for 8%

profile of v7, /device:TPU:0, one launch (start us, length us, event | category | flops | bytes accessed | tf_op | source)
XLA Modules:
  0.0 146.2 jit_solution(9977944453830531648)
XLA Ops:
  7.2 1.7 %pad_maximum_fusion = bf16[2,128,512]{2,1,0:T(8,128)(2,1)} fusion(bf16[2,128,256]{2,1,0:T(8,128)(2,1)} %bitcast.84, bf16[2,128,256]{2,1,0:T(8,128)(2,1)} %bitcast.85), kind=kLoop, calls=%fused_computation.44 | loop fusion | flops 524288 | bytes 524288 | tf_op jit(solution)/shard_map/concatenate | solution.py:175
  11.2 3.0 %collective-permute-start = (f32[2,32]{1,0:T(2,128)S(1)}, f32[2,32]{1,0:T(2,128)S(1)}, u32[]{:S(2)}, u32[]{:S(2)}) collective-permute-start(f32[2,32]{1,0:T(2,128)S(1)} %exp.26), channel_id=1, source_target_pairs={{0,2},{2,0},{4,6},{6,4},{8,10},{10,8},{12,14},{14,12},{1,3},{3,1},... | collective-permute-start | bytes 776 | tf_op jit(solution)/shard_map/ppermute | solution.py:30
  14.2 1.5 %copy.22 = f32[2,128,2048]{1,2,0:T(8,128)S(1)} copy(bf16[2,128,2048]{2,1,0:T(8,128)(2,1)} %bitcast.78) | data formatting | bytes 3145728 | tf_op jit(solution)/shard_map/convert_element_type | solution.py:186
  16.6 1.4 copy-done.6
  18.0 3.1 %reshape.126 = bf16[2,128,32,64]{3,2,1,0:T(8,128)(2,1)} reshape(bf16[256,2048]{1,0:T(8,128)(2,1)S(1)} %copy-done.6) | data formatting | bytes 2097152 | tf_op jit(solution)/shard_map/reshape | solution.py:85
  21.1 3.4 %copy.24 = bf16[2,128,32,64]{1,3,2,0:T(8,128)(2,1)S(1)} copy(bf16[2,128,32,64]{3,2,1,0:T(8,128)(2,1)} %reshape.126) | data formatting | bytes 2097152 | tf_op jit(solution)/shard_map/reshape | solution.py:85
  25.5 2.0 %collective-permute-start.2 = (f32[2,32]{1,0:T(2,128)S(1)}, f32[2,32]{1,0:T(2,128)S(1)}, u32[]{:S(2)}, u32[]{:S(2)}) collective-permute-start(f32[2,32]{1,0:T(2,128)S(1)} %exponential_multiply_fusion), channel_id=1, source_target_pairs={{0,4},{2,6},{4,0},{6,2},{8,12},{10,14},{12,8},{14,10},{1,5},{3,7},... | collective-permute-start | bytes 776 | tf_op jit(solution)/shard_map/ppermute | solution.py:30
  27.7 3.4 %bitcast_add_fusion = f32[2,128,32,64]{1,3,2,0:T(8,128)} fusion(bf16[2,128,32,64]{1,3,2,0:T(8,128)(2,1)S(1)} %copy.24, f32[2,32,128]{2,1,0:T(8,128)S(1)} %bitcast_bitcast_fusion.1, f32[2,32,128]{2,1,0:T(8,128)S(1)} %reduce_window_sum.11, f32[2,128,128]{2,1,0:T(8,128)S(1)} %fusion.26, pred[128,128]{1,0:T(8,128)(4,1)S(1)} %iota_compare_fusion, ...), kind=kOutput, calls=%fused_computation.6 | convolution fusion | flops 141033472 | bytes 3358848 | tf_op jit(solution)/shard_map/chij,cjhp->cihp/dot_general | solution.py:90
  31.4 2.7 %collective-permute-start.3 = (f32[2,32]{1,0:T(2,128)S(1)}, f32[2,32]{1,0:T(2,128)S(1)}, u32[]{:S(2)}, u32[]{:S(2)}) collective-permute-start(f32[2,32]{1,0:T(2,128)S(1)} %mul.334), channel_id=1, source_target_pairs={{0,8},{2,10},{4,12},{6,14},{8,0},{10,2},{12,4},{14,6},{1,9},{3,11}... | collective-permute-start | bytes 776 | tf_op jit(solution)/shard_map/ppermute | solution.py:30
  34.0 5.0 %collective-permute-done.1 = bf16[2,128,1024]{1,2,0:T(8,128)(2,1)} collective-permute-done((bf16[2,128,1024]{1,2,0:T(8,128)(2,1)}, bf16[2,128,1024]{1,2,0:T(8,128)(2,1)}, u32[]{:S(2)}, u32[]{:S(2)}) %collective-permute-start.1) | collective-permute-done | bytes 524320 | tf_op jit(solution)/shard_map/ppermute | solution.py:57
  39.1 1.2 convert_element_type.59
  41.4 1.8 %add_select_fusion.5 = f32[2,128,1024]{1,2,0:T(8,128)S(1)} fusion(f32[2,128,1024]{1,2,0:T(8,128)S(1)} %convert_element_type.59, f32[2,128,1024]{1,2,0:T(8,128)} %copy-done.2, f32[2,1024]{1,0:T(2,128)S(1)} %mul.344, f32[2,1024]{1,0:T(2,128)S(1)} %mul.341, pred[]{:T(512)S(6)} %eq.13), kind=kLoop, calls=%fused_computation.39 | loop fusion | flops 1310720 | bytes 3162113 | tf_op jit(solution)/shard_map/jit(_where)/select_n | solution.py:63
  43.2 0.9 convert_element_type.62
  44.1 1.8 %collective-permute-start.4 = (bf16[2,128,1024]{1,2,0:T(8,128)(2,1)}, bf16[2,128,1024]{1,2,0:T(8,128)(2,1)}, u32[]{:S(2)}, u32[]{:S(2)}) collective-permute-start(bf16[2,128,1024]{1,2,0:T(8,128)(2,1)} %convert_element_type.62), channel_id=1, source_target_pairs={{0,4},{2,6},{4,0},{6,2},{8,12},{10,14},{12,8},{14,10},{1,5},{3,7},... | collective-permute-start | bytes 1572872 | tf_op jit(solution)/shard_map/ppermute | solution.py:57
  46.3 17.9 %collective-permute-done.6 = bf16[2,128,1024]{1,2,0:T(8,128)(2,1)} collective-permute-done((bf16[2,128,1024]{1,2,0:T(8,128)(2,1)}, bf16[2,128,1024]{1,2,0:T(8,128)(2,1)}, u32[]{:S(2)}, u32[]{:S(2)}) %collective-permute-start.6) | collective-permute-done | bytes 524320 | tf_op jit(solution)/shard_map/ppermute | solution.py:57
  64.2 1.8 %fusion.11 = f32[2,128,1024]{1,2,0:T(8,128)S(1)} fusion(f32[2,128,1024]{1,2,0:T(8,128)} %copy-done.1, bf16[2,128,1024]{1,2,0:T(8,128)(2,1)} %collective-permute-done.6, f32[2,1024]{1,0:T(2,128)S(1)} %mul.383, f32[2,1024]{1,0:T(2,128)S(1)} %mul.380, pred[]{:T(512)S(6)} %eq.13), kind=kLoop, calls=%fused_computation.28 | loop fusion | flops 1572864 | bytes 2637825 | tf_op jit(solution)/shard_map/jit(_where)/select_n | solution.py:63
  67.0 1.5 %collective-permute-start.7 = (bf16[2,128,1024]{1,2,0:T(8,128)(2,1)}, bf16[2,128,1024]{1,2,0:T(8,128)(2,1)}, u32[]{:S(2)}, u32[]{:S(2)}) collective-permute-start(bf16[2,128,1024]{1,2,0:T(8,128)(2,1)} %convert_element_type.68), channel_id=1, source_target_pairs={{0,4},{2,6},{4,0},{6,2},{8,12},{10,14},{12,8},{14,10},{1,5},{3,7},... | collective-permute-start | bytes 1572872 | tf_op jit(solution)/shard_map/ppermute | solution.py:57
  68.9 2.5 %add_select_fusion.4 = f32[2,128,1024]{1,2,0:T(8,128)} fusion(f32[2,128,1024]{1,2,0:T(8,128)S(1)} %add_select_fusion.5, f32[2,1024]{1,0:T(2,128)S(1)} %mul.350, bf16[2,128,1024]{1,2,0:T(8,128)(2,1)} %collective-permute-done.4, f32[2,1024]{1,0:T(2,128)S(1)} %mul.347, pred[]{:T(512)S(6)} %eq.15), kind=kLoop, calls=%fused_computation.38 | loop fusion | flops 1572864 | bytes 2637825 | tf_op jit(solution)/shard_map/jit(_where)/select_n | solution.py:63
  72.1 2.1 %convert_element_type.64 = bf16[2,128,1024]{1,2,0:T(8,128)(2,1)} convert(f32[2,128,1024]{1,2,0:T(8,128)} %add_select_fusion.4) | non-fusion elementwise | flops 262144 | bytes 1572864 | tf_op jit(solution)/shard_map/convert_element_type | solution.py:57
  74.2 3.2 %collective-permute-start.5 = (bf16[2,128,1024]{1,2,0:T(8,128)(2,1)}, bf16[2,128,1024]{1,2,0:T(8,128)(2,1)}, u32[]{:S(2)}, u32[]{:S(2)}) collective-permute-start(bf16[2,128,1024]{1,2,0:T(8,128)(2,1)} %convert_element_type.64), channel_id=1, source_target_pairs={{0,8},{2,10},{4,12},{6,14},{8,0},{10,2},{12,4},{14,6},{1,9},{3,11}... | collective-permute-start | bytes 1572872 | tf_op jit(solution)/shard_map/ppermute | solution.py:57
  79.4 10.1 %collective-permute-done.7 = bf16[2,128,1024]{1,2,0:T(8,128)(2,1)} collective-permute-done((bf16[2,128,1024]{1,2,0:T(8,128)(2,1)}, bf16[2,128,1024]{1,2,0:T(8,128)(2,1)}, u32[]{:S(2)}, u32[]{:S(2)}) %collective-permute-start.7) | collective-permute-done | bytes 524320 | tf_op jit(solution)/shard_map/ppermute | solution.py:57
  89.5 1.7 %fusion.14 = f32[2,128,1024]{1,2,0:T(8,128)S(1)} fusion(f32[2,128,1024]{1,2,0:T(8,128)S(1)} %fusion.11, bf16[2,128,1024]{1,2,0:T(8,128)(2,1)} %collective-permute-done.7, f32[2,1024]{1,0:T(2,128)S(1)} %mul.389, f32[2,1024]{1,0:T(2,128)S(1)} %mul.386, pred[]{:T(512)S(6)} %eq.15), kind=kLoop, calls=%fused_computation.31 | loop fusion | flops 1572864 | bytes 2637825 | tf_op jit(solution)/shard_map/jit(_where)/select_n | solution.py:63
  91.6 12.0 %shard_map.104 = bf16[256,1024]{1,0:T(8,128)(2,1)} custom-call(bf16[256,1024]{1,0:T(8,128)(2,1)} %q_ref, bf16[2,1024,512]{2,1,0:T(8,128)(2,1)} %all-gather.2.cloned.1.call-done.k_ref.v_ref, bf16[2,1024,512]{2,1,0:T(8,128)(2,1)} %all-gather.2.cloned.1.call-done.k_ref.v_ref), custom_call_target="tpu_custom_call" | custom-call | flops 2147483648 | bytes 3145728 | tf_op jit(solution)/shard_map/pallas_call | solution.py:155
  103.6 1.1 convert_element_type.65
  105.6 4.7 %collective-permute-start.8 = (bf16[2,128,1024]{1,2,0:T(8,128)(2,1)}, bf16[2,128,1024]{1,2,0:T(8,128)(2,1)}, u32[]{:S(2)}, u32[]{:S(2)}) collective-permute-start(bf16[2,128,1024]{1,2,0:T(8,128)(2,1)} %convert_element_type.70), channel_id=1, source_target_pairs={{0,8},{2,10},{4,12},{6,14},{8,0},{10,2},{12,4},{14,6},{1,9},{3,11}... | collective-permute-start | bytes 1572872 | tf_op jit(solution)/shard_map/ppermute | solution.py:57
  111.0 1.9 %add_select_fusion.2 = f32[2,128,1024]{1,2,0:T(8,128)S(1)} fusion(f32[2,128,1024]{1,2,0:T(8,128)S(1)} %convert_element_type.59, f32[2,128,1024]{1,2,0:T(8,128)S(1)} %convert_element_type.65, f32[2,1024]{1,0:T(2,128)S(1)} %mul.359, f32[2,1024]{1,0:T(2,128)S(1)} %mul.356, f32[2,1024]{1,0:T(2,128)S(1)} %mul.353, ...), kind=kLoop, calls=%fused_computation.23 | loop fusion | flops 2359296 | bytes 3694595 | tf_op jit(solution)/shard_map/jit(_where)/select_n | solution.py:62
  113.0 0.9 slice_add_fusion.3
  114.6 18.3 %collective-permute-done.8 = bf16[2,128,1024]{1,2,0:T(8,128)(2,1)} collective-permute-done((bf16[2,128,1024]{1,2,0:T(8,128)(2,1)}, bf16[2,128,1024]{1,2,0:T(8,128)(2,1)}, u32[]{:S(2)}, u32[]{:S(2)}) %collective-permute-start.8) | collective-permute-done | bytes 524320 | tf_op jit(solution)/shard_map/ppermute | solution.py:57
  132.9 1.1 convert_element_type.71
  134.0 2.1 %add_select_fusion = f32[2,128,1024]{1,2,0:T(8,128)S(1)} fusion(bf16[2,128,1024]{1,2,0:T(8,128)(2,1)} %collective-permute-done.6, bf16[2,128,1024]{1,2,0:T(8,128)(2,1)} %collective-permute-done.7, f32[2,1024]{1,0:T(2,128)S(1)} %mul.398, f32[2,1024]{1,0:T(2,128)S(1)} %mul.395, f32[2,1024]{1,0:T(2,128)S(1)} %mul.392, pred[]{:T(512)S(6)} %eq.14, pred[]{:T(512)S(6)} %eq.15, ...), kind=kLoop, calls=%fused_computation.15 | loop fusion | flops 2883584 | bytes 2646019 | tf_op jit(solution)/shard_map/jit(_where)/select_n | solution.py:62
  136.2 0.9 slice_add_fusion.1
  138.0 1.3 copy.26
  (129 shorter events, 13.7 us)
Async XLA Ops:
  7.2 8.8 %copy-start = (bf16[256,128]{1,0:T(8,128)(2,1)S(1)}, bf16[256,128]{1,0:T(8,128)(2,1)}, u32[]{:S(2)}) copy-start(bf16[256,128]{1,0:T(8,128)(2,1)} %param.13) | copy-start | bytes 196612
  7.2 64.9 %all-gather.2.cloned.1.call-start = ((), (), s32[]{:S(2)}) async-start(), calls=%async_computation | async-start | bytes 2359296 | tf_op jit(solution)/shard_map/all_gather | solution.py:179
  7.2 8.5 %copy-start.9 = (f32[32,256]{1,0:T(8,128)S(1)}, f32[32,256]{1,0:T(8,128)}, u32[]{:S(2)}) copy-start(f32[32,256]{1,0:T(8,128)} %param.10) | copy-start | bytes 98308
  11.2 5.4 %collective-permute-start = (f32[2,32]{1,0:T(2,128)S(1)}, f32[2,32]{1,0:T(2,128)S(1)}, u32[]{:S(2)}, u32[]{:S(2)}) collective-permute-start(f32[2,32]{1,0:T(2,128)S(1)} %exp.26), channel_id=1, source_target_pairs={{0,2},{2,0},{4,6},{6,4},{8,10},{10,8},{12,14},{14,12},{1,3},{3,1},... | collective-permute-start | bytes 776 | tf_op jit(solution)/shard_map/ppermute | solution.py:30
  16.4 1.6 %copy-start.6 = (bf16[256,2048]{1,0:T(8,128)(2,1)S(1)}, bf16[256,2048]{1,0:T(8,128)(2,1)}, u32[]{:S(2)}) copy-start(bf16[256,2048]{1,0:T(8,128)(2,1)} %param.9) | copy-start | bytes 3145732
  16.6 7.9 %copy-start.2 = (f32[2,128,1024]{1,2,0:T(8,128)}, f32[2,128,1024]{1,2,0:T(8,128)S(1)}, u32[]{:S(2)}) copy-start(f32[2,128,1024]{1,2,0:T(8,128)S(1)} %get-tuple-element.49) | copy-start | bytes 3145732
  16.6 23.7 %copy-start.1 = (f32[2,128,1024]{1,2,0:T(8,128)}, f32[2,128,1024]{1,2,0:T(8,128)S(1)}, u32[]{:S(2)}) copy-start(f32[2,128,1024]{1,2,0:T(8,128)S(1)} %get-tuple-element.78) | copy-start | bytes 3145732
  21.1 6.4 %copy-start.8 = (bf16[256,128]{1,0:T(8,128)(2,1)S(1)}, bf16[256,128]{1,0:T(8,128)(2,1)}, u32[]{:S(2)}) copy-start(bf16[256,128]{1,0:T(8,128)(2,1)} %param.14) | copy-start | bytes 196612
  21.1 6.5 %copy-start.14 = (f32[32]{0:T(128)S(1)}, f32[32]{0:T(128)}, u32[]{:S(2)}) copy-start(f32[32]{0:T(128)} %param.12) | copy-start | bytes 388
  25.4 13.7 %collective-permute-start.1 = (bf16[2,128,1024]{1,2,0:T(8,128)(2,1)}, bf16[2,128,1024]{1,2,0:T(8,128)(2,1)}, u32[]{:S(2)}, u32[]{:S(2)}) collective-permute-start(bf16[2,128,1024]{1,2,0:T(8,128)(2,1)} %convert_element_type.58), channel_id=1, source_target_pairs={{0,2},{2,0},{4,6},{6,4},{8,10},{10,8},{12,14},{14,12},{1,3},{3,1},... | collective-permute-start | bytes 1572872 | tf_op jit(solution)/shard_map/ppermute | solution.py:57
  25.5 5.9 %collective-permute-start.2 = (f32[2,32]{1,0:T(2,128)S(1)}, f32[2,32]{1,0:T(2,128)S(1)}, u32[]{:S(2)}, u32[]{:S(2)}) collective-permute-start(f32[2,32]{1,0:T(2,128)S(1)} %exponential_multiply_fusion), channel_id=1, source_target_pairs={{0,4},{2,6},{4,0},{6,2},{8,12},{10,14},{12,8},{14,10},{1,5},{3,7},... | collective-permute-start | bytes 776 | tf_op jit(solution)/shard_map/ppermute | solution.py:30
  31.4 10.1 %collective-permute-start.3 = (f32[2,32]{1,0:T(2,128)S(1)}, f32[2,32]{1,0:T(2,128)S(1)}, u32[]{:S(2)}, u32[]{:S(2)}) collective-permute-start(f32[2,32]{1,0:T(2,128)S(1)} %mul.334), channel_id=1, source_target_pairs={{0,8},{2,10},{4,12},{6,14},{8,0},{10,2},{12,4},{14,6},{1,9},{3,11}... | collective-permute-start | bytes 776 | tf_op jit(solution)/shard_map/ppermute | solution.py:30
  41.1 23.1 %collective-permute-start.6 = (bf16[2,128,1024]{1,2,0:T(8,128)(2,1)}, bf16[2,128,1024]{1,2,0:T(8,128)(2,1)}, u32[]{:S(2)}, u32[]{:S(2)}) collective-permute-start(bf16[2,128,1024]{1,2,0:T(8,128)(2,1)} %convert_element_type.66), channel_id=1, source_target_pairs={{0,2},{2,0},{4,6},{6,4},{8,10},{10,8},{12,14},{14,12},{1,3},{3,1},... | collective-permute-start | bytes 1572872 | tf_op jit(solution)/shard_map/ppermute | solution.py:57
  44.1 24.8 %collective-permute-start.4 = (bf16[2,128,1024]{1,2,0:T(8,128)(2,1)}, bf16[2,128,1024]{1,2,0:T(8,128)(2,1)}, u32[]{:S(2)}, u32[]{:S(2)}) collective-permute-start(bf16[2,128,1024]{1,2,0:T(8,128)(2,1)} %convert_element_type.62), channel_id=1, source_target_pairs={{0,4},{2,6},{4,0},{6,2},{8,12},{10,14},{12,8},{14,10},{1,5},{3,7},... | collective-permute-start | bytes 1572872 | tf_op jit(solution)/shard_map/ppermute | solution.py:57
  67.0 22.5 %collective-permute-start.7 = (bf16[2,128,1024]{1,2,0:T(8,128)(2,1)}, bf16[2,128,1024]{1,2,0:T(8,128)(2,1)}, u32[]{:S(2)}, u32[]{:S(2)}) collective-permute-start(bf16[2,128,1024]{1,2,0:T(8,128)(2,1)} %convert_element_type.68), channel_id=1, source_target_pairs={{0,4},{2,6},{4,0},{6,2},{8,12},{10,14},{12,8},{14,10},{1,5},{3,7},... | collective-permute-start | bytes 1572872 | tf_op jit(solution)/shard_map/ppermute | solution.py:57
  74.2 29.5 %collective-permute-start.5 = (bf16[2,128,1024]{1,2,0:T(8,128)(2,1)}, bf16[2,128,1024]{1,2,0:T(8,128)(2,1)}, u32[]{:S(2)}, u32[]{:S(2)}) collective-permute-start(bf16[2,128,1024]{1,2,0:T(8,128)(2,1)} %convert_element_type.64), channel_id=1, source_target_pairs={{0,8},{2,10},{4,12},{6,14},{8,0},{10,2},{12,4},{14,6},{1,9},{3,11}... | collective-permute-start | bytes 1572872 | tf_op jit(solution)/shard_map/ppermute | solution.py:57
  91.1 13.6 %copy-start.4 = (f32[2,128,1024]{1,2,0:T(8,128)}, f32[2,128,1024]{1,2,0:T(8,128)S(1)}, u32[]{:S(2)}) copy-start(f32[2,128,1024]{1,2,0:T(8,128)S(1)} %fusion.14) | copy-start | bytes 3145732
  91.5 12.2 %copy-start.10 = (f32[2,1024]{1,0:T(2,128)}, f32[2,1024]{1,0:T(2,128)S(1)}, u32[]{:S(2)}) copy-start(f32[2,1024]{1,0:T(2,128)S(1)} %mul.369) | copy-start | bytes 24580
  91.6 12.0 %copy-start.11 = (f32[2,1024]{1,0:T(2,128)}, f32[2,1024]{1,0:T(2,128)S(1)}, u32[]{:S(2)}) copy-start(f32[2,1024]{1,0:T(2,128)S(1)} %mul.372) | copy-start | bytes 24580
  105.6 7.4 %copy-start.3 = (f32[2,128,1024]{1,2,0:T(8,128)S(1)}, f32[2,128,1024]{1,2,0:T(8,128)}, u32[]{:S(2)}) copy-start(f32[2,128,1024]{1,2,0:T(8,128)} %add_select_fusion.4) | copy-start | bytes 3145732
  105.6 7.4 %slice-start = ((f32[2,1024]{1,0:T(2,128)}), f32[1,1024]{1,0:T(1,128)S(1)}, s32[]{:S(2)}) async-start(f32[2,1024]{1,0:T(2,128)} %copy-done.10), calls=%async_computation.1 | async-start | bytes 8192 | tf_op jit(solution)/shard_map/slice | solution.py:78
  105.6 7.4 %slice-start.1 = ((f32[2,1024]{1,0:T(2,128)}), f32[1,1024]{1,0:T(1,128)S(1)}, s32[]{:S(2)}) async-start(f32[2,1024]{1,0:T(2,128)} %copy-done.11), calls=%async_computation.2 | async-start | bytes 8192 | tf_op jit(solution)/shard_map/slice | solution.py:78
  105.6 27.3 %collective-permute-start.8 = (bf16[2,128,1024]{1,2,0:T(8,128)(2,1)}, bf16[2,128,1024]{1,2,0:T(8,128)(2,1)}, u32[]{:S(2)}, u32[]{:S(2)}) collective-permute-start(bf16[2,128,1024]{1,2,0:T(8,128)(2,1)} %convert_element_type.70), channel_id=1, source_target_pairs={{0,8},{2,10},{4,12},{6,14},{8,0},{10,2},{12,4},{14,6},{1,9},{3,11}... | collective-permute-start | bytes 1572872 | tf_op jit(solution)/shard_map/ppermute | solution.py:57
  110.8 3.1 %copy-start.12 = (f32[2,1024]{1,0:T(2,128)}, f32[2,1024]{1,0:T(2,128)S(1)}, u32[]{:S(2)}) copy-start(f32[2,1024]{1,0:T(2,128)S(1)} %mul.407) | copy-start | bytes 24580
  111.0 2.9 %copy-start.13 = (f32[2,1024]{1,0:T(2,128)}, f32[2,1024]{1,0:T(2,128)S(1)}, u32[]{:S(2)}) copy-start(f32[2,1024]{1,0:T(2,128)S(1)} %mul.410) | copy-start | bytes 24580
  114.5 21.6 %copy-start.5 = (f32[2,128,1024]{1,2,0:T(8,128)S(1)}, f32[2,128,1024]{1,2,0:T(8,128)}, u32[]{:S(2)}) copy-start(f32[2,128,1024]{1,2,0:T(8,128)} %copy-done.4) | copy-start | bytes 3145732
  114.6 21.6 %slice-start.2 = ((f32[2,1024]{1,0:T(2,128)}), f32[1,1024]{1,0:T(1,128)S(1)}, s32[]{:S(2)}) async-start(f32[2,1024]{1,0:T(2,128)} %copy-done.12), calls=%async_computation.3 | async-start | bytes 8192 | tf_op jit(solution)/shard_map/slice | solution.py:78
  114.6 21.6 %slice-start.3 = ((f32[2,1024]{1,0:T(2,128)}), f32[1,1024]{1,0:T(1,128)S(1)}, s32[]{:S(2)}) async-start(f32[2,1024]{1,0:T(2,128)} %copy-done.13), calls=%async_computation.4 | async-start | bytes 8192 | tf_op jit(solution)/shard_map/slice | solution.py:78
  136.2 1.6 %copy-start.7 = (f32[2,128,32,64]{1,3,2,0:T(8,128)S(1)}, f32[2,128,32,64]{1,3,2,0:T(8,128)}, u32[]{:S(2)}) copy-start(f32[2,128,32,64]{1,3,2,0:T(8,128)} %bitcast_add_fusion) | copy-start | bytes 6291460
Sparse Core Ops, SparseCore 0:
  10.2 61.8 all-gather.1

commit v8 on v7

--- a/solution.py
+++ b/solution.py
@@ -80,16 +80,49 @@
     return (entering, results)
 
 
+def mamba_base_kernel(x_ref, inner_ref, cum_row_ref, cum_col_ref, step_ref, skip_ref, o_ref):
+    causal = lax.broadcasted_iota(jnp.int32, (BLOCK, BLOCK), 0) >= lax.broadcasted_iota(
+        jnp.int32, (BLOCK, BLOCK), 1
+    )
+    inner = inner_ref[0]
+    for e in range(cum_row_ref.shape[1]):
+        log_gap = jnp.where(causal, cum_col_ref[0, e] - cum_row_ref[0, e], -jnp.inf)
+        mixing = (inner * jnp.exp(log_gap) * step_ref[0, e]).astype(jnp.bfloat16)
+        x_head = x_ref[:, e * HEADDIM : (e + 1) * HEADDIM]
+        intra = jnp.dot(mixing, x_head, preferred_element_type=jnp.float32)
+        skip = skip_ref[:, e * HEADDIM : (e + 1) * HEADDIM] * x_head.astype(jnp.float32)
+        o_ref[0, :, e * HEADDIM : (e + 1) * HEADDIM] = intra + skip
+
+
 def mamba_base(x_in, steps, cum, b_blocks, c_blocks, d_skip):
     slots, heads = steps.shape[:2]
-    x_blocks = x_in.reshape(slots, BLOCK, heads, HEADDIM)
-    causal = jnp.arange(BLOCK)[:, None] >= jnp.arange(BLOCK)[None, :]
-    log_gap = jnp.where(causal, cum[:, :, :, None] - cum[:, :, None, :], -jnp.inf)
+    width = x_in.shape[1]
+    pair = 128 // HEADDIM
     inner = jnp.einsum("cin,cjn->cij", c_blocks, b_blocks, preferred_element_type=jnp.float32)
-    mixing = (inner[:, None] * jnp.exp(log_gap) * steps[:, :, None, :]).astype(jnp.bfloat16)
-    intra = jnp.einsum("chij,cjhp->cihp", mixing, x_blocks, preferred_element_type=jnp.float32)
-    base = intra + d_skip[None, None, :, None] * x_blocks.astype(jnp.float32)
-    return base.reshape(slots, BLOCK, heads * HEADDIM)
+    cum_row = cum[:, :, None, :]
+    cum_col = cum[:, :, :, None]
+    step_row = steps[:, :, None, :]
+    skip_row = spread(d_skip)[None, :]
+    cost = pl.CostEstimate(
+        flops=2 * slots * heads * BLOCK * BLOCK * (HEADDIM + 3),
+        transcendentals=slots * heads * BLOCK * BLOCK,
+        bytes_accessed=x_in.size * 2 + slots * BLOCK * width * 4,
+    )
+    return pl.pallas_call(
+        mamba_base_kernel,
+        out_shape=jax.ShapeDtypeStruct((slots, BLOCK, width), jnp.float32),
+        grid=(slots, heads // pair),
+        in_specs=[
+            pl.BlockSpec((BLOCK, pair * HEADDIM), lambda c, g: (c, g)),
+            pl.BlockSpec((1, BLOCK, BLOCK), lambda c, g: (c, 0, 0)),
+            pl.BlockSpec((1, pair, 1, BLOCK), lambda c, g: (c, g, 0, 0)),
+            pl.BlockSpec((1, pair, BLOCK, 1), lambda c, g: (c, g, 0, 0)),
+            pl.BlockSpec((1, pair, 1, BLOCK), lambda c, g: (c, g, 0, 0)),
+            pl.BlockSpec((1, pair * HEADDIM), lambda c, g: (0, g)),
+        ],
+        out_specs=pl.BlockSpec((1, BLOCK, pair * HEADDIM), lambda c, g: (c, 0, g)),
+        cost_estimate=cost,
+    )(x_in, inner, cum_row, cum_col, step_row, skip_row)
 
 
 KEY_CHUNK = 256

time: 147 us -> 147 us (level)
  Pallas kernels: 12 us -> 33.3 us
  waiting for transfers between devices: 52 us -> 37.9 us
  starting transfers between devices: 19.3 us -> 15.8 us
  matrix products: 5.14 us -> 2.67 us
    pallas_call x0 -> x1, Pallas kernels: none -> 21.3 us  [mamba_base(): pl.pallas_call(mamba_base_kernel, out_shape=jax.ShapeDtypeStruct((slots,...]
    ppermute x6, waiting for transfers between devices: 51.4 us -> 37.9 us  [entering_states(): lax.ppermute(totals[j].astype(jnp.bfloat16), 'seq', pairs)]
    reshape x2 -> x1, local copies, waits for them, and re-layouts: 6.49 us -> 2.9 us  [spread(): return jnp.repeat(a, HEADDIM, axis=-1)]
    dot_general x1 -> x0, matrix products: 3.36 us -> none  [mamba_base(): jnp.einsum('chij,cjhp->cihp', mixing, x_blocks, preferred_element_type=jn...]
    ppermute x6, starting transfers between devices: 11.5 us -> 8.53 us  [entering_states(): lax.ppermute(totals[j].astype(jnp.bfloat16), 'seq', pairs)]
    broadcast_in_dim x0 -> x1, local copies, waits for them, and re-layouts: none -> 2.68 us  [mamba_base(): cum_col = cum[:, :, :, None]]
    broadcast_in_dim x24 -> x26, local copies, waits for them, and re-layouts: 1.7 us -> 3.23 us  [spread(): return jnp.repeat(a, HEADDIM, axis=-1)]
  transfers between devices with their start and end apart: 10 -> 10, of which waited for: 5 -> 4; matrix products, arithmetic and copies ran while one was open for 25% -> 23% of each run, Pallas kernels for 8% -> 23%
where the time goes in v8:
time: 147 us; the launch traced here: 146 us
  waiting for transfers between devices  37.9 us (26%)
  Pallas kernels  33.3 us (23%)
  other arithmetic  27.1 us (18%)
  starting transfers between devices  15.8 us (11%)
  local copies, waits for them, and re-layouts  15.1 us (10%)
  between operations  14.4 us (10%)
  matrix products  2.67 us (2%)
    ppermute x6, waiting for transfers between devices, entering_states(): lax.ppermute(totals[j].astype(jnp.bfloat16), 'seq', pairs)  37.9 us
    pallas_call x1, Pallas kernels, mamba_base(): pl.pallas_call(mamba_base_kernel, out_shape=jax.ShapeDtypeStruct((slots,...  21.3 us
    pallas_call x1, Pallas kernels, attention_core(): pl.pallas_call(attention_kernel, out_shape=jax.ShapeDtypeStruct(queries.s...  12 us
    ppermute x6, starting transfers between devices, entering_states(): lax.ppermute(totals[j].astype(jnp.bfloat16), 'seq', pairs)  8.53 us
    select_n x4, other arithmetic, entering_states(): jnp.where(lower, spread(own_a)[:, None, :] * got + totals[j], spread(got_...  7.76 us
    ppermute x3, starting transfers between devices, decay_scan(): got = lax.ppermute(total, 'seq', [(i, i ^ span) for i in range(count)])  7.23 us
    convert_element_type x6, other arithmetic, entering_states(): totals[j].astype(jnp.bfloat16)  5.64 us
    select_n x2, other arithmetic, entering_states(): jnp.where(lower, spread(excl_a)[:, None, :] * got + excls[j], excls[j])  4.08 us
  transfers between devices with their start and end apart: 10, of which 4 were waited for; matrix products, arithmetic and copies ran while one was open for 23% of the time, Pallas kernels for 23%

profile of v8, /device:TPU:0, one launch (start us, length us, event | category | flops | bytes accessed | tf_op | source)
XLA Modules:
  0.0 146.4 jit_solution(10939709481575157349)
XLA Ops:
  7.2 1.7 %pad_maximum_fusion = bf16[2,128,512]{2,1,0:T(8,128)(2,1)} fusion(bf16[2,128,256]{2,1,0:T(8,128)(2,1)} %bitcast.85, bf16[2,128,256]{2,1,0:T(8,128)(2,1)} %bitcast.86), kind=kLoop, calls=%fused_computation.35 | loop fusion | flops 524288 | bytes 524288 | tf_op jit(solution)/shard_map/concatenate | solution.py:208
  11.2 3.0 %collective-permute-start = (f32[2,32]{1,0:T(2,128)S(1)}, f32[2,32]{1,0:T(2,128)S(1)}, u32[]{:S(2)}, u32[]{:S(2)}) collective-permute-start(f32[2,32]{1,0:T(2,128)S(1)} %exp.23), channel_id=1, source_target_pairs={{0,2},{2,0},{4,6},{6,4},{8,10},{10,8},{12,14},{14,12},{1,3},{3,1},... | collective-permute-start | bytes 776 | tf_op jit(solution)/shard_map/ppermute | solution.py:30
  14.2 1.5 %copy.17 = f32[2,128,2048]{1,2,0:T(8,128)S(1)} copy(bf16[2,128,2048]{2,1,0:T(8,128)(2,1)} %bitcast.77) | data formatting | bytes 3145728 | tf_op jit(solution)/shard_map/convert_element_type | solution.py:219
  17.9 2.7 %copy.18.cum_col_ref = f32[2,32,128,1]{3,2,1,0:T(8,128)} copy(f32[2,32,128,1]{2,1,0,3:T(8,128)S(1)} %bitcast.78) | data formatting | bytes 65536 | tf_op jit(solution)/shard_map/broadcast_in_dim | solution.py:103
  21.4 1.6 %collective-permute-start.2 = (f32[2,32]{1,0:T(2,128)S(1)}, f32[2,32]{1,0:T(2,128)S(1)}, u32[]{:S(2)}, u32[]{:S(2)}) collective-permute-start(f32[2,32]{1,0:T(2,128)S(1)} %exponential_multiply_fusion), channel_id=1, source_target_pairs={{0,4},{2,6},{4,0},{6,2},{8,12},{10,14},{12,8},{14,10},{1,5},{3,7},... | collective-permute-start | bytes 776 | tf_op jit(solution)/shard_map/ppermute | solution.py:30
  23.8 21.3 %shard_map.104 = f32[2,128,2048]{2,1,0:T(8,128)} custom-call(bf16[256,2048]{1,0:T(8,128)(2,1)} %x_ref, f32[2,128,128]{2,1,0:T(8,128)} %fusion.18.inner_ref, f32[2,32,1,128]{3,2,1,0:T(1,128)} %bitcast.79, f32[2,32,128,1]{3,2,1,0:T(8,128)} %copy.18.cum_col_ref, f32[2,32,1,128]{3,2,1,0:T(1,128)} %bitcast.84, f32[1,2048]{1,0:T(1,128)} %broadcast_in_dim_reshape.2.skip_ref), custom_call_target="tpu_custom_call" | custom-call | flops 140509184 | bytes 3145728 | tf_op jit(solution)/shard_map/pallas_call | solution.py:111
  45.4 2.7 %collective-permute-start.3 = (f32[2,32]{1,0:T(2,128)S(1)}, f32[2,32]{1,0:T(2,128)S(1)}, u32[]{:S(2)}, u32[]{:S(2)}) collective-permute-start(f32[2,32]{1,0:T(2,128)S(1)} %mul.304), channel_id=1, source_target_pairs={{0,8},{2,10},{4,12},{6,14},{8,0},{10,2},{12,4},{14,6},{1,9},{3,11}... | collective-permute-start | bytes 776 | tf_op jit(solution)/shard_map/ppermute | solution.py:30
  49.0 1.4 collective-permute-start.6
  50.5 1.8 %add_select_fusion.5 = f32[2,128,1024]{1,2,0:T(8,128)S(1)} fusion(f32[2,128,1024]{1,2,0:T(8,128)S(1)} %convert_element_type.53, f32[2,128,1024]{1,2,0:T(8,128)} %copy-done.2, f32[2,1024]{1,0:T(2,128)S(1)} %mul.314, f32[2,1024]{1,0:T(2,128)S(1)} %mul.311, pred[]{:T(512)S(6)} %eq.13), kind=kLoop, calls=%fused_computation.30 | loop fusion | flops 1310720 | bytes 3162113 | tf_op jit(solution)/shard_map/jit(_where)/select_n | solution.py:63
  52.3 0.9 convert_element_type.54
  54.1 12.8 %collective-permute-done.6 = bf16[2,128,1024]{1,2,0:T(8,128)(2,1)} collective-permute-done((bf16[2,128,1024]{1,2,0:T(8,128)(2,1)}, bf16[2,128,1024]{1,2,0:T(8,128)(2,1)}, u32[]{:S(2)}, u32[]{:S(2)}) %collective-permute-start.6) | collective-permute-done | bytes 524320 | tf_op jit(solution)/shard_map/ppermute | solution.py:57
  66.8 1.8 %fusion.4 = f32[2,128,1024]{1,2,0:T(8,128)S(1)} fusion(f32[2,128,1024]{1,2,0:T(8,128)} %copy-done.1, bf16[2,128,1024]{1,2,0:T(8,128)(2,1)} %collective-permute-done.6, f32[2,1024]{1,0:T(2,128)S(1)} %mul.353, f32[2,1024]{1,0:T(2,128)S(1)} %mul.350, pred[]{:T(512)S(6)} %eq.13), kind=kLoop, calls=%fused_computation.19 | loop fusion | flops 1572864 | bytes 2637825 | tf_op jit(solution)/shard_map/jit(_where)/select_n | solution.py:63
  69.5 1.5 %collective-permute-start.7 = (bf16[2,128,1024]{1,2,0:T(8,128)(2,1)}, bf16[2,128,1024]{1,2,0:T(8,128)(2,1)}, u32[]{:S(2)}, u32[]{:S(2)}) collective-permute-start(bf16[2,128,1024]{1,2,0:T(8,128)(2,1)} %convert_element_type.60), channel_id=1, source_target_pairs={{0,4},{2,6},{4,0},{6,2},{8,12},{10,14},{12,8},{14,10},{1,5},{3,7},... | collective-permute-start | bytes 1572872 | tf_op jit(solution)/shard_map/ppermute | solution.py:57
  71.1 1.5 broadcast_in_dim.124
  72.6 2.9 %copy.21 = f32[2,128,2048]{2,1,0:T(8,128)} copy(f32[2,128,2048]{1,2,0:T(8,128)} %bitcast.76) | data formatting | bytes 4194304 | tf_op jit(solution)/shard_map/reshape | solution.py:20
  75.9 2.5 %add_select_fusion.4 = f32[2,128,1024]{1,2,0:T(8,128)} fusion(f32[2,128,1024]{1,2,0:T(8,128)S(1)} %add_select_fusion.5, f32[2,1024]{1,0:T(2,128)S(1)} %mul.320, bf16[2,128,1024]{1,2,0:T(8,128)(2,1)} %collective-permute-done.4, f32[2,1024]{1,0:T(2,128)S(1)} %mul.317, pred[]{:T(512)S(6)} %eq.15), kind=kLoop, calls=%fused_computation.29 | loop fusion | flops 1572864 | bytes 2637825 | tf_op jit(solution)/shard_map/jit(_where)/select_n | solution.py:63
  78.4 2.1 %convert_element_type.56 = bf16[2,128,1024]{1,2,0:T(8,128)(2,1)} convert(f32[2,128,1024]{1,2,0:T(8,128)} %add_select_fusion.4) | non-fusion elementwise | flops 262144 | bytes 1572864 | tf_op jit(solution)/shard_map/convert_element_type | solution.py:57
  80.5 2.4 %collective-permute-start.5 = (bf16[2,128,1024]{1,2,0:T(8,128)(2,1)}, bf16[2,128,1024]{1,2,0:T(8,128)(2,1)}, u32[]{:S(2)}, u32[]{:S(2)}) collective-permute-start(bf16[2,128,1024]{1,2,0:T(8,128)(2,1)} %convert_element_type.56), channel_id=1, source_target_pairs={{0,8},{2,10},{4,12},{6,14},{8,0},{10,2},{12,4},{14,6},{1,9},{3,11}... | collective-permute-start | bytes 1572872 | tf_op jit(solution)/shard_map/ppermute | solution.py:57
  84.9 2.9 %collective-permute-done.7 = bf16[2,128,1024]{1,2,0:T(8,128)(2,1)} collective-permute-done((bf16[2,128,1024]{1,2,0:T(8,128)(2,1)}, bf16[2,128,1024]{1,2,0:T(8,128)(2,1)}, u32[]{:S(2)}, u32[]{:S(2)}) %collective-permute-start.7) | collective-permute-done | bytes 524320 | tf_op jit(solution)/shard_map/ppermute | solution.py:57
  87.8 1.7 %fusion.7 = f32[2,128,1024]{1,2,0:T(8,128)S(1)} fusion(f32[2,128,1024]{1,2,0:T(8,128)S(1)} %fusion.4, bf16[2,128,1024]{1,2,0:T(8,128)(2,1)} %collective-permute-done.7, f32[2,1024]{1,0:T(2,128)S(1)} %mul.359, f32[2,1024]{1,0:T(2,128)S(1)} %mul.356, pred[]{:T(512)S(6)} %eq.15), kind=kLoop, calls=%fused_computation.22 | loop fusion | flops 1572864 | bytes 2637825 | tf_op jit(solution)/shard_map/jit(_where)/select_n | solution.py:63
  90.0 12.0 %shard_map.105 = bf16[256,1024]{1,0:T(8,128)(2,1)} custom-call(bf16[256,1024]{1,0:T(8,128)(2,1)} %q_ref, bf16[2,1024,512]{2,1,0:T(8,128)(2,1)} %all-gather.2.cloned.1.call-done.k_ref.v_ref, bf16[2,1024,512]{2,1,0:T(8,128)(2,1)} %all-gather.2.cloned.1.call-done.k_ref.v_ref), custom_call_target="tpu_custom_call" | custom-call | flops 2147483648 | bytes 3145728 | tf_op jit(solution)/shard_map/pallas_call | solution.py:188
  102.0 3.9 %collective-permute-done.5 = bf16[2,128,1024]{1,2,0:T(8,128)(2,1)} collective-permute-done((bf16[2,128,1024]{1,2,0:T(8,128)(2,1)}, bf16[2,128,1024]{1,2,0:T(8,128)(2,1)}, u32[]{:S(2)}, u32[]{:S(2)}) %collective-permute-start.5) | collective-permute-done | bytes 524320 | tf_op jit(solution)/shard_map/ppermute | solution.py:57
  105.9 1.1 convert_element_type.57
  107.0 0.9 convert_element_type.62
  107.9 2.0 %collective-permute-start.8 = (bf16[2,128,1024]{1,2,0:T(8,128)(2,1)}, bf16[2,128,1024]{1,2,0:T(8,128)(2,1)}, u32[]{:S(2)}, u32[]{:S(2)}) collective-permute-start(bf16[2,128,1024]{1,2,0:T(8,128)(2,1)} %convert_element_type.62), channel_id=1, source_target_pairs={{0,8},{2,10},{4,12},{6,14},{8,0},{10,2},{12,4},{14,6},{1,9},{3,11}... | collective-permute-start | bytes 1572872 | tf_op jit(solution)/shard_map/ppermute | solution.py:57
  110.6 1.9 %add_select_fusion.2 = f32[2,128,1024]{1,2,0:T(8,128)S(1)} fusion(f32[2,128,1024]{1,2,0:T(8,128)S(1)} %convert_element_type.53, f32[2,128,1024]{1,2,0:T(8,128)S(1)} %convert_element_type.57, f32[2,1024]{1,0:T(2,128)S(1)} %mul.329, f32[2,1024]{1,0:T(2,128)S(1)} %mul.326, f32[2,1024]{1,0:T(2,128)S(1)} %mul.323, ...), kind=kLoop, calls=%fused_computation.14 | loop fusion | flops 2359296 | bytes 3694595 | tf_op jit(solution)/shard_map/jit(_where)/select_n | solution.py:62
  112.6 0.9 slice_add_fusion.3
  114.3 18.3 %collective-permute-done.8 = bf16[2,128,1024]{1,2,0:T(8,128)(2,1)} collective-permute-done((bf16[2,128,1024]{1,2,0:T(8,128)(2,1)}, bf16[2,128,1024]{1,2,0:T(8,128)(2,1)}, u32[]{:S(2)}, u32[]{:S(2)}) %collective-permute-start.8) | collective-permute-done | bytes 524320 | tf_op jit(solution)/shard_map/ppermute | solution.py:57
  132.6 1.1 convert_element_type.63
  133.7 2.1 %add_select_fusion = f32[2,128,1024]{1,2,0:T(8,128)S(1)} fusion(bf16[2,128,1024]{1,2,0:T(8,128)(2,1)} %collective-permute-done.6, bf16[2,128,1024]{1,2,0:T(8,128)(2,1)} %collective-permute-done.7, f32[2,1024]{1,0:T(2,128)S(1)} %mul.368, f32[2,1024]{1,0:T(2,128)S(1)} %mul.365, f32[2,1024]{1,0:T(2,128)S(1)} %mul.362, pred[]{:T(512)S(6)} %eq.14, pred[]{:T(512)S(6)} %eq.15, ...), kind=kLoop, calls=%fused_computation.6 | loop fusion | flops 2883584 | bytes 2646019 | tf_op jit(solution)/shard_map/jit(_where)/select_n | solution.py:62
  135.9 0.9 slice_add_fusion.1
  138.1 1.4 fusion.1
  (134 shorter events, 14.7 us)
Async XLA Ops:
  7.2 9.4 %copy-start = (bf16[256,128]{1,0:T(8,128)(2,1)S(1)}, bf16[256,128]{1,0:T(8,128)(2,1)}, u32[]{:S(2)}) copy-start(bf16[256,128]{1,0:T(8,128)(2,1)} %param.13) | copy-start | bytes 196612
  7.2 8.5 %copy-start.11 = (f32[32,256]{1,0:T(8,128)S(1)}, f32[32,256]{1,0:T(8,128)}, u32[]{:S(2)}) copy-start(f32[32,256]{1,0:T(8,128)} %param.10) | copy-start | bytes 98308
  7.2 71.2 %all-gather.2.cloned.1.call-start = ((), (), s32[]{:S(2)}) async-start(), calls=%async_computation | async-start | bytes 2359296 | tf_op jit(solution)/shard_map/all_gather | solution.py:212
  11.0 6.9 %copy-start.8 = (f32[2,32,128]{2,1,0:T(8,128)}, f32[2,32,128]{2,1,0:T(8,128)S(1)}, u32[]{:S(2)}) copy-start(f32[2,32,128]{2,1,0:T(8,128)S(1)} %reduce_window_sum.11) | copy-start | bytes 98308
  11.2 6.0 %collective-permute-start = (f32[2,32]{1,0:T(2,128)S(1)}, f32[2,32]{1,0:T(2,128)S(1)}, u32[]{:S(2)}, u32[]{:S(2)}) collective-permute-start(f32[2,32]{1,0:T(2,128)S(1)} %exp.23), channel_id=1, source_target_pairs={{0,2},{2,0},{4,6},{6,4},{8,10},{10,8},{12,14},{14,12},{1,3},{3,1},... | collective-permute-start | bytes 776 | tf_op jit(solution)/shard_map/ppermute | solution.py:30
  17.1 3.5 %copy-start.2 = (f32[2,128,1024]{1,2,0:T(8,128)}, f32[2,128,1024]{1,2,0:T(8,128)S(1)}, u32[]{:S(2)}) copy-start(f32[2,128,1024]{1,2,0:T(8,128)S(1)} %get-tuple-element.49) | copy-start | bytes 3145732
  17.2 31.0 %copy-start.1 = (f32[2,128,1024]{1,2,0:T(8,128)}, f32[2,128,1024]{1,2,0:T(8,128)S(1)}, u32[]{:S(2)}) copy-start(f32[2,128,1024]{1,2,0:T(8,128)S(1)} %get-tuple-element.78) | copy-start | bytes 3145732
  17.3 30.8 %collective-permute-start.1 = (bf16[2,128,1024]{1,2,0:T(8,128)(2,1)S(1)}, bf16[2,128,1024]{1,2,0:T(8,128)(2,1)S(1)}, u32[]{:S(2)}, u32[]{:S(2)}) collective-permute-start(bf16[2,128,1024]{1,2,0:T(8,128)(2,1)S(1)} %convert_element_type.52), channel_id=1, source_target_pairs={{0,2},{2,0},{4,6},{6,4},{8,10},{10,8},{12,14},{14,12},{1,3},{3,1},... | collective-permute-start | bytes 1572872 | tf_op jit(solution)/shard_map/ppermute | solution.py:57
  17.9 2.7 %copy-start.16 = (f32[32]{0:T(128)S(1)}, f32[32]{0:T(128)}, u32[]{:S(2)}) copy-start(f32[32]{0:T(128)} %param.12) | copy-start | bytes 388
  17.9 5.0 %copy-start.10 = (bf16[256,128]{1,0:T(8,128)(2,1)S(1)}, bf16[256,128]{1,0:T(8,128)(2,1)}, u32[]{:S(2)}) copy-start(bf16[256,128]{1,0:T(8,128)(2,1)} %param.14) | copy-start | bytes 196612
  21.4 24.1 %collective-permute-start.2 = (f32[2,32]{1,0:T(2,128)S(1)}, f32[2,32]{1,0:T(2,128)S(1)}, u32[]{:S(2)}, u32[]{:S(2)}) collective-permute-start(f32[2,32]{1,0:T(2,128)S(1)} %exponential_multiply_fusion), channel_id=1, source_target_pairs={{0,4},{2,6},{4,0},{6,2},{8,12},{10,14},{12,8},{14,10},{1,5},{3,7},... | collective-permute-start | bytes 776 | tf_op jit(solution)/shard_map/ppermute | solution.py:30
  45.4 5.1 %collective-permute-start.3 = (f32[2,32]{1,0:T(2,128)S(1)}, f32[2,32]{1,0:T(2,128)S(1)}, u32[]{:S(2)}, u32[]{:S(2)}) collective-permute-start(f32[2,32]{1,0:T(2,128)S(1)} %mul.304), channel_id=1, source_target_pairs={{0,8},{2,10},{4,12},{6,14},{8,0},{10,2},{12,4},{14,6},{1,9},{3,11}... | collective-permute-start | bytes 776 | tf_op jit(solution)/shard_map/ppermute | solution.py:30
  49.0 17.8 %collective-permute-start.6 = (bf16[2,128,1024]{1,2,0:T(8,128)(2,1)}, bf16[2,128,1024]{1,2,0:T(8,128)(2,1)}, u32[]{:S(2)}, u32[]{:S(2)}) collective-permute-start(bf16[2,128,1024]{1,2,0:T(8,128)(2,1)} %convert_element_type.58), channel_id=1, source_target_pairs={{0,2},{2,0},{4,6},{6,4},{8,10},{10,8},{12,14},{14,12},{1,3},{3,1},... | collective-permute-start | bytes 1572872 | tf_op jit(solution)/shard_map/ppermute | solution.py:57
  53.2 22.8 %collective-permute-start.4 = (bf16[2,128,1024]{1,2,0:T(8,128)(2,1)}, bf16[2,128,1024]{1,2,0:T(8,128)(2,1)}, u32[]{:S(2)}, u32[]{:S(2)}) collective-permute-start(bf16[2,128,1024]{1,2,0:T(8,128)(2,1)} %convert_element_type.54), channel_id=1, source_target_pairs={{0,4},{2,6},{4,0},{6,2},{8,12},{10,14},{12,8},{14,10},{1,5},{3,7},... | collective-permute-start | bytes 1572872 | tf_op jit(solution)/shard_map/ppermute | solution.py:57
  54.1 17.0 %copy-start.9 = (f32[2,32,128]{2,1,0:T(8,128)S(1)}, f32[2,32,128]{2,1,0:T(8,128)}, u32[]{:S(2)}) copy-start(f32[2,32,128]{2,1,0:T(8,128)} %copy-done.8) | copy-start | bytes 98308
  69.5 18.3 %collective-permute-start.7 = (bf16[2,128,1024]{1,2,0:T(8,128)(2,1)}, bf16[2,128,1024]{1,2,0:T(8,128)(2,1)}, u32[]{:S(2)}, u32[]{:S(2)}) collective-permute-start(bf16[2,128,1024]{1,2,0:T(8,128)(2,1)} %convert_element_type.60), channel_id=1, source_target_pairs={{0,4},{2,6},{4,0},{6,2},{8,12},{10,14},{12,8},{14,10},{1,5},{3,7},... | collective-permute-start | bytes 1572872 | tf_op jit(solution)/shard_map/ppermute | solution.py:57
  80.5 25.4 %collective-permute-start.5 = (bf16[2,128,1024]{1,2,0:T(8,128)(2,1)}, bf16[2,128,1024]{1,2,0:T(8,128)(2,1)}, u32[]{:S(2)}, u32[]{:S(2)}) collective-permute-start(bf16[2,128,1024]{1,2,0:T(8,128)(2,1)} %convert_element_type.56), channel_id=1, source_target_pairs={{0,8},{2,10},{4,12},{6,14},{8,0},{10,2},{12,4},{14,6},{1,9},{3,11}... | collective-permute-start | bytes 1572872 | tf_op jit(solution)/shard_map/ppermute | solution.py:57
  89.5 17.5 %copy-start.6 = (f32[2,128,1024]{1,2,0:T(8,128)}, f32[2,128,1024]{1,2,0:T(8,128)S(1)}, u32[]{:S(2)}) copy-start(f32[2,128,1024]{1,2,0:T(8,128)S(1)} %fusion.7) | copy-start | bytes 3145732
  89.8 12.1 %copy-start.12 = (f32[2,1024]{1,0:T(2,128)}, f32[2,1024]{1,0:T(2,128)S(1)}, u32[]{:S(2)}) copy-start(f32[2,1024]{1,0:T(2,128)S(1)} %mul.339) | copy-start | bytes 24580
  90.0 12.0 %copy-start.13 = (f32[2,1024]{1,0:T(2,128)}, f32[2,1024]{1,0:T(2,128)S(1)}, u32[]{:S(2)}) copy-start(f32[2,1024]{1,0:T(2,128)S(1)} %mul.342) | copy-start | bytes 24580
  107.9 4.7 %copy-start.5 = (f32[2,128,1024]{1,2,0:T(8,128)S(1)}, f32[2,128,1024]{1,2,0:T(8,128)}, u32[]{:S(2)}) copy-start(f32[2,128,1024]{1,2,0:T(8,128)} %add_select_fusion.4) | copy-start | bytes 3145732
  107.9 4.7 %slice-start = ((f32[2,1024]{1,0:T(2,128)}), f32[1,1024]{1,0:T(1,128)S(1)}, s32[]{:S(2)}) async-start(f32[2,1024]{1,0:T(2,128)} %copy-done.12), calls=%async_computation.1 | async-start | bytes 8192 | tf_op jit(solution)/shard_map/slice | solution.py:78
  107.9 4.7 %slice-start.1 = ((f32[2,1024]{1,0:T(2,128)}), f32[1,1024]{1,0:T(1,128)S(1)}, s32[]{:S(2)}) async-start(f32[2,1024]{1,0:T(2,128)} %copy-done.13), calls=%async_computation.2 | async-start | bytes 8192 | tf_op jit(solution)/shard_map/slice | solution.py:78
  107.9 24.7 %collective-permute-start.8 = (bf16[2,128,1024]{1,2,0:T(8,128)(2,1)}, bf16[2,128,1024]{1,2,0:T(8,128)(2,1)}, u32[]{:S(2)}, u32[]{:S(2)}) collective-permute-start(bf16[2,128,1024]{1,2,0:T(8,128)(2,1)} %convert_element_type.62), channel_id=1, source_target_pairs={{0,8},{2,10},{4,12},{6,14},{8,0},{10,2},{12,4},{14,6},{1,9},{3,11}... | collective-permute-start | bytes 1572872 | tf_op jit(solution)/shard_map/ppermute | solution.py:57
  110.4 3.1 %copy-start.14 = (f32[2,1024]{1,0:T(2,128)}, f32[2,1024]{1,0:T(2,128)S(1)}, u32[]{:S(2)}) copy-start(f32[2,1024]{1,0:T(2,128)S(1)} %mul.377) | copy-start | bytes 24580
  110.6 2.9 %copy-start.15 = (f32[2,1024]{1,0:T(2,128)}, f32[2,1024]{1,0:T(2,128)S(1)}, u32[]{:S(2)}) copy-start(f32[2,1024]{1,0:T(2,128)S(1)} %mul.380) | copy-start | bytes 24580
  114.3 21.6 %copy-start.7 = (f32[2,128,1024]{1,2,0:T(8,128)S(1)}, f32[2,128,1024]{1,2,0:T(8,128)}, u32[]{:S(2)}) copy-start(f32[2,128,1024]{1,2,0:T(8,128)} %copy-done.6) | copy-start | bytes 3145732
  114.3 21.6 %slice-start.2 = ((f32[2,1024]{1,0:T(2,128)}), f32[1,1024]{1,0:T(1,128)S(1)}, s32[]{:S(2)}) async-start(f32[2,1024]{1,0:T(2,128)} %copy-done.14), calls=%async_computation.3 | async-start | bytes 8192 | tf_op jit(solution)/shard_map/slice | solution.py:78
  114.3 21.6 %slice-start.3 = ((f32[2,1024]{1,0:T(2,128)}), f32[1,1024]{1,0:T(1,128)S(1)}, s32[]{:S(2)}) async-start(f32[2,1024]{1,0:T(2,128)} %copy-done.15), calls=%async_computation.4 | async-start | bytes 8192 | tf_op jit(solution)/shard_map/slice | solution.py:78
  135.9 1.6 %copy-start.3 = (f32[2,128,2048]{2,1,0:T(8,128)S(1)}, f32[2,128,2048]{2,1,0:T(8,128)}, u32[]{:S(2)}) copy-start(f32[2,128,2048]{2,1,0:T(8,128)} %shard_map.104) | copy-start | bytes 6291460
  135.9 2.2 %copy-start.4 = (f32[2,128,2048]{2,1,0:T(8,128)S(1)}, f32[2,128,2048]{2,1,0:T(8,128)}, u32[]{:S(2)}) copy-start(f32[2,128,2048]{2,1,0:T(8,128)} %copy.21) | copy-start | bytes 6291460
Sparse Core Ops, SparseCore 0:
  10.2 61.9 all-gather.1

commit v9 on v8

--- a/solution.py
+++ b/solution.py
@@ -45,27 +45,33 @@
     span = 1
     for step, known_all in enumerate(steps):
         pairs = [(i, i ^ span) for i in range(count)]
-        before = ()
+        gots = []
         for j in range(parts):
             hook = hooks.get((j, step if step + 1 < len(steps) else -1))
-            totals[j], known, args, unused = lax.optimization_barrier(
-                (totals[j], known_all, hook[1] if hook else (), before)
+            tie = gots[-1] if gots else ()
+            totals[j], known, args, tie = lax.optimization_barrier(
+                (totals[j], known_all, hook[1] if hook else (), tie)
             )
-            lower, excl_a, own_a, got_a = [
-                v if v.ndim == 0 else v[:, j * head_cut : (j + 1) * head_cut] for v in known
-            ]
+            if gots:
+                gots[-1] = tie
             got = lax.ppermute(totals[j].astype(jnp.bfloat16), "seq", pairs).astype(jnp.float32)
             if hook is not None:
                 done = hook[0](*args)
                 got, done = lax.optimization_barrier((got, done))
                 results[hook[0].__name__] = done
+            gots.append(got)
+        lower = known_all[0]
+        for j in range(parts):
+            unused, excl_a, own_a, got_a = [
+                v if v.ndim == 0 else v[:, j * head_cut : (j + 1) * head_cut] for v in known_all
+            ]
+            got = gots[j]
             excls[j] = jnp.where(lower, spread(excl_a)[:, None, :] * got + excls[j], excls[j])
             totals[j] = jnp.where(
                 lower,
                 spread(own_a)[:, None, :] * got + totals[j],
                 spread(got_a)[:, None, :] * totals[j] + got,
             )
-            before = got
         span *= 2
     entering = []
     for j in range(parts):
@@ -223,7 +229,7 @@
     decay = jnp.exp(log_total)
     parts = 2 if heads % 2 == 0 else 1
     hooks = {
-        (0, 0): (mamba_base, (x_in, steps, cum, b_blocks, c_blocks, d_skip)),
+        (1, 0): (mamba_base, (x_in, steps, cum, b_blocks, c_blocks, d_skip)),
         (0, -1): (attention_core, (queries, kv_piece)),
     }
     incoming, results = entering_states(decay, block_state, seq_count, my_index, hooks, parts)

time: 147 us -> 151 us (1.027)
  other arithmetic: 27.1 us -> 23.6 us
  waiting for transfers between devices: 37.9 us -> 41.4 us
  local copies, waits for them, and re-layouts: 15.1 us -> 17.7 us
    select_n x4, other arithmetic: 7.76 us -> 5.52 us  [entering_states(): jnp.where(lower, spread(own_a)[:, None, :] * got + totals[j], spread(got_...]
    unnamed x34, local copies, waits for them, and re-layouts: 0.66 us -> 2.83 us
    ppermute x3, waiting for transfers between devices: 0.01 us -> 1.86 us  [decay_scan(): got = lax.ppermute(total, 'seq', [(i, i ^ span) for i in range(count)])]
    select_n x2, other arithmetic: 4.08 us -> 2.38 us  [entering_states(): jnp.where(lower, spread(excl_a)[:, None, :] * got + excls[j], excls[j])]
    convert_element_type x6, other arithmetic: 5.64 us -> 4.02 us  [entering_states(): totals[j].astype(jnp.bfloat16)]
    ppermute x6, waiting for transfers between devices: 37.9 us -> 39.5 us  [entering_states(): lax.ppermute(totals[j].astype(jnp.bfloat16), 'seq', pairs)]
    convert_element_type x3 -> x5, other arithmetic: 2.29 us -> 3.63 us  [entering_states(): lax.ppermute(totals[j].astype(jnp.bfloat16), 'seq', pairs)]
    broadcast_in_dim x26 -> x24, local copies, waits for them, and re-layouts: 3.23 us -> 3.15 us  [spread(): return jnp.repeat(a, HEADDIM, axis=-1)]
  transfers between devices with their start and end apart: 10 -> 10, of which waited for: 4 -> 5; matrix products, arithmetic and copies ran while one was open for 23% -> 21% of each run, Pallas kernels for 23% -> 22%
where the time goes in v9:
time: 151 us; the launch traced here: 150 us
  waiting for transfers between devices  41.4 us (27%)
  Pallas kernels  33.3 us (22%)
  other arithmetic  23.6 us (16%)
  local copies, waits for them, and re-layouts  17.7 us (12%)
  starting transfers between devices  16.7 us (11%)
  between operations  14.4 us (10%)
  matrix products  2.66 us (2%)
    ppermute x6, waiting for transfers between devices, entering_states(): lax.ppermute(totals[j].astype(jnp.bfloat16), 'seq', pairs)  39.5 us
    pallas_call x1, Pallas kernels, mamba_base(): pl.pallas_call(mamba_base_kernel, out_shape=jax.ShapeDtypeStruct((slots,...  21.3 us
    pallas_call x1, Pallas kernels, attention_core(): pl.pallas_call(attention_kernel, out_shape=jax.ShapeDtypeStruct(queries.s...  12 us
    ppermute x6, starting transfers between devices, entering_states(): lax.ppermute(totals[j].astype(jnp.bfloat16), 'seq', pairs)  8.54 us
    ppermute x3, starting transfers between devices, decay_scan(): got = lax.ppermute(total, 'seq', [(i, i ^ span) for i in range(count)])  8.11 us
    select_n x4, other arithmetic, entering_states(): jnp.where(lower, spread(own_a)[:, None, :] * got + totals[j], spread(got_...  5.52 us
    convert_element_type x6, other arithmetic, entering_states(): totals[j].astype(jnp.bfloat16)  4.02 us
    convert_element_type x5, other arithmetic, entering_states(): lax.ppermute(totals[j].astype(jnp.bfloat16), 'seq', pairs)  3.63 us
  transfers between devices with their start and end apart: 10, of which 5 were waited for; matrix products, arithmetic and copies ran while one was open for 21% of the time, Pallas kernels for 22%

profile of v9, /device:TPU:0, one launch (start us, length us, event | category | flops | bytes accessed | tf_op | source)
XLA Modules:
  0.0 149.8 jit_solution(9502317029750547832)
XLA Ops:
  7.2 1.7 %pad_maximum_fusion = bf16[2,128,512]{2,1,0:T(8,128)(2,1)} fusion(bf16[2,128,256]{2,1,0:T(8,128)(2,1)} %bitcast.76, bf16[2,128,256]{2,1,0:T(8,128)(2,1)} %bitcast.77), kind=kLoop, calls=%fused_computation.30 | loop fusion | flops 524288 | bytes 524288 | tf_op jit(solution)/shard_map/concatenate | solution.py:214
  11.2 3.0 %collective-permute-start = (f32[2,32]{1,0:T(2,128)S(1)}, f32[2,32]{1,0:T(2,128)S(1)}, u32[]{:S(2)}, u32[]{:S(2)}) collective-permute-start(f32[2,32]{1,0:T(2,128)S(1)} %exp.23), channel_id=1, source_target_pairs={{0,2},{2,0},{4,6},{6,4},{8,10},{10,8},{12,14},{14,12},{1,3},{3,1},... | collective-permute-start | bytes 776 | tf_op jit(solution)/shard_map/ppermute | solution.py:30
  15.0 1.4 bitcast_bitcast_fusion.1
  16.5 1.5 copy.17
  19.0 1.5 %broadcast_in_dim.116 = f32[2,128,32,64]{1,3,2,0:T(8,128)} broadcast(f32[2,128,32]{1,2,0:T(8,128)S(1)} %exponential_bitcast_fusion), dimensions={0,1,2} | broadcast | bytes 2129920 | tf_op jit(solution)/shard_map/broadcast_in_dim | solution.py:20
  20.6 3.0 %copy.21 = f32[2,128,2048]{2,1,0:T(8,128)} copy(f32[2,128,2048]{1,2,0:T(8,128)} %bitcast.67) | data formatting | bytes 4194304 | tf_op jit(solution)/shard_map/reshape | solution.py:20
  24.0 2.1 %collective-permute-start.3 = (f32[2,32]{1,0:T(2,128)S(1)}, f32[2,32]{1,0:T(2,128)S(1)}, u32[]{:S(2)}, u32[]{:S(2)}) collective-permute-start(f32[2,32]{1,0:T(2,128)S(1)} %exponential_multiply_fusion), channel_id=1, source_target_pairs={{0,4},{2,6},{4,0},{6,2},{8,12},{10,14},{12,8},{14,10},{1,5},{3,7},... | collective-permute-start | bytes 776 | tf_op jit(solution)/shard_map/ppermute | solution.py:30
  26.6 1.1 collective-permute-done.3
  27.7 3.0 %collective-permute-start.4 = (f32[2,32]{1,0:T(2,128)S(1)}, f32[2,32]{1,0:T(2,128)S(1)}, u32[]{:S(2)}, u32[]{:S(2)}) collective-permute-start(f32[2,32]{1,0:T(2,128)S(1)} %mul.284), channel_id=1, source_target_pairs={{0,8},{2,10},{4,12},{6,14},{8,0},{10,2},{12,4},{14,6},{1,9},{3,11}... | collective-permute-start | bytes 776 | tf_op jit(solution)/shard_map/ppermute | solution.py:30
  32.2 7.2 %collective-permute-done.1 = bf16[2,128,1024]{1,2,0:T(8,128)(2,1)} collective-permute-done((bf16[2,128,1024]{1,2,0:T(8,128)(2,1)S(1)}, bf16[2,128,1024]{1,2,0:T(8,128)(2,1)}, u32[]{:S(2)}, u32[]{:S(2)}) %collective-permute-start.1) | collective-permute-done | bytes 524320 | tf_op jit(solution)/shard_map/ppermute | solution.py:57
  39.5 1.1 convert_element_type.53
  41.3 1.0 copy-done.2
  42.4 1.6 %collective-permute-start.5 = (bf16[2,128,1024]{1,2,0:T(8,128)(2,1)S(1)}, bf16[2,128,1024]{1,2,0:T(8,128)(2,1)}, u32[]{:S(2)}, u32[]{:S(2)}) collective-permute-start(bf16[2,128,1024]{1,2,0:T(8,128)(2,1)S(1)} %convert_element_type.56), channel_id=1, source_target_pairs={{0,4},{2,6},{4,0},{6,2},{8,12},{10,14},{12,8},{14,10},{1,5},{3,7},... | collective-permute-start | bytes 1572872 | tf_op jit(solution)/shard_map/ppermute | solution.py:57
  43.9 0.9 convert_element_type.54
  45.5 2.6 %copy.18.cum_col_ref = f32[2,32,128,1]{3,2,1,0:T(8,128)} copy(f32[2,32,128,1]{2,1,0,3:T(8,128)S(1)} %bitcast.69) | data formatting | bytes 65536 | tf_op jit(solution)/shard_map/broadcast_in_dim | solution.py:109
  49.7 21.3 %shard_map.104 = f32[2,128,2048]{2,1,0:T(8,128)} custom-call(bf16[256,2048]{1,0:T(8,128)(2,1)} %x_ref, f32[2,128,128]{2,1,0:T(8,128)} %fusion.23.inner_ref, f32[2,32,1,128]{3,2,1,0:T(1,128)} %bitcast.70, f32[2,32,128,1]{3,2,1,0:T(8,128)} %copy.18.cum_col_ref, f32[2,32,1,128]{3,2,1,0:T(1,128)} %bitcast.75, f32[1,2048]{1,0:T(1,128)} %broadcast_in_dim_reshape.2.skip_ref), custom_call_target="tpu_custom_call" | custom-call | flops 140509184 | bytes 3145728 | tf_op jit(solution)/shard_map/pallas_call | solution.py:117
  71.2 1.2 convert_element_type.57
  73.2 1.0 copy-done.1
  74.1 0.9 convert_element_type.58
  75.3 1.5 add_select_fusion.4
  76.8 2.1 %convert_element_type.60 = bf16[2,128,1024]{1,2,0:T(8,128)(2,1)} convert(f32[2,128,1024]{1,2,0:T(8,128)} %add_select_fusion.4) | non-fusion elementwise | flops 262144 | bytes 1572864 | tf_op jit(solution)/shard_map/convert_element_type | solution.py:57
  78.9 2.7 %collective-permute-start.7 = (bf16[2,128,1024]{1,2,0:T(8,128)(2,1)}, bf16[2,128,1024]{1,2,0:T(8,128)(2,1)}, u32[]{:S(2)}, u32[]{:S(2)}) collective-permute-start(bf16[2,128,1024]{1,2,0:T(8,128)(2,1)} %convert_element_type.60), channel_id=1, source_target_pairs={{0,8},{2,10},{4,12},{6,14},{8,0},{10,2},{12,4},{14,6},{1,9},{3,11}... | collective-permute-start | bytes 1572872 | tf_op jit(solution)/shard_map/ppermute | solution.py:57
  83.4 13.3 %collective-permute-done.6 = bf16[2,128,1024]{1,2,0:T(8,128)(2,1)} collective-permute-done((bf16[2,128,1024]{1,2,0:T(8,128)(2,1)}, bf16[2,128,1024]{1,2,0:T(8,128)(2,1)}, u32[]{:S(2)}, u32[]{:S(2)}) %collective-permute-start.6) | collective-permute-done | bytes 524320 | tf_op jit(solution)/shard_map/ppermute | solution.py:57
  96.7 2.6 %fusion.4 = f32[2,128,1024]{1,2,0:T(8,128)} fusion(f32[2,128,1024]{1,2,0:T(8,128)} %copy-done.1, bf16[2,128,1024]{1,2,0:T(8,128)(2,1)} %collective-permute-done.6, f32[2,1024]{1,0:T(2,128)S(1)} %mul.308, f32[2,1024]{1,0:T(2,128)S(1)} %mul.293, pred[]{:T(512)S(6)} %eq.15), kind=kLoop, calls=%fused_computation.16 | loop fusion | flops 1572864 | bytes 2637825 | tf_op jit(solution)/shard_map/jit(_where)/select_n | solution.py:70
  99.3 12.0 %shard_map.105 = bf16[256,1024]{1,0:T(8,128)(2,1)} custom-call(bf16[256,1024]{1,0:T(8,128)(2,1)} %q_ref, bf16[2,1024,512]{2,1,0:T(8,128)(2,1)} %all-gather.2.cloned.1.call-done.k_ref.v_ref, bf16[2,1024,512]{2,1,0:T(8,128)(2,1)} %all-gather.2.cloned.1.call-done.k_ref.v_ref), custom_call_target="tpu_custom_call" | custom-call | flops 2147483648 | bytes 3145728 | tf_op jit(solution)/shard_map/pallas_call | solution.py:194
  111.3 1.2 convert_element_type.61
  112.8 3.4 %collective-permute-start.8 = (bf16[2,128,1024]{1,2,0:T(8,128)(2,1)S(1)}, bf16[2,128,1024]{1,2,0:T(8,128)(2,1)S(1)}, u32[]{:S(2)}, u32[]{:S(2)}) collective-permute-start(bf16[2,128,1024]{1,2,0:T(8,128)(2,1)S(1)} %convert_element_type.62), channel_id=1, source_target_pairs={{0,8},{2,10},{4,12},{6,14},{8,0},{10,2},{12,4},{14,6},{1,9},{3,11}... | collective-permute-start | bytes 1572872 | tf_op jit(solution)/shard_map/ppermute | solution.py:57
  116.9 0.9 slice_add_fusion.3
  118.5 19.0 %collective-permute-done.8 = bf16[2,128,1024]{1,2,0:T(8,128)(2,1)S(1)} collective-permute-done((bf16[2,128,1024]{1,2,0:T(8,128)(2,1)S(1)}, bf16[2,128,1024]{1,2,0:T(8,128)(2,1)S(1)}, u32[]{:S(2)}, u32[]{:S(2)}) %collective-permute-start.8) | collective-permute-done | bytes 524320 | tf_op jit(solution)/shard_map/ppermute | solution.py:57
  137.6 1.7 %add_select_fusion = f32[2,128,1024]{1,2,0:T(8,128)S(1)} fusion(bf16[2,128,1024]{1,2,0:T(8,128)(2,1)} %collective-permute-done.6, f32[2,128,1024]{1,2,0:T(8,128)S(1)} %convert_element_type.55, f32[2,1024]{1,0:T(2,128)S(1)} %mul.342, f32[2,1024]{1,0:T(2,128)S(1)} %mul.339, pred[]{:T(512)S(6)} %eq.13, pred[]{:T(512)S(6)} %eq.15, pred[]{:T(512)S(6)} %eq.14, ...), kind=kLoop, calls=%fused_computation.6 | loop fusion | flops 2359296 | bytes 3162115 | tf_op jit(solution)/shard_map/jit(_where)/select_n | solution.py:69
  139.3 0.9 slice_add_fusion.1
  141.5 1.4 fusion.1
  (129 shorter events, 15.9 us)
Async XLA Ops:
  7.2 11.1 %copy-start = (bf16[256,128]{1,0:T(8,128)(2,1)S(1)}, bf16[256,128]{1,0:T(8,128)(2,1)}, u32[]{:S(2)}) copy-start(bf16[256,128]{1,0:T(8,128)(2,1)} %param.13) | copy-start | bytes 196612
  7.2 69.6 %all-gather.2.cloned.1.call-start = ((), (), s32[]{:S(2)}) async-start(), calls=%async_computation | async-start | bytes 2359296 | tf_op jit(solution)/shard_map/all_gather | solution.py:218
  11.0 34.5 %copy-start.10 = (f32[2,32,128]{2,1,0:T(8,128)}, f32[2,32,128]{2,1,0:T(8,128)S(1)}, u32[]{:S(2)}) copy-start(f32[2,32,128]{2,1,0:T(8,128)S(1)} %reduce_window_sum.11) | copy-start | bytes 98308
  11.2 12.4 %collective-permute-start = (f32[2,32]{1,0:T(2,128)S(1)}, f32[2,32]{1,0:T(2,128)S(1)}, u32[]{:S(2)}, u32[]{:S(2)}) collective-permute-start(f32[2,32]{1,0:T(2,128)S(1)} %exp.23), channel_id=1, source_target_pairs={{0,2},{2,0},{4,6},{6,4},{8,10},{10,8},{12,14},{14,12},{1,3},{3,1},... | collective-permute-start | bytes 776 | tf_op jit(solution)/shard_map/ppermute | solution.py:30
  18.9 25.0 %copy-start.4 = (f32[2,128,1024]{1,2,0:T(8,128)}, f32[2,128,1024]{1,2,0:T(8,128)S(1)}, u32[]{:S(2)}) copy-start(f32[2,128,1024]{1,2,0:T(8,128)S(1)} %get-tuple-element.29) | copy-start | bytes 3145732
  23.6 15.8 %collective-permute-start.1 = (bf16[2,128,1024]{1,2,0:T(8,128)(2,1)S(1)}, bf16[2,128,1024]{1,2,0:T(8,128)(2,1)}, u32[]{:S(2)}, u32[]{:S(2)}) collective-permute-start(bf16[2,128,1024]{1,2,0:T(8,128)(2,1)S(1)} %convert_element_type.52), channel_id=1, source_target_pairs={{0,2},{2,0},{4,6},{6,4},{8,10},{10,8},{12,14},{14,12},{1,3},{3,1},... | collective-permute-start | bytes 1572872 | tf_op jit(solution)/shard_map/ppermute | solution.py:57
  24.0 3.7 %collective-permute-start.3 = (f32[2,32]{1,0:T(2,128)S(1)}, f32[2,32]{1,0:T(2,128)S(1)}, u32[]{:S(2)}, u32[]{:S(2)}) collective-permute-start(f32[2,32]{1,0:T(2,128)S(1)} %exponential_multiply_fusion), channel_id=1, source_target_pairs={{0,4},{2,6},{4,0},{6,2},{8,12},{10,14},{12,8},{14,10},{1,5},{3,7},... | collective-permute-start | bytes 776 | tf_op jit(solution)/shard_map/ppermute | solution.py:30
  27.7 4.5 %collective-permute-start.4 = (f32[2,32]{1,0:T(2,128)S(1)}, f32[2,32]{1,0:T(2,128)S(1)}, u32[]{:S(2)}, u32[]{:S(2)}) collective-permute-start(f32[2,32]{1,0:T(2,128)S(1)} %mul.284), channel_id=1, source_target_pairs={{0,8},{2,10},{4,12},{6,14},{8,0},{10,2},{12,4},{14,6},{1,9},{3,11}... | collective-permute-start | bytes 776 | tf_op jit(solution)/shard_map/ppermute | solution.py:30
  31.3 10.0 %copy-start.12 = (f32[2,1024]{1,0:T(2,128)}, f32[2,1024]{1,0:T(2,128)S(1)}, u32[]{:S(2)}) copy-start(f32[2,1024]{1,0:T(2,128)S(1)} %mul.328) | copy-start | bytes 24580
  31.4 9.9 %copy-start.13 = (f32[2,1024]{1,0:T(2,128)}, f32[2,1024]{1,0:T(2,128)S(1)}, u32[]{:S(2)}) copy-start(f32[2,1024]{1,0:T(2,128)S(1)} %mul.351) | copy-start | bytes 24580
  41.3 1.0 copy-start.2
  42.4 28.8 %collective-permute-start.5 = (bf16[2,128,1024]{1,2,0:T(8,128)(2,1)S(1)}, bf16[2,128,1024]{1,2,0:T(8,128)(2,1)}, u32[]{:S(2)}, u32[]{:S(2)}) collective-permute-start(bf16[2,128,1024]{1,2,0:T(8,128)(2,1)S(1)} %convert_element_type.56), channel_id=1, source_target_pairs={{0,4},{2,6},{4,0},{6,2},{8,12},{10,14},{12,8},{14,10},{1,5},{3,7},... | collective-permute-start | bytes 1572872 | tf_op jit(solution)/shard_map/ppermute | solution.py:57
  44.8 26.3 %collective-permute-start.2 = (bf16[2,128,1024]{1,2,0:T(8,128)(2,1)}, bf16[2,128,1024]{1,2,0:T(8,128)(2,1)S(1)}, u32[]{:S(2)}, u32[]{:S(2)}) collective-permute-start(bf16[2,128,1024]{1,2,0:T(8,128)(2,1)} %convert_element_type.54), channel_id=1, source_target_pairs={{0,2},{2,0},{4,6},{6,4},{8,10},{10,8},{12,14},{14,12},{1,3},{3,1},... | collective-permute-start | bytes 1572872 | tf_op jit(solution)/shard_map/ppermute | solution.py:57
  45.5 2.7 %copy-start.16 = (f32[32]{0:T(128)S(1)}, f32[32]{0:T(128)}, u32[]{:S(2)}) copy-start(f32[32]{0:T(128)} %param.12) | copy-start | bytes 388
  45.5 3.4 %copy-start.11 = (bf16[256,128]{1,0:T(8,128)(2,1)S(1)}, bf16[256,128]{1,0:T(8,128)(2,1)}, u32[]{:S(2)}) copy-start(bf16[256,128]{1,0:T(8,128)(2,1)} %param.14) | copy-start | bytes 196612
  71.1 1.4 copy-start.5
  72.5 2.9 %copy-start.3 = (f32[2,128,1024]{1,2,0:T(8,128)S(1)}, f32[2,128,1024]{1,2,0:T(8,128)}, u32[]{:S(2)}) copy-start(f32[2,128,1024]{1,2,0:T(8,128)} %copy-done.2) | copy-start | bytes 3145732
  73.2 1.0 copy-start.1
  75.0 21.7 %collective-permute-start.6 = (bf16[2,128,1024]{1,2,0:T(8,128)(2,1)}, bf16[2,128,1024]{1,2,0:T(8,128)(2,1)}, u32[]{:S(2)}, u32[]{:S(2)}) collective-permute-start(bf16[2,128,1024]{1,2,0:T(8,128)(2,1)} %convert_element_type.58), channel_id=1, source_target_pairs={{0,4},{2,6},{4,0},{6,2},{8,12},{10,14},{12,8},{14,10},{1,5},{3,7},... | collective-permute-start | bytes 1572872 | tf_op jit(solution)/shard_map/ppermute | solution.py:57
  78.9 32.4 %collective-permute-start.7 = (bf16[2,128,1024]{1,2,0:T(8,128)(2,1)}, bf16[2,128,1024]{1,2,0:T(8,128)(2,1)}, u32[]{:S(2)}, u32[]{:S(2)}) collective-permute-start(bf16[2,128,1024]{1,2,0:T(8,128)(2,1)} %convert_element_type.60), channel_id=1, source_target_pairs={{0,8},{2,10},{4,12},{6,14},{8,0},{10,2},{12,4},{14,6},{1,9},{3,11}... | collective-permute-start | bytes 1572872 | tf_op jit(solution)/shard_map/ppermute | solution.py:57
  82.5 28.8 %copy-start.14 = (f32[2,1024]{1,0:T(2,128)}, f32[2,1024]{1,0:T(2,128)S(1)}, u32[]{:S(2)}) copy-start(f32[2,1024]{1,0:T(2,128)S(1)} %mul.331) | copy-start | bytes 24580
  83.4 27.9 %copy-start.15 = (f32[2,1024]{1,0:T(2,128)}, f32[2,1024]{1,0:T(2,128)S(1)}, u32[]{:S(2)}) copy-start(f32[2,1024]{1,0:T(2,128)S(1)} %mul.354) | copy-start | bytes 24580
  111.3 1.4 copy-start.9
  112.7 4.1 %copy-start.8 = (f32[2,128,1024]{1,2,0:T(8,128)S(1)}, f32[2,128,1024]{1,2,0:T(8,128)}, u32[]{:S(2)}) copy-start(f32[2,128,1024]{1,2,0:T(8,128)} %add_select_fusion.4) | copy-start | bytes 3145732
  112.7 4.1 %slice-start = ((f32[2,1024]{1,0:T(2,128)}), f32[1,1024]{1,0:T(1,128)S(1)}, s32[]{:S(2)}) async-start(f32[2,1024]{1,0:T(2,128)} %copy-done.12), calls=%async_computation.1 | async-start | bytes 8192 | tf_op jit(solution)/shard_map/slice | solution.py:84
  112.8 4.1 %slice-start.2 = ((f32[2,1024]{1,0:T(2,128)}), f32[1,1024]{1,0:T(1,128)S(1)}, s32[]{:S(2)}) async-start(f32[2,1024]{1,0:T(2,128)} %copy-done.14), calls=%async_computation.3 | async-start | bytes 8192 | tf_op jit(solution)/shard_map/slice | solution.py:84
  112.8 24.7 %collective-permute-start.8 = (bf16[2,128,1024]{1,2,0:T(8,128)(2,1)S(1)}, bf16[2,128,1024]{1,2,0:T(8,128)(2,1)S(1)}, u32[]{:S(2)}, u32[]{:S(2)}) collective-permute-start(bf16[2,128,1024]{1,2,0:T(8,128)(2,1)S(1)} %convert_element_type.62), channel_id=1, source_target_pairs={{0,8},{2,10},{4,12},{6,14},{8,0},{10,2},{12,4},{14,6},{1,9},{3,11}... | collective-permute-start | bytes 1572872 | tf_op jit(solution)/shard_map/ppermute | solution.py:57
  118.5 20.8 %slice-start.1 = ((f32[2,1024]{1,0:T(2,128)}), f32[1,1024]{1,0:T(1,128)S(1)}, s32[]{:S(2)}) async-start(f32[2,1024]{1,0:T(2,128)} %copy-done.13), calls=%async_computation.2 | async-start | bytes 8192 | tf_op jit(solution)/shard_map/slice | solution.py:84
  118.5 20.7 %slice-start.3 = ((f32[2,1024]{1,0:T(2,128)}), f32[1,1024]{1,0:T(1,128)S(1)}, s32[]{:S(2)}) async-start(f32[2,1024]{1,0:T(2,128)} %copy-done.15), calls=%async_computation.4 | async-start | bytes 8192 | tf_op jit(solution)/shard_map/slice | solution.py:84
  139.3 1.6 %copy-start.6 = (f32[2,128,2048]{2,1,0:T(8,128)S(1)}, f32[2,128,2048]{2,1,0:T(8,128)}, u32[]{:S(2)}) copy-start(f32[2,128,2048]{2,1,0:T(8,128)} %shard_map.104) | copy-start | bytes 6291460
  139.3 2.2 %copy-start.7 = (f32[2,128,2048]{2,1,0:T(8,128)S(1)}, f32[2,128,2048]{2,1,0:T(8,128)}, u32[]{:S(2)}) copy-start(f32[2,128,2048]{2,1,0:T(8,128)} %copy.21) | copy-start | bytes 6291460
Sparse Core Ops, SparseCore 0:
  14.3 60.4 all-gather.1

commit v10 on v9

--- a/solution.py
+++ b/solution.py
@@ -86,13 +86,15 @@
     return (entering, results)
 
 
-def mamba_base_kernel(x_ref, inner_ref, cum_row_ref, cum_col_ref, step_ref, skip_ref, o_ref):
-    causal = lax.broadcasted_iota(jnp.int32, (BLOCK, BLOCK), 0) >= lax.broadcasted_iota(
-        jnp.int32, (BLOCK, BLOCK), 1
-    )
+def mamba_base_kernel(x_ref, inner_ref, cum_ref, step_ref, skip_ref, o_ref):
+    rows = lax.broadcasted_iota(jnp.int32, (BLOCK, BLOCK), 0)
+    cols = lax.broadcasted_iota(jnp.int32, (BLOCK, BLOCK), 1)
+    causal = rows >= cols
     inner = inner_ref[0]
-    for e in range(cum_row_ref.shape[1]):
-        log_gap = jnp.where(causal, cum_col_ref[0, e] - cum_row_ref[0, e], -jnp.inf)
+    for e in range(cum_ref.shape[1]):
+        cum_row = cum_ref[0, e]
+        cum_col = jnp.sum(jnp.where(rows == cols, cum_row, 0.0), axis=1, keepdims=True)
+        log_gap = jnp.where(causal, cum_col - cum_row, -jnp.inf)
         mixing = (inner * jnp.exp(log_gap) * step_ref[0, e]).astype(jnp.bfloat16)
         x_head = x_ref[:, e * HEADDIM : (e + 1) * HEADDIM]
         intra = jnp.dot(mixing, x_head, preferred_element_type=jnp.float32)
@@ -103,10 +105,9 @@
 def mamba_base(x_in, steps, cum, b_blocks, c_blocks, d_skip):
     slots, heads = steps.shape[:2]
     width = x_in.shape[1]
-    pair = 128 // HEADDIM
+    group = 8 if heads % 8 == 0 else 128 // HEADDIM
     inner = jnp.einsum("cin,cjn->cij", c_blocks, b_blocks, preferred_element_type=jnp.float32)
     cum_row = cum[:, :, None, :]
-    cum_col = cum[:, :, :, None]
     step_row = steps[:, :, None, :]
     skip_row = spread(d_skip)[None, :]
     cost = pl.CostEstimate(
@@ -117,18 +118,17 @@
     return pl.pallas_call(
         mamba_base_kernel,
         out_shape=jax.ShapeDtypeStruct((slots, BLOCK, width), jnp.float32),
-        grid=(slots, heads // pair),
+        grid=(slots, heads // group),
         in_specs=[
-            pl.BlockSpec((BLOCK, pair * HEADDIM), lambda c, g: (c, g)),
+            pl.BlockSpec((BLOCK, group * HEADDIM), lambda c, g: (c, g)),
             pl.BlockSpec((1, BLOCK, BLOCK), lambda c, g: (c, 0, 0)),
-            pl.BlockSpec((1, pair, 1, BLOCK), lambda c, g: (c, g, 0, 0)),
-            pl.BlockSpec((1, pair, BLOCK, 1), lambda c, g: (c, g, 0, 0)),
-            pl.BlockSpec((1, pair, 1, BLOCK), lambda c, g: (c, g, 0, 0)),
-            pl.BlockSpec((1, pair * HEADDIM), lambda c, g: (0, g)),
+            pl.BlockSpec((1, group, 1, BLOCK), lambda c, g: (c, g, 0, 0)),
+            pl.BlockSpec((1, group, 1, BLOCK), lambda c, g: (c, g, 0, 0)),
+            pl.BlockSpec((1, group * HEADDIM), lambda c, g: (0, g)),
         ],
-        out_specs=pl.BlockSpec((1, BLOCK, pair * HEADDIM), lambda c, g: (c, 0, g)),
+        out_specs=pl.BlockSpec((1, BLOCK, group * HEADDIM), lambda c, g: (c, 0, g)),
         cost_estimate=cost,
-    )(x_in, inner, cum_row, cum_col, step_row, skip_row)
+    )(x_in, inner, cum_row, step_row, skip_row)
 
 
 KEY_CHUNK = 256

time: 151 us -> 150 us (level)
  Pallas kernels: 33.3 us -> 20.8 us
  waiting for transfers between devices: 41.4 us -> 51.2 us
  starting transfers between devices: 16.7 us -> 21.1 us
  local copies, waits for them, and re-layouts: 17.7 us -> 15 us
    pallas_call x1, Pallas kernels: 21.3 us -> 8.88 us  [mamba_base(): pl.pallas_call(mamba_base_kernel, out_shape=jax.ShapeDtypeStruct((slots,...]
    ppermute x6, waiting for transfers between devices: 39.5 us -> 48.6 us  [entering_states(): lax.ppermute(totals[j].astype(jnp.bfloat16), 'seq', pairs)]
    ppermute x6, starting transfers between devices: 8.54 us -> 12.9 us  [entering_states(): lax.ppermute(totals[j].astype(jnp.bfloat16), 'seq', pairs)]
    broadcast_in_dim x1 -> x0, local copies, waits for them, and re-layouts: 2.65 us -> none  [mamba_base(): cum_col = cum[:, :, :, None]]
  transfers between devices with their start and end apart: 10 -> 10, of which waited for: 5 -> 7; matrix products, arithmetic and copies ran while one was open for 21% -> 19% of each run, Pallas kernels for 22% -> 14%
where the time goes in v10:
time: 150 us; the launch traced here: 149 us
  waiting for transfers between devices  51.2 us (34%)
  other arithmetic  23.6 us (16%)
  starting transfers between devices  21.1 us (14%)
  Pallas kernels  20.8 us (14%)
  local copies, waits for them, and re-layouts  15 us (10%)
  between operations  14.4 us (10%)
  matrix products  2.65 us (2%)
    ppermute x6, waiting for transfers between devices, entering_states(): lax.ppermute(totals[j].astype(jnp.bfloat16), 'seq', pairs)  48.6 us
    ppermute x6, starting transfers between devices, entering_states(): lax.ppermute(totals[j].astype(jnp.bfloat16), 'seq', pairs)  12.9 us
    pallas_call x1, Pallas kernels, attention_core(): pl.pallas_call(attention_kernel, out_shape=jax.ShapeDtypeStruct(queries.s...  12 us
    pallas_call x1, Pallas kernels, mamba_base(): pl.pallas_call(mamba_base_kernel, out_shape=jax.ShapeDtypeStruct((slots,...  8.88 us
    ppermute x3, starting transfers between devices, decay_scan(): got = lax.ppermute(total, 'seq', [(i, i ^ span) for i in range(count)])  8.13 us
    select_n x4, other arithmetic, entering_states(): jnp.where(lower, spread(own_a)[:, None, :] * got + totals[j], spread(got_...  5.54 us
    convert_element_type x6, other arithmetic, entering_states(): totals[j].astype(jnp.bfloat16)  4.05 us
    convert_element_type x5, other arithmetic, entering_states(): lax.ppermute(totals[j].astype(jnp.bfloat16), 'seq', pairs)  3.56 us
  transfers between devices with their start and end apart: 10, of which 7 were waited for; matrix products, arithmetic and copies ran while one was open for 19% of the time, Pallas kernels for 14%

profile of v10, /device:TPU:0, one launch (start us, length us, event | category | flops | bytes accessed | tf_op | source)
XLA Modules:
  0.0 148.8 jit_solution(12791657366419858491)
XLA Ops:
  7.2 1.7 %pad_maximum_fusion = bf16[2,128,512]{2,1,0:T(8,128)(2,1)} fusion(bf16[2,128,256]{2,1,0:T(8,128)(2,1)} %bitcast.74, bf16[2,128,256]{2,1,0:T(8,128)(2,1)} %bitcast.75), kind=kLoop, calls=%fused_computation.30 | loop fusion | flops 524288 | bytes 524288 | tf_op jit(solution)/shard_map/concatenate | solution.py:214
  11.2 3.0 %collective-permute-start = (f32[2,32]{1,0:T(2,128)S(1)}, f32[2,32]{1,0:T(2,128)S(1)}, u32[]{:S(2)}, u32[]{:S(2)}) collective-permute-start(f32[2,32]{1,0:T(2,128)S(1)} %exp.23), channel_id=1, source_target_pairs={{0,2},{2,0},{4,6},{6,4},{8,10},{10,8},{12,14},{14,12},{1,3},{3,1},... | collective-permute-start | bytes 776 | tf_op jit(solution)/shard_map/ppermute | solution.py:30
  15.1 1.4 bitcast_bitcast_fusion.1
  16.5 1.5 copy.17
  19.1 1.6 %broadcast_in_dim.112 = f32[2,128,32,64]{1,3,2,0:T(8,128)} broadcast(f32[2,128,32]{1,2,0:T(8,128)S(1)} %exponential_bitcast_fusion), dimensions={0,1,2} | broadcast | bytes 2129920 | tf_op jit(solution)/shard_map/broadcast_in_dim | solution.py:20
  20.6 3.0 %copy.20 = f32[2,128,2048]{2,1,0:T(8,128)} copy(f32[2,128,2048]{1,2,0:T(8,128)} %bitcast.66) | data formatting | bytes 4194304 | tf_op jit(solution)/shard_map/reshape | solution.py:20
  24.0 2.1 %collective-permute-start.3 = (f32[2,32]{1,0:T(2,128)S(1)}, f32[2,32]{1,0:T(2,128)S(1)}, u32[]{:S(2)}, u32[]{:S(2)}) collective-permute-start(f32[2,32]{1,0:T(2,128)S(1)} %exponential_multiply_fusion), channel_id=1, source_target_pairs={{0,4},{2,6},{4,0},{6,2},{8,12},{10,14},{12,8},{14,10},{1,5},{3,7},... | collective-permute-start | bytes 776 | tf_op jit(solution)/shard_map/ppermute | solution.py:30
  26.6 1.1 collective-permute-done.3
  27.7 3.0 %collective-permute-start.4 = (f32[2,32]{1,0:T(2,128)S(1)}, f32[2,32]{1,0:T(2,128)S(1)}, u32[]{:S(2)}, u32[]{:S(2)}) collective-permute-start(f32[2,32]{1,0:T(2,128)S(1)} %mul.284), channel_id=1, source_target_pairs={{0,8},{2,10},{4,12},{6,14},{8,0},{10,2},{12,4},{14,6},{1,9},{3,11}... | collective-permute-start | bytes 776 | tf_op jit(solution)/shard_map/ppermute | solution.py:30
  32.3 7.2 %collective-permute-done.1 = bf16[2,128,1024]{1,2,0:T(8,128)(2,1)} collective-permute-done((bf16[2,128,1024]{1,2,0:T(8,128)(2,1)S(1)}, bf16[2,128,1024]{1,2,0:T(8,128)(2,1)}, u32[]{:S(2)}, u32[]{:S(2)}) %collective-permute-start.1) | collective-permute-done | bytes 524320 | tf_op jit(solution)/shard_map/ppermute | solution.py:57
  39.5 1.1 convert_element_type.53
  41.4 0.9 copy-done.2
  42.4 1.6 %collective-permute-start.5 = (bf16[2,128,1024]{1,2,0:T(8,128)(2,1)S(1)}, bf16[2,128,1024]{1,2,0:T(8,128)(2,1)}, u32[]{:S(2)}, u32[]{:S(2)}) collective-permute-start(bf16[2,128,1024]{1,2,0:T(8,128)(2,1)S(1)} %convert_element_type.56), channel_id=1, source_target_pairs={{0,4},{2,6},{4,0},{6,2},{8,12},{10,14},{12,8},{14,10},{1,5},{3,7},... | collective-permute-start | bytes 1572872 | tf_op jit(solution)/shard_map/ppermute | solution.py:57
  43.9 0.9 convert_element_type.54
  47.1 8.9 %shard_map.104 = f32[2,128,2048]{2,1,0:T(8,128)} custom-call(bf16[256,2048]{1,0:T(8,128)(2,1)} %x_ref, f32[2,128,128]{2,1,0:T(8,128)} %fusion.23.inner_ref, f32[2,32,1,128]{3,2,1,0:T(1,128)} %bitcast.69, f32[2,32,1,128]{3,2,1,0:T(1,128)} %bitcast.73, f32[1,2048]{1,0:T(1,128)} %broadcast_in_dim_reshape.2.skip_ref), custom_call_target="tpu_custom_call" | custom-call | flops 140509184 | bytes 3145728 | tf_op jit(solution)/shard_map/pallas_call | solution.py:118
  56.0 11.6 %collective-permute-done.2 = bf16[2,128,1024]{1,2,0:T(8,128)(2,1)S(1)} collective-permute-done((bf16[2,128,1024]{1,2,0:T(8,128)(2,1)}, bf16[2,128,1024]{1,2,0:T(8,128)(2,1)S(1)}, u32[]{:S(2)}, u32[]{:S(2)}) %collective-permute-start.2) | collective-permute-done | bytes 524320 | tf_op jit(solution)/shard_map/ppermute | solution.py:57
  67.7 1.1 convert_element_type.57
  69.5 1.0 copy-done.1
  71.3 1.5 collective-permute-start.6
  72.8 1.5 %add_select_fusion.4 = f32[2,128,1024]{1,2,0:T(8,128)} fusion(f32[2,128,1024]{1,2,0:T(8,128)S(1)} %convert_element_type.57, f32[2,128,1024]{1,2,0:T(8,128)S(1)} %copy-done.3, f32[2,1024]{1,0:T(2,128)S(1)} %mul.314, f32[2,1024]{1,0:T(2,128)S(1)} %mul.311, pred[]{:T(512)S(6)} %eq.15), kind=kLoop, calls=%fused_computation.23 | loop fusion | flops 1310720 | bytes 3162113 | tf_op jit(solution)/shard_map/jit(_where)/select_n | solution.py:70
  75.1 2.1 %convert_element_type.60 = bf16[2,128,1024]{1,2,0:T(8,128)(2,1)} convert(f32[2,128,1024]{1,2,0:T(8,128)} %add_select_fusion.4) | non-fusion elementwise | flops 262144 | bytes 1572864 | tf_op jit(solution)/shard_map/convert_element_type | solution.py:57
  77.2 3.0 %collective-permute-start.7 = (bf16[2,128,1024]{1,2,0:T(8,128)(2,1)}, bf16[2,128,1024]{1,2,0:T(8,128)(2,1)}, u32[]{:S(2)}, u32[]{:S(2)}) collective-permute-start(bf16[2,128,1024]{1,2,0:T(8,128)(2,1)} %convert_element_type.60), channel_id=1, source_target_pairs={{0,8},{2,10},{4,12},{6,14},{8,0},{10,2},{12,4},{14,6},{1,9},{3,11}... | collective-permute-start | bytes 1572872 | tf_op jit(solution)/shard_map/ppermute | solution.py:57
  82.1 10.3 %collective-permute-done.6 = bf16[2,128,1024]{1,2,0:T(8,128)(2,1)} collective-permute-done((bf16[2,128,1024]{1,2,0:T(8,128)(2,1)}, bf16[2,128,1024]{1,2,0:T(8,128)(2,1)}, u32[]{:S(2)}, u32[]{:S(2)}) %collective-permute-start.6) | collective-permute-done | bytes 524320 | tf_op jit(solution)/shard_map/ppermute | solution.py:57
  92.4 2.6 %fusion.4 = f32[2,128,1024]{1,2,0:T(8,128)} fusion(f32[2,128,1024]{1,2,0:T(8,128)} %copy-done.1, bf16[2,128,1024]{1,2,0:T(8,128)(2,1)} %collective-permute-done.6, f32[2,1024]{1,0:T(2,128)S(1)} %mul.308, f32[2,1024]{1,0:T(2,128)S(1)} %mul.293, pred[]{:T(512)S(6)} %eq.15), kind=kLoop, calls=%fused_computation.16 | loop fusion | flops 1572864 | bytes 2637825 | tf_op jit(solution)/shard_map/jit(_where)/select_n | solution.py:70
  95.0 12.0 %shard_map.105 = bf16[256,1024]{1,0:T(8,128)(2,1)} custom-call(bf16[256,1024]{1,0:T(8,128)(2,1)} %q_ref, bf16[2,1024,512]{2,1,0:T(8,128)(2,1)} %all-gather.2.cloned.1.call-done.k_ref.v_ref, bf16[2,1024,512]{2,1,0:T(8,128)(2,1)} %all-gather.2.cloned.1.call-done.k_ref.v_ref), custom_call_target="tpu_custom_call" | custom-call | flops 2147483648 | bytes 3145728 | tf_op jit(solution)/shard_map/pallas_call | solution.py:194
  107.0 1.2 convert_element_type.61
  108.5 6.2 %collective-permute-start.8 = (bf16[2,128,1024]{1,2,0:T(8,128)(2,1)S(1)}, bf16[2,128,1024]{1,2,0:T(8,128)(2,1)S(1)}, u32[]{:S(2)}, u32[]{:S(2)}) collective-permute-start(bf16[2,128,1024]{1,2,0:T(8,128)(2,1)S(1)} %convert_element_type.62), channel_id=1, source_target_pairs={{0,8},{2,10},{4,12},{6,14},{8,0},{10,2},{12,4},{14,6},{1,9},{3,11}... | collective-permute-start | bytes 1572872 | tf_op jit(solution)/shard_map/ppermute | solution.py:57
  115.4 0.9 slice_add_fusion.3
  117.1 19.5 %collective-permute-done.8 = bf16[2,128,1024]{1,2,0:T(8,128)(2,1)S(1)} collective-permute-done((bf16[2,128,1024]{1,2,0:T(8,128)(2,1)S(1)}, bf16[2,128,1024]{1,2,0:T(8,128)(2,1)S(1)}, u32[]{:S(2)}, u32[]{:S(2)}) %collective-permute-start.8) | collective-permute-done | bytes 524320 | tf_op jit(solution)/shard_map/ppermute | solution.py:57
  136.6 1.7 %add_select_fusion = f32[2,128,1024]{1,2,0:T(8,128)S(1)} fusion(bf16[2,128,1024]{1,2,0:T(8,128)(2,1)} %collective-permute-done.6, f32[2,128,1024]{1,2,0:T(8,128)S(1)} %convert_element_type.55, f32[2,1024]{1,0:T(2,128)S(1)} %mul.342, f32[2,1024]{1,0:T(2,128)S(1)} %mul.339, pred[]{:T(512)S(6)} %eq.13, pred[]{:T(512)S(6)} %eq.15, pred[]{:T(512)S(6)} %eq.14, ...), kind=kLoop, calls=%fused_computation.6 | loop fusion | flops 2359296 | bytes 3162115 | tf_op jit(solution)/shard_map/jit(_where)/select_n | solution.py:69
  138.3 0.9 slice_add_fusion.1
  140.5 1.4 fusion.1
  (128 shorter events, 17.1 us)
Async XLA Ops:
  7.2 11.2 %copy-start = (bf16[256,128]{1,0:T(8,128)(2,1)S(1)}, bf16[256,128]{1,0:T(8,128)(2,1)}, u32[]{:S(2)}) copy-start(bf16[256,128]{1,0:T(8,128)(2,1)} %param.13) | copy-start | bytes 196612
  7.2 67.9 %all-gather.2.cloned.1.call-start = ((), (), s32[]{:S(2)}) async-start(), calls=%async_computation | async-start | bytes 2359296 | tf_op jit(solution)/shard_map/all_gather | solution.py:218
  11.0 7.3 %copy-start.10 = (f32[2,32,128]{2,1,0:T(8,128)}, f32[2,32,128]{2,1,0:T(8,128)S(1)}, u32[]{:S(2)}) copy-start(f32[2,32,128]{2,1,0:T(8,128)S(1)} %reduce_window_sum.11) | copy-start | bytes 98308
  11.2 12.4 %collective-permute-start = (f32[2,32]{1,0:T(2,128)S(1)}, f32[2,32]{1,0:T(2,128)S(1)}, u32[]{:S(2)}, u32[]{:S(2)}) collective-permute-start(f32[2,32]{1,0:T(2,128)S(1)} %exp.23), channel_id=1, source_target_pairs={{0,2},{2,0},{4,6},{6,4},{8,10},{10,8},{12,14},{14,12},{1,3},{3,1},... | collective-permute-start | bytes 776 | tf_op jit(solution)/shard_map/ppermute | solution.py:30
  18.9 25.0 %copy-start.4 = (f32[2,128,1024]{1,2,0:T(8,128)}, f32[2,128,1024]{1,2,0:T(8,128)S(1)}, u32[]{:S(2)}) copy-start(f32[2,128,1024]{1,2,0:T(8,128)S(1)} %get-tuple-element.29) | copy-start | bytes 3145732
  23.7 15.8 %collective-permute-start.1 = (bf16[2,128,1024]{1,2,0:T(8,128)(2,1)S(1)}, bf16[2,128,1024]{1,2,0:T(8,128)(2,1)}, u32[]{:S(2)}, u32[]{:S(2)}) collective-permute-start(bf16[2,128,1024]{1,2,0:T(8,128)(2,1)S(1)} %convert_element_type.52), channel_id=1, source_target_pairs={{0,2},{2,0},{4,6},{6,4},{8,10},{10,8},{12,14},{14,12},{1,3},{3,1},... | collective-permute-start | bytes 1572872 | tf_op jit(solution)/shard_map/ppermute | solution.py:57
  24.0 3.7 %collective-permute-start.3 = (f32[2,32]{1,0:T(2,128)S(1)}, f32[2,32]{1,0:T(2,128)S(1)}, u32[]{:S(2)}, u32[]{:S(2)}) collective-permute-start(f32[2,32]{1,0:T(2,128)S(1)} %exponential_multiply_fusion), channel_id=1, source_target_pairs={{0,4},{2,6},{4,0},{6,2},{8,12},{10,14},{12,8},{14,10},{1,5},{3,7},... | collective-permute-start | bytes 776 | tf_op jit(solution)/shard_map/ppermute | solution.py:30
  27.7 4.5 %collective-permute-start.4 = (f32[2,32]{1,0:T(2,128)S(1)}, f32[2,32]{1,0:T(2,128)S(1)}, u32[]{:S(2)}, u32[]{:S(2)}) collective-permute-start(f32[2,32]{1,0:T(2,128)S(1)} %mul.284), channel_id=1, source_target_pairs={{0,8},{2,10},{4,12},{6,14},{8,0},{10,2},{12,4},{14,6},{1,9},{3,11}... | collective-permute-start | bytes 776 | tf_op jit(solution)/shard_map/ppermute | solution.py:30
  31.3 10.0 %copy-start.12 = (f32[2,1024]{1,0:T(2,128)}, f32[2,1024]{1,0:T(2,128)S(1)}, u32[]{:S(2)}) copy-start(f32[2,1024]{1,0:T(2,128)S(1)} %mul.328) | copy-start | bytes 24580
  31.5 9.9 %copy-start.13 = (f32[2,1024]{1,0:T(2,128)}, f32[2,1024]{1,0:T(2,128)S(1)}, u32[]{:S(2)}) copy-start(f32[2,1024]{1,0:T(2,128)S(1)} %mul.351) | copy-start | bytes 24580
  41.3 1.0 copy-start.2
  41.3 4.2 %copy-start.16 = (f32[32]{0:T(128)S(1)}, f32[32]{0:T(128)}, u32[]{:S(2)}) copy-start(f32[32]{0:T(128)} %param.12) | copy-start | bytes 388
  41.4 4.9 %copy-start.11 = (bf16[256,128]{1,0:T(8,128)(2,1)S(1)}, bf16[256,128]{1,0:T(8,128)(2,1)}, u32[]{:S(2)}) copy-start(bf16[256,128]{1,0:T(8,128)(2,1)} %param.14) | copy-start | bytes 196612
  42.4 25.3 %collective-permute-start.5 = (bf16[2,128,1024]{1,2,0:T(8,128)(2,1)S(1)}, bf16[2,128,1024]{1,2,0:T(8,128)(2,1)}, u32[]{:S(2)}, u32[]{:S(2)}) collective-permute-start(bf16[2,128,1024]{1,2,0:T(8,128)(2,1)S(1)} %convert_element_type.56), channel_id=1, source_target_pairs={{0,4},{2,6},{4,0},{6,2},{8,12},{10,14},{12,8},{14,10},{1,5},{3,7},... | collective-permute-start | bytes 1572872 | tf_op jit(solution)/shard_map/ppermute | solution.py:57
  44.8 22.8 %collective-permute-start.2 = (bf16[2,128,1024]{1,2,0:T(8,128)(2,1)}, bf16[2,128,1024]{1,2,0:T(8,128)(2,1)S(1)}, u32[]{:S(2)}, u32[]{:S(2)}) collective-permute-start(bf16[2,128,1024]{1,2,0:T(8,128)(2,1)} %convert_element_type.54), channel_id=1, source_target_pairs={{0,2},{2,0},{4,6},{6,4},{8,10},{10,8},{12,14},{14,12},{1,3},{3,1},... | collective-permute-start | bytes 1572872 | tf_op jit(solution)/shard_map/ppermute | solution.py:57
  56.0 12.8 %copy-start.5 = (f32[2,128,1024]{1,2,0:T(8,128)S(1)}, f32[2,128,1024]{1,2,0:T(8,128)}, u32[]{:S(2)}) copy-start(f32[2,128,1024]{1,2,0:T(8,128)} %copy-done.4) | copy-start | bytes 3145732
  68.8 4.1 %copy-start.3 = (f32[2,128,1024]{1,2,0:T(8,128)S(1)}, f32[2,128,1024]{1,2,0:T(8,128)}, u32[]{:S(2)}) copy-start(f32[2,128,1024]{1,2,0:T(8,128)} %copy-done.2) | copy-start | bytes 3145732
  69.5 1.0 copy-start.1
  71.3 21.0 %collective-permute-start.6 = (bf16[2,128,1024]{1,2,0:T(8,128)(2,1)}, bf16[2,128,1024]{1,2,0:T(8,128)(2,1)}, u32[]{:S(2)}, u32[]{:S(2)}) collective-permute-start(bf16[2,128,1024]{1,2,0:T(8,128)(2,1)} %convert_element_type.58), channel_id=1, source_target_pairs={{0,4},{2,6},{4,0},{6,2},{8,12},{10,14},{12,8},{14,10},{1,5},{3,7},... | collective-permute-start | bytes 1572872 | tf_op jit(solution)/shard_map/ppermute | solution.py:57
  77.2 29.8 %collective-permute-start.7 = (bf16[2,128,1024]{1,2,0:T(8,128)(2,1)}, bf16[2,128,1024]{1,2,0:T(8,128)(2,1)}, u32[]{:S(2)}, u32[]{:S(2)}) collective-permute-start(bf16[2,128,1024]{1,2,0:T(8,128)(2,1)} %convert_element_type.60), channel_id=1, source_target_pairs={{0,8},{2,10},{4,12},{6,14},{8,0},{10,2},{12,4},{14,6},{1,9},{3,11}... | collective-permute-start | bytes 1572872 | tf_op jit(solution)/shard_map/ppermute | solution.py:57
  81.1 25.8 %copy-start.14 = (f32[2,1024]{1,0:T(2,128)}, f32[2,1024]{1,0:T(2,128)S(1)}, u32[]{:S(2)}) copy-start(f32[2,1024]{1,0:T(2,128)S(1)} %mul.331) | copy-start | bytes 24580
  82.0 24.9 %copy-start.15 = (f32[2,1024]{1,0:T(2,128)}, f32[2,1024]{1,0:T(2,128)S(1)}, u32[]{:S(2)}) copy-start(f32[2,1024]{1,0:T(2,128)S(1)} %mul.354) | copy-start | bytes 24580
  107.0 1.4 copy-start.9
  108.4 7.0 %copy-start.8 = (f32[2,128,1024]{1,2,0:T(8,128)S(1)}, f32[2,128,1024]{1,2,0:T(8,128)}, u32[]{:S(2)}) copy-start(f32[2,128,1024]{1,2,0:T(8,128)} %add_select_fusion.4) | copy-start | bytes 3145732
  108.4 7.0 %slice-start = ((f32[2,1024]{1,0:T(2,128)}), f32[1,1024]{1,0:T(1,128)S(1)}, s32[]{:S(2)}) async-start(f32[2,1024]{1,0:T(2,128)} %copy-done.12), calls=%async_computation.1 | async-start | bytes 8192 | tf_op jit(solution)/shard_map/slice | solution.py:84
  108.5 7.0 %slice-start.2 = ((f32[2,1024]{1,0:T(2,128)}), f32[1,1024]{1,0:T(1,128)S(1)}, s32[]{:S(2)}) async-start(f32[2,1024]{1,0:T(2,128)} %copy-done.14), calls=%async_computation.3 | async-start | bytes 8192 | tf_op jit(solution)/shard_map/slice | solution.py:84
  108.5 28.1 %collective-permute-start.8 = (bf16[2,128,1024]{1,2,0:T(8,128)(2,1)S(1)}, bf16[2,128,1024]{1,2,0:T(8,128)(2,1)S(1)}, u32[]{:S(2)}, u32[]{:S(2)}) collective-permute-start(bf16[2,128,1024]{1,2,0:T(8,128)(2,1)S(1)} %convert_element_type.62), channel_id=1, source_target_pairs={{0,8},{2,10},{4,12},{6,14},{8,0},{10,2},{12,4},{14,6},{1,9},{3,11}... | collective-permute-start | bytes 1572872 | tf_op jit(solution)/shard_map/ppermute | solution.py:57
  117.1 21.2 %slice-start.1 = ((f32[2,1024]{1,0:T(2,128)}), f32[1,1024]{1,0:T(1,128)S(1)}, s32[]{:S(2)}) async-start(f32[2,1024]{1,0:T(2,128)} %copy-done.13), calls=%async_computation.2 | async-start | bytes 8192 | tf_op jit(solution)/shard_map/slice | solution.py:84
  117.1 21.2 %slice-start.3 = ((f32[2,1024]{1,0:T(2,128)}), f32[1,1024]{1,0:T(1,128)S(1)}, s32[]{:S(2)}) async-start(f32[2,1024]{1,0:T(2,128)} %copy-done.15), calls=%async_computation.4 | async-start | bytes 8192 | tf_op jit(solution)/shard_map/slice | solution.py:84
  138.3 1.6 %copy-start.6 = (f32[2,128,2048]{2,1,0:T(8,128)S(1)}, f32[2,128,2048]{2,1,0:T(8,128)}, u32[]{:S(2)}) copy-start(f32[2,128,2048]{2,1,0:T(8,128)} %copy.20) | copy-start | bytes 6291460
  138.3 2.2 %copy-start.7 = (f32[2,128,2048]{2,1,0:T(8,128)S(1)}, f32[2,128,2048]{2,1,0:T(8,128)}, u32[]{:S(2)}) copy-start(f32[2,128,2048]{2,1,0:T(8,128)} %shard_map.104) | copy-start | bytes 6291460
Sparse Core Ops, SparseCore 0:
  14.3 60.7 all-gather.1

commit v11 on v10

--- a/solution.py
+++ b/solution.py
@@ -229,7 +229,7 @@
     decay = jnp.exp(log_total)
     parts = 2 if heads % 2 == 0 else 1
     hooks = {
-        (1, 0): (mamba_base, (x_in, steps, cum, b_blocks, c_blocks, d_skip)),
+        (0, 0): (mamba_base, (x_in, steps, cum, b_blocks, c_blocks, d_skip)),
         (0, -1): (attention_core, (queries, kv_piece)),
     }
     incoming, results = entering_states(decay, block_state, seq_count, my_index, hooks, parts)

time: 150 us -> 150 us (level)
  the two profiles are of different devices: /device:TPU:0 before, /device:TPU:31 now
where the time goes in v11:
time: 150 us; the launch traced here: 149 us
  waiting for transfers between devices  59.7 us (40%)
  Pallas kernels  29.8 us (20%)
  other arithmetic  23.5 us (16%)
  local copies, waits for them, and re-layouts  14.4 us (10%)
  between operations  14.4 us (10%)
  starting transfers between devices  4.69 us (3%)
  matrix products  2.65 us (2%)
    ppermute x6, waiting for transfers between devices, entering_states(): lax.ppermute(totals[j].astype(jnp.bfloat16), 'seq', pairs)  56.5 us
    pallas_call x1, Pallas kernels, attention_core(): pl.pallas_call(attention_kernel, out_shape=jax.ShapeDtypeStruct(queries.s...  21 us
    pallas_call x1, Pallas kernels, mamba_base(): pl.pallas_call(mamba_base_kernel, out_shape=jax.ShapeDtypeStruct((slots,...  8.88 us
    select_n x4, other arithmetic, entering_states(): jnp.where(lower, spread(own_a)[:, None, :] * got + totals[j], spread(got_...  6.45 us
    convert_element_type x6, other arithmetic, entering_states(): totals[j].astype(jnp.bfloat16)  4.08 us
    ppermute x6, starting transfers between devices, entering_states(): lax.ppermute(totals[j].astype(jnp.bfloat16), 'seq', pairs)  4.05 us
    ppermute x3, waiting for transfers between devices, decay_scan(): got = lax.ppermute(total, 'seq', [(i, i ^ span) for i in range(count)])  3.2 us
    broadcast_in_dim x24, local copies, waits for them, and re-layouts, spread(): return jnp.repeat(a, HEADDIM, axis=-1)  3.12 us
  transfers between devices with their start and end apart: 10, of which 4 were waited for; matrix products, arithmetic and copies ran while one was open for 19% of the time, Pallas kernels for 20%

profile of v11, /device:TPU:31, one launch (start us, length us, event | category | flops | bytes accessed | tf_op | source)
XLA Modules:
  0.0 149.2 jit_solution(14338578287757071477)
XLA Ops:
  7.2 1.7 %pad_maximum_fusion = bf16[2,128,512]{2,1,0:T(8,128)(2,1)} fusion(bf16[2,128,256]{2,1,0:T(8,128)(2,1)} %bitcast.74, bf16[2,128,256]{2,1,0:T(8,128)(2,1)} %bitcast.75), kind=kLoop, calls=%fused_computation.34 | loop fusion | flops 524288 | bytes 524288 | tf_op jit(solution)/shard_map/concatenate | solution.py:214
  9.6 0.8 broadcast_multiply_fusion
  11.5 0.8 fusion.13
  12.4 1.4 bitcast_bitcast_fusion.1
  13.8 1.5 copy.17
  16.4 1.5 %broadcast_in_dim.112 = f32[2,128,32,64]{1,3,2,0:T(8,128)} broadcast(f32[2,128,32]{1,2,0:T(8,128)S(1)} %exponential_bitcast_fusion), dimensions={0,1,2} | broadcast | bytes 2129920 | tf_op jit(solution)/shard_map/broadcast_in_dim | solution.py:20
  17.9 3.0 %copy.20 = f32[2,128,2048]{2,1,0:T(8,128)} copy(f32[2,128,2048]{1,2,0:T(8,128)} %bitcast.66) | data formatting | bytes 4194304 | tf_op jit(solution)/shard_map/reshape | solution.py:20
  20.9 1.3 collective-permute-start.1
  22.5 0.8 fusion.25.inner_ref
  24.4 8.9 %shard_map.104 = f32[2,128,2048]{2,1,0:T(8,128)} custom-call(bf16[256,2048]{1,0:T(8,128)(2,1)} %x_ref, f32[2,128,128]{2,1,0:T(8,128)} %fusion.25.inner_ref, f32[2,32,1,128]{3,2,1,0:T(1,128)} %bitcast.69, f32[2,32,1,128]{3,2,1,0:T(1,128)} %bitcast.73, f32[1,2048]{1,0:T(1,128)} %broadcast_in_dim_reshape.2.skip_ref), custom_call_target="tpu_custom_call" | custom-call | flops 140509184 | bytes 3145728 | tf_op jit(solution)/shard_map/pallas_call | solution.py:118
  33.8 3.2 %collective-permute-done.3 = f32[2,32]{1,0:T(2,128)S(1)} collective-permute-done((f32[2,32]{1,0:T(2,128)S(1)}, f32[2,32]{1,0:T(2,128)S(1)}, u32[]{:S(2)}, u32[]{:S(2)}) %collective-permute-start.3) | collective-permute-done | bytes 288 | tf_op jit(solution)/shard_map/ppermute | solution.py:30
  37.0 1.1 convert_element_type.53
  38.1 0.7 add_select_fusion.5
  38.9 1.0 copy-done.1
  39.9 0.9 convert_element_type.56
  40.7 1.3 collective-permute-start.5
  43.3 25.6 %collective-permute-done.5 = bf16[2,128,1024]{1,2,0:T(8,128)(2,1)S(1)} collective-permute-done((bf16[2,128,1024]{1,2,0:T(8,128)(2,1)}, bf16[2,128,1024]{1,2,0:T(8,128)(2,1)S(1)}, u32[]{:S(2)}, u32[]{:S(2)}) %collective-permute-start.5) | collective-permute-done | bytes 524320 | tf_op jit(solution)/shard_map/ppermute | solution.py:57
  68.9 1.8 %fusion.4 = f32[2,128,1024]{1,2,0:T(8,128)S(1)} fusion(f32[2,128,1024]{1,2,0:T(8,128)S(1)} %copy-done.4, bf16[2,128,1024]{1,2,0:T(8,128)(2,1)} %collective-permute-done.4, f32[2,1024]{1,0:T(2,128)S(1)} %mul.298, f32[2,1024]{1,0:T(2,128)S(1)} %mul.295, pred[]{:T(512)S(6)} %eq.13), kind=kLoop, calls=%fused_computation.19 | loop fusion | flops 1572864 | bytes 2637825 | tf_op jit(solution)/shard_map/jit(_where)/select_n | solution.py:70
  70.7 0.9 convert_element_type.58
  71.6 1.5 %add_select_fusion.4 = f32[2,128,1024]{1,2,0:T(8,128)} fusion(f32[2,128,1024]{1,2,0:T(8,128)S(1)} %convert_element_type.57, f32[2,128,1024]{1,2,0:T(8,128)S(1)} %copy-done.2, f32[2,1024]{1,0:T(2,128)S(1)} %mul.314, f32[2,1024]{1,0:T(2,128)S(1)} %mul.311, pred[]{:T(512)S(6)} %eq.15), kind=kLoop, calls=%fused_computation.28 | loop fusion | flops 1310720 | bytes 3162113 | tf_op jit(solution)/shard_map/jit(_where)/select_n | solution.py:70
  73.1 2.1 %convert_element_type.60 = bf16[2,128,1024]{1,2,0:T(8,128)(2,1)} convert(f32[2,128,1024]{1,2,0:T(8,128)} %add_select_fusion.4) | non-fusion elementwise | flops 262144 | bytes 1572864 | tf_op jit(solution)/shard_map/convert_element_type | solution.py:57
  75.2 1.1 collective-permute-start.7
  78.2 11.7 %collective-permute-done.6 = bf16[2,128,1024]{1,2,0:T(8,128)(2,1)} collective-permute-done((bf16[2,128,1024]{1,2,0:T(8,128)(2,1)}, bf16[2,128,1024]{1,2,0:T(8,128)(2,1)}, u32[]{:S(2)}, u32[]{:S(2)}) %collective-permute-start.6) | collective-permute-done | bytes 524320 | tf_op jit(solution)/shard_map/ppermute | solution.py:57
  89.9 2.4 %fusion.6 = f32[2,128,1024]{1,2,0:T(8,128)} fusion(f32[2,128,1024]{1,2,0:T(8,128)S(1)} %fusion.4, bf16[2,128,1024]{1,2,0:T(8,128)(2,1)} %collective-permute-done.6, f32[2,1024]{1,0:T(2,128)S(1)} %mul.308, f32[2,1024]{1,0:T(2,128)S(1)} %mul.293, pred[]{:T(512)S(6)} %eq.15), kind=kLoop, calls=%fused_computation.21 | loop fusion | flops 1572864 | bytes 2637825 | tf_op jit(solution)/shard_map/jit(_where)/select_n | solution.py:70
  92.3 21.0 %shard_map.105 = bf16[256,1024]{1,0:T(8,128)(2,1)} custom-call(bf16[256,1024]{1,0:T(8,128)(2,1)} %q_ref, bf16[2,1024,512]{2,1,0:T(8,128)(2,1)} %all-gather.2.cloned.1.call-done.k_ref.v_ref, bf16[2,1024,512]{2,1,0:T(8,128)(2,1)} %all-gather.2.cloned.1.call-done.k_ref.v_ref), custom_call_target="tpu_custom_call" | custom-call | flops 2147483648 | bytes 3145728 | tf_op jit(solution)/shard_map/pallas_call | solution.py:194
  113.3 1.2 convert_element_type.61
  114.9 0.7 add_select_fusion.2
  116.0 0.9 slice_add_fusion.3
  117.6 19.2 %collective-permute-done.8 = bf16[2,128,1024]{1,2,0:T(8,128)(2,1)S(1)} collective-permute-done((bf16[2,128,1024]{1,2,0:T(8,128)(2,1)S(1)}, bf16[2,128,1024]{1,2,0:T(8,128)(2,1)S(1)}, u32[]{:S(2)}, u32[]{:S(2)}) %collective-permute-start.8) | collective-permute-done | bytes 524320 | tf_op jit(solution)/shard_map/ppermute | solution.py:57
  136.9 1.8 %add_select_fusion = f32[2,128,1024]{1,2,0:T(8,128)S(1)} fusion(bf16[2,128,1024]{1,2,0:T(8,128)(2,1)} %collective-permute-done.4, bf16[2,128,1024]{1,2,0:T(8,128)(2,1)} %collective-permute-done.6, f32[2,1024]{1,0:T(2,128)S(1)} %mul.342, f32[2,1024]{1,0:T(2,128)S(1)} %mul.339, pred[]{:T(512)S(6)} %eq.13, pred[]{:T(512)S(6)} %eq.15, pred[]{:T(512)S(6)} %eq.14, ...), kind=kLoop, calls=%fused_computation.6 | loop fusion | flops 2621440 | bytes 2637827 | tf_op jit(solution)/shard_map/jit(_where)/select_n | solution.py:69
  138.7 0.9 slice_add_fusion.1
  141.0 1.4 fusion.1
  (125 shorter events, 10.8 us)
Async XLA Ops:
  7.2 8.5 %copy-start = (bf16[256,128]{1,0:T(8,128)(2,1)S(1)}, bf16[256,128]{1,0:T(8,128)(2,1)}, u32[]{:S(2)}) copy-start(bf16[256,128]{1,0:T(8,128)(2,1)} %param.13) | copy-start | bytes 196612
  7.2 65.9 %all-gather.2.cloned.1.call-start = ((), (), s32[]{:S(2)}) async-start(), calls=%async_computation | async-start | bytes 2359296 | tf_op jit(solution)/shard_map/all_gather | solution.py:218
  11.0 4.6 %copy-start.9 = (f32[2,32,128]{2,1,0:T(8,128)}, f32[2,32,128]{2,1,0:T(8,128)S(1)}, u32[]{:S(2)}) copy-start(f32[2,32,128]{2,1,0:T(8,128)S(1)} %reduce_window_sum.11) | copy-start | bytes 98308
  11.2 9.7 %collective-permute-start = (f32[2,32]{1,0:T(2,128)S(1)}, f32[2,32]{1,0:T(2,128)S(1)}, u32[]{:S(2)}, u32[]{:S(2)}) collective-permute-start(f32[2,32]{1,0:T(2,128)S(1)} %exp.23), channel_id=1, source_target_pairs={{0,2},{2,0},{4,6},{6,4},{8,10},{10,8},{12,14},{14,12},{1,3},{3,1},... | collective-permute-start | bytes 776 | tf_op jit(solution)/shard_map/ppermute | solution.py:30
  16.2 25.8 %copy-start.3 = (f32[2,128,1024]{1,2,0:T(8,128)}, f32[2,128,1024]{1,2,0:T(8,128)S(1)}, u32[]{:S(2)}) copy-start(f32[2,128,1024]{1,2,0:T(8,128)S(1)} %get-tuple-element.37) | copy-start | bytes 3145732
  17.9 4.6 %copy-start.10 = (bf16[256,128]{1,0:T(8,128)(2,1)S(1)}, bf16[256,128]{1,0:T(8,128)(2,1)}, u32[]{:S(2)}) copy-start(bf16[256,128]{1,0:T(8,128)(2,1)} %param.14) | copy-start | bytes 196612
  17.9 5.5 %copy-start.15 = (f32[32]{0:T(128)S(1)}, f32[32]{0:T(128)}, u32[]{:S(2)}) copy-start(f32[32]{0:T(128)} %param.12) | copy-start | bytes 388
  20.9 16.1 %collective-permute-start.1 = (bf16[2,128,1024]{1,2,0:T(8,128)(2,1)S(1)}, bf16[2,128,1024]{1,2,0:T(8,128)(2,1)}, u32[]{:S(2)}, u32[]{:S(2)}) collective-permute-start(bf16[2,128,1024]{1,2,0:T(8,128)(2,1)S(1)} %convert_element_type.52), channel_id=1, source_target_pairs={{0,2},{2,0},{4,6},{6,4},{8,10},{10,8},{12,14},{14,12},{1,3},{3,1},... | collective-permute-start | bytes 1572872 | tf_op jit(solution)/shard_map/ppermute | solution.py:57
  22.2 11.4 %collective-permute-start.2 = (f32[2,32]{1,0:T(2,128)S(1)}, f32[2,32]{1,0:T(2,128)S(1)}, u32[]{:S(2)}, u32[]{:S(2)}) collective-permute-start(f32[2,32]{1,0:T(2,128)S(1)} %exponential_multiply_fusion), channel_id=1, source_target_pairs={{0,4},{2,6},{4,0},{6,2},{8,12},{10,14},{12,8},{14,10},{1,5},{3,7},... | collective-permute-start | bytes 776 | tf_op jit(solution)/shard_map/ppermute | solution.py:30
  33.6 3.4 %collective-permute-start.3 = (f32[2,32]{1,0:T(2,128)S(1)}, f32[2,32]{1,0:T(2,128)S(1)}, u32[]{:S(2)}, u32[]{:S(2)}) collective-permute-start(f32[2,32]{1,0:T(2,128)S(1)} %mul.284), channel_id=1, source_target_pairs={{0,8},{2,10},{4,12},{6,14},{8,0},{10,2},{12,4},{14,6},{1,9},{3,11}... | collective-permute-start | bytes 776 | tf_op jit(solution)/shard_map/ppermute | solution.py:30
  38.9 1.0 copy-start.1
  40.7 28.1 %collective-permute-start.5 = (bf16[2,128,1024]{1,2,0:T(8,128)(2,1)}, bf16[2,128,1024]{1,2,0:T(8,128)(2,1)S(1)}, u32[]{:S(2)}, u32[]{:S(2)}) collective-permute-start(bf16[2,128,1024]{1,2,0:T(8,128)(2,1)} %convert_element_type.56), channel_id=1, source_target_pairs={{0,4},{2,6},{4,0},{6,2},{8,12},{10,14},{12,8},{14,10},{1,5},{3,7},... | collective-permute-start | bytes 1572872 | tf_op jit(solution)/shard_map/ppermute | solution.py:57
  42.1 26.8 %collective-permute-start.4 = (bf16[2,128,1024]{1,2,0:T(8,128)(2,1)S(1)}, bf16[2,128,1024]{1,2,0:T(8,128)(2,1)}, u32[]{:S(2)}, u32[]{:S(2)}) collective-permute-start(bf16[2,128,1024]{1,2,0:T(8,128)(2,1)S(1)} %convert_element_type.54), channel_id=1, source_target_pairs={{0,2},{2,0},{4,6},{6,4},{8,10},{10,8},{12,14},{14,12},{1,3},{3,1},... | collective-permute-start | bytes 1572872 | tf_op jit(solution)/shard_map/ppermute | solution.py:57
  42.9 27.7 %copy-start.11 = (f32[2,1024]{1,0:T(2,128)}, f32[2,1024]{1,0:T(2,128)S(1)}, u32[]{:S(2)}) copy-start(f32[2,1024]{1,0:T(2,128)S(1)} %mul.328) | copy-start | bytes 24580
  43.1 27.6 %copy-start.12 = (f32[2,1024]{1,0:T(2,128)}, f32[2,1024]{1,0:T(2,128)S(1)}, u32[]{:S(2)}) copy-start(f32[2,1024]{1,0:T(2,128)S(1)} %mul.351) | copy-start | bytes 24580
  43.1 25.8 %copy-start.4 = (f32[2,128,1024]{1,2,0:T(8,128)S(1)}, f32[2,128,1024]{1,2,0:T(8,128)}, u32[]{:S(2)}) copy-start(f32[2,128,1024]{1,2,0:T(8,128)} %copy-done.3) | copy-start | bytes 3145732
  68.9 2.7 %copy-start.2 = (f32[2,128,1024]{1,2,0:T(8,128)S(1)}, f32[2,128,1024]{1,2,0:T(8,128)}, u32[]{:S(2)}) copy-start(f32[2,128,1024]{1,2,0:T(8,128)} %copy-done.1) | copy-start | bytes 3145732
  71.6 18.3 %collective-permute-start.6 = (bf16[2,128,1024]{1,2,0:T(8,128)(2,1)}, bf16[2,128,1024]{1,2,0:T(8,128)(2,1)}, u32[]{:S(2)}, u32[]{:S(2)}) collective-permute-start(bf16[2,128,1024]{1,2,0:T(8,128)(2,1)} %convert_element_type.58), channel_id=1, source_target_pairs={{0,4},{2,6},{4,0},{6,2},{8,12},{10,14},{12,8},{14,10},{1,5},{3,7},... | collective-permute-start | bytes 1572872 | tf_op jit(solution)/shard_map/ppermute | solution.py:57
  75.2 38.1 %collective-permute-start.7 = (bf16[2,128,1024]{1,2,0:T(8,128)(2,1)}, bf16[2,128,1024]{1,2,0:T(8,128)(2,1)}, u32[]{:S(2)}, u32[]{:S(2)}) collective-permute-start(bf16[2,128,1024]{1,2,0:T(8,128)(2,1)} %convert_element_type.60), channel_id=1, source_target_pairs={{0,8},{2,10},{4,12},{6,14},{8,0},{10,2},{12,4},{14,6},{1,9},{3,11}... | collective-permute-start | bytes 1572872 | tf_op jit(solution)/shard_map/ppermute | solution.py:57
  77.3 36.0 %copy-start.13 = (f32[2,1024]{1,0:T(2,128)}, f32[2,1024]{1,0:T(2,128)S(1)}, u32[]{:S(2)}) copy-start(f32[2,1024]{1,0:T(2,128)S(1)} %mul.331) | copy-start | bytes 24580
  78.2 35.1 %copy-start.14 = (f32[2,1024]{1,0:T(2,128)}, f32[2,1024]{1,0:T(2,128)S(1)}, u32[]{:S(2)}) copy-start(f32[2,1024]{1,0:T(2,128)S(1)} %mul.354) | copy-start | bytes 24580
  113.3 1.4 copy-start.8
  114.8 1.2 copy-start.7
  114.8 1.2 slice-start
  114.8 1.2 slice-start.2
  114.8 22.1 %collective-permute-start.8 = (bf16[2,128,1024]{1,2,0:T(8,128)(2,1)S(1)}, bf16[2,128,1024]{1,2,0:T(8,128)(2,1)S(1)}, u32[]{:S(2)}, u32[]{:S(2)}) collective-permute-start(bf16[2,128,1024]{1,2,0:T(8,128)(2,1)S(1)} %convert_element_type.62), channel_id=1, source_target_pairs={{0,8},{2,10},{4,12},{6,14},{8,0},{10,2},{12,4},{14,6},{1,9},{3,11}... | collective-permute-start | bytes 1572872 | tf_op jit(solution)/shard_map/ppermute | solution.py:57
  117.6 21.1 %slice-start.1 = ((f32[2,1024]{1,0:T(2,128)}), f32[1,1024]{1,0:T(1,128)S(1)}, s32[]{:S(2)}) async-start(f32[2,1024]{1,0:T(2,128)} %copy-done.12), calls=%async_computation.2 | async-start | bytes 8192 | tf_op jit(solution)/shard_map/slice | solution.py:84
  117.6 21.1 %slice-start.3 = ((f32[2,1024]{1,0:T(2,128)}), f32[1,1024]{1,0:T(1,128)S(1)}, s32[]{:S(2)}) async-start(f32[2,1024]{1,0:T(2,128)} %copy-done.14), calls=%async_computation.4 | async-start | bytes 8192 | tf_op jit(solution)/shard_map/slice | solution.py:84
  138.7 1.6 %copy-start.5 = (f32[2,128,2048]{2,1,0:T(8,128)S(1)}, f32[2,128,2048]{2,1,0:T(8,128)}, u32[]{:S(2)}) copy-start(f32[2,128,2048]{2,1,0:T(8,128)} %copy.20) | copy-start | bytes 6291460
  138.7 2.2 %copy-start.6 = (f32[2,128,2048]{2,1,0:T(8,128)S(1)}, f32[2,128,2048]{2,1,0:T(8,128)}, u32[]{:S(2)}) copy-start(f32[2,128,2048]{2,1,0:T(8,128)} %shard_map.104) | copy-start | bytes 6291460
Sparse Core Ops, SparseCore 0:
  11.6 59.4 all-gather.1

commit v12 on v10

--- a/solution.py
+++ b/solution.py
@@ -48,11 +48,11 @@
         gots = []
         for j in range(parts):
             hook = hooks.get((j, step if step + 1 < len(steps) else -1))
-            tie = gots[-1] if gots else ()
+            tie = gots[-1] if gots and step + 1 < len(steps) else ()
             totals[j], known, args, tie = lax.optimization_barrier(
                 (totals[j], known_all, hook[1] if hook else (), tie)
             )
-            if gots:
+            if gots and step + 1 < len(steps):
                 gots[-1] = tie
             got = lax.ppermute(totals[j].astype(jnp.bfloat16), "seq", pairs).astype(jnp.float32)
             if hook is not None:
@@ -230,7 +230,7 @@
     parts = 2 if heads % 2 == 0 else 1
     hooks = {
         (1, 0): (mamba_base, (x_in, steps, cum, b_blocks, c_blocks, d_skip)),
-        (0, -1): (attention_core, (queries, kv_piece)),
+        (1, 1): (attention_core, (queries, kv_piece)),
     }
     incoming, results = entering_states(decay, block_state, seq_count, my_index, hooks, parts)
     c_wide = c_blocks.astype(jnp.float32)

time: 150 us -> 148 us (0.987)
  waiting for transfers between devices: 51.2 us -> 44.9 us
  other arithmetic: 23.6 us -> 27 us
    ppermute x6, waiting for transfers between devices: 48.6 us -> 38.5 us  [entering_states(): lax.ppermute(totals[j].astype(jnp.bfloat16), 'seq', pairs)]
    all_gather x1, waiting for transfers between devices: 0.76 us -> 4.66 us  [local(): kv_piece = lax.all_gather(kv_cat, 'seq', axis=1, tiled=True)]
    convert_element_type x5 -> x6, other arithmetic: 3.56 us -> 5.71 us  [entering_states(): lax.ppermute(totals[j].astype(jnp.bfloat16), 'seq', pairs)]
where the time goes in v12:
time: 148 us; the launch traced here: 147 us
  waiting for transfers between devices  44.9 us (30%)
  other arithmetic  27 us (18%)
  starting transfers between devices  21.5 us (15%)
  Pallas kernels  20.9 us (14%)
  local copies, waits for them, and re-layouts  15.2 us (10%)
  between operations  14.5 us (10%)
  matrix products  2.66 us (2%)
    ppermute x6, waiting for transfers between devices, entering_states(): lax.ppermute(totals[j].astype(jnp.bfloat16), 'seq', pairs)  38.5 us
    ppermute x6, starting transfers between devices, entering_states(): lax.ppermute(totals[j].astype(jnp.bfloat16), 'seq', pairs)  13.3 us
    pallas_call x1, Pallas kernels, attention_core(): pl.pallas_call(attention_kernel, out_shape=jax.ShapeDtypeStruct(queries.s...  12 us
    pallas_call x1, Pallas kernels, mamba_base(): pl.pallas_call(mamba_base_kernel, out_shape=jax.ShapeDtypeStruct((slots,...  8.88 us
    ppermute x3, starting transfers between devices, decay_scan(): got = lax.ppermute(total, 'seq', [(i, i ^ span) for i in range(count)])  8.16 us
    convert_element_type x6, other arithmetic, entering_states(): lax.ppermute(totals[j].astype(jnp.bfloat16), 'seq', pairs)  5.71 us
    convert_element_type x6, other arithmetic, entering_states(): totals[j].astype(jnp.bfloat16)  4.96 us
    select_n x4, other arithmetic, entering_states(): jnp.where(lower, spread(own_a)[:, None, :] * got + totals[j], spread(got_...  4.69 us
  transfers between devices with their start and end apart: 10, of which 7 were waited for; matrix products, arithmetic and copies ran while one was open for 19% of the time, Pallas kernels for 14%

profile of v12, /device:TPU:0, one launch (start us, length us, event | category | flops | bytes accessed | tf_op | source)
XLA Modules:
  0.0 146.7 jit_solution(12462708392501847207)
XLA Ops:
  7.2 1.7 %pad_maximum_fusion = bf16[2,128,512]{2,1,0:T(8,128)(2,1)} fusion(bf16[2,128,256]{2,1,0:T(8,128)(2,1)} %bitcast.74, bf16[2,128,256]{2,1,0:T(8,128)(2,1)} %bitcast.75), kind=kLoop, calls=%fused_computation.26 | loop fusion | flops 524288 | bytes 524288 | tf_op jit(solution)/shard_map/concatenate | solution.py:214
  11.2 3.0 %collective-permute-start = (f32[2,32]{1,0:T(2,128)S(1)}, f32[2,32]{1,0:T(2,128)S(1)}, u32[]{:S(2)}, u32[]{:S(2)}) collective-permute-start(f32[2,32]{1,0:T(2,128)S(1)} %exp.23), channel_id=1, source_target_pairs={{0,2},{2,0},{4,6},{6,4},{8,10},{10,8},{12,14},{14,12},{1,3},{3,1},... | collective-permute-start | bytes 776 | tf_op jit(solution)/shard_map/ppermute | solution.py:30
  15.0 1.4 bitcast_bitcast_fusion.1
  16.5 1.5 %copy.17 = f32[2,128,2048]{1,2,0:T(8,128)S(1)} copy(bf16[2,128,2048]{2,1,0:T(8,128)(2,1)} %bitcast.67) | data formatting | bytes 3145728 | tf_op jit(solution)/shard_map/convert_element_type | solution.py:225
  19.1 1.5 %broadcast_in_dim.112 = f32[2,128,32,64]{1,3,2,0:T(8,128)} broadcast(f32[2,128,32]{1,2,0:T(8,128)S(1)} %exponential_bitcast_fusion), dimensions={0,1,2} | broadcast | bytes 2129920 | tf_op jit(solution)/shard_map/broadcast_in_dim | solution.py:20
  20.6 2.9 %copy.20 = f32[2,128,2048]{2,1,0:T(8,128)} copy(f32[2,128,2048]{1,2,0:T(8,128)} %bitcast.66) | data formatting | bytes 4194304 | tf_op jit(solution)/shard_map/reshape | solution.py:20
  23.9 2.1 %collective-permute-start.3 = (f32[2,32]{1,0:T(2,128)S(1)}, f32[2,32]{1,0:T(2,128)S(1)}, u32[]{:S(2)}, u32[]{:S(2)}) collective-permute-start(f32[2,32]{1,0:T(2,128)S(1)} %exponential_multiply_fusion), channel_id=1, source_target_pairs={{0,4},{2,6},{4,0},{6,2},{8,12},{10,14},{12,8},{14,10},{1,5},{3,7},... | collective-permute-start | bytes 776 | tf_op jit(solution)/shard_map/ppermute | solution.py:30
  26.6 1.0 collective-permute-done.3
  27.6 3.0 %collective-permute-start.4 = (f32[2,32]{1,0:T(2,128)S(1)}, f32[2,32]{1,0:T(2,128)S(1)}, u32[]{:S(2)}, u32[]{:S(2)}) collective-permute-start(f32[2,32]{1,0:T(2,128)S(1)} %mul.284), channel_id=1, source_target_pairs={{0,8},{2,10},{4,12},{6,14},{8,0},{10,2},{12,4},{14,6},{1,9},{3,11}... | collective-permute-start | bytes 776 | tf_op jit(solution)/shard_map/ppermute | solution.py:30
  32.3 7.2 %collective-permute-done.1 = bf16[2,128,1024]{1,2,0:T(8,128)(2,1)} collective-permute-done((bf16[2,128,1024]{1,2,0:T(8,128)(2,1)S(1)}, bf16[2,128,1024]{1,2,0:T(8,128)(2,1)}, u32[]{:S(2)}, u32[]{:S(2)}) %collective-permute-start.1) | collective-permute-done | bytes 524320 | tf_op jit(solution)/shard_map/ppermute | solution.py:57
  39.5 1.1 convert_element_type.53
  42.4 1.6 %collective-permute-start.5 = (bf16[2,128,1024]{1,2,0:T(8,128)(2,1)S(1)}, bf16[2,128,1024]{1,2,0:T(8,128)(2,1)}, u32[]{:S(2)}, u32[]{:S(2)}) collective-permute-start(bf16[2,128,1024]{1,2,0:T(8,128)(2,1)S(1)} %convert_element_type.56), channel_id=1, source_target_pairs={{0,4},{2,6},{4,0},{6,2},{8,12},{10,14},{12,8},{14,10},{1,5},{3,7},... | collective-permute-start | bytes 1572872 | tf_op jit(solution)/shard_map/ppermute | solution.py:57
  47.1 8.9 %shard_map.104 = f32[2,128,2048]{2,1,0:T(8,128)} custom-call(bf16[256,2048]{1,0:T(8,128)(2,1)} %x_ref, f32[2,128,128]{2,1,0:T(8,128)} %fusion.21.inner_ref, f32[2,32,1,128]{3,2,1,0:T(1,128)} %bitcast.69, f32[2,32,1,128]{3,2,1,0:T(1,128)} %bitcast.73, f32[1,2048]{1,0:T(1,128)} %broadcast_in_dim_reshape.2.skip_ref), custom_call_target="tpu_custom_call" | custom-call | flops 140509184 | bytes 3145728 | tf_op jit(solution)/shard_map/pallas_call | solution.py:118
  55.9 11.7 %collective-permute-done.2 = bf16[2,128,1024]{1,2,0:T(8,128)(2,1)S(1)} collective-permute-done((bf16[2,128,1024]{1,2,0:T(8,128)(2,1)}, bf16[2,128,1024]{1,2,0:T(8,128)(2,1)S(1)}, u32[]{:S(2)}, u32[]{:S(2)}) %collective-permute-start.2) | collective-permute-done | bytes 524320 | tf_op jit(solution)/shard_map/ppermute | solution.py:57
  67.7 1.1 convert_element_type.57
  68.9 1.5 %add_select_fusion.7 = f32[2,128,1024]{1,2,0:T(8,128)} fusion(f32[2,128,1024]{1,2,0:T(8,128)S(1)} %convert_element_type.55, f32[2,128,1024]{1,2,0:T(8,128)S(1)} %copy-done.6, f32[2,1024]{1,0:T(2,128)S(1)} %mul.298, f32[2,1024]{1,0:T(2,128)S(1)} %mul.295, pred[]{:T(512)S(6)} %eq.13), kind=kLoop, calls=%fused_computation.21 | loop fusion | flops 1310720 | bytes 3162113 | tf_op jit(solution)/shard_map/jit(_where)/select_n | solution.py:70
  70.4 4.7 %all-gather.2.cloned.1.call-done.k_ref.v_ref = bf16[2,1024,512]{2,1,0:T(8,128)(2,1)} async-done(((bf16[2,128,512]{2,1,0:T(8,128)(2,1)}), bf16[2,1024,512]{2,1,0:T(8,128)(2,1)}) %all-gather.2.cloned.1.call-update) | async-done | bytes 2097168 | tf_op jit(solution)/shard_map/all_gather | solution.py:218
  75.0 2.1 %convert_element_type.60 = bf16[2,128,1024]{1,2,0:T(8,128)(2,1)} convert(f32[2,128,1024]{1,2,0:T(8,128)} %add_select_fusion.7) | non-fusion elementwise | flops 262144 | bytes 1572864 | tf_op jit(solution)/shard_map/convert_element_type | solution.py:57
  77.1 2.2 %collective-permute-start.7 = (bf16[2,128,1024]{1,2,0:T(8,128)(2,1)}, bf16[2,128,1024]{1,2,0:T(8,128)(2,1)}, u32[]{:S(2)}, u32[]{:S(2)}) collective-permute-start(bf16[2,128,1024]{1,2,0:T(8,128)(2,1)} %convert_element_type.60), channel_id=1, source_target_pairs={{0,4},{2,6},{4,0},{6,2},{8,12},{10,14},{12,8},{14,10},{1,5},{3,7},... | collective-permute-start | bytes 1572872 | tf_op jit(solution)/shard_map/ppermute | solution.py:57
  80.9 1.8 %add_select_fusion.5 = f32[2,128,1024]{1,2,0:T(8,128)S(1)} fusion(f32[2,128,1024]{1,2,0:T(8,128)S(1)} %convert_element_type.57, f32[2,128,1024]{1,2,0:T(8,128)} %copy-done.3, f32[2,1024]{1,0:T(2,128)S(1)} %mul.308, f32[2,1024]{1,0:T(2,128)S(1)} %mul.293, pred[]{:T(512)S(6)} %eq.15), kind=kLoop, calls=%fused_computation.19 | loop fusion | flops 1310720 | bytes 3162113 | tf_op jit(solution)/shard_map/jit(_where)/select_n | solution.py:70
  82.7 1.0 copy-done.9
  84.9 12.0 %shard_map.105 = bf16[256,1024]{1,0:T(8,128)(2,1)} custom-call(bf16[256,1024]{1,0:T(8,128)(2,1)} %q_ref, bf16[2,1024,512]{2,1,0:T(8,128)(2,1)} %all-gather.2.cloned.1.call-done.k_ref.v_ref, bf16[2,1024,512]{2,1,0:T(8,128)(2,1)} %all-gather.2.cloned.1.call-done.k_ref.v_ref), custom_call_target="tpu_custom_call" | custom-call | flops 2147483648 | bytes 3145728 | tf_op jit(solution)/shard_map/pallas_call | solution.py:194
  96.9 1.2 convert_element_type.61
  99.9 8.6 %collective-permute-start.8 = (bf16[2,128,1024]{1,2,0:T(8,128)(2,1)}, bf16[2,128,1024]{1,2,0:T(8,128)(2,1)}, u32[]{:S(2)}, u32[]{:S(2)}) collective-permute-start(bf16[2,128,1024]{1,2,0:T(8,128)(2,1)} %convert_element_type.62), channel_id=1, source_target_pairs={{0,8},{2,10},{4,12},{6,14},{8,0},{10,2},{12,4},{14,6},{1,9},{3,11}... | collective-permute-start | bytes 1572872 | tf_op jit(solution)/shard_map/ppermute | solution.py:57
  108.9 1.4 collective-permute-done.6
  110.3 1.1 convert_element_type.59
  111.4 1.8 %add_select_fusion.2 = f32[2,128,1024]{1,2,0:T(8,128)S(1)} fusion(f32[2,128,1024]{1,2,0:T(8,128)S(1)} %convert_element_type.53, f32[2,128,1024]{1,2,0:T(8,128)S(1)} %convert_element_type.57, f32[2,1024]{1,0:T(2,128)S(1)} %mul.312, f32[2,1024]{1,0:T(2,128)S(1)} %mul.291, pred[]{:T(512)S(6)} %eq.13, pred[]{:T(512)S(6)} %eq.15, pred[]{:T(512)S(6)} %eq.14, ...), kind=kLoop, calls=%fused_computation.8 | loop fusion | flops 2097152 | bytes 3686403 | tf_op jit(solution)/shard_map/jit(_where)/select_n | solution.py:69
  113.2 18.1 %collective-permute-done.8 = bf16[2,128,1024]{1,2,0:T(8,128)(2,1)} collective-permute-done((bf16[2,128,1024]{1,2,0:T(8,128)(2,1)}, bf16[2,128,1024]{1,2,0:T(8,128)(2,1)}, u32[]{:S(2)}, u32[]{:S(2)}) %collective-permute-start.8) | collective-permute-done | bytes 524320 | tf_op jit(solution)/shard_map/ppermute | solution.py:57
  131.4 1.1 convert_element_type.63
  132.6 1.8 %add_select_fusion = f32[2,128,1024]{1,2,0:T(8,128)S(1)} fusion(f32[2,128,1024]{1,2,0:T(8,128)S(1)} %convert_element_type.55, f32[2,128,1024]{1,2,0:T(8,128)S(1)} %copy-done.2, f32[2,1024]{1,0:T(2,128)S(1)} %mul.342, f32[2,1024]{1,0:T(2,128)S(1)} %mul.333, pred[]{:T(512)S(6)} %eq.13, pred[]{:T(512)S(6)} %eq.15, pred[]{:T(512)S(6)} %eq.14, ...), kind=kLoop, calls=%fused_computation.6 | loop fusion | flops 2097152 | bytes 3686403 | tf_op jit(solution)/shard_map/jit(_where)/select_n | solution.py:69
  134.4 1.7 %slice_add_fusion.1 = (f32[1,128,1024]{1,2,0:T(8,128)S(1)}, f32[1,128,1024]{1,2,0:T(8,128)S(1)}, f32[1,128,1024]{1,2,0:T(8,128)S(1)}, f32[1,128,1024]{1,2,0:T(8,128)S(1)}) fusion(f32[2,128,1024]{1,2,0:T(8,128)S(1)} %add_select_fusion, f32[1024]{0:T(1024)S(1)} %mul.331, f32[1,1024]{1,0:T(1,128)S(1)} %slice-done.3, f32[2,128,1024]{1,2,0:T(8,128)S(1)} %copy-done.12, ...), kind=kLoop, calls=%fused_computation.23 | loop fusion | flops 2359296 | bytes 6332417 | tf_op jit(solution)/shard_map/add | solution.py:83
  138.4 1.4 fusion.1
  (136 shorter events, 19.0 us)
Async XLA Ops:
  7.2 11.2 %copy-start = (bf16[256,128]{1,0:T(8,128)(2,1)S(1)}, bf16[256,128]{1,0:T(8,128)(2,1)}, u32[]{:S(2)}) copy-start(bf16[256,128]{1,0:T(8,128)(2,1)} %param.13) | copy-start | bytes 196612
  7.2 67.9 %all-gather.2.cloned.1.call-start = ((), (), s32[]{:S(2)}) async-start(), calls=%async_computation | async-start | bytes 2359296 | tf_op jit(solution)/shard_map/all_gather | solution.py:218
  11.0 7.3 %copy-start.13 = (f32[2,32,128]{2,1,0:T(8,128)}, f32[2,32,128]{2,1,0:T(8,128)S(1)}, u32[]{:S(2)}) copy-start(f32[2,32,128]{2,1,0:T(8,128)S(1)} %reduce_window_sum.11) | copy-start | bytes 98308
  11.2 12.4 %collective-permute-start = (f32[2,32]{1,0:T(2,128)S(1)}, f32[2,32]{1,0:T(2,128)S(1)}, u32[]{:S(2)}, u32[]{:S(2)}) collective-permute-start(f32[2,32]{1,0:T(2,128)S(1)} %exp.23), channel_id=1, source_target_pairs={{0,2},{2,0},{4,6},{6,4},{8,10},{10,8},{12,14},{14,12},{1,3},{3,1},... | collective-permute-start | bytes 776 | tf_op jit(solution)/shard_map/ppermute | solution.py:30
  18.9 25.0 %copy-start.5 = (f32[2,128,1024]{1,2,0:T(8,128)}, f32[2,128,1024]{1,2,0:T(8,128)S(1)}, u32[]{:S(2)}) copy-start(f32[2,128,1024]{1,2,0:T(8,128)S(1)} %get-tuple-element.28) | copy-start | bytes 3145732
  23.6 15.9 %collective-permute-start.1 = (bf16[2,128,1024]{1,2,0:T(8,128)(2,1)S(1)}, bf16[2,128,1024]{1,2,0:T(8,128)(2,1)}, u32[]{:S(2)}, u32[]{:S(2)}) collective-permute-start(bf16[2,128,1024]{1,2,0:T(8,128)(2,1)S(1)} %convert_element_type.52), channel_id=1, source_target_pairs={{0,2},{2,0},{4,6},{6,4},{8,10},{10,8},{12,14},{14,12},{1,3},{3,1},... | collective-permute-start | bytes 1572872 | tf_op jit(solution)/shard_map/ppermute | solution.py:57
  23.9 3.7 %collective-permute-start.3 = (f32[2,32]{1,0:T(2,128)S(1)}, f32[2,32]{1,0:T(2,128)S(1)}, u32[]{:S(2)}, u32[]{:S(2)}) collective-permute-start(f32[2,32]{1,0:T(2,128)S(1)} %exponential_multiply_fusion), channel_id=1, source_target_pairs={{0,4},{2,6},{4,0},{6,2},{8,12},{10,14},{12,8},{14,10},{1,5},{3,7},... | collective-permute-start | bytes 776 | tf_op jit(solution)/shard_map/ppermute | solution.py:30
  27.6 4.6 %collective-permute-start.4 = (f32[2,32]{1,0:T(2,128)S(1)}, f32[2,32]{1,0:T(2,128)S(1)}, u32[]{:S(2)}, u32[]{:S(2)}) collective-permute-start(f32[2,32]{1,0:T(2,128)S(1)} %mul.284), channel_id=1, source_target_pairs={{0,8},{2,10},{4,12},{6,14},{8,0},{10,2},{12,4},{14,6},{1,9},{3,11}... | collective-permute-start | bytes 776 | tf_op jit(solution)/shard_map/ppermute | solution.py:30
  31.2 10.1 %copy-start.15 = (f32[2,1024]{1,0:T(2,128)}, f32[2,1024]{1,0:T(2,128)S(1)}, u32[]{:S(2)}) copy-start(f32[2,1024]{1,0:T(2,128)S(1)} %mul.322) | copy-start | bytes 24580
  31.4 9.9 %copy-start.16 = (f32[2,1024]{1,0:T(2,128)}, f32[2,1024]{1,0:T(2,128)S(1)}, u32[]{:S(2)}) copy-start(f32[2,1024]{1,0:T(2,128)S(1)} %mul.351) | copy-start | bytes 24580
  42.3 3.2 %copy-start.19 = (f32[32]{0:T(128)S(1)}, f32[32]{0:T(128)}, u32[]{:S(2)}) copy-start(f32[32]{0:T(128)} %param.12) | copy-start | bytes 388
  42.3 3.9 %copy-start.14 = (bf16[256,128]{1,0:T(8,128)(2,1)S(1)}, bf16[256,128]{1,0:T(8,128)(2,1)}, u32[]{:S(2)}) copy-start(bf16[256,128]{1,0:T(8,128)(2,1)} %param.14) | copy-start | bytes 196612
  42.4 25.4 %collective-permute-start.5 = (bf16[2,128,1024]{1,2,0:T(8,128)(2,1)S(1)}, bf16[2,128,1024]{1,2,0:T(8,128)(2,1)}, u32[]{:S(2)}, u32[]{:S(2)}) collective-permute-start(bf16[2,128,1024]{1,2,0:T(8,128)(2,1)S(1)} %convert_element_type.56), channel_id=1, source_target_pairs={{0,4},{2,6},{4,0},{6,2},{8,12},{10,14},{12,8},{14,10},{1,5},{3,7},... | collective-permute-start | bytes 1572872 | tf_op jit(solution)/shard_map/ppermute | solution.py:57
  44.8 22.9 %collective-permute-start.2 = (bf16[2,128,1024]{1,2,0:T(8,128)(2,1)}, bf16[2,128,1024]{1,2,0:T(8,128)(2,1)S(1)}, u32[]{:S(2)}, u32[]{:S(2)}) collective-permute-start(bf16[2,128,1024]{1,2,0:T(8,128)(2,1)} %convert_element_type.54), channel_id=1, source_target_pairs={{0,2},{2,0},{4,6},{6,4},{8,10},{10,8},{12,14},{14,12},{1,3},{3,1},... | collective-permute-start | bytes 1572872 | tf_op jit(solution)/shard_map/ppermute | solution.py:57
  55.9 12.9 %copy-start.6 = (f32[2,128,1024]{1,2,0:T(8,128)S(1)}, f32[2,128,1024]{1,2,0:T(8,128)}, u32[]{:S(2)}) copy-start(f32[2,128,1024]{1,2,0:T(8,128)} %copy-done.5) | copy-start | bytes 3145732
  77.1 19.8 %collective-permute-start.7 = (bf16[2,128,1024]{1,2,0:T(8,128)(2,1)}, bf16[2,128,1024]{1,2,0:T(8,128)(2,1)}, u32[]{:S(2)}, u32[]{:S(2)}) collective-permute-start(bf16[2,128,1024]{1,2,0:T(8,128)(2,1)} %convert_element_type.60), channel_id=1, source_target_pairs={{0,4},{2,6},{4,0},{6,2},{8,12},{10,14},{12,8},{14,10},{1,5},{3,7},... | collective-permute-start | bytes 1572872 | tf_op jit(solution)/shard_map/ppermute | solution.py:57
  84.6 25.7 %collective-permute-start.6 = (bf16[2,128,1024]{1,2,0:T(8,128)(2,1)}, bf16[2,128,1024]{1,2,0:T(8,128)(2,1)}, u32[]{:S(2)}, u32[]{:S(2)}) collective-permute-start(bf16[2,128,1024]{1,2,0:T(8,128)(2,1)} %convert_element_type.58), channel_id=1, source_target_pairs={{0,8},{2,10},{4,12},{6,14},{8,0},{10,2},{12,4},{14,6},{1,9},{3,11}... | collective-permute-start | bytes 1572872 | tf_op jit(solution)/shard_map/ppermute | solution.py:57
  96.9 1.4 copy-start.4
  98.3 1.7 %copy-start.1 = (f32[2,128,1024]{1,2,0:T(8,128)}, f32[2,128,1024]{1,2,0:T(8,128)S(1)}, u32[]{:S(2)}) copy-start(f32[2,128,1024]{1,2,0:T(8,128)S(1)} %convert_element_type.61) | copy-start | bytes 3145732
  99.0 9.5 %copy-start.11 = (f32[2,128,1024]{1,2,0:T(8,128)}, f32[2,128,1024]{1,2,0:T(8,128)S(1)}, u32[]{:S(2)}) copy-start(f32[2,128,1024]{1,2,0:T(8,128)S(1)} %add_select_fusion.4) | copy-start | bytes 3145732
  99.9 31.4 %collective-permute-start.8 = (bf16[2,128,1024]{1,2,0:T(8,128)(2,1)}, bf16[2,128,1024]{1,2,0:T(8,128)(2,1)}, u32[]{:S(2)}, u32[]{:S(2)}) collective-permute-start(bf16[2,128,1024]{1,2,0:T(8,128)(2,1)} %convert_element_type.62), channel_id=1, source_target_pairs={{0,8},{2,10},{4,12},{6,14},{8,0},{10,2},{12,4},{14,6},{1,9},{3,11}... | collective-permute-start | bytes 1572872 | tf_op jit(solution)/shard_map/ppermute | solution.py:57
  108.8 4.5 %copy-start.17 = (f32[2,1024]{1,0:T(2,128)}, f32[2,1024]{1,0:T(2,128)S(1)}, u32[]{:S(2)}) copy-start(f32[2,1024]{1,0:T(2,128)S(1)} %mul.325) | copy-start | bytes 24580
  108.9 4.3 %copy-start.18 = (f32[2,1024]{1,0:T(2,128)}, f32[2,1024]{1,0:T(2,128)S(1)}, u32[]{:S(2)}) copy-start(f32[2,1024]{1,0:T(2,128)S(1)} %mul.354) | copy-start | bytes 24580
  111.4 21.0 %copy-start.2 = (f32[2,128,1024]{1,2,0:T(8,128)S(1)}, f32[2,128,1024]{1,2,0:T(8,128)}, u32[]{:S(2)}) copy-start(f32[2,128,1024]{1,2,0:T(8,128)} %copy-done.1) | copy-start | bytes 3145732
  132.5 1.9 %copy-start.10 = (f32[2,128,1024]{1,2,0:T(8,128)S(1)}, f32[2,128,1024]{1,2,0:T(8,128)}, u32[]{:S(2)}) copy-start(f32[2,128,1024]{1,2,0:T(8,128)} %copy-done.9) | copy-start | bytes 3145732
  132.5 1.9 %copy-start.12 = (f32[2,128,1024]{1,2,0:T(8,128)S(1)}, f32[2,128,1024]{1,2,0:T(8,128)}, u32[]{:S(2)}) copy-start(f32[2,128,1024]{1,2,0:T(8,128)} %copy-done.11) | copy-start | bytes 3145732
  132.5 1.9 %slice-start = ((f32[2,1024]{1,0:T(2,128)}), f32[1,1024]{1,0:T(1,128)S(1)}, s32[]{:S(2)}) async-start(f32[2,1024]{1,0:T(2,128)} %copy-done.15), calls=%async_computation.1 | async-start | bytes 8192 | tf_op jit(solution)/shard_map/slice | solution.py:84
  132.5 1.9 %slice-start.1 = ((f32[2,1024]{1,0:T(2,128)}), f32[1,1024]{1,0:T(1,128)S(1)}, s32[]{:S(2)}) async-start(f32[2,1024]{1,0:T(2,128)} %copy-done.16), calls=%async_computation.2 | async-start | bytes 8192 | tf_op jit(solution)/shard_map/slice | solution.py:84
  132.5 1.9 %slice-start.2 = ((f32[2,1024]{1,0:T(2,128)}), f32[1,1024]{1,0:T(1,128)S(1)}, s32[]{:S(2)}) async-start(f32[2,1024]{1,0:T(2,128)} %copy-done.17), calls=%async_computation.3 | async-start | bytes 8192 | tf_op jit(solution)/shard_map/slice | solution.py:84
  132.5 1.9 %slice-start.3 = ((f32[2,1024]{1,0:T(2,128)}), f32[1,1024]{1,0:T(1,128)S(1)}, s32[]{:S(2)}) async-start(f32[2,1024]{1,0:T(2,128)} %copy-done.18), calls=%async_computation.4 | async-start | bytes 8192 | tf_op jit(solution)/shard_map/slice | solution.py:84
  136.2 1.6 %copy-start.7 = (f32[2,128,2048]{2,1,0:T(8,128)S(1)}, f32[2,128,2048]{2,1,0:T(8,128)}, u32[]{:S(2)}) copy-start(f32[2,128,2048]{2,1,0:T(8,128)} %copy.20) | copy-start | bytes 6291460
  136.2 2.2 %copy-start.8 = (f32[2,128,2048]{2,1,0:T(8,128)S(1)}, f32[2,128,2048]{2,1,0:T(8,128)}, u32[]{:S(2)}) copy-start(f32[2,128,2048]{2,1,0:T(8,128)} %shard_map.104) | copy-start | bytes 6291460
  (2 other events, 1.9 us)
Sparse Core Ops, SparseCore 0:
  14.3 60.6 all-gather.1

commit v13 on v12

--- a/solution.py
+++ b/solution.py
@@ -131,6 +131,36 @@
     )(x_in, inner, cum_row, step_row, skip_row)
 
 
+def block_state_kernel(b_ref, f_ref, x_ref, o_ref):
+    scaled = (f_ref[0] * x_ref[...].astype(jnp.float32)).astype(jnp.bfloat16)
+    o_ref[0] = jnp.dot(b_ref[0], scaled, preferred_element_type=jnp.float32)
+
+
+def block_states(b_blocks, factor, x_in):
+    slots, tokens, state = b_blocks.shape
+    width = x_in.shape[1]
+    cut = 512 if width % 512 == 0 else width
+    b_t = b_blocks.transpose(0, 2, 1)
+    spread_factor = spread(factor)
+    cost = pl.CostEstimate(
+        flops=2 * slots * state * tokens * width,
+        transcendentals=0,
+        bytes_accessed=x_in.size * 2 + spread_factor.size * 4 + slots * state * width * 4,
+    )
+    return pl.pallas_call(
+        block_state_kernel,
+        out_shape=jax.ShapeDtypeStruct((slots, state, width), jnp.float32),
+        grid=(slots, width // cut),
+        in_specs=[
+            pl.BlockSpec((1, state, tokens), lambda c, k: (c, 0, 0)),
+            pl.BlockSpec((1, tokens, cut), lambda c, k: (c, 0, k)),
+            pl.BlockSpec((tokens, cut), lambda c, k: (c, k)),
+        ],
+        out_specs=pl.BlockSpec((1, state, cut), lambda c, k: (c, 0, k)),
+        cost_estimate=cost,
+    )(b_t, spread_factor, x_in)
+
+
 KEY_CHUNK = 256
 
 
@@ -221,11 +251,9 @@
     cum = jnp.cumsum(steps * rate[None, :, None], axis=2)
     log_total = cum[:, :, -1]
     factor = (jnp.exp(log_total[:, :, None] - cum) * steps).transpose(0, 2, 1)
-    x3 = x_in.reshape(slots, BLOCK, width)
-    scaled = (spread(factor) * x3.astype(jnp.float32)).astype(jnp.bfloat16)
     b_blocks = b_in.reshape(slots, BLOCK, STATE)
     c_blocks = c_in.reshape(slots, BLOCK, STATE)
-    block_state = jnp.einsum("ctn,ctk->cnk", b_blocks, scaled, preferred_element_type=jnp.float32)
+    block_state = block_states(b_blocks, factor, x_in)
     decay = jnp.exp(log_total)
     parts = 2 if heads % 2 == 0 else 1
     hooks = {

time: 148 us -> 144 us (0.973)
  Pallas kernels: 20.9 us -> 27.4 us
  waiting for transfers between devices: 44.9 us -> 38.5 us
  other arithmetic: 27 us -> 23.7 us
  local copies, waits for them, and re-layouts: 15.2 us -> 17.5 us
  starting transfers between devices: 21.5 us -> 19.6 us
    pallas_call x0 -> x1, Pallas kernels: none -> 6.53 us  [block_states(): pl.pallas_call(block_state_kernel, out_shape=jax.ShapeDtypeStruct((slots,...]
    all_gather x1, waiting for transfers between devices: 4.66 us -> 0.01 us  [local(): kv_piece = lax.all_gather(kv_cat, 'seq', axis=1, tiled=True)]
    ppermute x6, waiting for transfers between devices: 38.5 us -> 36.5 us  [entering_states(): lax.ppermute(totals[j].astype(jnp.bfloat16), 'seq', pairs)]
    reshape x1 -> x2, local copies, waits for them, and re-layouts: 2.94 us -> 4.76 us  [spread(): return jnp.repeat(a, HEADDIM, axis=-1)]
    ppermute x6, starting transfers between devices: 13.3 us -> 11.5 us  [entering_states(): lax.ppermute(totals[j].astype(jnp.bfloat16), 'seq', pairs)]
    slice x1, local copies, waits for them, and re-layouts: 0.14 us -> 1.68 us  [entering_states(): block_state[:, :, j * width_cut:(j + 1) * width_cut]]
    select_n x4, other arithmetic: 4.69 us -> 3.17 us  [entering_states(): jnp.where(lower, spread(own_a)[:, None, :] * got + totals[j], spread(got_...]
    unnamed x40 -> x42, local copies, waits for them, and re-layouts: 2.94 us -> 3.18 us
  transfers between devices with their start and end apart: 10 -> 10, of which waited for: 7 -> 7; matrix products, arithmetic and copies ran while one was open for 19% -> 20% of each run, Pallas kernels for 14% -> 19%
where the time goes in v13:
time: 144 us; the launch traced here: 143 us
  waiting for transfers between devices  38.5 us (27%)
  Pallas kernels  27.4 us (19%)
  other arithmetic  23.7 us (16%)
  starting transfers between devices  19.6 us (14%)
  local copies, waits for them, and re-layouts  17.5 us (12%)
  between operations  14.4 us (10%)
  matrix products  2.11 us (1%)
    ppermute x6, waiting for transfers between devices, entering_states(): lax.ppermute(totals[j].astype(jnp.bfloat16), 'seq', pairs)  36.5 us
    pallas_call x1, Pallas kernels, attention_core(): pl.pallas_call(attention_kernel, out_shape=jax.ShapeDtypeStruct(queries.s...  12 us
    ppermute x6, starting transfers between devices, entering_states(): lax.ppermute(totals[j].astype(jnp.bfloat16), 'seq', pairs)  11.5 us
    pallas_call x1, Pallas kernels, mamba_base(): pl.pallas_call(mamba_base_kernel, out_shape=jax.ShapeDtypeStruct((slots,...  8.88 us
    ppermute x3, starting transfers between devices, decay_scan(): got = lax.ppermute(total, 'seq', [(i, i ^ span) for i in range(count)])  8.04 us
    pallas_call x1, Pallas kernels, block_states(): pl.pallas_call(block_state_kernel, out_shape=jax.ShapeDtypeStruct((slots,...  6.53 us
    convert_element_type x6, other arithmetic, entering_states(): lax.ppermute(totals[j].astype(jnp.bfloat16), 'seq', pairs)  5.92 us
    convert_element_type x6, other arithmetic, entering_states(): totals[j].astype(jnp.bfloat16)  5.03 us
  transfers between devices with their start and end apart: 10, of which 7 were waited for; matrix products, arithmetic and copies ran while one was open for 20% of the time, Pallas kernels for 19%

profile of v13, /device:TPU:0, one launch (start us, length us, event | category | flops | bytes accessed | tf_op | source)
XLA Modules:
  0.0 143.1 jit_solution(8710937188053335809)
XLA Ops:
  7.2 1.7 %pad_maximum_fusion = bf16[2,128,512]{2,1,0:T(8,128)(2,1)} fusion(bf16[2,128,256]{2,1,0:T(8,128)(2,1)} %bitcast.67, bf16[2,128,256]{2,1,0:T(8,128)(2,1)} %bitcast.68), kind=kLoop, calls=%fused_computation.23 | loop fusion | flops 524288 | bytes 524288 | tf_op jit(solution)/shard_map/concatenate | solution.py:244
  11.2 3.0 %collective-permute-start = (f32[2,32]{1,0:T(2,128)S(1)}, f32[2,32]{1,0:T(2,128)S(1)}, u32[]{:S(2)}, u32[]{:S(2)}) collective-permute-start(f32[2,32]{1,0:T(2,128)S(1)} %exp.23), channel_id=1, source_target_pairs={{0,2},{2,0},{4,6},{6,4},{8,10},{10,8},{12,14},{14,12},{1,3},{3,1},... | collective-permute-start | bytes 776 | tf_op jit(solution)/shard_map/ppermute | solution.py:30
  15.3 1.8 %copy.21.f_ref = f32[2,128,2048]{2,1,0:T(8,128)} copy(f32[2,128,2048]{1,2,0:T(8,128)S(1)} %bitcast.59) | data formatting | bytes 4194304 | tf_op jit(solution)/shard_map/reshape | solution.py:20
  18.0 6.5 %shard_map.104 = f32[2,128,2048]{2,1,0:T(8,128)} custom-call(bf16[2,128,128]{2,1,0:T(8,128)(2,1)} %bitcast.65, f32[2,128,2048]{2,1,0:T(8,128)} %copy.21.f_ref, bf16[256,2048]{1,0:T(8,128)(2,1)} %x_ref.1), custom_call_target="tpu_custom_call" | custom-call | flops 134217728 | bytes 5242880 | tf_op jit(solution)/shard_map/pallas_call | solution.py:150
  25.2 1.7 %fusion.11 = (f32[2,128,1024]{2,1,0:T(8,128)S(1)}, f32[2,128,1024]{2,1,0:T(8,128)S(1)}) fusion(f32[2,128,2048]{2,1,0:T(8,128)} %shard_map.104), kind=kLoop, calls=%fused_computation.43 | loop fusion | bytes 4194304 | tf_op jit(solution)/shard_map/slice | solution.py:42
  27.0 1.5 %broadcast_in_dim.112 = f32[2,128,32,64]{1,3,2,0:T(8,128)} broadcast(f32[2,128,32]{1,2,0:T(8,128)S(1)} %exponential_bitcast_fusion), dimensions={0,1,2} | broadcast | bytes 2129920 | tf_op jit(solution)/shard_map/broadcast_in_dim | solution.py:20
  28.5 2.9 %copy.26 = f32[2,128,2048]{2,1,0:T(8,128)} copy(f32[2,128,2048]{1,2,0:T(8,128)} %bitcast.60) | data formatting | bytes 4194304 | tf_op jit(solution)/shard_map/reshape | solution.py:20
  31.9 2.1 %collective-permute-start.3 = (f32[2,32]{1,0:T(2,128)S(1)}, f32[2,32]{1,0:T(2,128)S(1)}, u32[]{:S(2)}, u32[]{:S(2)}) collective-permute-start(f32[2,32]{1,0:T(2,128)S(1)} %exponential_multiply_fusion), channel_id=1, source_target_pairs={{0,4},{2,6},{4,0},{6,2},{8,12},{10,14},{12,8},{14,10},{1,5},{3,7},... | collective-permute-start | bytes 776 | tf_op jit(solution)/shard_map/ppermute | solution.py:30
  34.5 1.2 collective-permute-done.3
  35.7 2.9 %collective-permute-start.4 = (f32[2,32]{1,0:T(2,128)S(1)}, f32[2,32]{1,0:T(2,128)S(1)}, u32[]{:S(2)}, u32[]{:S(2)}) collective-permute-start(f32[2,32]{1,0:T(2,128)S(1)} %mul.280), channel_id=1, source_target_pairs={{0,8},{2,10},{4,12},{6,14},{8,0},{10,2},{12,4},{14,6},{1,9},{3,11}... | collective-permute-start | bytes 776 | tf_op jit(solution)/shard_map/ppermute | solution.py:30
  40.2 7.8 %collective-permute-done.1 = bf16[2,128,1024]{2,1,0:T(8,128)(2,1)} collective-permute-done((bf16[2,128,1024]{2,1,0:T(8,128)(2,1)S(1)}, bf16[2,128,1024]{2,1,0:T(8,128)(2,1)}, u32[]{:S(2)}, u32[]{:S(2)}) %collective-permute-start.1) | collective-permute-done | bytes 524320 | tf_op jit(solution)/shard_map/ppermute | solution.py:57
  48.0 1.1 convert_element_type.41
  50.5 1.7 %collective-permute-start.5 = (bf16[2,128,1024]{2,1,0:T(8,128)(2,1)S(1)}, bf16[2,128,1024]{2,1,0:T(8,128)(2,1)}, u32[]{:S(2)}, u32[]{:S(2)}) collective-permute-start(bf16[2,128,1024]{2,1,0:T(8,128)(2,1)S(1)} %convert_element_type.44), channel_id=1, source_target_pairs={{0,4},{2,6},{4,0},{6,2},{8,12},{10,14},{12,8},{14,10},{1,5},{3,7},... | collective-permute-start | bytes 1572872 | tf_op jit(solution)/shard_map/ppermute | solution.py:57
  55.3 8.9 %shard_map.105 = f32[2,128,2048]{2,1,0:T(8,128)} custom-call(bf16[256,2048]{1,0:T(8,128)(2,1)} %x_ref.1, f32[2,128,128]{2,1,0:T(8,128)} %fusion.20.inner_ref, f32[2,32,1,128]{3,2,1,0:T(1,128)} %bitcast.62, f32[2,32,1,128]{3,2,1,0:T(1,128)} %bitcast.66, f32[1,2048]{1,0:T(1,128)} %broadcast_in_dim_reshape.2.skip_ref), custom_call_target="tpu_custom_call" | custom-call | flops 140509184 | bytes 3145728 | tf_op jit(solution)/shard_map/pallas_call | solution.py:118
  64.2 3.2 %collective-permute-done.2 = bf16[2,128,1024]{2,1,0:T(8,128)(2,1)S(1)} collective-permute-done((bf16[2,128,1024]{2,1,0:T(8,128)(2,1)}, bf16[2,128,1024]{2,1,0:T(8,128)(2,1)S(1)}, u32[]{:S(2)}, u32[]{:S(2)}) %collective-permute-start.2) | collective-permute-done | bytes 524320 | tf_op jit(solution)/shard_map/ppermute | solution.py:57
  67.6 4.0 %collective-permute-done.5 = bf16[2,128,1024]{2,1,0:T(8,128)(2,1)} collective-permute-done((bf16[2,128,1024]{2,1,0:T(8,128)(2,1)S(1)}, bf16[2,128,1024]{2,1,0:T(8,128)(2,1)}, u32[]{:S(2)}, u32[]{:S(2)}) %collective-permute-start.5) | collective-permute-done | bytes 524320 | tf_op jit(solution)/shard_map/ppermute | solution.py:57
  71.6 1.1 convert_element_type.45
  72.7 1.2 add_select_fusion.7
  73.9 2.1 %convert_element_type.48 = bf16[2,128,1024]{2,1,0:T(8,128)(2,1)} convert(f32[2,128,1024]{2,1,0:T(8,128)} %add_select_fusion.7) | non-fusion elementwise | flops 262144 | bytes 1572864 | tf_op jit(solution)/shard_map/convert_element_type | solution.py:57
  77.9 1.5 %add_select_fusion.5 = f32[2,128,1024]{2,1,0:T(8,128)S(1)} fusion(f32[2,128,1024]{2,1,0:T(8,128)S(1)} %convert_element_type.45, f32[2,128,1024]{2,1,0:T(8,128)} %copy-done.3, f32[2,1024]{1,0:T(2,128)S(1)} %mul.304, f32[2,1024]{1,0:T(2,128)S(1)} %mul.289, pred[]{:T(512)S(6)} %eq.15), kind=kLoop, calls=%fused_computation.16 | loop fusion | flops 1310720 | bytes 3162113 | tf_op jit(solution)/shard_map/jit(_where)/select_n | solution.py:70
  81.3 2.7 %collective-permute-start.6 = (bf16[2,128,1024]{2,1,0:T(8,128)(2,1)}, bf16[2,128,1024]{2,1,0:T(8,128)(2,1)}, u32[]{:S(2)}, u32[]{:S(2)}) collective-permute-start(bf16[2,128,1024]{2,1,0:T(8,128)(2,1)} %convert_element_type.46), channel_id=1, source_target_pairs={{0,8},{2,10},{4,12},{6,14},{8,0},{10,2},{12,4},{14,6},{1,9},{3,11}... | collective-permute-start | bytes 1572872 | tf_op jit(solution)/shard_map/ppermute | solution.py:57
  84.0 12.0 %shard_map.106 = bf16[256,1024]{1,0:T(8,128)(2,1)} custom-call(bf16[256,1024]{1,0:T(8,128)(2,1)} %q_ref, bf16[2,1024,512]{2,1,0:T(8,128)(2,1)} %all-gather.2.cloned.1.call-done.k_ref.v_ref, bf16[2,1024,512]{2,1,0:T(8,128)(2,1)} %all-gather.2.cloned.1.call-done.k_ref.v_ref), custom_call_target="tpu_custom_call" | custom-call | flops 2147483648 | bytes 3145728 | tf_op jit(solution)/shard_map/pallas_call | solution.py:224
  95.9 1.2 convert_element_type.49
  97.6 1.0 convert_element_type.50
  98.6 6.3 %collective-permute-start.8 = (bf16[2,128,1024]{2,1,0:T(8,128)(2,1)}, bf16[2,128,1024]{2,1,0:T(8,128)(2,1)}, u32[]{:S(2)}, u32[]{:S(2)}) collective-permute-start(bf16[2,128,1024]{2,1,0:T(8,128)(2,1)} %convert_element_type.50), channel_id=1, source_target_pairs={{0,8},{2,10},{4,12},{6,14},{8,0},{10,2},{12,4},{14,6},{1,9},{3,11}... | collective-permute-start | bytes 1572872 | tf_op jit(solution)/shard_map/ppermute | solution.py:57
  105.3 14.6 %collective-permute-done.6 = bf16[2,128,1024]{2,1,0:T(8,128)(2,1)} collective-permute-done((bf16[2,128,1024]{2,1,0:T(8,128)(2,1)}, bf16[2,128,1024]{2,1,0:T(8,128)(2,1)}, u32[]{:S(2)}, u32[]{:S(2)}) %collective-permute-start.6) | collective-permute-done | bytes 524320 | tf_op jit(solution)/shard_map/ppermute | solution.py:57
  119.8 1.1 convert_element_type.47
  121.0 1.4 %add_select_fusion.2 = f32[2,128,1024]{2,1,0:T(8,128)S(1)} fusion(f32[2,128,1024]{2,1,0:T(8,128)S(1)} %convert_element_type.41, f32[2,128,1024]{2,1,0:T(8,128)S(1)} %convert_element_type.45, f32[2,1024]{1,0:T(2,128)S(1)} %mul.308, f32[2,1024]{1,0:T(2,128)S(1)} %mul.287, pred[]{:T(512)S(6)} %eq.13, pred[]{:T(512)S(6)} %eq.15, pred[]{:T(512)S(6)} %eq.14, ...), kind=kLoop, calls=%fused_computation.5 | loop fusion | flops 2097152 | bytes 3686403 | tf_op jit(solution)/shard_map/jit(_where)/select_n | solution.py:69
  122.4 6.8 %collective-permute-done.8 = bf16[2,128,1024]{2,1,0:T(8,128)(2,1)} collective-permute-done((bf16[2,128,1024]{2,1,0:T(8,128)(2,1)}, bf16[2,128,1024]{2,1,0:T(8,128)(2,1)}, u32[]{:S(2)}, u32[]{:S(2)}) %collective-permute-start.8) | collective-permute-done | bytes 524320 | tf_op jit(solution)/shard_map/ppermute | solution.py:57
  129.3 1.1 convert_element_type.51
  130.5 1.5 %add_select_fusion = f32[2,128,1024]{2,1,0:T(8,128)S(1)} fusion(f32[2,128,1024]{2,1,0:T(8,128)S(1)} %convert_element_type.43, f32[2,128,1024]{2,1,0:T(8,128)S(1)} %copy-done.2, f32[2,1024]{1,0:T(2,128)S(1)} %mul.338, f32[2,1024]{1,0:T(2,128)S(1)} %mul.329, pred[]{:T(512)S(6)} %eq.13, pred[]{:T(512)S(6)} %eq.15, pred[]{:T(512)S(6)} %eq.14, ...), kind=kLoop, calls=%fused_computation.3 | loop fusion | flops 2097152 | bytes 3686403 | tf_op jit(solution)/shard_map/jit(_where)/select_n | solution.py:69
  134.9 1.4 fusion.1
  (139 shorter events, 19.4 us)
Async XLA Ops:
  7.2 42.0 %copy-start = (bf16[256,128]{1,0:T(8,128)(2,1)S(1)}, bf16[256,128]{1,0:T(8,128)(2,1)}, u32[]{:S(2)}) copy-start(bf16[256,128]{1,0:T(8,128)(2,1)} %param.14) | copy-start | bytes 196612
  7.2 66.8 %all-gather.2.cloned.1.call-start = ((), (), s32[]{:S(2)}) async-start(), calls=%async_computation | async-start | bytes 2359296 | tf_op jit(solution)/shard_map/all_gather | solution.py:248
  11.0 14.2 %copy-start.13 = (f32[2,32,128]{2,1,0:T(8,128)}, f32[2,32,128]{2,1,0:T(8,128)S(1)}, u32[]{:S(2)}) copy-start(f32[2,32,128]{2,1,0:T(8,128)S(1)} %reduce_window_sum.11) | copy-start | bytes 98308
  11.2 20.3 %collective-permute-start = (f32[2,32]{1,0:T(2,128)S(1)}, f32[2,32]{1,0:T(2,128)S(1)}, u32[]{:S(2)}, u32[]{:S(2)}) collective-permute-start(f32[2,32]{1,0:T(2,128)S(1)} %exp.23), channel_id=1, source_target_pairs={{0,2},{2,0},{4,6},{6,4},{8,10},{10,8},{12,14},{14,12},{1,3},{3,1},... | collective-permute-start | bytes 776 | tf_op jit(solution)/shard_map/ppermute | solution.py:30
  15.3 1.9 %copy-start.15 = (bf16[256,128]{1,0:T(8,128)(2,1)S(1)}, bf16[256,128]{1,0:T(8,128)(2,1)}, u32[]{:S(2)}) copy-start(bf16[256,128]{1,0:T(8,128)(2,1)} %param.13) | copy-start | bytes 196612
  18.0 6.5 %copy-start.14 = (f32[32,256]{1,0:T(8,128)S(1)}, f32[32,256]{1,0:T(8,128)}, u32[]{:S(2)}) copy-start(f32[32,256]{1,0:T(8,128)} %param.10) | copy-start | bytes 98308
  26.9 25.4 %copy-start.5 = (f32[2,128,1024]{2,1,0:T(8,128)}, f32[2,128,1024]{2,1,0:T(8,128)S(1)}, u32[]{:S(2)}) copy-start(f32[2,128,1024]{2,1,0:T(8,128)S(1)} %get-tuple-element.28) | copy-start | bytes 3145732
  31.5 16.5 %collective-permute-start.1 = (bf16[2,128,1024]{2,1,0:T(8,128)(2,1)S(1)}, bf16[2,128,1024]{2,1,0:T(8,128)(2,1)}, u32[]{:S(2)}, u32[]{:S(2)}) collective-permute-start(bf16[2,128,1024]{2,1,0:T(8,128)(2,1)S(1)} %convert_element_type.40), channel_id=1, source_target_pairs={{0,2},{2,0},{4,6},{6,4},{8,10},{10,8},{12,14},{14,12},{1,3},{3,1},... | collective-permute-start | bytes 1572872 | tf_op jit(solution)/shard_map/ppermute | solution.py:57
  31.9 3.8 %collective-permute-start.3 = (f32[2,32]{1,0:T(2,128)S(1)}, f32[2,32]{1,0:T(2,128)S(1)}, u32[]{:S(2)}, u32[]{:S(2)}) collective-permute-start(f32[2,32]{1,0:T(2,128)S(1)} %exponential_multiply_fusion), channel_id=1, source_target_pairs={{0,4},{2,6},{4,0},{6,2},{8,12},{10,14},{12,8},{14,10},{1,5},{3,7},... | collective-permute-start | bytes 776 | tf_op jit(solution)/shard_map/ppermute | solution.py:30
  35.7 4.5 %collective-permute-start.4 = (f32[2,32]{1,0:T(2,128)S(1)}, f32[2,32]{1,0:T(2,128)S(1)}, u32[]{:S(2)}, u32[]{:S(2)}) collective-permute-start(f32[2,32]{1,0:T(2,128)S(1)} %mul.280), channel_id=1, source_target_pairs={{0,8},{2,10},{4,12},{6,14},{8,0},{10,2},{12,4},{14,6},{1,9},{3,11}... | collective-permute-start | bytes 776 | tf_op jit(solution)/shard_map/ppermute | solution.py:30
  39.2 10.2 %copy-start.16 = (f32[2,1024]{1,0:T(2,128)}, f32[2,1024]{1,0:T(2,128)S(1)}, u32[]{:S(2)}) copy-start(f32[2,1024]{1,0:T(2,128)S(1)} %mul.318) | copy-start | bytes 24580
  39.3 10.1 %copy-start.17 = (f32[2,1024]{1,0:T(2,128)}, f32[2,1024]{1,0:T(2,128)S(1)}, u32[]{:S(2)}) copy-start(f32[2,1024]{1,0:T(2,128)S(1)} %mul.347) | copy-start | bytes 24580
  50.4 3.3 %copy-start.20 = (f32[32]{0:T(128)S(1)}, f32[32]{0:T(128)}, u32[]{:S(2)}) copy-start(f32[32]{0:T(128)} %param.12) | copy-start | bytes 388
  50.5 21.1 %collective-permute-start.5 = (bf16[2,128,1024]{2,1,0:T(8,128)(2,1)S(1)}, bf16[2,128,1024]{2,1,0:T(8,128)(2,1)}, u32[]{:S(2)}, u32[]{:S(2)}) collective-permute-start(bf16[2,128,1024]{2,1,0:T(8,128)(2,1)S(1)} %convert_element_type.44), channel_id=1, source_target_pairs={{0,4},{2,6},{4,0},{6,2},{8,12},{10,14},{12,8},{14,10},{1,5},{3,7},... | collective-permute-start | bytes 1572872 | tf_op jit(solution)/shard_map/ppermute | solution.py:57
  53.1 14.3 %collective-permute-start.2 = (bf16[2,128,1024]{2,1,0:T(8,128)(2,1)}, bf16[2,128,1024]{2,1,0:T(8,128)(2,1)S(1)}, u32[]{:S(2)}, u32[]{:S(2)}) collective-permute-start(bf16[2,128,1024]{2,1,0:T(8,128)(2,1)} %convert_element_type.42), channel_id=1, source_target_pairs={{0,2},{2,0},{4,6},{6,4},{8,10},{10,8},{12,14},{14,12},{1,3},{3,1},... | collective-permute-start | bytes 1572872 | tf_op jit(solution)/shard_map/ppermute | solution.py:57
  64.2 8.5 %copy-start.6 = (f32[2,128,1024]{2,1,0:T(8,128)S(1)}, f32[2,128,1024]{2,1,0:T(8,128)}, u32[]{:S(2)}) copy-start(f32[2,128,1024]{2,1,0:T(8,128)} %copy-done.5) | copy-start | bytes 3145732
  76.1 19.9 %collective-permute-start.7 = (bf16[2,128,1024]{2,1,0:T(8,128)(2,1)}, bf16[2,128,1024]{2,1,0:T(8,128)(2,1)}, u32[]{:S(2)}, u32[]{:S(2)}) collective-permute-start(bf16[2,128,1024]{2,1,0:T(8,128)(2,1)} %convert_element_type.48), channel_id=1, source_target_pairs={{0,4},{2,6},{4,0},{6,2},{8,12},{10,14},{12,8},{14,10},{1,5},{3,7},... | collective-permute-start | bytes 1572872 | tf_op jit(solution)/shard_map/ppermute | solution.py:57
  81.3 38.5 %collective-permute-start.6 = (bf16[2,128,1024]{2,1,0:T(8,128)(2,1)}, bf16[2,128,1024]{2,1,0:T(8,128)(2,1)}, u32[]{:S(2)}, u32[]{:S(2)}) collective-permute-start(bf16[2,128,1024]{2,1,0:T(8,128)(2,1)} %convert_element_type.46), channel_id=1, source_target_pairs={{0,8},{2,10},{4,12},{6,14},{8,0},{10,2},{12,4},{14,6},{1,9},{3,11}... | collective-permute-start | bytes 1572872 | tf_op jit(solution)/shard_map/ppermute | solution.py:57
  95.9 1.4 copy-start.4
  97.6 7.3 %copy-start.11 = (f32[2,128,1024]{2,1,0:T(8,128)}, f32[2,128,1024]{2,1,0:T(8,128)S(1)}, u32[]{:S(2)}) copy-start(f32[2,128,1024]{2,1,0:T(8,128)S(1)} %add_select_fusion.4) | copy-start | bytes 3145732
  98.6 30.7 %collective-permute-start.8 = (bf16[2,128,1024]{2,1,0:T(8,128)(2,1)}, bf16[2,128,1024]{2,1,0:T(8,128)(2,1)}, u32[]{:S(2)}, u32[]{:S(2)}) collective-permute-start(bf16[2,128,1024]{2,1,0:T(8,128)(2,1)} %convert_element_type.50), channel_id=1, source_target_pairs={{0,8},{2,10},{4,12},{6,14},{8,0},{10,2},{12,4},{14,6},{1,9},{3,11}... | collective-permute-start | bytes 1572872 | tf_op jit(solution)/shard_map/ppermute | solution.py:57
  105.1 17.3 %copy-start.18 = (f32[2,1024]{1,0:T(2,128)}, f32[2,1024]{1,0:T(2,128)S(1)}, u32[]{:S(2)}) copy-start(f32[2,1024]{1,0:T(2,128)S(1)} %mul.321) | copy-start | bytes 24580
  105.3 17.2 %copy-start.19 = (f32[2,1024]{1,0:T(2,128)}, f32[2,1024]{1,0:T(2,128)S(1)}, u32[]{:S(2)}) copy-start(f32[2,1024]{1,0:T(2,128)S(1)} %mul.350) | copy-start | bytes 24580
  121.0 9.5 %copy-start.2 = (f32[2,128,1024]{2,1,0:T(8,128)S(1)}, f32[2,128,1024]{2,1,0:T(8,128)}, u32[]{:S(2)}) copy-start(f32[2,128,1024]{2,1,0:T(8,128)} %copy-done.1) | copy-start | bytes 3145732
  130.4 1.6 %copy-start.10 = (f32[2,128,1024]{2,1,0:T(8,128)S(1)}, f32[2,128,1024]{2,1,0:T(8,128)}, u32[]{:S(2)}) copy-start(f32[2,128,1024]{2,1,0:T(8,128)} %copy-done.9) | copy-start | bytes 3145732
  130.5 1.7 %copy-start.12 = (f32[2,128,1024]{2,1,0:T(8,128)S(1)}, f32[2,128,1024]{2,1,0:T(8,128)}, u32[]{:S(2)}) copy-start(f32[2,128,1024]{2,1,0:T(8,128)} %copy-done.11) | copy-start | bytes 3145732
  130.5 1.7 %slice-start = ((f32[2,1024]{1,0:T(2,128)}), f32[1,1024]{1,0:T(1,128)S(1)}, s32[]{:S(2)}) async-start(f32[2,1024]{1,0:T(2,128)} %copy-done.16), calls=%async_computation.1 | async-start | bytes 8192 | tf_op jit(solution)/shard_map/slice | solution.py:84
  130.5 1.7 %slice-start.1 = ((f32[2,1024]{1,0:T(2,128)}), f32[1,1024]{1,0:T(1,128)S(1)}, s32[]{:S(2)}) async-start(f32[2,1024]{1,0:T(2,128)} %copy-done.17), calls=%async_computation.2 | async-start | bytes 8192 | tf_op jit(solution)/shard_map/slice | solution.py:84
  130.5 1.7 %slice-start.2 = ((f32[2,1024]{1,0:T(2,128)}), f32[1,1024]{1,0:T(1,128)S(1)}, s32[]{:S(2)}) async-start(f32[2,1024]{1,0:T(2,128)} %copy-done.18), calls=%async_computation.3 | async-start | bytes 8192 | tf_op jit(solution)/shard_map/slice | solution.py:84
  130.5 1.7 %slice-start.3 = ((f32[2,1024]{1,0:T(2,128)}), f32[1,1024]{1,0:T(1,128)S(1)}, s32[]{:S(2)}) async-start(f32[2,1024]{1,0:T(2,128)} %copy-done.19), calls=%async_computation.4 | async-start | bytes 8192 | tf_op jit(solution)/shard_map/slice | solution.py:84
  132.7 1.6 %copy-start.7 = (f32[2,128,2048]{2,1,0:T(8,128)S(1)}, f32[2,128,2048]{2,1,0:T(8,128)}, u32[]{:S(2)}) copy-start(f32[2,128,2048]{2,1,0:T(8,128)} %copy.26) | copy-start | bytes 6291460
  132.7 2.2 %copy-start.8 = (f32[2,128,2048]{2,1,0:T(8,128)S(1)}, f32[2,128,2048]{2,1,0:T(8,128)}, u32[]{:S(2)}) copy-start(f32[2,128,2048]{2,1,0:T(8,128)} %shard_map.105) | copy-start | bytes 6291460
  (3 other events, 3.2 us)
Sparse Core Ops, SparseCore 0:
  14.3 56.7 all-gather.1

commit v14 on v13

--- a/solution.py
+++ b/solution.py
@@ -115,7 +115,8 @@
         transcendentals=slots * heads * BLOCK * BLOCK,
         bytes_accessed=x_in.size * 2 + slots * BLOCK * width * 4,
     )
-    return pl.pallas_call(
+    carried_scale = spread(jnp.exp(cum).transpose(0, 2, 1))
+    return carried_scale, pl.pallas_call(
         mamba_base_kernel,
         out_shape=jax.ShapeDtypeStruct((slots, BLOCK, width), jnp.float32),
         grid=(slots, heads // group),
@@ -269,8 +270,9 @@
         ],
         axis=2,
     )
-    carried = carried * spread(jnp.exp(cum).transpose(0, 2, 1))
-    mamba_out = (results["mamba_base"] + carried).astype(jnp.bfloat16).reshape(tok_rows, width)
+    carried_scale, base = results["mamba_base"]
+    carried = carried * carried_scale
+    mamba_out = (base + carried).astype(jnp.bfloat16).reshape(tok_rows, width)
     return (mamba_out, results["attention_core"])
 
 

time: 144 us -> 142 us (0.986)
  waiting for transfers between devices: 38.5 us -> 34.4 us
    ppermute x6, waiting for transfers between devices: 36.5 us -> 30.9 us  [entering_states(): lax.ppermute(totals[j].astype(jnp.bfloat16), 'seq', pairs)]
    optimization_barrier x0 -> x1, local copies, waits for them, and re-layouts: none -> 2.91 us  [entering_states(): got, done = lax.optimization_barrier((got, done))]
    reshape x2 -> x1, local copies, waits for them, and re-layouts: 4.76 us -> 1.86 us  [spread(): return jnp.repeat(a, HEADDIM, axis=-1)]
    all_gather x1, waiting for transfers between devices: 0.01 us -> 1.7 us  [local(): kv_piece = lax.all_gather(kv_cat, 'seq', axis=1, tiled=True)]
    unnamed x42 -> x44, local copies, waits for them, and re-layouts: 3.18 us -> 3.05 us
  transfers between devices with their start and end apart: 10 -> 10, of which waited for: 7 -> 8; matrix products, arithmetic and copies ran while one was open for 20% -> 21% of each run, Pallas kernels for 19% -> 19%
where the time goes in v14:
time: 142 us; the launch traced here: 141 us
  waiting for transfers between devices  34.4 us (24%)
  Pallas kernels  27.4 us (19%)
  other arithmetic  24.8 us (17%)
  starting transfers between devices  20 us (14%)
  local copies, waits for them, and re-layouts  18.1 us (13%)
  between operations  14.4 us (10%)
  matrix products  2.14 us (2%)
    ppermute x6, waiting for transfers between devices, entering_states(): lax.ppermute(totals[j].astype(jnp.bfloat16), 'seq', pairs)  30.9 us
    pallas_call x1, Pallas kernels, attention_core(): pl.pallas_call(attention_kernel, out_shape=jax.ShapeDtypeStruct(queries.s...  12 us
    ppermute x6, starting transfers between devices, entering_states(): lax.ppermute(totals[j].astype(jnp.bfloat16), 'seq', pairs)  11.8 us
    pallas_call x1, Pallas kernels, mamba_base(): pl.pallas_call(mamba_base_kernel, out_shape=jax.ShapeDtypeStruct((slots,...  8.85 us
    ppermute x3, starting transfers between devices, decay_scan(): got = lax.ppermute(total, 'seq', [(i, i ^ span) for i in range(count)])  8.19 us
    convert_element_type x6, other arithmetic, entering_states(): lax.ppermute(totals[j].astype(jnp.bfloat16), 'seq', pairs)  6.89 us
    pallas_call x1, Pallas kernels, block_states(): pl.pallas_call(block_state_kernel, out_shape=jax.ShapeDtypeStruct((slots,...  6.53 us
    convert_element_type x6, other arithmetic, entering_states(): totals[j].astype(jnp.bfloat16)  5.13 us
  transfers between devices with their start and end apart: 10, of which 8 were waited for; matrix products, arithmetic and copies ran while one was open for 21% of the time, Pallas kernels for 19%

profile of v14, /device:TPU:0, one launch (start us, length us, event | category | flops | bytes accessed | tf_op | source)
XLA Modules:
  0.0 141.3 jit_solution(14892115981307612221)
XLA Ops:
  7.9 1.7 %pad_maximum_fusion = bf16[2,128,512]{2,1,0:T(8,128)(2,1)} fusion(bf16[2,128,256]{2,1,0:T(8,128)(2,1)} %bitcast.67, bf16[2,128,256]{2,1,0:T(8,128)(2,1)} %bitcast.68), kind=kLoop, calls=%fused_computation.23 | loop fusion | flops 524288 | bytes 524288 | tf_op jit(solution)/shard_map/concatenate | solution.py:245
  11.1 3.0 %collective-permute-start = (f32[2,32]{1,0:T(2,128)S(1)}, f32[2,32]{1,0:T(2,128)S(1)}, u32[]{:S(2)}, u32[]{:S(2)}) collective-permute-start(f32[2,32]{1,0:T(2,128)S(1)} %exp.19), channel_id=1, source_target_pairs={{0,2},{2,0},{4,6},{6,4},{8,10},{10,8},{12,14},{14,12},{1,3},{3,1},... | collective-permute-start | bytes 776 | tf_op jit(solution)/shard_map/ppermute | solution.py:30
  15.1 1.6 %copy.18 = bf16[2,128,128]{1,2,0:T(8,128)(2,1)} copy(bf16[2,128,128]{2,1,0:T(8,128)(2,1)} %bitcast.63) | data formatting | bytes 131072 | tf_op jit(solution)/shard_map/reshape | solution.py:255
  16.8 1.9 %copy.21.f_ref = f32[2,128,2048]{2,1,0:T(8,128)} copy(f32[2,128,2048]{1,2,0:T(8,128)S(1)} %bitcast.60) | data formatting | bytes 4194304 | tf_op jit(solution)/shard_map/reshape | solution.py:20
  18.8 6.5 %shard_map.104 = f32[2,128,2048]{2,1,0:T(8,128)} custom-call(bf16[2,128,128]{2,1,0:T(8,128)(2,1)} %bitcast.65, f32[2,128,2048]{2,1,0:T(8,128)} %copy.21.f_ref, bf16[256,2048]{1,0:T(8,128)(2,1)} %x_ref.1), custom_call_target="tpu_custom_call" | custom-call | flops 134217728 | bytes 5242880 | tf_op jit(solution)/shard_map/pallas_call | solution.py:151
  26.0 1.7 %fusion.11 = (f32[2,128,1024]{2,1,0:T(8,128)S(1)}, f32[2,128,1024]{2,1,0:T(8,128)S(1)}) fusion(f32[2,128,2048]{2,1,0:T(8,128)} %shard_map.104), kind=kLoop, calls=%fused_computation.43 | loop fusion | bytes 4194304 | tf_op jit(solution)/shard_map/slice | solution.py:42
  28.2 2.1 %collective-permute-start.3 = (f32[2,32]{1,0:T(2,128)S(1)}, f32[2,32]{1,0:T(2,128)S(1)}, u32[]{:S(2)}, u32[]{:S(2)}) collective-permute-start(f32[2,32]{1,0:T(2,128)S(1)} %exponential_multiply_fusion), channel_id=1, source_target_pairs={{0,4},{2,6},{4,0},{6,2},{8,12},{10,14},{12,8},{14,10},{1,5},{3,7},... | collective-permute-start | bytes 776 | tf_op jit(solution)/shard_map/ppermute | solution.py:30
  31.9 3.0 %collective-permute-start.4 = (f32[2,32]{1,0:T(2,128)S(1)}, f32[2,32]{1,0:T(2,128)S(1)}, u32[]{:S(2)}, u32[]{:S(2)}) collective-permute-start(f32[2,32]{1,0:T(2,128)S(1)} %mul.280), channel_id=1, source_target_pairs={{0,8},{2,10},{4,12},{6,14},{8,0},{10,2},{12,4},{14,6},{1,9},{3,11}... | collective-permute-start | bytes 776 | tf_op jit(solution)/shard_map/ppermute | solution.py:30
  36.7 4.8 %collective-permute-done.1 = bf16[2,128,1024]{2,1,0:T(8,128)(2,1)} collective-permute-done((bf16[2,128,1024]{2,1,0:T(8,128)(2,1)S(1)}, bf16[2,128,1024]{2,1,0:T(8,128)(2,1)}, u32[]{:S(2)}, u32[]{:S(2)}) %collective-permute-start.1) | collective-permute-done | bytes 524320 | tf_op jit(solution)/shard_map/ppermute | solution.py:57
  41.5 1.2 convert_element_type.41
  45.1 1.9 %collective-permute-start.5 = (bf16[2,128,1024]{2,1,0:T(8,128)(2,1)S(1)}, bf16[2,128,1024]{2,1,0:T(8,128)(2,1)}, u32[]{:S(2)}, u32[]{:S(2)}) collective-permute-start(bf16[2,128,1024]{2,1,0:T(8,128)(2,1)S(1)} %convert_element_type.44), channel_id=1, source_target_pairs={{0,4},{2,6},{4,0},{6,2},{8,12},{10,14},{12,8},{14,10},{1,5},{3,7},... | collective-permute-start | bytes 1572872 | tf_op jit(solution)/shard_map/ppermute | solution.py:57
  48.6 8.9 %shard_map.105 = f32[2,128,2048]{2,1,0:T(8,128)} custom-call(bf16[256,2048]{1,0:T(8,128)(2,1)} %x_ref.1, f32[2,128,128]{2,1,0:T(8,128)} %fusion.20.inner_ref, f32[2,32,1,128]{3,2,1,0:T(1,128)} %bitcast.62, f32[2,32,1,128]{3,2,1,0:T(1,128)} %bitcast.66, f32[1,2048]{1,0:T(1,128)} %broadcast_in_dim_reshape.2.skip_ref), custom_call_target="tpu_custom_call" | custom-call | flops 140509184 | bytes 3145728 | tf_op jit(solution)/shard_map/pallas_call | solution.py:119
  57.5 8.7 %collective-permute-done.2 = bf16[2,128,1024]{2,1,0:T(8,128)(2,1)} collective-permute-done((bf16[2,128,1024]{2,1,0:T(8,128)(2,1)}, bf16[2,128,1024]{2,1,0:T(8,128)(2,1)}, u32[]{:S(2)}, u32[]{:S(2)}) %collective-permute-start.2) | collective-permute-done | bytes 524320 | tf_op jit(solution)/shard_map/ppermute | solution.py:57
  66.3 1.1 convert_element_type.43
  67.4 1.5 %broadcast_in_dim.87 = f32[2,128,32,64]{1,3,2,0:T(8,128)} broadcast(f32[2,128,32]{1,2,0:T(8,128)S(1)} %exponential_bitcast_fusion), dimensions={0,1,2} | broadcast | bytes 2129920 | tf_op jit(solution)/shard_map/broadcast_in_dim | solution.py:20
  68.9 1.1 convert_element_type.45
  70.1 1.2 add_select_fusion.7
  71.3 1.7 %all-gather.2.cloned.1.call-done.k_ref.v_ref = bf16[2,1024,512]{2,1,0:T(8,128)(2,1)} async-done(((bf16[2,128,512]{2,1,0:T(8,128)(2,1)}), bf16[2,1024,512]{2,1,0:T(8,128)(2,1)}) %all-gather.2.cloned.1.call-update) | async-done | bytes 2097168 | tf_op jit(solution)/shard_map/all_gather | solution.py:249
  73.0 2.1 %convert_element_type.48 = bf16[2,128,1024]{2,1,0:T(8,128)(2,1)} convert(f32[2,128,1024]{2,1,0:T(8,128)} %add_select_fusion.7) | non-fusion elementwise | flops 262144 | bytes 1572864 | tf_op jit(solution)/shard_map/convert_element_type | solution.py:57
  75.1 1.5 %collective-permute-start.7 = (bf16[2,128,1024]{2,1,0:T(8,128)(2,1)}, bf16[2,128,1024]{2,1,0:T(8,128)(2,1)}, u32[]{:S(2)}, u32[]{:S(2)}) collective-permute-start(bf16[2,128,1024]{2,1,0:T(8,128)(2,1)} %convert_element_type.48), channel_id=1, source_target_pairs={{0,4},{2,6},{4,0},{6,2},{8,12},{10,14},{12,8},{14,10},{1,5},{3,7},... | collective-permute-start | bytes 1572872 | tf_op jit(solution)/shard_map/ppermute | solution.py:57
  77.3 1.5 %add_select_fusion.5 = f32[2,128,1024]{2,1,0:T(8,128)S(1)} fusion(f32[2,128,1024]{2,1,0:T(8,128)S(1)} %convert_element_type.45, f32[2,128,1024]{2,1,0:T(8,128)} %copy-done.3, f32[2,1024]{1,0:T(2,128)S(1)} %mul.304, f32[2,1024]{1,0:T(2,128)S(1)} %mul.289, pred[]{:T(512)S(6)} %eq.15), kind=kLoop, calls=%fused_computation.16 | loop fusion | flops 1310720 | bytes 3162113 | tf_op jit(solution)/shard_map/jit(_where)/select_n | solution.py:70
  80.6 1.1 collective-permute-start.6
  81.8 12.0 %shard_map.106 = bf16[256,1024]{1,0:T(8,128)(2,1)} custom-call(bf16[256,1024]{1,0:T(8,128)(2,1)} %q_ref, bf16[2,1024,512]{2,1,0:T(8,128)(2,1)} %all-gather.2.cloned.1.call-done.k_ref.v_ref, bf16[2,1024,512]{2,1,0:T(8,128)(2,1)} %all-gather.2.cloned.1.call-done.k_ref.v_ref), custom_call_target="tpu_custom_call" | custom-call | flops 2147483648 | bytes 3145728 | tf_op jit(solution)/shard_map/pallas_call | solution.py:225
  94.8 1.1 convert_element_type.49
  97.4 6.9 %collective-permute-start.8 = (bf16[2,128,1024]{2,1,0:T(8,128)(2,1)}, bf16[2,128,1024]{2,1,0:T(8,128)(2,1)}, u32[]{:S(2)}, u32[]{:S(2)}) collective-permute-start(bf16[2,128,1024]{2,1,0:T(8,128)(2,1)} %convert_element_type.50), channel_id=1, source_target_pairs={{0,8},{2,10},{4,12},{6,14},{8,0},{10,2},{12,4},{14,6},{1,9},{3,11}... | collective-permute-start | bytes 1572872 | tf_op jit(solution)/shard_map/ppermute | solution.py:57
  105.6 2.9 %copy.26 = f32[2,128,2048]{2,1,0:T(8,128)} copy(f32[2,128,2048]{1,2,0:T(8,128)} %bitcast.59) | data formatting | bytes 4194304 | tf_op jit(solution)/shard_map/optimization_barrier | solution.py:60
  108.5 9.3 %collective-permute-done.6 = bf16[2,128,1024]{2,1,0:T(8,128)(2,1)} collective-permute-done((bf16[2,128,1024]{2,1,0:T(8,128)(2,1)}, bf16[2,128,1024]{2,1,0:T(8,128)(2,1)}, u32[]{:S(2)}, u32[]{:S(2)}) %collective-permute-start.6) | collective-permute-done | bytes 524320 | tf_op jit(solution)/shard_map/ppermute | solution.py:57
  117.8 1.1 convert_element_type.47
  119.0 1.4 %add_select_fusion.2 = f32[2,128,1024]{2,1,0:T(8,128)S(1)} fusion(f32[2,128,1024]{2,1,0:T(8,128)S(1)} %convert_element_type.41, f32[2,128,1024]{2,1,0:T(8,128)S(1)} %convert_element_type.45, f32[2,1024]{1,0:T(2,128)S(1)} %mul.308, f32[2,1024]{1,0:T(2,128)S(1)} %mul.287, pred[]{:T(512)S(6)} %eq.13, pred[]{:T(512)S(6)} %eq.15, pred[]{:T(512)S(6)} %eq.14, ...), kind=kLoop, calls=%fused_computation.5 | loop fusion | flops 2097152 | bytes 3686403 | tf_op jit(solution)/shard_map/jit(_where)/select_n | solution.py:69
  120.5 7.0 %collective-permute-done.8 = bf16[2,128,1024]{2,1,0:T(8,128)(2,1)} collective-permute-done((bf16[2,128,1024]{2,1,0:T(8,128)(2,1)}, bf16[2,128,1024]{2,1,0:T(8,128)(2,1)}, u32[]{:S(2)}, u32[]{:S(2)}) %collective-permute-start.8) | collective-permute-done | bytes 524320 | tf_op jit(solution)/shard_map/ppermute | solution.py:57
  128.7 1.5 %add_select_fusion = f32[2,128,1024]{2,1,0:T(8,128)S(1)} fusion(f32[2,128,1024]{2,1,0:T(8,128)S(1)} %convert_element_type.43, f32[2,128,1024]{2,1,0:T(8,128)S(1)} %copy-done.2, f32[2,1024]{1,0:T(2,128)S(1)} %mul.338, f32[2,1024]{1,0:T(2,128)S(1)} %mul.329, pred[]{:T(512)S(6)} %eq.13, pred[]{:T(512)S(6)} %eq.15, pred[]{:T(512)S(6)} %eq.14, ...), kind=kLoop, calls=%fused_computation.3 | loop fusion | flops 2097152 | bytes 3686403 | tf_op jit(solution)/shard_map/jit(_where)/select_n | solution.py:69
  133.0 1.4 fusion.1
  (141 shorter events, 22.2 us)
Async XLA Ops:
  7.2 35.5 %copy-start = (bf16[256,128]{1,0:T(8,128)(2,1)S(1)}, bf16[256,128]{1,0:T(8,128)(2,1)}, u32[]{:S(2)}) copy-start(bf16[256,128]{1,0:T(8,128)(2,1)} %param.14) | copy-start | bytes 196612
  7.2 65.8 %all-gather.2.cloned.1.call-start = ((), (), s32[]{:S(2)}) async-start(), calls=%async_computation | async-start | bytes 2359296 | tf_op jit(solution)/shard_map/all_gather | solution.py:249
  11.0 7.7 %copy-start.13 = (f32[2,32,128]{2,1,0:T(8,128)}, f32[2,32,128]{2,1,0:T(8,128)S(1)}, u32[]{:S(2)}) copy-start(f32[2,32,128]{2,1,0:T(8,128)S(1)} %reduce_window_sum.11) | copy-start | bytes 98308
  11.1 16.7 %collective-permute-start = (f32[2,32]{1,0:T(2,128)S(1)}, f32[2,32]{1,0:T(2,128)S(1)}, u32[]{:S(2)}, u32[]{:S(2)}) collective-permute-start(f32[2,32]{1,0:T(2,128)S(1)} %exp.19), channel_id=1, source_target_pairs={{0,2},{2,0},{4,6},{6,4},{8,10},{10,8},{12,14},{14,12},{1,3},{3,1},... | collective-permute-start | bytes 776 | tf_op jit(solution)/shard_map/ppermute | solution.py:30
  18.8 6.5 %copy-start.15 = (f32[32,256]{1,0:T(8,128)S(1)}, f32[32,256]{1,0:T(8,128)}, u32[]{:S(2)}) copy-start(f32[32,256]{1,0:T(8,128)} %param.10) | copy-start | bytes 98308
  27.6 15.9 %copy-start.5 = (f32[2,128,1024]{2,1,0:T(8,128)}, f32[2,128,1024]{2,1,0:T(8,128)S(1)}, u32[]{:S(2)}) copy-start(f32[2,128,1024]{2,1,0:T(8,128)S(1)} %get-tuple-element.29) | copy-start | bytes 3145732
  27.9 13.6 %collective-permute-start.1 = (bf16[2,128,1024]{2,1,0:T(8,128)(2,1)S(1)}, bf16[2,128,1024]{2,1,0:T(8,128)(2,1)}, u32[]{:S(2)}, u32[]{:S(2)}) collective-permute-start(bf16[2,128,1024]{2,1,0:T(8,128)(2,1)S(1)} %convert_element_type.40), channel_id=1, source_target_pairs={{0,2},{2,0},{4,6},{6,4},{8,10},{10,8},{12,14},{14,12},{1,3},{3,1},... | collective-permute-start | bytes 1572872 | tf_op jit(solution)/shard_map/ppermute | solution.py:57
  28.2 3.7 %collective-permute-start.3 = (f32[2,32]{1,0:T(2,128)S(1)}, f32[2,32]{1,0:T(2,128)S(1)}, u32[]{:S(2)}, u32[]{:S(2)}) collective-permute-start(f32[2,32]{1,0:T(2,128)S(1)} %exponential_multiply_fusion), channel_id=1, source_target_pairs={{0,4},{2,6},{4,0},{6,2},{8,12},{10,14},{12,8},{14,10},{1,5},{3,7},... | collective-permute-start | bytes 776 | tf_op jit(solution)/shard_map/ppermute | solution.py:30
  31.9 4.6 %collective-permute-start.4 = (f32[2,32]{1,0:T(2,128)S(1)}, f32[2,32]{1,0:T(2,128)S(1)}, u32[]{:S(2)}, u32[]{:S(2)}) collective-permute-start(f32[2,32]{1,0:T(2,128)S(1)} %mul.280), channel_id=1, source_target_pairs={{0,8},{2,10},{4,12},{6,14},{8,0},{10,2},{12,4},{14,6},{1,9},{3,11}... | collective-permute-start | bytes 776 | tf_op jit(solution)/shard_map/ppermute | solution.py:30
  35.4 8.6 %copy-start.17 = (f32[2,1024]{1,0:T(2,128)}, f32[2,1024]{1,0:T(2,128)S(1)}, u32[]{:S(2)}) copy-start(f32[2,1024]{1,0:T(2,128)S(1)} %mul.347) | copy-start | bytes 24580
  35.7 8.3 %copy-start.18 = (f32[2,1024]{1,0:T(2,128)}, f32[2,1024]{1,0:T(2,128)S(1)}, u32[]{:S(2)}) copy-start(f32[2,1024]{1,0:T(2,128)S(1)} %mul.318) | copy-start | bytes 24580
  43.5 3.5 %copy-start.21 = (f32[32]{0:T(128)S(1)}, f32[32]{0:T(128)}, u32[]{:S(2)}) copy-start(f32[32]{0:T(128)} %param.12) | copy-start | bytes 388
  43.5 4.3 %copy-start.16 = (bf16[256,128]{1,0:T(8,128)(2,1)S(1)}, bf16[256,128]{1,0:T(8,128)(2,1)}, u32[]{:S(2)}) copy-start(bf16[256,128]{1,0:T(8,128)(2,1)} %param.13) | copy-start | bytes 196612
  43.5 22.7 %collective-permute-start.2 = (bf16[2,128,1024]{2,1,0:T(8,128)(2,1)}, bf16[2,128,1024]{2,1,0:T(8,128)(2,1)}, u32[]{:S(2)}, u32[]{:S(2)}) collective-permute-start(bf16[2,128,1024]{2,1,0:T(8,128)(2,1)} %convert_element_type.42), channel_id=1, source_target_pairs={{0,2},{2,0},{4,6},{6,4},{8,10},{10,8},{12,14},{14,12},{1,3},{3,1},... | collective-permute-start | bytes 1572872 | tf_op jit(solution)/shard_map/ppermute | solution.py:57
  45.1 12.4 %copy-start.14 = (f32[2,32,128]{2,1,0:T(8,128)S(1)}, f32[2,32,128]{2,1,0:T(8,128)}, u32[]{:S(2)}) copy-start(f32[2,32,128]{2,1,0:T(8,128)} %copy-done.13) | copy-start | bytes 98308
  45.1 23.8 %collective-permute-start.5 = (bf16[2,128,1024]{2,1,0:T(8,128)(2,1)S(1)}, bf16[2,128,1024]{2,1,0:T(8,128)(2,1)}, u32[]{:S(2)}, u32[]{:S(2)}) collective-permute-start(bf16[2,128,1024]{2,1,0:T(8,128)(2,1)S(1)} %convert_element_type.44), channel_id=1, source_target_pairs={{0,4},{2,6},{4,0},{6,2},{8,12},{10,14},{12,8},{14,10},{1,5},{3,7},... | collective-permute-start | bytes 1572872 | tf_op jit(solution)/shard_map/ppermute | solution.py:57
  67.4 2.7 %copy-start.6 = (f32[2,128,1024]{2,1,0:T(8,128)S(1)}, f32[2,128,1024]{2,1,0:T(8,128)}, u32[]{:S(2)}) copy-start(f32[2,128,1024]{2,1,0:T(8,128)} %copy-done.5) | copy-start | bytes 3145732
  75.1 19.7 %collective-permute-start.7 = (bf16[2,128,1024]{2,1,0:T(8,128)(2,1)}, bf16[2,128,1024]{2,1,0:T(8,128)(2,1)}, u32[]{:S(2)}, u32[]{:S(2)}) collective-permute-start(bf16[2,128,1024]{2,1,0:T(8,128)(2,1)} %convert_element_type.48), channel_id=1, source_target_pairs={{0,4},{2,6},{4,0},{6,2},{8,12},{10,14},{12,8},{14,10},{1,5},{3,7},... | collective-permute-start | bytes 1572872 | tf_op jit(solution)/shard_map/ppermute | solution.py:57
  77.3 3.3 %copy-start.19 = (f32[2,1024]{1,0:T(2,128)}, f32[2,1024]{1,0:T(2,128)S(1)}, u32[]{:S(2)}) copy-start(f32[2,1024]{1,0:T(2,128)S(1)} %mul.350) | copy-start | bytes 24580
  80.6 37.2 %collective-permute-start.6 = (bf16[2,128,1024]{2,1,0:T(8,128)(2,1)}, bf16[2,128,1024]{2,1,0:T(8,128)(2,1)}, u32[]{:S(2)}, u32[]{:S(2)}) collective-permute-start(bf16[2,128,1024]{2,1,0:T(8,128)(2,1)} %convert_element_type.46), channel_id=1, source_target_pairs={{0,8},{2,10},{4,12},{6,14},{8,0},{10,2},{12,4},{14,6},{1,9},{3,11}... | collective-permute-start | bytes 1572872 | tf_op jit(solution)/shard_map/ppermute | solution.py:57
  93.8 2.2 %copy-start.4 = (f32[2,128,1024]{2,1,0:T(8,128)S(1)}, f32[2,128,1024]{2,1,0:T(8,128)}, u32[]{:S(2)}) copy-start(f32[2,128,1024]{2,1,0:T(8,128)} %add_select_fusion.7) | copy-start | bytes 3145732
  96.3 8.1 %copy-start.11 = (f32[2,128,1024]{2,1,0:T(8,128)}, f32[2,128,1024]{2,1,0:T(8,128)S(1)}, u32[]{:S(2)}) copy-start(f32[2,128,1024]{2,1,0:T(8,128)S(1)} %add_select_fusion.4) | copy-start | bytes 3145732
  97.4 30.0 %collective-permute-start.8 = (bf16[2,128,1024]{2,1,0:T(8,128)(2,1)}, bf16[2,128,1024]{2,1,0:T(8,128)(2,1)}, u32[]{:S(2)}, u32[]{:S(2)}) collective-permute-start(bf16[2,128,1024]{2,1,0:T(8,128)(2,1)} %convert_element_type.50), channel_id=1, source_target_pairs={{0,8},{2,10},{4,12},{6,14},{8,0},{10,2},{12,4},{14,6},{1,9},{3,11}... | collective-permute-start | bytes 1572872 | tf_op jit(solution)/shard_map/ppermute | solution.py:57
  105.2 3.3 %copy-start.20 = (f32[2,1024]{1,0:T(2,128)}, f32[2,1024]{1,0:T(2,128)S(1)}, u32[]{:S(2)}) copy-start(f32[2,1024]{1,0:T(2,128)S(1)} %mul.321) | copy-start | bytes 24580
  119.0 9.6 %copy-start.2 = (f32[2,128,1024]{2,1,0:T(8,128)S(1)}, f32[2,128,1024]{2,1,0:T(8,128)}, u32[]{:S(2)}) copy-start(f32[2,128,1024]{2,1,0:T(8,128)} %copy-done.1) | copy-start | bytes 3145732
  128.6 1.7 %copy-start.12 = (f32[2,128,1024]{2,1,0:T(8,128)S(1)}, f32[2,128,1024]{2,1,0:T(8,128)}, u32[]{:S(2)}) copy-start(f32[2,128,1024]{2,1,0:T(8,128)} %copy-done.11) | copy-start | bytes 3145732
  128.6 1.7 %slice-start = ((f32[2,1024]{1,0:T(2,128)}), f32[1,1024]{1,0:T(1,128)S(1)}, s32[]{:S(2)}) async-start(f32[2,1024]{1,0:T(2,128)} %copy-done.17), calls=%async_computation.1 | async-start | bytes 8192 | tf_op jit(solution)/shard_map/slice | solution.py:84
  128.6 1.7 %slice-start.1 = ((f32[2,1024]{1,0:T(2,128)}), f32[1,1024]{1,0:T(1,128)S(1)}, s32[]{:S(2)}) async-start(f32[2,1024]{1,0:T(2,128)} %copy-done.18), calls=%async_computation.2 | async-start | bytes 8192 | tf_op jit(solution)/shard_map/slice | solution.py:84
  128.6 1.7 %slice-start.2 = ((f32[2,1024]{1,0:T(2,128)}), f32[1,1024]{1,0:T(1,128)S(1)}, s32[]{:S(2)}) async-start(f32[2,1024]{1,0:T(2,128)} %copy-done.19), calls=%async_computation.3 | async-start | bytes 8192 | tf_op jit(solution)/shard_map/slice | solution.py:84
  128.7 1.7 %slice-start.3 = ((f32[2,1024]{1,0:T(2,128)}), f32[1,1024]{1,0:T(1,128)S(1)}, s32[]{:S(2)}) async-start(f32[2,1024]{1,0:T(2,128)} %copy-done.20), calls=%async_computation.4 | async-start | bytes 8192 | tf_op jit(solution)/shard_map/slice | solution.py:84
  130.8 1.6 %copy-start.7 = (f32[2,128,2048]{2,1,0:T(8,128)S(1)}, f32[2,128,2048]{2,1,0:T(8,128)}, u32[]{:S(2)}) copy-start(f32[2,128,2048]{2,1,0:T(8,128)} %shard_map.105) | copy-start | bytes 6291460
  130.8 2.2 %copy-start.8 = (f32[2,128,2048]{2,1,0:T(8,128)S(1)}, f32[2,128,2048]{2,1,0:T(8,128)}, u32[]{:S(2)}) copy-start(f32[2,128,2048]{2,1,0:T(8,128)} %copy.26) | copy-start | bytes 6291460
  (4 other events, 4.9 us)
Sparse Core Ops, SparseCore 0:
  14.3 58.6 all-gather.1

commit v15 on v14

--- a/solution.py
+++ b/solution.py
@@ -37,9 +37,9 @@
 
 def entering_states(decay, block_state, count, mine, hooks, parts):
     steps, excl_decay, total_decay = decay_scan(decay, count, mine)
-    heads, width = decay.shape[1], block_state.shape[2]
-    head_cut, width_cut = heads // parts, width // parts
-    totals = [block_state[:, :, j * width_cut : (j + 1) * width_cut] for j in range(parts)]
+    heads = decay.shape[1]
+    head_cut = heads // parts
+    totals = [block_state[j] for j in range(parts)]
     excls = [jnp.zeros_like(t) for t in totals]
     results = {}
     span = 1
@@ -134,13 +134,13 @@
 
 def block_state_kernel(b_ref, f_ref, x_ref, o_ref):
     scaled = (f_ref[0] * x_ref[...].astype(jnp.float32)).astype(jnp.bfloat16)
-    o_ref[0] = jnp.dot(b_ref[0], scaled, preferred_element_type=jnp.float32)
-
-
-def block_states(b_blocks, factor, x_in):
+    o_ref[0, 0] = jnp.dot(b_ref[0], scaled, preferred_element_type=jnp.float32)
+
+
+def block_states(b_blocks, factor, x_in, parts):
     slots, tokens, state = b_blocks.shape
     width = x_in.shape[1]
-    cut = 512 if width % 512 == 0 else width
+    cut = width // parts
     b_t = b_blocks.transpose(0, 2, 1)
     spread_factor = spread(factor)
     cost = pl.CostEstimate(
@@ -150,14 +150,14 @@
     )
     return pl.pallas_call(
         block_state_kernel,
-        out_shape=jax.ShapeDtypeStruct((slots, state, width), jnp.float32),
-        grid=(slots, width // cut),
+        out_shape=jax.ShapeDtypeStruct((parts, slots, state, cut), jnp.float32),
+        grid=(slots, parts),
         in_specs=[
             pl.BlockSpec((1, state, tokens), lambda c, k: (c, 0, 0)),
             pl.BlockSpec((1, tokens, cut), lambda c, k: (c, 0, k)),
             pl.BlockSpec((tokens, cut), lambda c, k: (c, k)),
         ],
-        out_specs=pl.BlockSpec((1, state, cut), lambda c, k: (c, 0, k)),
+        out_specs=pl.BlockSpec((1, 1, state, cut), lambda c, k: (k, c, 0, 0)),
         cost_estimate=cost,
     )(b_t, spread_factor, x_in)
 
@@ -254,9 +254,9 @@
     factor = (jnp.exp(log_total[:, :, None] - cum) * steps).transpose(0, 2, 1)
     b_blocks = b_in.reshape(slots, BLOCK, STATE)
     c_blocks = c_in.reshape(slots, BLOCK, STATE)
-    block_state = block_states(b_blocks, factor, x_in)
+    parts = 2 if heads % 2 == 0 else 1
+    block_state = block_states(b_blocks, factor, x_in, parts)
     decay = jnp.exp(log_total)
-    parts = 2 if heads % 2 == 0 else 1
     hooks = {
         (1, 0): (mamba_base, (x_in, steps, cum, b_blocks, c_blocks, d_skip)),
         (1, 1): (attention_core, (queries, kv_piece)),

time: 142 us -> 144 us (1.014)
  waiting for transfers between devices: 34.4 us -> 38.8 us
  Pallas kernels: 27.4 us -> 25.3 us
    ppermute x6, waiting for transfers between devices: 30.9 us -> 33.4 us  [entering_states(): lax.ppermute(totals[j].astype(jnp.bfloat16), 'seq', pairs)]
    pallas_call x1, Pallas kernels: 6.53 us -> 4.4 us  [block_states(): pl.pallas_call(block_state_kernel, out_shape=jax.ShapeDtypeStruct((parts,...]
    all_gather x1, waiting for transfers between devices: 1.7 us -> 3.59 us  [local(): kv_piece = lax.all_gather(kv_cat, 'seq', axis=1, tiled=True)]
    slice x1 -> x0, local copies, waits for them, and re-layouts: 1.68 us -> none  [entering_states(): block_state[:, :, j * width_cut:(j + 1) * width_cut]]
    squeeze x0 -> x1, local copies, waits for them, and re-layouts: none -> 1.68 us  [entering_states(): totals = [block_state[j] for j in range(parts)]]
  transfers between devices with their start and end apart: 10 -> 10, of which waited for: 8 -> 8; matrix products, arithmetic and copies ran while one was open for 21% -> 21% of each run, Pallas kernels for 19% -> 18%
where the time goes in v15:
time: 144 us; the launch traced here: 143 us
  waiting for transfers between devices  38.8 us (27%)
  Pallas kernels  25.3 us (18%)
  other arithmetic  24.8 us (17%)
  starting transfers between devices  19.7 us (14%)
  local copies, waits for them, and re-layouts  18.1 us (13%)
  between operations  14.4 us (10%)
  matrix products  2.13 us (1%)
    ppermute x6, waiting for transfers between devices, entering_states(): lax.ppermute(totals[j].astype(jnp.bfloat16), 'seq', pairs)  33.4 us
    pallas_call x1, Pallas kernels, attention_core(): pl.pallas_call(attention_kernel, out_shape=jax.ShapeDtypeStruct(queries.s...  12 us
    ppermute x6, starting transfers between devices, entering_states(): lax.ppermute(totals[j].astype(jnp.bfloat16), 'seq', pairs)  11.5 us
    pallas_call x1, Pallas kernels, mamba_base(): pl.pallas_call(mamba_base_kernel, out_shape=jax.ShapeDtypeStruct((slots,...  8.86 us
    ppermute x3, starting transfers between devices, decay_scan(): got = lax.ppermute(total, 'seq', [(i, i ^ span) for i in range(count)])  8.22 us
    convert_element_type x6, other arithmetic, entering_states(): lax.ppermute(totals[j].astype(jnp.bfloat16), 'seq', pairs)  6.92 us
    convert_element_type x6, other arithmetic, entering_states(): totals[j].astype(jnp.bfloat16)  5.13 us
    pallas_call x1, Pallas kernels, block_states(): pl.pallas_call(block_state_kernel, out_shape=jax.ShapeDtypeStruct((parts,...  4.4 us
  transfers between devices with their start and end apart: 10, of which 8 were waited for; matrix products, arithmetic and copies ran while one was open for 21% of the time, Pallas kernels for 18%

profile of v15, /device:TPU:0, one launch (start us, length us, event | category | flops | bytes accessed | tf_op | source)
XLA Modules:
  0.0 143.3 jit_solution(13012555038615930460)
XLA Ops:
  7.9 1.7 %pad_maximum_fusion = bf16[2,128,512]{2,1,0:T(8,128)(2,1)} fusion(bf16[2,128,256]{2,1,0:T(8,128)(2,1)} %bitcast.71, bf16[2,128,256]{2,1,0:T(8,128)(2,1)} %bitcast.72), kind=kLoop, calls=%fused_computation.25 | loop fusion | flops 524288 | bytes 524288 | tf_op jit(solution)/shard_map/concatenate | solution.py:245
  11.1 3.0 %collective-permute-start = (f32[2,32]{1,0:T(2,128)S(1)}, f32[2,32]{1,0:T(2,128)S(1)}, u32[]{:S(2)}, u32[]{:S(2)}) collective-permute-start(f32[2,32]{1,0:T(2,128)S(1)} %exp.19), channel_id=1, source_target_pairs={{0,2},{2,0},{4,6},{6,4},{8,10},{10,8},{12,14},{14,12},{1,3},{3,1},... | collective-permute-start | bytes 776 | tf_op jit(solution)/shard_map/ppermute | solution.py:30
  15.1 1.6 %copy.18 = bf16[2,128,128]{1,2,0:T(8,128)(2,1)} copy(bf16[2,128,128]{2,1,0:T(8,128)(2,1)} %bitcast.67) | data formatting | bytes 131072 | tf_op jit(solution)/shard_map/reshape | solution.py:255
  16.8 1.9 %copy.21.f_ref = f32[2,128,2048]{2,1,0:T(8,128)} copy(f32[2,128,2048]{1,2,0:T(8,128)S(1)} %bitcast.64) | data formatting | bytes 4194304 | tf_op jit(solution)/shard_map/reshape | solution.py:20
  18.8 4.4 %shard_map.104 = f32[2,2,128,1024]{3,2,1,0:T(8,128)} custom-call(bf16[2,128,128]{2,1,0:T(8,128)(2,1)} %bitcast.69, f32[2,128,2048]{2,1,0:T(8,128)} %copy.21.f_ref, bf16[256,2048]{1,0:T(8,128)(2,1)} %x_ref.1), custom_call_target="tpu_custom_call" | custom-call | flops 134217728 | bytes 5242880 | tf_op jit(solution)/shard_map/pallas_call | solution.py:151
  23.8 1.7 %slice_bitcast_fusion = (f32[2,128,1024]{2,1,0:T(8,128)S(1)}, f32[2,128,1024]{2,1,0:T(8,128)S(1)}) fusion(f32[2,2,128,1024]{3,2,1,0:T(8,128)} %shard_map.104), kind=kLoop, calls=%fused_computation.9 | loop fusion | bytes 4194304 | tf_op jit(solution)/shard_map/squeeze | solution.py:42
  26.1 2.2 %collective-permute-start.3 = (f32[2,32]{1,0:T(2,128)S(1)}, f32[2,32]{1,0:T(2,128)S(1)}, u32[]{:S(2)}, u32[]{:S(2)}) collective-permute-start(f32[2,32]{1,0:T(2,128)S(1)} %exponential_multiply_fusion), channel_id=1, source_target_pairs={{0,4},{2,6},{4,0},{6,2},{8,12},{10,14},{12,8},{14,10},{1,5},{3,7},... | collective-permute-start | bytes 776 | tf_op jit(solution)/shard_map/ppermute | solution.py:30
  29.9 3.0 %collective-permute-start.4 = (f32[2,32]{1,0:T(2,128)S(1)}, f32[2,32]{1,0:T(2,128)S(1)}, u32[]{:S(2)}, u32[]{:S(2)}) collective-permute-start(f32[2,32]{1,0:T(2,128)S(1)} %mul.280), channel_id=1, source_target_pairs={{0,8},{2,10},{4,12},{6,14},{8,0},{10,2},{12,4},{14,6},{1,9},{3,11}... | collective-permute-start | bytes 776 | tf_op jit(solution)/shard_map/ppermute | solution.py:30
  34.6 4.9 %collective-permute-done.1 = bf16[2,128,1024]{2,1,0:T(8,128)(2,1)} collective-permute-done((bf16[2,128,1024]{2,1,0:T(8,128)(2,1)S(1)}, bf16[2,128,1024]{2,1,0:T(8,128)(2,1)}, u32[]{:S(2)}, u32[]{:S(2)}) %collective-permute-start.1) | collective-permute-done | bytes 524320 | tf_op jit(solution)/shard_map/ppermute | solution.py:57
  39.4 1.1 convert_element_type.41
  43.1 1.8 %collective-permute-start.5 = (bf16[2,128,1024]{2,1,0:T(8,128)(2,1)S(1)}, bf16[2,128,1024]{2,1,0:T(8,128)(2,1)}, u32[]{:S(2)}, u32[]{:S(2)}) collective-permute-start(bf16[2,128,1024]{2,1,0:T(8,128)(2,1)S(1)} %convert_element_type.44), channel_id=1, source_target_pairs={{0,4},{2,6},{4,0},{6,2},{8,12},{10,14},{12,8},{14,10},{1,5},{3,7},... | collective-permute-start | bytes 1572872 | tf_op jit(solution)/shard_map/ppermute | solution.py:57
  46.6 8.9 %shard_map.105 = f32[2,128,2048]{2,1,0:T(8,128)} custom-call(bf16[256,2048]{1,0:T(8,128)(2,1)} %x_ref.1, f32[2,128,128]{2,1,0:T(8,128)} %fusion.19.inner_ref, f32[2,32,1,128]{3,2,1,0:T(1,128)} %bitcast.66, f32[2,32,1,128]{3,2,1,0:T(1,128)} %bitcast.70, f32[1,2048]{1,0:T(1,128)} %broadcast_in_dim_reshape.2.skip_ref), custom_call_target="tpu_custom_call" | custom-call | flops 140509184 | bytes 3145728 | tf_op jit(solution)/shard_map/pallas_call | solution.py:119
  55.5 10.2 %collective-permute-done.2 = bf16[2,128,1024]{2,1,0:T(8,128)(2,1)} collective-permute-done((bf16[2,128,1024]{2,1,0:T(8,128)(2,1)}, bf16[2,128,1024]{2,1,0:T(8,128)(2,1)}, u32[]{:S(2)}, u32[]{:S(2)}) %collective-permute-start.2) | collective-permute-done | bytes 524320 | tf_op jit(solution)/shard_map/ppermute | solution.py:57
  65.6 1.2 convert_element_type.43
  66.8 1.5 %broadcast_in_dim.87 = f32[2,128,32,64]{1,3,2,0:T(8,128)} broadcast(f32[2,128,32]{1,2,0:T(8,128)S(1)} %exponential_bitcast_fusion), dimensions={0,1,2} | broadcast | bytes 2129920 | tf_op jit(solution)/shard_map/broadcast_in_dim | solution.py:20
  68.3 1.1 convert_element_type.45
  69.5 1.2 add_select_fusion.7
  70.7 3.6 %all-gather.2.cloned.1.call-done.k_ref.v_ref = bf16[2,1024,512]{2,1,0:T(8,128)(2,1)} async-done(((bf16[2,128,512]{2,1,0:T(8,128)(2,1)}), bf16[2,1024,512]{2,1,0:T(8,128)(2,1)}) %all-gather.2.cloned.1.call-update) | async-done | bytes 2097168 | tf_op jit(solution)/shard_map/all_gather | solution.py:249
  74.3 2.1 %convert_element_type.48 = bf16[2,128,1024]{2,1,0:T(8,128)(2,1)} convert(f32[2,128,1024]{2,1,0:T(8,128)} %add_select_fusion.7) | non-fusion elementwise | flops 262144 | bytes 1572864 | tf_op jit(solution)/shard_map/convert_element_type | solution.py:57
  76.4 1.6 %collective-permute-start.7 = (bf16[2,128,1024]{2,1,0:T(8,128)(2,1)}, bf16[2,128,1024]{2,1,0:T(8,128)(2,1)}, u32[]{:S(2)}, u32[]{:S(2)}) collective-permute-start(bf16[2,128,1024]{2,1,0:T(8,128)(2,1)} %convert_element_type.48), channel_id=1, source_target_pairs={{0,4},{2,6},{4,0},{6,2},{8,12},{10,14},{12,8},{14,10},{1,5},{3,7},... | collective-permute-start | bytes 1572872 | tf_op jit(solution)/shard_map/ppermute | solution.py:57
  78.7 1.5 %add_select_fusion.5 = f32[2,128,1024]{2,1,0:T(8,128)S(1)} fusion(f32[2,128,1024]{2,1,0:T(8,128)S(1)} %convert_element_type.45, f32[2,128,1024]{2,1,0:T(8,128)} %copy-done.3, f32[2,1024]{1,0:T(2,128)S(1)} %mul.304, f32[2,1024]{1,0:T(2,128)S(1)} %mul.289, pred[]{:T(512)S(6)} %eq.15), kind=kLoop, calls=%fused_computation.18 | loop fusion | flops 1310720 | bytes 3162113 | tf_op jit(solution)/shard_map/jit(_where)/select_n | solution.py:70
  82.9 12.0 %shard_map.106 = bf16[256,1024]{1,0:T(8,128)(2,1)} custom-call(bf16[256,1024]{1,0:T(8,128)(2,1)} %q_ref, bf16[2,1024,512]{2,1,0:T(8,128)(2,1)} %all-gather.2.cloned.1.call-done.k_ref.v_ref, bf16[2,1024,512]{2,1,0:T(8,128)(2,1)} %all-gather.2.cloned.1.call-done.k_ref.v_ref), custom_call_target="tpu_custom_call" | custom-call | flops 2147483648 | bytes 3145728 | tf_op jit(solution)/shard_map/pallas_call | solution.py:225
  94.9 1.4 %collective-permute-done.7 = bf16[2,128,1024]{2,1,0:T(8,128)(2,1)} collective-permute-done((bf16[2,128,1024]{2,1,0:T(8,128)(2,1)}, bf16[2,128,1024]{2,1,0:T(8,128)(2,1)}, u32[]{:S(2)}, u32[]{:S(2)}) %collective-permute-start.7) | collective-permute-done | bytes 524320 | tf_op jit(solution)/shard_map/ppermute | solution.py:57
  96.3 1.1 convert_element_type.49
  98.9 6.8 %collective-permute-start.8 = (bf16[2,128,1024]{2,1,0:T(8,128)(2,1)}, bf16[2,128,1024]{2,1,0:T(8,128)(2,1)}, u32[]{:S(2)}, u32[]{:S(2)}) collective-permute-start(bf16[2,128,1024]{2,1,0:T(8,128)(2,1)} %convert_element_type.50), channel_id=1, source_target_pairs={{0,8},{2,10},{4,12},{6,14},{8,0},{10,2},{12,4},{14,6},{1,9},{3,11}... | collective-permute-start | bytes 1572872 | tf_op jit(solution)/shard_map/ppermute | solution.py:57
  107.0 2.9 %copy.26 = f32[2,128,2048]{2,1,0:T(8,128)} copy(f32[2,128,2048]{1,2,0:T(8,128)} %bitcast.63) | data formatting | bytes 4194304 | tf_op jit(solution)/shard_map/optimization_barrier | solution.py:60
  109.9 9.9 %collective-permute-done.6 = bf16[2,128,1024]{2,1,0:T(8,128)(2,1)} collective-permute-done((bf16[2,128,1024]{2,1,0:T(8,128)(2,1)}, bf16[2,128,1024]{2,1,0:T(8,128)(2,1)}, u32[]{:S(2)}, u32[]{:S(2)}) %collective-permute-start.6) | collective-permute-done | bytes 524320 | tf_op jit(solution)/shard_map/ppermute | solution.py:57
  119.8 1.1 convert_element_type.47
  121.0 1.4 %add_select_fusion.2 = f32[2,128,1024]{2,1,0:T(8,128)S(1)} fusion(f32[2,128,1024]{2,1,0:T(8,128)S(1)} %convert_element_type.41, f32[2,128,1024]{2,1,0:T(8,128)S(1)} %convert_element_type.45, f32[2,1024]{1,0:T(2,128)S(1)} %mul.308, f32[2,1024]{1,0:T(2,128)S(1)} %mul.287, pred[]{:T(512)S(6)} %eq.13, pred[]{:T(512)S(6)} %eq.15, pred[]{:T(512)S(6)} %eq.14, ...), kind=kLoop, calls=%fused_computation.5 | loop fusion | flops 2097152 | bytes 3686403 | tf_op jit(solution)/shard_map/jit(_where)/select_n | solution.py:69
  122.5 7.0 %collective-permute-done.8 = bf16[2,128,1024]{2,1,0:T(8,128)(2,1)} collective-permute-done((bf16[2,128,1024]{2,1,0:T(8,128)(2,1)}, bf16[2,128,1024]{2,1,0:T(8,128)(2,1)}, u32[]{:S(2)}, u32[]{:S(2)}) %collective-permute-start.8) | collective-permute-done | bytes 524320 | tf_op jit(solution)/shard_map/ppermute | solution.py:57
  130.7 1.5 %add_select_fusion = f32[2,128,1024]{2,1,0:T(8,128)S(1)} fusion(f32[2,128,1024]{2,1,0:T(8,128)S(1)} %convert_element_type.43, f32[2,128,1024]{2,1,0:T(8,128)S(1)} %copy-done.2, f32[2,1024]{1,0:T(2,128)S(1)} %mul.338, f32[2,1024]{1,0:T(2,128)S(1)} %mul.329, pred[]{:T(512)S(6)} %eq.13, pred[]{:T(512)S(6)} %eq.15, pred[]{:T(512)S(6)} %eq.14, ...), kind=kLoop, calls=%fused_computation.3 | loop fusion | flops 2097152 | bytes 3686403 | tf_op jit(solution)/shard_map/jit(_where)/select_n | solution.py:69
  135.0 1.4 fusion.1
  (141 shorter events, 22.1 us)
Async XLA Ops:
  7.2 33.4 %copy-start = (bf16[256,128]{1,0:T(8,128)(2,1)S(1)}, bf16[256,128]{1,0:T(8,128)(2,1)}, u32[]{:S(2)}) copy-start(bf16[256,128]{1,0:T(8,128)(2,1)} %param.14) | copy-start | bytes 196612
  7.2 67.1 %all-gather.2.cloned.1.call-start = ((), (), s32[]{:S(2)}) async-start(), calls=%async_computation | async-start | bytes 2359296 | tf_op jit(solution)/shard_map/all_gather | solution.py:249
  11.0 7.7 %copy-start.13 = (f32[2,32,128]{2,1,0:T(8,128)}, f32[2,32,128]{2,1,0:T(8,128)S(1)}, u32[]{:S(2)}) copy-start(f32[2,32,128]{2,1,0:T(8,128)S(1)} %reduce_window_sum.11) | copy-start | bytes 98308
  11.1 14.5 %collective-permute-start = (f32[2,32]{1,0:T(2,128)S(1)}, f32[2,32]{1,0:T(2,128)S(1)}, u32[]{:S(2)}, u32[]{:S(2)}) collective-permute-start(f32[2,32]{1,0:T(2,128)S(1)} %exp.19), channel_id=1, source_target_pairs={{0,2},{2,0},{4,6},{6,4},{8,10},{10,8},{12,14},{14,12},{1,3},{3,1},... | collective-permute-start | bytes 776 | tf_op jit(solution)/shard_map/ppermute | solution.py:30
  18.8 4.4 %copy-start.15 = (f32[32,256]{1,0:T(8,128)S(1)}, f32[32,256]{1,0:T(8,128)}, u32[]{:S(2)}) copy-start(f32[32,256]{1,0:T(8,128)} %param.10) | copy-start | bytes 98308
  25.5 16.0 %copy-start.5 = (f32[2,128,1024]{2,1,0:T(8,128)}, f32[2,128,1024]{2,1,0:T(8,128)S(1)}, u32[]{:S(2)}) copy-start(f32[2,128,1024]{2,1,0:T(8,128)S(1)} %get-tuple-element.29) | copy-start | bytes 3145732
  25.8 13.7 %collective-permute-start.1 = (bf16[2,128,1024]{2,1,0:T(8,128)(2,1)S(1)}, bf16[2,128,1024]{2,1,0:T(8,128)(2,1)}, u32[]{:S(2)}, u32[]{:S(2)}) collective-permute-start(bf16[2,128,1024]{2,1,0:T(8,128)(2,1)S(1)} %convert_element_type.40), channel_id=1, source_target_pairs={{0,2},{2,0},{4,6},{6,4},{8,10},{10,8},{12,14},{14,12},{1,3},{3,1},... | collective-permute-start | bytes 1572872 | tf_op jit(solution)/shard_map/ppermute | solution.py:57
  26.1 3.8 %collective-permute-start.3 = (f32[2,32]{1,0:T(2,128)S(1)}, f32[2,32]{1,0:T(2,128)S(1)}, u32[]{:S(2)}, u32[]{:S(2)}) collective-permute-start(f32[2,32]{1,0:T(2,128)S(1)} %exponential_multiply_fusion), channel_id=1, source_target_pairs={{0,4},{2,6},{4,0},{6,2},{8,12},{10,14},{12,8},{14,10},{1,5},{3,7},... | collective-permute-start | bytes 776 | tf_op jit(solution)/shard_map/ppermute | solution.py:30
  29.9 4.6 %collective-permute-start.4 = (f32[2,32]{1,0:T(2,128)S(1)}, f32[2,32]{1,0:T(2,128)S(1)}, u32[]{:S(2)}, u32[]{:S(2)}) collective-permute-start(f32[2,32]{1,0:T(2,128)S(1)} %mul.280), channel_id=1, source_target_pairs={{0,8},{2,10},{4,12},{6,14},{8,0},{10,2},{12,4},{14,6},{1,9},{3,11}... | collective-permute-start | bytes 776 | tf_op jit(solution)/shard_map/ppermute | solution.py:30
  33.3 8.7 %copy-start.17 = (f32[2,1024]{1,0:T(2,128)}, f32[2,1024]{1,0:T(2,128)S(1)}, u32[]{:S(2)}) copy-start(f32[2,1024]{1,0:T(2,128)S(1)} %mul.347) | copy-start | bytes 24580
  33.7 8.4 %copy-start.18 = (f32[2,1024]{1,0:T(2,128)}, f32[2,1024]{1,0:T(2,128)S(1)}, u32[]{:S(2)}) copy-start(f32[2,1024]{1,0:T(2,128)S(1)} %mul.318) | copy-start | bytes 24580
  41.5 3.5 %copy-start.21 = (f32[32]{0:T(128)S(1)}, f32[32]{0:T(128)}, u32[]{:S(2)}) copy-start(f32[32]{0:T(128)} %param.12) | copy-start | bytes 388
  41.5 4.2 %copy-start.16 = (bf16[256,128]{1,0:T(8,128)(2,1)S(1)}, bf16[256,128]{1,0:T(8,128)(2,1)}, u32[]{:S(2)}) copy-start(bf16[256,128]{1,0:T(8,128)(2,1)} %param.13) | copy-start | bytes 196612
  41.5 24.1 %collective-permute-start.2 = (bf16[2,128,1024]{2,1,0:T(8,128)(2,1)}, bf16[2,128,1024]{2,1,0:T(8,128)(2,1)}, u32[]{:S(2)}, u32[]{:S(2)}) collective-permute-start(bf16[2,128,1024]{2,1,0:T(8,128)(2,1)} %convert_element_type.42), channel_id=1, source_target_pairs={{0,2},{2,0},{4,6},{6,4},{8,10},{10,8},{12,14},{14,12},{1,3},{3,1},... | collective-permute-start | bytes 1572872 | tf_op jit(solution)/shard_map/ppermute | solution.py:57
  43.1 12.3 %copy-start.14 = (f32[2,32,128]{2,1,0:T(8,128)S(1)}, f32[2,32,128]{2,1,0:T(8,128)}, u32[]{:S(2)}) copy-start(f32[2,32,128]{2,1,0:T(8,128)} %copy-done.13) | copy-start | bytes 98308
  43.1 25.2 %collective-permute-start.5 = (bf16[2,128,1024]{2,1,0:T(8,128)(2,1)S(1)}, bf16[2,128,1024]{2,1,0:T(8,128)(2,1)}, u32[]{:S(2)}, u32[]{:S(2)}) collective-permute-start(bf16[2,128,1024]{2,1,0:T(8,128)(2,1)S(1)} %convert_element_type.44), channel_id=1, source_target_pairs={{0,4},{2,6},{4,0},{6,2},{8,12},{10,14},{12,8},{14,10},{1,5},{3,7},... | collective-permute-start | bytes 1572872 | tf_op jit(solution)/shard_map/ppermute | solution.py:57
  66.8 2.7 %copy-start.6 = (f32[2,128,1024]{2,1,0:T(8,128)S(1)}, f32[2,128,1024]{2,1,0:T(8,128)}, u32[]{:S(2)}) copy-start(f32[2,128,1024]{2,1,0:T(8,128)} %copy-done.5) | copy-start | bytes 3145732
  76.4 19.9 %collective-permute-start.7 = (bf16[2,128,1024]{2,1,0:T(8,128)(2,1)}, bf16[2,128,1024]{2,1,0:T(8,128)(2,1)}, u32[]{:S(2)}, u32[]{:S(2)}) collective-permute-start(bf16[2,128,1024]{2,1,0:T(8,128)(2,1)} %convert_element_type.48), channel_id=1, source_target_pairs={{0,4},{2,6},{4,0},{6,2},{8,12},{10,14},{12,8},{14,10},{1,5},{3,7},... | collective-permute-start | bytes 1572872 | tf_op jit(solution)/shard_map/ppermute | solution.py:57
  78.7 3.3 %copy-start.19 = (f32[2,1024]{1,0:T(2,128)}, f32[2,1024]{1,0:T(2,128)S(1)}, u32[]{:S(2)}) copy-start(f32[2,1024]{1,0:T(2,128)S(1)} %mul.350) | copy-start | bytes 24580
  82.0 37.8 %collective-permute-start.6 = (bf16[2,128,1024]{2,1,0:T(8,128)(2,1)}, bf16[2,128,1024]{2,1,0:T(8,128)(2,1)}, u32[]{:S(2)}, u32[]{:S(2)}) collective-permute-start(bf16[2,128,1024]{2,1,0:T(8,128)(2,1)} %convert_element_type.46), channel_id=1, source_target_pairs={{0,8},{2,10},{4,12},{6,14},{8,0},{10,2},{12,4},{14,6},{1,9},{3,11}... | collective-permute-start | bytes 1572872 | tf_op jit(solution)/shard_map/ppermute | solution.py:57
  94.9 2.6 %copy-start.4 = (f32[2,128,1024]{2,1,0:T(8,128)S(1)}, f32[2,128,1024]{2,1,0:T(8,128)}, u32[]{:S(2)}) copy-start(f32[2,128,1024]{2,1,0:T(8,128)} %add_select_fusion.7) | copy-start | bytes 3145732
  97.8 7.9 %copy-start.11 = (f32[2,128,1024]{2,1,0:T(8,128)}, f32[2,128,1024]{2,1,0:T(8,128)S(1)}, u32[]{:S(2)}) copy-start(f32[2,128,1024]{2,1,0:T(8,128)S(1)} %add_select_fusion.4) | copy-start | bytes 3145732
  98.9 30.5 %collective-permute-start.8 = (bf16[2,128,1024]{2,1,0:T(8,128)(2,1)}, bf16[2,128,1024]{2,1,0:T(8,128)(2,1)}, u32[]{:S(2)}, u32[]{:S(2)}) collective-permute-start(bf16[2,128,1024]{2,1,0:T(8,128)(2,1)} %convert_element_type.50), channel_id=1, source_target_pairs={{0,8},{2,10},{4,12},{6,14},{8,0},{10,2},{12,4},{14,6},{1,9},{3,11}... | collective-permute-start | bytes 1572872 | tf_op jit(solution)/shard_map/ppermute | solution.py:57
  106.6 3.3 %copy-start.20 = (f32[2,1024]{1,0:T(2,128)}, f32[2,1024]{1,0:T(2,128)S(1)}, u32[]{:S(2)}) copy-start(f32[2,1024]{1,0:T(2,128)S(1)} %mul.321) | copy-start | bytes 24580
  121.0 9.6 %copy-start.2 = (f32[2,128,1024]{2,1,0:T(8,128)S(1)}, f32[2,128,1024]{2,1,0:T(8,128)}, u32[]{:S(2)}) copy-start(f32[2,128,1024]{2,1,0:T(8,128)} %copy-done.1) | copy-start | bytes 3145732
  130.6 1.7 %copy-start.12 = (f32[2,128,1024]{2,1,0:T(8,128)S(1)}, f32[2,128,1024]{2,1,0:T(8,128)}, u32[]{:S(2)}) copy-start(f32[2,128,1024]{2,1,0:T(8,128)} %copy-done.11) | copy-start | bytes 3145732
  130.6 1.7 %slice-start = ((f32[2,1024]{1,0:T(2,128)}), f32[1,1024]{1,0:T(1,128)S(1)}, s32[]{:S(2)}) async-start(f32[2,1024]{1,0:T(2,128)} %copy-done.17), calls=%async_computation.1 | async-start | bytes 8192 | tf_op jit(solution)/shard_map/slice | solution.py:84
  130.6 1.7 %slice-start.1 = ((f32[2,1024]{1,0:T(2,128)}), f32[1,1024]{1,0:T(1,128)S(1)}, s32[]{:S(2)}) async-start(f32[2,1024]{1,0:T(2,128)} %copy-done.18), calls=%async_computation.2 | async-start | bytes 8192 | tf_op jit(solution)/shard_map/slice | solution.py:84
  130.6 1.7 %slice-start.2 = ((f32[2,1024]{1,0:T(2,128)}), f32[1,1024]{1,0:T(1,128)S(1)}, s32[]{:S(2)}) async-start(f32[2,1024]{1,0:T(2,128)} %copy-done.19), calls=%async_computation.3 | async-start | bytes 8192 | tf_op jit(solution)/shard_map/slice | solution.py:84
  130.6 1.7 %slice-start.3 = ((f32[2,1024]{1,0:T(2,128)}), f32[1,1024]{1,0:T(1,128)S(1)}, s32[]{:S(2)}) async-start(f32[2,1024]{1,0:T(2,128)} %copy-done.20), calls=%async_computation.4 | async-start | bytes 8192 | tf_op jit(solution)/shard_map/slice | solution.py:84
  132.8 1.6 %copy-start.7 = (f32[2,128,2048]{2,1,0:T(8,128)S(1)}, f32[2,128,2048]{2,1,0:T(8,128)}, u32[]{:S(2)}) copy-start(f32[2,128,2048]{2,1,0:T(8,128)} %shard_map.105) | copy-start | bytes 6291460
  132.8 2.2 %copy-start.8 = (f32[2,128,2048]{2,1,0:T(8,128)S(1)}, f32[2,128,2048]{2,1,0:T(8,128)}, u32[]{:S(2)}) copy-start(f32[2,128,2048]{2,1,0:T(8,128)} %copy.26) | copy-start | bytes 6291460
  (4 other events, 4.9 us)
Sparse Core Ops, SparseCore 0:
  14.3 59.9 all-gather.1

commit v16 on v14

--- a/solution.py
+++ b/solution.py
@@ -245,7 +245,6 @@
     kv_cat = jnp.concatenate(
         [key_rows.reshape(slots, BLOCK, -1), values.reshape(slots, BLOCK, -1)], axis=2
     )
-    kv_cat, x_in, step_size = lax.optimization_barrier((kv_cat, x_in, step_size))
     kv_piece = lax.all_gather(kv_cat, "seq", axis=1, tiled=True)
     rate = -jnp.exp(a_log)
     steps = step_size.reshape(heads, slots, BLOCK).transpose(1, 0, 2)

time: 142 us -> 142 us (level)
  transfers between devices with their start and end apart: 10 -> 10, of which waited for: 8 -> 8; matrix products, arithmetic and copies ran while one was open for 21% -> 22% of each run, Pallas kernels for 19% -> 19%
where the time goes in v16:
time: 142 us; the launch traced here: 141 us
  waiting for transfers between devices  34.5 us (24%)
  Pallas kernels  27.3 us (19%)
  other arithmetic  24.8 us (17%)
  starting transfers between devices  20 us (14%)
  local copies, waits for them, and re-layouts  18.1 us (13%)
  between operations  14.4 us (10%)
  matrix products  2.13 us (2%)
    ppermute x6, waiting for transfers between devices, entering_states(): lax.ppermute(totals[j].astype(jnp.bfloat16), 'seq', pairs)  31 us
    pallas_call x1, Pallas kernels, attention_core(): pl.pallas_call(attention_kernel, out_shape=jax.ShapeDtypeStruct(queries.s...  12 us
    ppermute x6, starting transfers between devices, entering_states(): lax.ppermute(totals[j].astype(jnp.bfloat16), 'seq', pairs)  11.8 us
    pallas_call x1, Pallas kernels, mamba_base(): pl.pallas_call(mamba_base_kernel, out_shape=jax.ShapeDtypeStruct((slots,...  8.85 us
    ppermute x3, starting transfers between devices, decay_scan(): got = lax.ppermute(total, 'seq', [(i, i ^ span) for i in range(count)])  8.19 us
    convert_element_type x6, other arithmetic, entering_states(): lax.ppermute(totals[j].astype(jnp.bfloat16), 'seq', pairs)  6.89 us
    pallas_call x1, Pallas kernels, block_states(): pl.pallas_call(block_state_kernel, out_shape=jax.ShapeDtypeStruct((slots,...  6.53 us
    convert_element_type x6, other arithmetic, entering_states(): totals[j].astype(jnp.bfloat16)  5.13 us
  transfers between devices with their start and end apart: 10, of which 8 were waited for; matrix products, arithmetic and copies ran while one was open for 22% of the time, Pallas kernels for 19%

profile of v16, /device:TPU:0, one launch (start us, length us, event | category | flops | bytes accessed | tf_op | source)
XLA Modules:
  0.0 141.3 jit_solution(17174544752418699886)
XLA Ops:
  9.5 3.0 %collective-permute-start = (f32[2,32]{1,0:T(2,128)S(1)}, f32[2,32]{1,0:T(2,128)S(1)}, u32[]{:S(2)}, u32[]{:S(2)}) collective-permute-start(f32[2,32]{1,0:T(2,128)S(1)} %exp.19), channel_id=1, source_target_pairs={{0,2},{2,0},{4,6},{6,4},{8,10},{10,8},{12,14},{14,12},{1,3},{3,1},... | collective-permute-start | bytes 776 | tf_op jit(solution)/shard_map/ppermute | solution.py:30
  12.5 1.7 %pad_maximum_fusion = bf16[2,128,512]{2,1,0:T(8,128)(2,1)} fusion(bf16[2,128,256]{2,1,0:T(8,128)(2,1)} %bitcast.67, bf16[2,128,256]{2,1,0:T(8,128)(2,1)} %bitcast.68), kind=kLoop, calls=%fused_computation.23 | loop fusion | flops 524288 | bytes 524288 | tf_op jit(solution)/shard_map/concatenate | solution.py:245
  15.1 1.6 %copy.18 = bf16[2,128,128]{1,2,0:T(8,128)(2,1)} copy(bf16[2,128,128]{2,1,0:T(8,128)(2,1)} %bitcast.63) | data formatting | bytes 131072 | tf_op jit(solution)/shard_map/reshape | solution.py:254
  16.8 1.9 %copy.21.f_ref = f32[2,128,2048]{2,1,0:T(8,128)} copy(f32[2,128,2048]{1,2,0:T(8,128)S(1)} %bitcast.60) | data formatting | bytes 4194304 | tf_op jit(solution)/shard_map/reshape | solution.py:20
  18.8 6.5 %shard_map.104 = f32[2,128,2048]{2,1,0:T(8,128)} custom-call(bf16[2,128,128]{2,1,0:T(8,128)(2,1)} %bitcast.65, f32[2,128,2048]{2,1,0:T(8,128)} %copy.21.f_ref, bf16[256,2048]{1,0:T(8,128)(2,1)} %x_ref.2), custom_call_target="tpu_custom_call" | custom-call | flops 134217728 | bytes 5242880 | tf_op jit(solution)/shard_map/pallas_call | solution.py:151
  26.0 1.7 %fusion.11 = (f32[2,128,1024]{2,1,0:T(8,128)S(1)}, f32[2,128,1024]{2,1,0:T(8,128)S(1)}) fusion(f32[2,128,2048]{2,1,0:T(8,128)} %shard_map.104), kind=kLoop, calls=%fused_computation.43 | loop fusion | bytes 4194304 | tf_op jit(solution)/shard_map/slice | solution.py:42
  28.2 2.2 %collective-permute-start.3 = (f32[2,32]{1,0:T(2,128)S(1)}, f32[2,32]{1,0:T(2,128)S(1)}, u32[]{:S(2)}, u32[]{:S(2)}) collective-permute-start(f32[2,32]{1,0:T(2,128)S(1)} %exponential_multiply_fusion), channel_id=1, source_target_pairs={{0,4},{2,6},{4,0},{6,2},{8,12},{10,14},{12,8},{14,10},{1,5},{3,7},... | collective-permute-start | bytes 776 | tf_op jit(solution)/shard_map/ppermute | solution.py:30
  31.9 3.0 %collective-permute-start.4 = (f32[2,32]{1,0:T(2,128)S(1)}, f32[2,32]{1,0:T(2,128)S(1)}, u32[]{:S(2)}, u32[]{:S(2)}) collective-permute-start(f32[2,32]{1,0:T(2,128)S(1)} %mul.280), channel_id=1, source_target_pairs={{0,8},{2,10},{4,12},{6,14},{8,0},{10,2},{12,4},{14,6},{1,9},{3,11}... | collective-permute-start | bytes 776 | tf_op jit(solution)/shard_map/ppermute | solution.py:30
  36.7 4.8 %collective-permute-done.1 = bf16[2,128,1024]{2,1,0:T(8,128)(2,1)} collective-permute-done((bf16[2,128,1024]{2,1,0:T(8,128)(2,1)S(1)}, bf16[2,128,1024]{2,1,0:T(8,128)(2,1)}, u32[]{:S(2)}, u32[]{:S(2)}) %collective-permute-start.1) | collective-permute-done | bytes 524320 | tf_op jit(solution)/shard_map/ppermute | solution.py:57
  41.5 1.2 convert_element_type.41
  45.1 1.9 %collective-permute-start.5 = (bf16[2,128,1024]{2,1,0:T(8,128)(2,1)S(1)}, bf16[2,128,1024]{2,1,0:T(8,128)(2,1)}, u32[]{:S(2)}, u32[]{:S(2)}) collective-permute-start(bf16[2,128,1024]{2,1,0:T(8,128)(2,1)S(1)} %convert_element_type.44), channel_id=1, source_target_pairs={{0,4},{2,6},{4,0},{6,2},{8,12},{10,14},{12,8},{14,10},{1,5},{3,7},... | collective-permute-start | bytes 1572872 | tf_op jit(solution)/shard_map/ppermute | solution.py:57
  48.6 8.9 %shard_map.105 = f32[2,128,2048]{2,1,0:T(8,128)} custom-call(bf16[256,2048]{1,0:T(8,128)(2,1)} %x_ref.2, f32[2,128,128]{2,1,0:T(8,128)} %fusion.20.inner_ref, f32[2,32,1,128]{3,2,1,0:T(1,128)} %bitcast.62, f32[2,32,1,128]{3,2,1,0:T(1,128)} %bitcast.66, f32[1,2048]{1,0:T(1,128)} %broadcast_in_dim_reshape.2.skip_ref), custom_call_target="tpu_custom_call" | custom-call | flops 140509184 | bytes 3145728 | tf_op jit(solution)/shard_map/pallas_call | solution.py:119
  57.5 8.8 %collective-permute-done.2 = bf16[2,128,1024]{2,1,0:T(8,128)(2,1)} collective-permute-done((bf16[2,128,1024]{2,1,0:T(8,128)(2,1)}, bf16[2,128,1024]{2,1,0:T(8,128)(2,1)}, u32[]{:S(2)}, u32[]{:S(2)}) %collective-permute-start.2) | collective-permute-done | bytes 524320 | tf_op jit(solution)/shard_map/ppermute | solution.py:57
  66.3 1.1 convert_element_type.43
  67.4 1.5 %broadcast_in_dim.87 = f32[2,128,32,64]{1,3,2,0:T(8,128)} broadcast(f32[2,128,32]{1,2,0:T(8,128)S(1)} %exponential_bitcast_fusion), dimensions={0,1,2} | broadcast | bytes 2129920 | tf_op jit(solution)/shard_map/broadcast_in_dim | solution.py:20
  68.9 1.1 convert_element_type.45
  70.1 1.2 add_select_fusion.7
  71.3 1.7 %all-gather.2.cloned.1.call-done.k_ref.v_ref = bf16[2,1024,512]{2,1,0:T(8,128)(2,1)} async-done(((bf16[2,128,512]{2,1,0:T(8,128)(2,1)}), bf16[2,1024,512]{2,1,0:T(8,128)(2,1)}) %all-gather.2.cloned.1.call-update) | async-done | bytes 2097168 | tf_op jit(solution)/shard_map/all_gather | solution.py:248
  73.0 2.1 %convert_element_type.48 = bf16[2,128,1024]{2,1,0:T(8,128)(2,1)} convert(f32[2,128,1024]{2,1,0:T(8,128)} %add_select_fusion.7) | non-fusion elementwise | flops 262144 | bytes 1572864 | tf_op jit(solution)/shard_map/convert_element_type | solution.py:57
  75.2 1.5 %collective-permute-start.7 = (bf16[2,128,1024]{2,1,0:T(8,128)(2,1)}, bf16[2,128,1024]{2,1,0:T(8,128)(2,1)}, u32[]{:S(2)}, u32[]{:S(2)}) collective-permute-start(bf16[2,128,1024]{2,1,0:T(8,128)(2,1)} %convert_element_type.48), channel_id=1, source_target_pairs={{0,4},{2,6},{4,0},{6,2},{8,12},{10,14},{12,8},{14,10},{1,5},{3,7},... | collective-permute-start | bytes 1572872 | tf_op jit(solution)/shard_map/ppermute | solution.py:57
  77.3 1.5 %add_select_fusion.5 = f32[2,128,1024]{2,1,0:T(8,128)S(1)} fusion(f32[2,128,1024]{2,1,0:T(8,128)S(1)} %convert_element_type.45, f32[2,128,1024]{2,1,0:T(8,128)} %copy-done.3, f32[2,1024]{1,0:T(2,128)S(1)} %mul.304, f32[2,1024]{1,0:T(2,128)S(1)} %mul.289, pred[]{:T(512)S(6)} %eq.15), kind=kLoop, calls=%fused_computation.16 | loop fusion | flops 1310720 | bytes 3162113 | tf_op jit(solution)/shard_map/jit(_where)/select_n | solution.py:70
  81.8 12.0 %shard_map.106 = bf16[256,1024]{1,0:T(8,128)(2,1)} custom-call(bf16[256,1024]{1,0:T(8,128)(2,1)} %q_ref, bf16[2,1024,512]{2,1,0:T(8,128)(2,1)} %all-gather.2.cloned.1.call-done.k_ref.v_ref, bf16[2,1024,512]{2,1,0:T(8,128)(2,1)} %all-gather.2.cloned.1.call-done.k_ref.v_ref), custom_call_target="tpu_custom_call" | custom-call | flops 2147483648 | bytes 3145728 | tf_op jit(solution)/shard_map/pallas_call | solution.py:225
  94.8 1.1 convert_element_type.49
  97.4 7.0 %collective-permute-start.8 = (bf16[2,128,1024]{2,1,0:T(8,128)(2,1)}, bf16[2,128,1024]{2,1,0:T(8,128)(2,1)}, u32[]{:S(2)}, u32[]{:S(2)}) collective-permute-start(bf16[2,128,1024]{2,1,0:T(8,128)(2,1)} %convert_element_type.50), channel_id=1, source_target_pairs={{0,8},{2,10},{4,12},{6,14},{8,0},{10,2},{12,4},{14,6},{1,9},{3,11}... | collective-permute-start | bytes 1572872 | tf_op jit(solution)/shard_map/ppermute | solution.py:57
  105.6 2.9 %copy.26 = f32[2,128,2048]{2,1,0:T(8,128)} copy(f32[2,128,2048]{1,2,0:T(8,128)} %bitcast.59) | data formatting | bytes 4194304 | tf_op jit(solution)/shard_map/optimization_barrier | solution.py:60
  108.5 9.3 %collective-permute-done.6 = bf16[2,128,1024]{2,1,0:T(8,128)(2,1)} collective-permute-done((bf16[2,128,1024]{2,1,0:T(8,128)(2,1)}, bf16[2,128,1024]{2,1,0:T(8,128)(2,1)}, u32[]{:S(2)}, u32[]{:S(2)}) %collective-permute-start.6) | collective-permute-done | bytes 524320 | tf_op jit(solution)/shard_map/ppermute | solution.py:57
  117.9 1.1 convert_element_type.47
  119.0 1.4 %add_select_fusion.2 = f32[2,128,1024]{2,1,0:T(8,128)S(1)} fusion(f32[2,128,1024]{2,1,0:T(8,128)S(1)} %convert_element_type.41, f32[2,128,1024]{2,1,0:T(8,128)S(1)} %convert_element_type.45, f32[2,1024]{1,0:T(2,128)S(1)} %mul.308, f32[2,1024]{1,0:T(2,128)S(1)} %mul.287, pred[]{:T(512)S(6)} %eq.13, pred[]{:T(512)S(6)} %eq.15, pred[]{:T(512)S(6)} %eq.14, ...), kind=kLoop, calls=%fused_computation.5 | loop fusion | flops 2097152 | bytes 3686403 | tf_op jit(solution)/shard_map/jit(_where)/select_n | solution.py:69
  120.5 7.0 %collective-permute-done.8 = bf16[2,128,1024]{2,1,0:T(8,128)(2,1)} collective-permute-done((bf16[2,128,1024]{2,1,0:T(8,128)(2,1)}, bf16[2,128,1024]{2,1,0:T(8,128)(2,1)}, u32[]{:S(2)}, u32[]{:S(2)}) %collective-permute-start.8) | collective-permute-done | bytes 524320 | tf_op jit(solution)/shard_map/ppermute | solution.py:57
  127.5 1.1 convert_element_type.51
  128.7 1.5 %add_select_fusion = f32[2,128,1024]{2,1,0:T(8,128)S(1)} fusion(f32[2,128,1024]{2,1,0:T(8,128)S(1)} %convert_element_type.43, f32[2,128,1024]{2,1,0:T(8,128)S(1)} %copy-done.2, f32[2,1024]{1,0:T(2,128)S(1)} %mul.338, f32[2,1024]{1,0:T(2,128)S(1)} %mul.329, pred[]{:T(512)S(6)} %eq.13, pred[]{:T(512)S(6)} %eq.15, pred[]{:T(512)S(6)} %eq.14, ...), kind=kLoop, calls=%fused_computation.3 | loop fusion | flops 2097152 | bytes 3686403 | tf_op jit(solution)/shard_map/jit(_where)/select_n | solution.py:69
  133.1 1.4 fusion.1
  (141 shorter events, 22.2 us)
Async XLA Ops:
  7.2 35.5 %copy-start = (bf16[256,128]{1,0:T(8,128)(2,1)S(1)}, bf16[256,128]{1,0:T(8,128)(2,1)}, u32[]{:S(2)}) copy-start(bf16[256,128]{1,0:T(8,128)(2,1)} %param.14) | copy-start | bytes 196612
  7.2 65.8 %all-gather.2.cloned.1.call-start = ((), (), s32[]{:S(2)}) async-start(), calls=%async_computation | async-start | bytes 2359296 | tf_op jit(solution)/shard_map/all_gather | solution.py:248
  9.3 9.4 %copy-start.13 = (f32[2,32,128]{2,1,0:T(8,128)}, f32[2,32,128]{2,1,0:T(8,128)S(1)}, u32[]{:S(2)}) copy-start(f32[2,32,128]{2,1,0:T(8,128)S(1)} %reduce_window_sum.11) | copy-start | bytes 98308
  9.5 18.4 %collective-permute-start = (f32[2,32]{1,0:T(2,128)S(1)}, f32[2,32]{1,0:T(2,128)S(1)}, u32[]{:S(2)}, u32[]{:S(2)}) collective-permute-start(f32[2,32]{1,0:T(2,128)S(1)} %exp.19), channel_id=1, source_target_pairs={{0,2},{2,0},{4,6},{6,4},{8,10},{10,8},{12,14},{14,12},{1,3},{3,1},... | collective-permute-start | bytes 776 | tf_op jit(solution)/shard_map/ppermute | solution.py:30
  18.8 6.5 %copy-start.15 = (f32[32,256]{1,0:T(8,128)S(1)}, f32[32,256]{1,0:T(8,128)}, u32[]{:S(2)}) copy-start(f32[32,256]{1,0:T(8,128)} %param.10) | copy-start | bytes 98308
  27.6 15.9 %copy-start.5 = (f32[2,128,1024]{2,1,0:T(8,128)}, f32[2,128,1024]{2,1,0:T(8,128)S(1)}, u32[]{:S(2)}) copy-start(f32[2,128,1024]{2,1,0:T(8,128)S(1)} %get-tuple-element.24) | copy-start | bytes 3145732
  27.9 13.6 %collective-permute-start.1 = (bf16[2,128,1024]{2,1,0:T(8,128)(2,1)S(1)}, bf16[2,128,1024]{2,1,0:T(8,128)(2,1)}, u32[]{:S(2)}, u32[]{:S(2)}) collective-permute-start(bf16[2,128,1024]{2,1,0:T(8,128)(2,1)S(1)} %convert_element_type.40), channel_id=1, source_target_pairs={{0,2},{2,0},{4,6},{6,4},{8,10},{10,8},{12,14},{14,12},{1,3},{3,1},... | collective-permute-start | bytes 1572872 | tf_op jit(solution)/shard_map/ppermute | solution.py:57
  28.2 3.7 %collective-permute-start.3 = (f32[2,32]{1,0:T(2,128)S(1)}, f32[2,32]{1,0:T(2,128)S(1)}, u32[]{:S(2)}, u32[]{:S(2)}) collective-permute-start(f32[2,32]{1,0:T(2,128)S(1)} %exponential_multiply_fusion), channel_id=1, source_target_pairs={{0,4},{2,6},{4,0},{6,2},{8,12},{10,14},{12,8},{14,10},{1,5},{3,7},... | collective-permute-start | bytes 776 | tf_op jit(solution)/shard_map/ppermute | solution.py:30
  31.9 4.6 %collective-permute-start.4 = (f32[2,32]{1,0:T(2,128)S(1)}, f32[2,32]{1,0:T(2,128)S(1)}, u32[]{:S(2)}, u32[]{:S(2)}) collective-permute-start(f32[2,32]{1,0:T(2,128)S(1)} %mul.280), channel_id=1, source_target_pairs={{0,8},{2,10},{4,12},{6,14},{8,0},{10,2},{12,4},{14,6},{1,9},{3,11}... | collective-permute-start | bytes 776 | tf_op jit(solution)/shard_map/ppermute | solution.py:30
  35.4 8.6 %copy-start.17 = (f32[2,1024]{1,0:T(2,128)}, f32[2,1024]{1,0:T(2,128)S(1)}, u32[]{:S(2)}) copy-start(f32[2,1024]{1,0:T(2,128)S(1)} %mul.347) | copy-start | bytes 24580
  35.7 8.3 %copy-start.18 = (f32[2,1024]{1,0:T(2,128)}, f32[2,1024]{1,0:T(2,128)S(1)}, u32[]{:S(2)}) copy-start(f32[2,1024]{1,0:T(2,128)S(1)} %mul.318) | copy-start | bytes 24580
  43.5 3.5 %copy-start.21 = (f32[32]{0:T(128)S(1)}, f32[32]{0:T(128)}, u32[]{:S(2)}) copy-start(f32[32]{0:T(128)} %param.12) | copy-start | bytes 388
  43.5 4.3 %copy-start.16 = (bf16[256,128]{1,0:T(8,128)(2,1)S(1)}, bf16[256,128]{1,0:T(8,128)(2,1)}, u32[]{:S(2)}) copy-start(bf16[256,128]{1,0:T(8,128)(2,1)} %param.13) | copy-start | bytes 196612
  43.5 22.7 %collective-permute-start.2 = (bf16[2,128,1024]{2,1,0:T(8,128)(2,1)}, bf16[2,128,1024]{2,1,0:T(8,128)(2,1)}, u32[]{:S(2)}, u32[]{:S(2)}) collective-permute-start(bf16[2,128,1024]{2,1,0:T(8,128)(2,1)} %convert_element_type.42), channel_id=1, source_target_pairs={{0,2},{2,0},{4,6},{6,4},{8,10},{10,8},{12,14},{14,12},{1,3},{3,1},... | collective-permute-start | bytes 1572872 | tf_op jit(solution)/shard_map/ppermute | solution.py:57
  45.1 12.4 %copy-start.14 = (f32[2,32,128]{2,1,0:T(8,128)S(1)}, f32[2,32,128]{2,1,0:T(8,128)}, u32[]{:S(2)}) copy-start(f32[2,32,128]{2,1,0:T(8,128)} %copy-done.13) | copy-start | bytes 98308
  45.1 23.8 %collective-permute-start.5 = (bf16[2,128,1024]{2,1,0:T(8,128)(2,1)S(1)}, bf16[2,128,1024]{2,1,0:T(8,128)(2,1)}, u32[]{:S(2)}, u32[]{:S(2)}) collective-permute-start(bf16[2,128,1024]{2,1,0:T(8,128)(2,1)S(1)} %convert_element_type.44), channel_id=1, source_target_pairs={{0,4},{2,6},{4,0},{6,2},{8,12},{10,14},{12,8},{14,10},{1,5},{3,7},... | collective-permute-start | bytes 1572872 | tf_op jit(solution)/shard_map/ppermute | solution.py:57
  67.4 2.7 %copy-start.6 = (f32[2,128,1024]{2,1,0:T(8,128)S(1)}, f32[2,128,1024]{2,1,0:T(8,128)}, u32[]{:S(2)}) copy-start(f32[2,128,1024]{2,1,0:T(8,128)} %copy-done.5) | copy-start | bytes 3145732
  75.2 19.7 %collective-permute-start.7 = (bf16[2,128,1024]{2,1,0:T(8,128)(2,1)}, bf16[2,128,1024]{2,1,0:T(8,128)(2,1)}, u32[]{:S(2)}, u32[]{:S(2)}) collective-permute-start(bf16[2,128,1024]{2,1,0:T(8,128)(2,1)} %convert_element_type.48), channel_id=1, source_target_pairs={{0,4},{2,6},{4,0},{6,2},{8,12},{10,14},{12,8},{14,10},{1,5},{3,7},... | collective-permute-start | bytes 1572872 | tf_op jit(solution)/shard_map/ppermute | solution.py:57
  77.3 3.3 %copy-start.19 = (f32[2,1024]{1,0:T(2,128)}, f32[2,1024]{1,0:T(2,128)S(1)}, u32[]{:S(2)}) copy-start(f32[2,1024]{1,0:T(2,128)S(1)} %mul.350) | copy-start | bytes 24580
  80.6 37.2 %collective-permute-start.6 = (bf16[2,128,1024]{2,1,0:T(8,128)(2,1)}, bf16[2,128,1024]{2,1,0:T(8,128)(2,1)}, u32[]{:S(2)}, u32[]{:S(2)}) collective-permute-start(bf16[2,128,1024]{2,1,0:T(8,128)(2,1)} %convert_element_type.46), channel_id=1, source_target_pairs={{0,8},{2,10},{4,12},{6,14},{8,0},{10,2},{12,4},{14,6},{1,9},{3,11}... | collective-permute-start | bytes 1572872 | tf_op jit(solution)/shard_map/ppermute | solution.py:57
  93.8 2.2 %copy-start.4 = (f32[2,128,1024]{2,1,0:T(8,128)S(1)}, f32[2,128,1024]{2,1,0:T(8,128)}, u32[]{:S(2)}) copy-start(f32[2,128,1024]{2,1,0:T(8,128)} %add_select_fusion.7) | copy-start | bytes 3145732
  96.3 8.1 %copy-start.11 = (f32[2,128,1024]{2,1,0:T(8,128)}, f32[2,128,1024]{2,1,0:T(8,128)S(1)}, u32[]{:S(2)}) copy-start(f32[2,128,1024]{2,1,0:T(8,128)S(1)} %add_select_fusion.4) | copy-start | bytes 3145732
  97.4 30.0 %collective-permute-start.8 = (bf16[2,128,1024]{2,1,0:T(8,128)(2,1)}, bf16[2,128,1024]{2,1,0:T(8,128)(2,1)}, u32[]{:S(2)}, u32[]{:S(2)}) collective-permute-start(bf16[2,128,1024]{2,1,0:T(8,128)(2,1)} %convert_element_type.50), channel_id=1, source_target_pairs={{0,8},{2,10},{4,12},{6,14},{8,0},{10,2},{12,4},{14,6},{1,9},{3,11}... | collective-permute-start | bytes 1572872 | tf_op jit(solution)/shard_map/ppermute | solution.py:57
  105.2 3.3 %copy-start.20 = (f32[2,1024]{1,0:T(2,128)}, f32[2,1024]{1,0:T(2,128)S(1)}, u32[]{:S(2)}) copy-start(f32[2,1024]{1,0:T(2,128)S(1)} %mul.321) | copy-start | bytes 24580
  119.0 9.6 %copy-start.2 = (f32[2,128,1024]{2,1,0:T(8,128)S(1)}, f32[2,128,1024]{2,1,0:T(8,128)}, u32[]{:S(2)}) copy-start(f32[2,128,1024]{2,1,0:T(8,128)} %copy-done.1) | copy-start | bytes 3145732
  128.6 1.7 %copy-start.12 = (f32[2,128,1024]{2,1,0:T(8,128)S(1)}, f32[2,128,1024]{2,1,0:T(8,128)}, u32[]{:S(2)}) copy-start(f32[2,128,1024]{2,1,0:T(8,128)} %copy-done.11) | copy-start | bytes 3145732
  128.6 1.7 %slice-start = ((f32[2,1024]{1,0:T(2,128)}), f32[1,1024]{1,0:T(1,128)S(1)}, s32[]{:S(2)}) async-start(f32[2,1024]{1,0:T(2,128)} %copy-done.17), calls=%async_computation.1 | async-start | bytes 8192 | tf_op jit(solution)/shard_map/slice | solution.py:84
  128.6 1.7 %slice-start.1 = ((f32[2,1024]{1,0:T(2,128)}), f32[1,1024]{1,0:T(1,128)S(1)}, s32[]{:S(2)}) async-start(f32[2,1024]{1,0:T(2,128)} %copy-done.18), calls=%async_computation.2 | async-start | bytes 8192 | tf_op jit(solution)/shard_map/slice | solution.py:84
  128.7 1.7 %slice-start.2 = ((f32[2,1024]{1,0:T(2,128)}), f32[1,1024]{1,0:T(1,128)S(1)}, s32[]{:S(2)}) async-start(f32[2,1024]{1,0:T(2,128)} %copy-done.19), calls=%async_computation.3 | async-start | bytes 8192 | tf_op jit(solution)/shard_map/slice | solution.py:84
  128.7 1.7 %slice-start.3 = ((f32[2,1024]{1,0:T(2,128)}), f32[1,1024]{1,0:T(1,128)S(1)}, s32[]{:S(2)}) async-start(f32[2,1024]{1,0:T(2,128)} %copy-done.20), calls=%async_computation.4 | async-start | bytes 8192 | tf_op jit(solution)/shard_map/slice | solution.py:84
  130.8 1.6 %copy-start.7 = (f32[2,128,2048]{2,1,0:T(8,128)S(1)}, f32[2,128,2048]{2,1,0:T(8,128)}, u32[]{:S(2)}) copy-start(f32[2,128,2048]{2,1,0:T(8,128)} %shard_map.105) | copy-start | bytes 6291460
  130.8 2.2 %copy-start.8 = (f32[2,128,2048]{2,1,0:T(8,128)S(1)}, f32[2,128,2048]{2,1,0:T(8,128)}, u32[]{:S(2)}) copy-start(f32[2,128,2048]{2,1,0:T(8,128)} %copy.26) | copy-start | bytes 6291460
  (4 other events, 4.9 us)
Sparse Core Ops, SparseCore 0:
  14.3 58.6 all-gather.1

commit v17 on v16

--- a/solution.py
+++ b/solution.py
@@ -162,7 +162,7 @@
     )(b_t, spread_factor, x_in)
 
 
-KEY_CHUNK = 256
+KEY_CHUNK = 512
 
 
 def attention_kernel(q_ref, k_ref, v_ref, o_ref):

time: 142 us -> 142 us (level)
  waiting for transfers between devices: 34.5 us -> 38.8 us
  starting transfers between devices: 20 us -> 16.8 us
    ppermute x6, waiting for transfers between devices: 31 us -> 35.3 us  [entering_states(): lax.ppermute(totals[j].astype(jnp.bfloat16), 'seq', pairs)]
    ppermute x6, starting transfers between devices: 11.8 us -> 8.59 us  [entering_states(): lax.ppermute(totals[j].astype(jnp.bfloat16), 'seq', pairs)]
where the time goes in v17:
time: 142 us; the launch traced here: 141 us
  waiting for transfers between devices  38.8 us (27%)
  Pallas kernels  26.2 us (18%)
  other arithmetic  24.8 us (17%)
  local copies, waits for them, and re-layouts  18.1 us (13%)
  starting transfers between devices  16.8 us (12%)
  between operations  14.4 us (10%)
  matrix products  2.13 us (2%)
    ppermute x6, waiting for transfers between devices, entering_states(): lax.ppermute(totals[j].astype(jnp.bfloat16), 'seq', pairs)  35.3 us
    pallas_call x1, Pallas kernels, attention_core(): pl.pallas_call(attention_kernel, out_shape=jax.ShapeDtypeStruct(queries.s...  10.9 us
    pallas_call x1, Pallas kernels, mamba_base(): pl.pallas_call(mamba_base_kernel, out_shape=jax.ShapeDtypeStruct((slots,...  8.85 us
    ppermute x6, starting transfers between devices, entering_states(): lax.ppermute(totals[j].astype(jnp.bfloat16), 'seq', pairs)  8.59 us
    ppermute x3, starting transfers between devices, decay_scan(): got = lax.ppermute(total, 'seq', [(i, i ^ span) for i in range(count)])  8.19 us
    convert_element_type x6, other arithmetic, entering_states(): lax.ppermute(totals[j].astype(jnp.bfloat16), 'seq', pairs)  6.89 us
    pallas_call x1, Pallas kernels, block_states(): pl.pallas_call(block_state_kernel, out_shape=jax.ShapeDtypeStruct((slots,...  6.53 us
    convert_element_type x6, other arithmetic, entering_states(): totals[j].astype(jnp.bfloat16)  5.13 us
  transfers between devices with their start and end apart: 10, of which 8 were waited for; matrix products, arithmetic and copies ran while one was open for 22% of the time, Pallas kernels for 19%

profile of v17, /device:TPU:0, one launch (start us, length us, event | category | flops | bytes accessed | tf_op | source)
XLA Modules:
  0.0 141.3 jit_solution(977323585117420065)
XLA Ops:
  9.5 3.0 %collective-permute-start = (f32[2,32]{1,0:T(2,128)S(1)}, f32[2,32]{1,0:T(2,128)S(1)}, u32[]{:S(2)}, u32[]{:S(2)}) collective-permute-start(f32[2,32]{1,0:T(2,128)S(1)} %exp.19), channel_id=1, source_target_pairs={{0,2},{2,0},{4,6},{6,4},{8,10},{10,8},{12,14},{14,12},{1,3},{3,1},... | collective-permute-start | bytes 776 | tf_op jit(solution)/shard_map/ppermute | solution.py:30
  12.5 1.7 %pad_maximum_fusion = bf16[2,128,512]{2,1,0:T(8,128)(2,1)} fusion(bf16[2,128,256]{2,1,0:T(8,128)(2,1)} %bitcast.67, bf16[2,128,256]{2,1,0:T(8,128)(2,1)} %bitcast.68), kind=kLoop, calls=%fused_computation.23 | loop fusion | flops 524288 | bytes 524288 | tf_op jit(solution)/shard_map/concatenate | solution.py:245
  15.1 1.6 %copy.18 = bf16[2,128,128]{1,2,0:T(8,128)(2,1)} copy(bf16[2,128,128]{2,1,0:T(8,128)(2,1)} %bitcast.63) | data formatting | bytes 131072 | tf_op jit(solution)/shard_map/reshape | solution.py:254
  16.8 1.9 %copy.21.f_ref = f32[2,128,2048]{2,1,0:T(8,128)} copy(f32[2,128,2048]{1,2,0:T(8,128)S(1)} %bitcast.60) | data formatting | bytes 4194304 | tf_op jit(solution)/shard_map/reshape | solution.py:20
  18.8 6.5 %shard_map.104 = f32[2,128,2048]{2,1,0:T(8,128)} custom-call(bf16[2,128,128]{2,1,0:T(8,128)(2,1)} %bitcast.65, f32[2,128,2048]{2,1,0:T(8,128)} %copy.21.f_ref, bf16[256,2048]{1,0:T(8,128)(2,1)} %x_ref.2), custom_call_target="tpu_custom_call" | custom-call | flops 134217728 | bytes 5242880 | tf_op jit(solution)/shard_map/pallas_call | solution.py:151
  26.0 1.7 %fusion.11 = (f32[2,128,1024]{2,1,0:T(8,128)S(1)}, f32[2,128,1024]{2,1,0:T(8,128)S(1)}) fusion(f32[2,128,2048]{2,1,0:T(8,128)} %shard_map.104), kind=kLoop, calls=%fused_computation.43 | loop fusion | bytes 4194304 | tf_op jit(solution)/shard_map/slice | solution.py:42
  28.2 2.2 %collective-permute-start.3 = (f32[2,32]{1,0:T(2,128)S(1)}, f32[2,32]{1,0:T(2,128)S(1)}, u32[]{:S(2)}, u32[]{:S(2)}) collective-permute-start(f32[2,32]{1,0:T(2,128)S(1)} %exponential_multiply_fusion), channel_id=1, source_target_pairs={{0,4},{2,6},{4,0},{6,2},{8,12},{10,14},{12,8},{14,10},{1,5},{3,7},... | collective-permute-start | bytes 776 | tf_op jit(solution)/shard_map/ppermute | solution.py:30
  31.9 3.0 %collective-permute-start.4 = (f32[2,32]{1,0:T(2,128)S(1)}, f32[2,32]{1,0:T(2,128)S(1)}, u32[]{:S(2)}, u32[]{:S(2)}) collective-permute-start(f32[2,32]{1,0:T(2,128)S(1)} %mul.280), channel_id=1, source_target_pairs={{0,8},{2,10},{4,12},{6,14},{8,0},{10,2},{12,4},{14,6},{1,9},{3,11}... | collective-permute-start | bytes 776 | tf_op jit(solution)/shard_map/ppermute | solution.py:30
  36.7 4.8 %collective-permute-done.1 = bf16[2,128,1024]{2,1,0:T(8,128)(2,1)} collective-permute-done((bf16[2,128,1024]{2,1,0:T(8,128)(2,1)S(1)}, bf16[2,128,1024]{2,1,0:T(8,128)(2,1)}, u32[]{:S(2)}, u32[]{:S(2)}) %collective-permute-start.1) | collective-permute-done | bytes 524320 | tf_op jit(solution)/shard_map/ppermute | solution.py:57
  41.5 1.2 convert_element_type.41
  45.1 1.9 %collective-permute-start.5 = (bf16[2,128,1024]{2,1,0:T(8,128)(2,1)S(1)}, bf16[2,128,1024]{2,1,0:T(8,128)(2,1)}, u32[]{:S(2)}, u32[]{:S(2)}) collective-permute-start(bf16[2,128,1024]{2,1,0:T(8,128)(2,1)S(1)} %convert_element_type.44), channel_id=1, source_target_pairs={{0,4},{2,6},{4,0},{6,2},{8,12},{10,14},{12,8},{14,10},{1,5},{3,7},... | collective-permute-start | bytes 1572872 | tf_op jit(solution)/shard_map/ppermute | solution.py:57
  48.6 8.9 %shard_map.105 = f32[2,128,2048]{2,1,0:T(8,128)} custom-call(bf16[256,2048]{1,0:T(8,128)(2,1)} %x_ref.2, f32[2,128,128]{2,1,0:T(8,128)} %fusion.20.inner_ref, f32[2,32,1,128]{3,2,1,0:T(1,128)} %bitcast.62, f32[2,32,1,128]{3,2,1,0:T(1,128)} %bitcast.66, f32[1,2048]{1,0:T(1,128)} %broadcast_in_dim_reshape.2.skip_ref), custom_call_target="tpu_custom_call" | custom-call | flops 140509184 | bytes 3145728 | tf_op jit(solution)/shard_map/pallas_call | solution.py:119
  57.5 8.8 %collective-permute-done.2 = bf16[2,128,1024]{2,1,0:T(8,128)(2,1)} collective-permute-done((bf16[2,128,1024]{2,1,0:T(8,128)(2,1)}, bf16[2,128,1024]{2,1,0:T(8,128)(2,1)}, u32[]{:S(2)}, u32[]{:S(2)}) %collective-permute-start.2) | collective-permute-done | bytes 524320 | tf_op jit(solution)/shard_map/ppermute | solution.py:57
  66.3 1.1 convert_element_type.43
  67.4 1.5 %broadcast_in_dim.87 = f32[2,128,32,64]{1,3,2,0:T(8,128)} broadcast(f32[2,128,32]{1,2,0:T(8,128)S(1)} %exponential_bitcast_fusion), dimensions={0,1,2} | broadcast | bytes 2129920 | tf_op jit(solution)/shard_map/broadcast_in_dim | solution.py:20
  68.9 1.1 convert_element_type.45
  70.1 1.2 add_select_fusion.7
  71.3 1.7 %all-gather.2.cloned.1.call-done.k_ref.v_ref = bf16[2,1024,512]{2,1,0:T(8,128)(2,1)} async-done(((bf16[2,128,512]{2,1,0:T(8,128)(2,1)}), bf16[2,1024,512]{2,1,0:T(8,128)(2,1)}) %all-gather.2.cloned.1.call-update) | async-done | bytes 2097168 | tf_op jit(solution)/shard_map/all_gather | solution.py:248
  73.0 2.1 %convert_element_type.48 = bf16[2,128,1024]{2,1,0:T(8,128)(2,1)} convert(f32[2,128,1024]{2,1,0:T(8,128)} %add_select_fusion.7) | non-fusion elementwise | flops 262144 | bytes 1572864 | tf_op jit(solution)/shard_map/convert_element_type | solution.py:57
  75.2 1.5 %collective-permute-start.7 = (bf16[2,128,1024]{2,1,0:T(8,128)(2,1)}, bf16[2,128,1024]{2,1,0:T(8,128)(2,1)}, u32[]{:S(2)}, u32[]{:S(2)}) collective-permute-start(bf16[2,128,1024]{2,1,0:T(8,128)(2,1)} %convert_element_type.48), channel_id=1, source_target_pairs={{0,4},{2,6},{4,0},{6,2},{8,12},{10,14},{12,8},{14,10},{1,5},{3,7},... | collective-permute-start | bytes 1572872 | tf_op jit(solution)/shard_map/ppermute | solution.py:57
  77.3 1.5 %add_select_fusion.5 = f32[2,128,1024]{2,1,0:T(8,128)S(1)} fusion(f32[2,128,1024]{2,1,0:T(8,128)S(1)} %convert_element_type.45, f32[2,128,1024]{2,1,0:T(8,128)} %copy-done.3, f32[2,1024]{1,0:T(2,128)S(1)} %mul.304, f32[2,1024]{1,0:T(2,128)S(1)} %mul.289, pred[]{:T(512)S(6)} %eq.15), kind=kLoop, calls=%fused_computation.16 | loop fusion | flops 1310720 | bytes 3162113 | tf_op jit(solution)/shard_map/jit(_where)/select_n | solution.py:70
  81.8 10.9 %shard_map.106 = bf16[256,1024]{1,0:T(8,128)(2,1)} custom-call(bf16[256,1024]{1,0:T(8,128)(2,1)} %q_ref, bf16[2,1024,512]{2,1,0:T(8,128)(2,1)} %all-gather.2.cloned.1.call-done.k_ref.v_ref, bf16[2,1024,512]{2,1,0:T(8,128)(2,1)} %all-gather.2.cloned.1.call-done.k_ref.v_ref), custom_call_target="tpu_custom_call" | custom-call | flops 2147483648 | bytes 3145728 | tf_op jit(solution)/shard_map/pallas_call | solution.py:225
  92.6 2.2 %collective-permute-done.7 = bf16[2,128,1024]{2,1,0:T(8,128)(2,1)} collective-permute-done((bf16[2,128,1024]{2,1,0:T(8,128)(2,1)}, bf16[2,128,1024]{2,1,0:T(8,128)(2,1)}, u32[]{:S(2)}, u32[]{:S(2)}) %collective-permute-start.7) | collective-permute-done | bytes 524320 | tf_op jit(solution)/shard_map/ppermute | solution.py:57
  94.8 1.1 convert_element_type.49
  97.4 3.7 %collective-permute-start.8 = (bf16[2,128,1024]{2,1,0:T(8,128)(2,1)}, bf16[2,128,1024]{2,1,0:T(8,128)(2,1)}, u32[]{:S(2)}, u32[]{:S(2)}) collective-permute-start(bf16[2,128,1024]{2,1,0:T(8,128)(2,1)} %convert_element_type.50), channel_id=1, source_target_pairs={{0,8},{2,10},{4,12},{6,14},{8,0},{10,2},{12,4},{14,6},{1,9},{3,11}... | collective-permute-start | bytes 1572872 | tf_op jit(solution)/shard_map/ppermute | solution.py:57
  102.4 2.9 %copy.26 = f32[2,128,2048]{2,1,0:T(8,128)} copy(f32[2,128,2048]{1,2,0:T(8,128)} %bitcast.59) | data formatting | bytes 4194304 | tf_op jit(solution)/shard_map/optimization_barrier | solution.py:60
  105.3 13.9 %collective-permute-done.6 = bf16[2,128,1024]{2,1,0:T(8,128)(2,1)} collective-permute-done((bf16[2,128,1024]{2,1,0:T(8,128)(2,1)}, bf16[2,128,1024]{2,1,0:T(8,128)(2,1)}, u32[]{:S(2)}, u32[]{:S(2)}) %collective-permute-start.6) | collective-permute-done | bytes 524320 | tf_op jit(solution)/shard_map/ppermute | solution.py:57
  119.2 1.1 convert_element_type.47
  120.4 1.4 %add_select_fusion.2 = f32[2,128,1024]{2,1,0:T(8,128)S(1)} fusion(f32[2,128,1024]{2,1,0:T(8,128)S(1)} %convert_element_type.41, f32[2,128,1024]{2,1,0:T(8,128)S(1)} %convert_element_type.45, f32[2,1024]{1,0:T(2,128)S(1)} %mul.308, f32[2,1024]{1,0:T(2,128)S(1)} %mul.287, pred[]{:T(512)S(6)} %eq.13, pred[]{:T(512)S(6)} %eq.15, pred[]{:T(512)S(6)} %eq.14, ...), kind=kLoop, calls=%fused_computation.5 | loop fusion | flops 2097152 | bytes 3686403 | tf_op jit(solution)/shard_map/jit(_where)/select_n | solution.py:69
  121.8 5.6 %collective-permute-done.8 = bf16[2,128,1024]{2,1,0:T(8,128)(2,1)} collective-permute-done((bf16[2,128,1024]{2,1,0:T(8,128)(2,1)}, bf16[2,128,1024]{2,1,0:T(8,128)(2,1)}, u32[]{:S(2)}, u32[]{:S(2)}) %collective-permute-start.8) | collective-permute-done | bytes 524320 | tf_op jit(solution)/shard_map/ppermute | solution.py:57
  128.7 1.5 %add_select_fusion = f32[2,128,1024]{2,1,0:T(8,128)S(1)} fusion(f32[2,128,1024]{2,1,0:T(8,128)S(1)} %convert_element_type.43, f32[2,128,1024]{2,1,0:T(8,128)S(1)} %copy-done.2, f32[2,1024]{1,0:T(2,128)S(1)} %mul.338, f32[2,1024]{1,0:T(2,128)S(1)} %mul.329, pred[]{:T(512)S(6)} %eq.13, pred[]{:T(512)S(6)} %eq.15, pred[]{:T(512)S(6)} %eq.14, ...), kind=kLoop, calls=%fused_computation.3 | loop fusion | flops 2097152 | bytes 3686403 | tf_op jit(solution)/shard_map/jit(_where)/select_n | solution.py:69
  133.1 1.4 fusion.1
  (141 shorter events, 22.3 us)
Async XLA Ops:
  7.2 35.5 %copy-start = (bf16[256,128]{1,0:T(8,128)(2,1)S(1)}, bf16[256,128]{1,0:T(8,128)(2,1)}, u32[]{:S(2)}) copy-start(bf16[256,128]{1,0:T(8,128)(2,1)} %param.14) | copy-start | bytes 196612
  7.2 65.8 %all-gather.2.cloned.1.call-start = ((), (), s32[]{:S(2)}) async-start(), calls=%async_computation | async-start | bytes 2359296 | tf_op jit(solution)/shard_map/all_gather | solution.py:248
  9.3 9.4 %copy-start.13 = (f32[2,32,128]{2,1,0:T(8,128)}, f32[2,32,128]{2,1,0:T(8,128)S(1)}, u32[]{:S(2)}) copy-start(f32[2,32,128]{2,1,0:T(8,128)S(1)} %reduce_window_sum.11) | copy-start | bytes 98308
  9.5 18.4 %collective-permute-start = (f32[2,32]{1,0:T(2,128)S(1)}, f32[2,32]{1,0:T(2,128)S(1)}, u32[]{:S(2)}, u32[]{:S(2)}) collective-permute-start(f32[2,32]{1,0:T(2,128)S(1)} %exp.19), channel_id=1, source_target_pairs={{0,2},{2,0},{4,6},{6,4},{8,10},{10,8},{12,14},{14,12},{1,3},{3,1},... | collective-permute-start | bytes 776 | tf_op jit(solution)/shard_map/ppermute | solution.py:30
  18.8 6.5 %copy-start.15 = (f32[32,256]{1,0:T(8,128)S(1)}, f32[32,256]{1,0:T(8,128)}, u32[]{:S(2)}) copy-start(f32[32,256]{1,0:T(8,128)} %param.10) | copy-start | bytes 98308
  27.6 15.9 %copy-start.5 = (f32[2,128,1024]{2,1,0:T(8,128)}, f32[2,128,1024]{2,1,0:T(8,128)S(1)}, u32[]{:S(2)}) copy-start(f32[2,128,1024]{2,1,0:T(8,128)S(1)} %get-tuple-element.24) | copy-start | bytes 3145732
  27.9 13.6 %collective-permute-start.1 = (bf16[2,128,1024]{2,1,0:T(8,128)(2,1)S(1)}, bf16[2,128,1024]{2,1,0:T(8,128)(2,1)}, u32[]{:S(2)}, u32[]{:S(2)}) collective-permute-start(bf16[2,128,1024]{2,1,0:T(8,128)(2,1)S(1)} %convert_element_type.40), channel_id=1, source_target_pairs={{0,2},{2,0},{4,6},{6,4},{8,10},{10,8},{12,14},{14,12},{1,3},{3,1},... | collective-permute-start | bytes 1572872 | tf_op jit(solution)/shard_map/ppermute | solution.py:57
  28.2 3.7 %collective-permute-start.3 = (f32[2,32]{1,0:T(2,128)S(1)}, f32[2,32]{1,0:T(2,128)S(1)}, u32[]{:S(2)}, u32[]{:S(2)}) collective-permute-start(f32[2,32]{1,0:T(2,128)S(1)} %exponential_multiply_fusion), channel_id=1, source_target_pairs={{0,4},{2,6},{4,0},{6,2},{8,12},{10,14},{12,8},{14,10},{1,5},{3,7},... | collective-permute-start | bytes 776 | tf_op jit(solution)/shard_map/ppermute | solution.py:30
  31.9 4.6 %collective-permute-start.4 = (f32[2,32]{1,0:T(2,128)S(1)}, f32[2,32]{1,0:T(2,128)S(1)}, u32[]{:S(2)}, u32[]{:S(2)}) collective-permute-start(f32[2,32]{1,0:T(2,128)S(1)} %mul.280), channel_id=1, source_target_pairs={{0,8},{2,10},{4,12},{6,14},{8,0},{10,2},{12,4},{14,6},{1,9},{3,11}... | collective-permute-start | bytes 776 | tf_op jit(solution)/shard_map/ppermute | solution.py:30
  35.4 8.6 %copy-start.17 = (f32[2,1024]{1,0:T(2,128)}, f32[2,1024]{1,0:T(2,128)S(1)}, u32[]{:S(2)}) copy-start(f32[2,1024]{1,0:T(2,128)S(1)} %mul.347) | copy-start | bytes 24580
  35.7 8.3 %copy-start.18 = (f32[2,1024]{1,0:T(2,128)}, f32[2,1024]{1,0:T(2,128)S(1)}, u32[]{:S(2)}) copy-start(f32[2,1024]{1,0:T(2,128)S(1)} %mul.318) | copy-start | bytes 24580
  43.5 3.5 %copy-start.21 = (f32[32]{0:T(128)S(1)}, f32[32]{0:T(128)}, u32[]{:S(2)}) copy-start(f32[32]{0:T(128)} %param.12) | copy-start | bytes 388
  43.5 4.3 %copy-start.16 = (bf16[256,128]{1,0:T(8,128)(2,1)S(1)}, bf16[256,128]{1,0:T(8,128)(2,1)}, u32[]{:S(2)}) copy-start(bf16[256,128]{1,0:T(8,128)(2,1)} %param.13) | copy-start | bytes 196612
  43.5 22.7 %collective-permute-start.2 = (bf16[2,128,1024]{2,1,0:T(8,128)(2,1)}, bf16[2,128,1024]{2,1,0:T(8,128)(2,1)}, u32[]{:S(2)}, u32[]{:S(2)}) collective-permute-start(bf16[2,128,1024]{2,1,0:T(8,128)(2,1)} %convert_element_type.42), channel_id=1, source_target_pairs={{0,2},{2,0},{4,6},{6,4},{8,10},{10,8},{12,14},{14,12},{1,3},{3,1},... | collective-permute-start | bytes 1572872 | tf_op jit(solution)/shard_map/ppermute | solution.py:57
  45.1 12.4 %copy-start.14 = (f32[2,32,128]{2,1,0:T(8,128)S(1)}, f32[2,32,128]{2,1,0:T(8,128)}, u32[]{:S(2)}) copy-start(f32[2,32,128]{2,1,0:T(8,128)} %copy-done.13) | copy-start | bytes 98308
  45.1 23.8 %collective-permute-start.5 = (bf16[2,128,1024]{2,1,0:T(8,128)(2,1)S(1)}, bf16[2,128,1024]{2,1,0:T(8,128)(2,1)}, u32[]{:S(2)}, u32[]{:S(2)}) collective-permute-start(bf16[2,128,1024]{2,1,0:T(8,128)(2,1)S(1)} %convert_element_type.44), channel_id=1, source_target_pairs={{0,4},{2,6},{4,0},{6,2},{8,12},{10,14},{12,8},{14,10},{1,5},{3,7},... | collective-permute-start | bytes 1572872 | tf_op jit(solution)/shard_map/ppermute | solution.py:57
  67.4 2.7 %copy-start.6 = (f32[2,128,1024]{2,1,0:T(8,128)S(1)}, f32[2,128,1024]{2,1,0:T(8,128)}, u32[]{:S(2)}) copy-start(f32[2,128,1024]{2,1,0:T(8,128)} %copy-done.5) | copy-start | bytes 3145732
  75.2 19.7 %collective-permute-start.7 = (bf16[2,128,1024]{2,1,0:T(8,128)(2,1)}, bf16[2,128,1024]{2,1,0:T(8,128)(2,1)}, u32[]{:S(2)}, u32[]{:S(2)}) collective-permute-start(bf16[2,128,1024]{2,1,0:T(8,128)(2,1)} %convert_element_type.48), channel_id=1, source_target_pairs={{0,4},{2,6},{4,0},{6,2},{8,12},{10,14},{12,8},{14,10},{1,5},{3,7},... | collective-permute-start | bytes 1572872 | tf_op jit(solution)/shard_map/ppermute | solution.py:57
  77.3 3.3 %copy-start.19 = (f32[2,1024]{1,0:T(2,128)}, f32[2,1024]{1,0:T(2,128)S(1)}, u32[]{:S(2)}) copy-start(f32[2,1024]{1,0:T(2,128)S(1)} %mul.350) | copy-start | bytes 24580
  80.6 38.5 %collective-permute-start.6 = (bf16[2,128,1024]{2,1,0:T(8,128)(2,1)}, bf16[2,128,1024]{2,1,0:T(8,128)(2,1)}, u32[]{:S(2)}, u32[]{:S(2)}) collective-permute-start(bf16[2,128,1024]{2,1,0:T(8,128)(2,1)} %convert_element_type.46), channel_id=1, source_target_pairs={{0,8},{2,10},{4,12},{6,14},{8,0},{10,2},{12,4},{14,6},{1,9},{3,11}... | collective-permute-start | bytes 1572872 | tf_op jit(solution)/shard_map/ppermute | solution.py:57
  92.6 3.4 %copy-start.4 = (f32[2,128,1024]{2,1,0:T(8,128)S(1)}, f32[2,128,1024]{2,1,0:T(8,128)}, u32[]{:S(2)}) copy-start(f32[2,128,1024]{2,1,0:T(8,128)} %add_select_fusion.7) | copy-start | bytes 3145732
  96.3 4.9 %copy-start.11 = (f32[2,128,1024]{2,1,0:T(8,128)}, f32[2,128,1024]{2,1,0:T(8,128)S(1)}, u32[]{:S(2)}) copy-start(f32[2,128,1024]{2,1,0:T(8,128)S(1)} %add_select_fusion.4) | copy-start | bytes 3145732
  97.4 30.0 %collective-permute-start.8 = (bf16[2,128,1024]{2,1,0:T(8,128)(2,1)}, bf16[2,128,1024]{2,1,0:T(8,128)(2,1)}, u32[]{:S(2)}, u32[]{:S(2)}) collective-permute-start(bf16[2,128,1024]{2,1,0:T(8,128)(2,1)} %convert_element_type.50), channel_id=1, source_target_pairs={{0,8},{2,10},{4,12},{6,14},{8,0},{10,2},{12,4},{14,6},{1,9},{3,11}... | collective-permute-start | bytes 1572872 | tf_op jit(solution)/shard_map/ppermute | solution.py:57
  102.0 3.3 %copy-start.20 = (f32[2,1024]{1,0:T(2,128)}, f32[2,1024]{1,0:T(2,128)S(1)}, u32[]{:S(2)}) copy-start(f32[2,1024]{1,0:T(2,128)S(1)} %mul.321) | copy-start | bytes 24580
  120.4 8.3 %copy-start.2 = (f32[2,128,1024]{2,1,0:T(8,128)S(1)}, f32[2,128,1024]{2,1,0:T(8,128)}, u32[]{:S(2)}) copy-start(f32[2,128,1024]{2,1,0:T(8,128)} %copy-done.1) | copy-start | bytes 3145732
  128.6 1.7 %copy-start.12 = (f32[2,128,1024]{2,1,0:T(8,128)S(1)}, f32[2,128,1024]{2,1,0:T(8,128)}, u32[]{:S(2)}) copy-start(f32[2,128,1024]{2,1,0:T(8,128)} %copy-done.11) | copy-start | bytes 3145732
  128.6 1.7 %slice-start = ((f32[2,1024]{1,0:T(2,128)}), f32[1,1024]{1,0:T(1,128)S(1)}, s32[]{:S(2)}) async-start(f32[2,1024]{1,0:T(2,128)} %copy-done.17), calls=%async_computation.1 | async-start | bytes 8192 | tf_op jit(solution)/shard_map/slice | solution.py:84
  128.6 1.7 %slice-start.1 = ((f32[2,1024]{1,0:T(2,128)}), f32[1,1024]{1,0:T(1,128)S(1)}, s32[]{:S(2)}) async-start(f32[2,1024]{1,0:T(2,128)} %copy-done.18), calls=%async_computation.2 | async-start | bytes 8192 | tf_op jit(solution)/shard_map/slice | solution.py:84
  128.7 1.7 %slice-start.2 = ((f32[2,1024]{1,0:T(2,128)}), f32[1,1024]{1,0:T(1,128)S(1)}, s32[]{:S(2)}) async-start(f32[2,1024]{1,0:T(2,128)} %copy-done.19), calls=%async_computation.3 | async-start | bytes 8192 | tf_op jit(solution)/shard_map/slice | solution.py:84
  128.7 1.7 %slice-start.3 = ((f32[2,1024]{1,0:T(2,128)}), f32[1,1024]{1,0:T(1,128)S(1)}, s32[]{:S(2)}) async-start(f32[2,1024]{1,0:T(2,128)} %copy-done.20), calls=%async_computation.4 | async-start | bytes 8192 | tf_op jit(solution)/shard_map/slice | solution.py:84
  130.8 1.6 %copy-start.7 = (f32[2,128,2048]{2,1,0:T(8,128)S(1)}, f32[2,128,2048]{2,1,0:T(8,128)}, u32[]{:S(2)}) copy-start(f32[2,128,2048]{2,1,0:T(8,128)} %shard_map.105) | copy-start | bytes 6291460
  130.8 2.2 %copy-start.8 = (f32[2,128,2048]{2,1,0:T(8,128)S(1)}, f32[2,128,2048]{2,1,0:T(8,128)}, u32[]{:S(2)}) copy-start(f32[2,128,2048]{2,1,0:T(8,128)} %copy.26) | copy-start | bytes 6291460
  (4 other events, 4.9 us)
Sparse Core Ops, SparseCore 0:
  14.3 58.6 all-gather.1

commit v18 on v16

--- a/solution.py
+++ b/solution.py
@@ -132,9 +132,8 @@
     )(x_in, inner, cum_row, step_row, skip_row)
 
 
-def block_state_kernel(b_ref, f_ref, x_ref, o_ref):
-    scaled = (f_ref[0] * x_ref[...].astype(jnp.float32)).astype(jnp.bfloat16)
-    o_ref[0] = jnp.dot(b_ref[0], scaled, preferred_element_type=jnp.float32)
+def block_state_kernel(b_ref, f_ref, o_ref):
+    o_ref[0] = jnp.dot(b_ref[0], f_ref[0], preferred_element_type=jnp.float32)
 
 
 def block_states(b_blocks, factor, x_in):
@@ -142,11 +141,12 @@
     width = x_in.shape[1]
     cut = 512 if width % 512 == 0 else width
     b_t = b_blocks.transpose(0, 2, 1)
-    spread_factor = spread(factor)
+    tokens_x = x_in.reshape(slots, tokens, width).astype(jnp.float32)
+    spread_factor = (spread(factor) * tokens_x).astype(jnp.bfloat16)
     cost = pl.CostEstimate(
         flops=2 * slots * state * tokens * width,
         transcendentals=0,
-        bytes_accessed=x_in.size * 2 + spread_factor.size * 4 + slots * state * width * 4,
+        bytes_accessed=spread_factor.size * 2 + slots * state * width * 4,
     )
     return pl.pallas_call(
         block_state_kernel,
@@ -155,11 +155,10 @@
         in_specs=[
             pl.BlockSpec((1, state, tokens), lambda c, k: (c, 0, 0)),
             pl.BlockSpec((1, tokens, cut), lambda c, k: (c, 0, k)),
-            pl.BlockSpec((tokens, cut), lambda c, k: (c, k)),
         ],
         out_specs=pl.BlockSpec((1, state, cut), lambda c, k: (c, 0, k)),
         cost_estimate=cost,
-    )(b_t, spread_factor, x_in)
+    )(b_t, spread_factor)
 
 
 KEY_CHUNK = 256

time: 142 us -> 143 us (level)
  other arithmetic: 24.8 us -> 27.6 us
    convert_element_type x0 -> x1, other arithmetic: none -> 2.88 us  [block_states(): spread_factor = (spread(factor) * tokens_x).astype(jnp.bfloat16)]
    all_gather x1, waiting for transfers between devices: 1.71 us -> 0.01 us  [local(): kv_piece = lax.all_gather(kv_cat, 'seq', axis=1, tiled=True)]
    unnamed x44 -> x46, local copies, waits for them, and re-layouts: 3.05 us -> 3.08 us
  transfers between devices with their start and end apart: 10 -> 10, of which waited for: 8 -> 8; matrix products, arithmetic and copies ran while one was open for 22% -> 24% of each run, Pallas kernels for 19% -> 19%
where the time goes in v18:
time: 143 us; the launch traced here: 142 us
  waiting for transfers between devices  33.5 us (23%)
  other arithmetic  27.6 us (19%)
  Pallas kernels  27 us (19%)
  starting transfers between devices  20.1 us (14%)
  local copies, waits for them, and re-layouts  17.3 us (12%)
  between operations  14.4 us (10%)
  matrix products  2.13 us (1%)
    ppermute x6, waiting for transfers between devices, entering_states(): lax.ppermute(totals[j].astype(jnp.bfloat16), 'seq', pairs)  31.7 us
    pallas_call x1, Pallas kernels, attention_core(): pl.pallas_call(attention_kernel, out_shape=jax.ShapeDtypeStruct(queries.s...  12 us
    ppermute x6, starting transfers between devices, entering_states(): lax.ppermute(totals[j].astype(jnp.bfloat16), 'seq', pairs)  11.8 us
    pallas_call x1, Pallas kernels, mamba_base(): pl.pallas_call(mamba_base_kernel, out_shape=jax.ShapeDtypeStruct((slots,...  8.9 us
    ppermute x3, starting transfers between devices, decay_scan(): got = lax.ppermute(total, 'seq', [(i, i ^ span) for i in range(count)])  8.2 us
    convert_element_type x6, other arithmetic, entering_states(): lax.ppermute(totals[j].astype(jnp.bfloat16), 'seq', pairs)  6.87 us
    pallas_call x1, Pallas kernels, block_states(): pl.pallas_call(block_state_kernel, out_shape=jax.ShapeDtypeStruct((slots,...  6.1 us
    convert_element_type x6, other arithmetic, entering_states(): totals[j].astype(jnp.bfloat16)  5.12 us
  transfers between devices with their start and end apart: 10, of which 8 were waited for; matrix products, arithmetic and copies ran while one was open for 24% of the time, Pallas kernels for 19%

profile of v18, /device:TPU:0, one launch (start us, length us, event | category | flops | bytes accessed | tf_op | source)
XLA Modules:
  0.0 142.2 jit_solution(16701975203178268509)
XLA Ops:
  9.5 3.0 %collective-permute-start = (f32[2,32]{1,0:T(2,128)S(1)}, f32[2,32]{1,0:T(2,128)S(1)}, u32[]{:S(2)}, u32[]{:S(2)}) collective-permute-start(f32[2,32]{1,0:T(2,128)S(1)} %exp.19), channel_id=1, source_target_pairs={{0,2},{2,0},{4,6},{6,4},{8,10},{10,8},{12,14},{14,12},{1,3},{3,1},... | collective-permute-start | bytes 776 | tf_op jit(solution)/shard_map/ppermute | solution.py:30
  12.5 1.7 %pad_maximum_fusion = bf16[2,128,512]{2,1,0:T(8,128)(2,1)} fusion(bf16[2,128,256]{2,1,0:T(8,128)(2,1)} %bitcast.70, bf16[2,128,256]{2,1,0:T(8,128)(2,1)} %bitcast.71), kind=kLoop, calls=%fused_computation.25 | loop fusion | flops 524288 | bytes 524288 | tf_op jit(solution)/shard_map/concatenate | solution.py:244
  15.2 1.8 %copy.21 = f32[2,128,2048]{2,1,0:T(8,128)} copy(f32[2,128,2048]{1,2,0:T(8,128)S(1)} %bitcast.62) | data formatting | bytes 4194304 | tf_op jit(solution)/shard_map/reshape | solution.py:20
  17.0 2.9 %fusion.2.f_ref = bf16[2,128,2048]{2,1,0:T(8,128)(2,1)} fusion(f32[2,128,2048]{2,1,0:T(8,128)} %copy.21, bf16[2,128,2048]{2,1,0:T(8,128)(2,1)S(1)} %bitcast.63), kind=kLoop, calls=%fused_computation.4 | loop fusion | flops 1572864 | bytes 4194304 | tf_op jit(solution)/shard_map/convert_element_type | solution.py:145
  20.9 6.1 %shard_map.104 = f32[2,128,2048]{2,1,0:T(8,128)} custom-call(bf16[2,128,128]{2,1,0:T(8,128)(2,1)} %bitcast.66, bf16[2,128,2048]{2,1,0:T(8,128)(2,1)} %fusion.2.f_ref), custom_call_target="tpu_custom_call" | custom-call | flops 134217728 | bytes 3145728 | tf_op jit(solution)/shard_map/pallas_call | solution.py:151
  27.6 1.7 %fusion.12 = (f32[2,128,1024]{2,1,0:T(8,128)S(1)}, f32[2,128,1024]{2,1,0:T(8,128)S(1)}) fusion(f32[2,128,2048]{2,1,0:T(8,128)} %shard_map.104), kind=kLoop, calls=%fused_computation.45 | loop fusion | bytes 4194304 | tf_op jit(solution)/shard_map/slice | solution.py:42
  29.9 2.1 %collective-permute-start.3 = (f32[2,32]{1,0:T(2,128)S(1)}, f32[2,32]{1,0:T(2,128)S(1)}, u32[]{:S(2)}, u32[]{:S(2)}) collective-permute-start(f32[2,32]{1,0:T(2,128)S(1)} %exponential_multiply_fusion), channel_id=1, source_target_pairs={{0,4},{2,6},{4,0},{6,2},{8,12},{10,14},{12,8},{14,10},{1,5},{3,7},... | collective-permute-start | bytes 776 | tf_op jit(solution)/shard_map/ppermute | solution.py:30
  33.6 3.1 %collective-permute-start.4 = (f32[2,32]{1,0:T(2,128)S(1)}, f32[2,32]{1,0:T(2,128)S(1)}, u32[]{:S(2)}, u32[]{:S(2)}) collective-permute-start(f32[2,32]{1,0:T(2,128)S(1)} %mul.284), channel_id=1, source_target_pairs={{0,8},{2,10},{4,12},{6,14},{8,0},{10,2},{12,4},{14,6},{1,9},{3,11}... | collective-permute-start | bytes 776 | tf_op jit(solution)/shard_map/ppermute | solution.py:30
  38.3 4.8 %collective-permute-done.1 = bf16[2,128,1024]{2,1,0:T(8,128)(2,1)} collective-permute-done((bf16[2,128,1024]{2,1,0:T(8,128)(2,1)S(1)}, bf16[2,128,1024]{2,1,0:T(8,128)(2,1)}, u32[]{:S(2)}, u32[]{:S(2)}) %collective-permute-start.1) | collective-permute-done | bytes 524320 | tf_op jit(solution)/shard_map/ppermute | solution.py:57
  43.1 1.1 convert_element_type.53
  46.8 1.9 %collective-permute-start.5 = (bf16[2,128,1024]{2,1,0:T(8,128)(2,1)S(1)}, bf16[2,128,1024]{2,1,0:T(8,128)(2,1)}, u32[]{:S(2)}, u32[]{:S(2)}) collective-permute-start(bf16[2,128,1024]{2,1,0:T(8,128)(2,1)S(1)} %convert_element_type.56), channel_id=1, source_target_pairs={{0,4},{2,6},{4,0},{6,2},{8,12},{10,14},{12,8},{14,10},{1,5},{3,7},... | collective-permute-start | bytes 1572872 | tf_op jit(solution)/shard_map/ppermute | solution.py:57
  50.3 8.9 %shard_map.105 = f32[2,128,2048]{2,1,0:T(8,128)} custom-call(bf16[256,2048]{1,0:T(8,128)(2,1)} %x_ref, f32[2,128,128]{2,1,0:T(8,128)} %fusion.21.inner_ref, f32[2,32,1,128]{3,2,1,0:T(1,128)} %bitcast.65, f32[2,32,1,128]{3,2,1,0:T(1,128)} %bitcast.69, f32[1,2048]{1,0:T(1,128)} %broadcast_in_dim_reshape.2.skip_ref), custom_call_target="tpu_custom_call" | custom-call | flops 140509184 | bytes 3145728 | tf_op jit(solution)/shard_map/pallas_call | solution.py:119
  59.2 6.9 %collective-permute-done.2 = bf16[2,128,1024]{2,1,0:T(8,128)(2,1)} collective-permute-done((bf16[2,128,1024]{2,1,0:T(8,128)(2,1)}, bf16[2,128,1024]{2,1,0:T(8,128)(2,1)}, u32[]{:S(2)}, u32[]{:S(2)}) %collective-permute-start.2) | collective-permute-done | bytes 524320 | tf_op jit(solution)/shard_map/ppermute | solution.py:57
  66.1 1.1 convert_element_type.55
  67.3 1.5 %broadcast_in_dim.87 = f32[2,128,32,64]{1,3,2,0:T(8,128)} broadcast(f32[2,128,32]{1,2,0:T(8,128)S(1)} %exponential_bitcast_fusion), dimensions={0,1,2} | broadcast | bytes 2129920 | tf_op jit(solution)/shard_map/broadcast_in_dim | solution.py:20
  68.8 1.7 %collective-permute-done.5 = bf16[2,128,1024]{2,1,0:T(8,128)(2,1)} collective-permute-done((bf16[2,128,1024]{2,1,0:T(8,128)(2,1)S(1)}, bf16[2,128,1024]{2,1,0:T(8,128)(2,1)}, u32[]{:S(2)}, u32[]{:S(2)}) %collective-permute-start.5) | collective-permute-done | bytes 524320 | tf_op jit(solution)/shard_map/ppermute | solution.py:57
  70.5 1.1 convert_element_type.57
  71.7 1.2 add_select_fusion.7
  72.9 2.1 %convert_element_type.60 = bf16[2,128,1024]{2,1,0:T(8,128)(2,1)} convert(f32[2,128,1024]{2,1,0:T(8,128)} %add_select_fusion.7) | non-fusion elementwise | flops 262144 | bytes 1572864 | tf_op jit(solution)/shard_map/convert_element_type | solution.py:57
  75.0 1.3 collective-permute-start.7
  77.0 1.5 %add_select_fusion.5 = f32[2,128,1024]{2,1,0:T(8,128)S(1)} fusion(f32[2,128,1024]{2,1,0:T(8,128)S(1)} %convert_element_type.57, f32[2,128,1024]{2,1,0:T(8,128)} %copy-done.3, f32[2,1024]{1,0:T(2,128)S(1)} %mul.308, f32[2,1024]{1,0:T(2,128)S(1)} %mul.293, pred[]{:T(512)S(6)} %eq.15), kind=kLoop, calls=%fused_computation.18 | loop fusion | flops 1310720 | bytes 3162113 | tf_op jit(solution)/shard_map/jit(_where)/select_n | solution.py:70
  80.3 2.0 %collective-permute-start.6 = (bf16[2,128,1024]{2,1,0:T(8,128)(2,1)}, bf16[2,128,1024]{2,1,0:T(8,128)(2,1)}, u32[]{:S(2)}, u32[]{:S(2)}) collective-permute-start(bf16[2,128,1024]{2,1,0:T(8,128)(2,1)} %convert_element_type.58), channel_id=1, source_target_pairs={{0,8},{2,10},{4,12},{6,14},{8,0},{10,2},{12,4},{14,6},{1,9},{3,11}... | collective-permute-start | bytes 1572872 | tf_op jit(solution)/shard_map/ppermute | solution.py:57
  82.3 12.0 %shard_map.106 = bf16[256,1024]{1,0:T(8,128)(2,1)} custom-call(bf16[256,1024]{1,0:T(8,128)(2,1)} %q_ref, bf16[2,1024,512]{2,1,0:T(8,128)(2,1)} %all-gather.2.cloned.1.call-done.k_ref.v_ref, bf16[2,1024,512]{2,1,0:T(8,128)(2,1)} %all-gather.2.cloned.1.call-done.k_ref.v_ref), custom_call_target="tpu_custom_call" | custom-call | flops 2147483648 | bytes 3145728 | tf_op jit(solution)/shard_map/pallas_call | solution.py:224
  95.1 1.1 convert_element_type.61
  97.7 6.3 %collective-permute-start.8 = (bf16[2,128,1024]{2,1,0:T(8,128)(2,1)}, bf16[2,128,1024]{2,1,0:T(8,128)(2,1)}, u32[]{:S(2)}, u32[]{:S(2)}) collective-permute-start(bf16[2,128,1024]{2,1,0:T(8,128)(2,1)} %convert_element_type.62), channel_id=1, source_target_pairs={{0,8},{2,10},{4,12},{6,14},{8,0},{10,2},{12,4},{14,6},{1,9},{3,11}... | collective-permute-start | bytes 1572872 | tf_op jit(solution)/shard_map/ppermute | solution.py:57
  105.3 2.9 %copy.26 = f32[2,128,2048]{2,1,0:T(8,128)} copy(f32[2,128,2048]{1,2,0:T(8,128)} %bitcast.61) | data formatting | bytes 4194304 | tf_op jit(solution)/shard_map/optimization_barrier | solution.py:60
  108.2 10.5 %collective-permute-done.6 = bf16[2,128,1024]{2,1,0:T(8,128)(2,1)} collective-permute-done((bf16[2,128,1024]{2,1,0:T(8,128)(2,1)}, bf16[2,128,1024]{2,1,0:T(8,128)(2,1)}, u32[]{:S(2)}, u32[]{:S(2)}) %collective-permute-start.6) | collective-permute-done | bytes 524320 | tf_op jit(solution)/shard_map/ppermute | solution.py:57
  118.7 1.1 convert_element_type.59
  119.9 1.4 %add_select_fusion.2 = f32[2,128,1024]{2,1,0:T(8,128)S(1)} fusion(f32[2,128,1024]{2,1,0:T(8,128)S(1)} %convert_element_type.53, f32[2,128,1024]{2,1,0:T(8,128)S(1)} %convert_element_type.57, f32[2,1024]{1,0:T(2,128)S(1)} %mul.312, f32[2,1024]{1,0:T(2,128)S(1)} %mul.291, pred[]{:T(512)S(6)} %eq.13, pred[]{:T(512)S(6)} %eq.15, pred[]{:T(512)S(6)} %eq.14, ...), kind=kLoop, calls=%fused_computation.7 | loop fusion | flops 2097152 | bytes 3686403 | tf_op jit(solution)/shard_map/jit(_where)/select_n | solution.py:69
  121.3 7.0 %collective-permute-done.8 = bf16[2,128,1024]{2,1,0:T(8,128)(2,1)} collective-permute-done((bf16[2,128,1024]{2,1,0:T(8,128)(2,1)}, bf16[2,128,1024]{2,1,0:T(8,128)(2,1)}, u32[]{:S(2)}, u32[]{:S(2)}) %collective-permute-start.8) | collective-permute-done | bytes 524320 | tf_op jit(solution)/shard_map/ppermute | solution.py:57
  129.5 1.5 %add_select_fusion = f32[2,128,1024]{2,1,0:T(8,128)S(1)} fusion(f32[2,128,1024]{2,1,0:T(8,128)S(1)} %convert_element_type.55, f32[2,128,1024]{2,1,0:T(8,128)S(1)} %copy-done.2, f32[2,1024]{1,0:T(2,128)S(1)} %mul.342, f32[2,1024]{1,0:T(2,128)S(1)} %mul.333, pred[]{:T(512)S(6)} %eq.13, pred[]{:T(512)S(6)} %eq.15, pred[]{:T(512)S(6)} %eq.14, ...), kind=kLoop, calls=%fused_computation.5 | loop fusion | flops 2097152 | bytes 3686403 | tf_op jit(solution)/shard_map/jit(_where)/select_n | solution.py:69
  133.9 1.4 fusion.1
  (144 shorter events, 22.8 us)
Async XLA Ops:
  7.2 37.1 %copy-start = (bf16[256,128]{1,0:T(8,128)(2,1)S(1)}, bf16[256,128]{1,0:T(8,128)(2,1)}, u32[]{:S(2)}) copy-start(bf16[256,128]{1,0:T(8,128)(2,1)} %param.14) | copy-start | bytes 196612
  7.2 65.7 %all-gather.2.cloned.1.call-start = ((), (), s32[]{:S(2)}) async-start(), calls=%async_computation | async-start | bytes 2359296 | tf_op jit(solution)/shard_map/all_gather | solution.py:247
  9.3 7.7 %copy-start.14 = (f32[2,32,128]{2,1,0:T(8,128)}, f32[2,32,128]{2,1,0:T(8,128)S(1)}, u32[]{:S(2)}) copy-start(f32[2,32,128]{2,1,0:T(8,128)S(1)} %reduce_window_sum.11) | copy-start | bytes 98308
  9.5 20.0 %collective-permute-start = (f32[2,32]{1,0:T(2,128)S(1)}, f32[2,32]{1,0:T(2,128)S(1)}, u32[]{:S(2)}, u32[]{:S(2)}) collective-permute-start(f32[2,32]{1,0:T(2,128)S(1)} %exp.19), channel_id=1, source_target_pairs={{0,2},{2,0},{4,6},{6,4},{8,10},{10,8},{12,14},{14,12},{1,3},{3,1},... | collective-permute-start | bytes 776 | tf_op jit(solution)/shard_map/ppermute | solution.py:30
  15.2 1.9 %copy-start.13 = (bf16[256,2048]{1,0:T(8,128)(2,1)S(1)}, bf16[256,2048]{1,0:T(8,128)(2,1)}, u32[]{:S(2)}) copy-start(bf16[256,2048]{1,0:T(8,128)(2,1)} %x_ref) | copy-start | bytes 3145732
  17.0 3.0 %copy-start.17 = (bf16[256,128]{1,0:T(8,128)(2,1)S(1)}, bf16[256,128]{1,0:T(8,128)(2,1)}, u32[]{:S(2)}) copy-start(bf16[256,128]{1,0:T(8,128)(2,1)} %param.13) | copy-start | bytes 196612
  19.9 7.1 %copy-start.16 = (f32[32,256]{1,0:T(8,128)S(1)}, f32[32,256]{1,0:T(8,128)}, u32[]{:S(2)}) copy-start(f32[32,256]{1,0:T(8,128)} %param.10) | copy-start | bytes 98308
  29.3 15.8 %copy-start.5 = (f32[2,128,1024]{2,1,0:T(8,128)}, f32[2,128,1024]{2,1,0:T(8,128)S(1)}, u32[]{:S(2)}) copy-start(f32[2,128,1024]{2,1,0:T(8,128)S(1)} %get-tuple-element.24) | copy-start | bytes 3145732
  29.6 13.5 %collective-permute-start.1 = (bf16[2,128,1024]{2,1,0:T(8,128)(2,1)S(1)}, bf16[2,128,1024]{2,1,0:T(8,128)(2,1)}, u32[]{:S(2)}, u32[]{:S(2)}) collective-permute-start(bf16[2,128,1024]{2,1,0:T(8,128)(2,1)S(1)} %convert_element_type.52), channel_id=1, source_target_pairs={{0,2},{2,0},{4,6},{6,4},{8,10},{10,8},{12,14},{14,12},{1,3},{3,1},... | collective-permute-start | bytes 1572872 | tf_op jit(solution)/shard_map/ppermute | solution.py:57
  29.9 3.7 %collective-permute-start.3 = (f32[2,32]{1,0:T(2,128)S(1)}, f32[2,32]{1,0:T(2,128)S(1)}, u32[]{:S(2)}, u32[]{:S(2)}) collective-permute-start(f32[2,32]{1,0:T(2,128)S(1)} %exponential_multiply_fusion), channel_id=1, source_target_pairs={{0,4},{2,6},{4,0},{6,2},{8,12},{10,14},{12,8},{14,10},{1,5},{3,7},... | collective-permute-start | bytes 776 | tf_op jit(solution)/shard_map/ppermute | solution.py:30
  33.6 4.6 %collective-permute-start.4 = (f32[2,32]{1,0:T(2,128)S(1)}, f32[2,32]{1,0:T(2,128)S(1)}, u32[]{:S(2)}, u32[]{:S(2)}) collective-permute-start(f32[2,32]{1,0:T(2,128)S(1)} %mul.284), channel_id=1, source_target_pairs={{0,8},{2,10},{4,12},{6,14},{8,0},{10,2},{12,4},{14,6},{1,9},{3,11}... | collective-permute-start | bytes 776 | tf_op jit(solution)/shard_map/ppermute | solution.py:30
  37.1 8.6 %copy-start.18 = (f32[2,1024]{1,0:T(2,128)}, f32[2,1024]{1,0:T(2,128)S(1)}, u32[]{:S(2)}) copy-start(f32[2,1024]{1,0:T(2,128)S(1)} %mul.351) | copy-start | bytes 24580
  37.4 8.3 %copy-start.19 = (f32[2,1024]{1,0:T(2,128)}, f32[2,1024]{1,0:T(2,128)S(1)}, u32[]{:S(2)}) copy-start(f32[2,1024]{1,0:T(2,128)S(1)} %mul.322) | copy-start | bytes 24580
  45.1 3.6 %copy-start.22 = (f32[32]{0:T(128)S(1)}, f32[32]{0:T(128)}, u32[]{:S(2)}) copy-start(f32[32]{0:T(128)} %param.12) | copy-start | bytes 388
  45.2 21.0 %collective-permute-start.2 = (bf16[2,128,1024]{2,1,0:T(8,128)(2,1)}, bf16[2,128,1024]{2,1,0:T(8,128)(2,1)}, u32[]{:S(2)}, u32[]{:S(2)}) collective-permute-start(bf16[2,128,1024]{2,1,0:T(8,128)(2,1)} %convert_element_type.54), channel_id=1, source_target_pairs={{0,2},{2,0},{4,6},{6,4},{8,10},{10,8},{12,14},{14,12},{1,3},{3,1},... | collective-permute-start | bytes 1572872 | tf_op jit(solution)/shard_map/ppermute | solution.py:57
  46.8 12.5 %copy-start.15 = (f32[2,32,128]{2,1,0:T(8,128)S(1)}, f32[2,32,128]{2,1,0:T(8,128)}, u32[]{:S(2)}) copy-start(f32[2,32,128]{2,1,0:T(8,128)} %copy-done.14) | copy-start | bytes 98308
  46.8 23.7 %collective-permute-start.5 = (bf16[2,128,1024]{2,1,0:T(8,128)(2,1)S(1)}, bf16[2,128,1024]{2,1,0:T(8,128)(2,1)}, u32[]{:S(2)}, u32[]{:S(2)}) collective-permute-start(bf16[2,128,1024]{2,1,0:T(8,128)(2,1)S(1)} %convert_element_type.56), channel_id=1, source_target_pairs={{0,4},{2,6},{4,0},{6,2},{8,12},{10,14},{12,8},{14,10},{1,5},{3,7},... | collective-permute-start | bytes 1572872 | tf_op jit(solution)/shard_map/ppermute | solution.py:57
  67.3 4.4 %copy-start.6 = (f32[2,128,1024]{2,1,0:T(8,128)S(1)}, f32[2,128,1024]{2,1,0:T(8,128)}, u32[]{:S(2)}) copy-start(f32[2,128,1024]{2,1,0:T(8,128)} %copy-done.5) | copy-start | bytes 3145732
  75.0 20.1 %collective-permute-start.7 = (bf16[2,128,1024]{2,1,0:T(8,128)(2,1)}, bf16[2,128,1024]{2,1,0:T(8,128)(2,1)}, u32[]{:S(2)}, u32[]{:S(2)}) collective-permute-start(bf16[2,128,1024]{2,1,0:T(8,128)(2,1)} %convert_element_type.60), channel_id=1, source_target_pairs={{0,4},{2,6},{4,0},{6,2},{8,12},{10,14},{12,8},{14,10},{1,5},{3,7},... | collective-permute-start | bytes 1572872 | tf_op jit(solution)/shard_map/ppermute | solution.py:57
  77.0 3.3 %copy-start.20 = (f32[2,1024]{1,0:T(2,128)}, f32[2,1024]{1,0:T(2,128)S(1)}, u32[]{:S(2)}) copy-start(f32[2,1024]{1,0:T(2,128)S(1)} %mul.354) | copy-start | bytes 24580
  80.3 38.4 %collective-permute-start.6 = (bf16[2,128,1024]{2,1,0:T(8,128)(2,1)}, bf16[2,128,1024]{2,1,0:T(8,128)(2,1)}, u32[]{:S(2)}, u32[]{:S(2)}) collective-permute-start(bf16[2,128,1024]{2,1,0:T(8,128)(2,1)} %convert_element_type.58), channel_id=1, source_target_pairs={{0,8},{2,10},{4,12},{6,14},{8,0},{10,2},{12,4},{14,6},{1,9},{3,11}... | collective-permute-start | bytes 1572872 | tf_op jit(solution)/shard_map/ppermute | solution.py:57
  94.3 2.0 %copy-start.4 = (f32[2,128,1024]{2,1,0:T(8,128)S(1)}, f32[2,128,1024]{2,1,0:T(8,128)}, u32[]{:S(2)}) copy-start(f32[2,128,1024]{2,1,0:T(8,128)} %add_select_fusion.7) | copy-start | bytes 3145732
  96.6 7.4 %copy-start.11 = (f32[2,128,1024]{2,1,0:T(8,128)}, f32[2,128,1024]{2,1,0:T(8,128)S(1)}, u32[]{:S(2)}) copy-start(f32[2,128,1024]{2,1,0:T(8,128)S(1)} %add_select_fusion.4) | copy-start | bytes 3145732
  97.7 30.6 %collective-permute-start.8 = (bf16[2,128,1024]{2,1,0:T(8,128)(2,1)}, bf16[2,128,1024]{2,1,0:T(8,128)(2,1)}, u32[]{:S(2)}, u32[]{:S(2)}) collective-permute-start(bf16[2,128,1024]{2,1,0:T(8,128)(2,1)} %convert_element_type.62), channel_id=1, source_target_pairs={{0,8},{2,10},{4,12},{6,14},{8,0},{10,2},{12,4},{14,6},{1,9},{3,11}... | collective-permute-start | bytes 1572872 | tf_op jit(solution)/shard_map/ppermute | solution.py:57
  104.9 3.3 %copy-start.21 = (f32[2,1024]{1,0:T(2,128)}, f32[2,1024]{1,0:T(2,128)S(1)}, u32[]{:S(2)}) copy-start(f32[2,1024]{1,0:T(2,128)S(1)} %mul.325) | copy-start | bytes 24580
  119.9 9.6 %copy-start.2 = (f32[2,128,1024]{2,1,0:T(8,128)S(1)}, f32[2,128,1024]{2,1,0:T(8,128)}, u32[]{:S(2)}) copy-start(f32[2,128,1024]{2,1,0:T(8,128)} %copy-done.1) | copy-start | bytes 3145732
  129.5 1.7 %copy-start.12 = (f32[2,128,1024]{2,1,0:T(8,128)S(1)}, f32[2,128,1024]{2,1,0:T(8,128)}, u32[]{:S(2)}) copy-start(f32[2,128,1024]{2,1,0:T(8,128)} %copy-done.11) | copy-start | bytes 3145732
  129.5 1.7 %slice-start = ((f32[2,1024]{1,0:T(2,128)}), f32[1,1024]{1,0:T(1,128)S(1)}, s32[]{:S(2)}) async-start(f32[2,1024]{1,0:T(2,128)} %copy-done.18), calls=%async_computation.1 | async-start | bytes 8192 | tf_op jit(solution)/shard_map/slice | solution.py:84
  129.5 1.7 %slice-start.1 = ((f32[2,1024]{1,0:T(2,128)}), f32[1,1024]{1,0:T(1,128)S(1)}, s32[]{:S(2)}) async-start(f32[2,1024]{1,0:T(2,128)} %copy-done.19), calls=%async_computation.2 | async-start | bytes 8192 | tf_op jit(solution)/shard_map/slice | solution.py:84
  129.5 1.7 %slice-start.2 = ((f32[2,1024]{1,0:T(2,128)}), f32[1,1024]{1,0:T(1,128)S(1)}, s32[]{:S(2)}) async-start(f32[2,1024]{1,0:T(2,128)} %copy-done.20), calls=%async_computation.3 | async-start | bytes 8192 | tf_op jit(solution)/shard_map/slice | solution.py:84
  129.5 1.7 %slice-start.3 = ((f32[2,1024]{1,0:T(2,128)}), f32[1,1024]{1,0:T(1,128)S(1)}, s32[]{:S(2)}) async-start(f32[2,1024]{1,0:T(2,128)} %copy-done.21), calls=%async_computation.4 | async-start | bytes 8192 | tf_op jit(solution)/shard_map/slice | solution.py:84
  131.7 2.2 %copy-start.8 = (f32[2,128,2048]{2,1,0:T(8,128)S(1)}, f32[2,128,2048]{2,1,0:T(8,128)}, u32[]{:S(2)}) copy-start(f32[2,128,2048]{2,1,0:T(8,128)} %copy.26) | copy-start | bytes 6291460
  (5 other events, 6.5 us)
Sparse Core Ops, SparseCore 0:
  14.3 57.8 all-gather.1

commit v19 on v16

--- a/solution.py
+++ b/solution.py
@@ -49,8 +49,9 @@
         for j in range(parts):
             hook = hooks.get((j, step if step + 1 < len(steps) else -1))
             tie = gots[-1] if gots and step + 1 < len(steps) else ()
+            waited = known_all if step > 0 else ()
             totals[j], known, args, tie = lax.optimization_barrier(
-                (totals[j], known_all, hook[1] if hook else (), tie)
+                (totals[j], waited, hook[1] if hook else (), tie)
             )
             if gots and step + 1 < len(steps):
                 gots[-1] = tie

time: 142 us -> 142 us (level)
    ppermute x3, waiting for transfers between devices: 1.79 us -> 15 us  [decay_scan(): got = lax.ppermute(total, 'seq', [(i, i ^ span) for i in range(count)])]
    ppermute x6, waiting for transfers between devices: 31 us -> 18.8 us  [entering_states(): lax.ppermute(totals[j].astype(jnp.bfloat16), 'seq', pairs)]
    ppermute x3, starting transfers between devices: 8.19 us -> 3.86 us  [decay_scan(): got = lax.ppermute(total, 'seq', [(i, i ^ span) for i in range(count)])]
    ppermute x6, starting transfers between devices: 11.8 us -> 14.9 us  [entering_states(): lax.ppermute(totals[j].astype(jnp.bfloat16), 'seq', pairs)]
    all_gather x1, waiting for transfers between devices: 1.71 us -> 0.01 us  [local(): kv_piece = lax.all_gather(kv_cat, 'seq', axis=1, tiled=True)]
  transfers between devices with their start and end apart: 10 -> 10, of which waited for: 8 -> 5; matrix products, arithmetic and copies ran while one was open for 22% -> 24% of each run, Pallas kernels for 19% -> 19%
where the time goes in v19:
time: 142 us; the launch traced here: 141 us
  waiting for transfers between devices  33.8 us (24%)
  Pallas kernels  27.3 us (19%)
  other arithmetic  25.8 us (18%)
  starting transfers between devices  18.8 us (13%)
  local copies, waits for them, and re-layouts  18.2 us (13%)
  between operations  14.4 us (10%)
  matrix products  2.13 us (2%)
    ppermute x6, waiting for transfers between devices, entering_states(): lax.ppermute(totals[j].astype(jnp.bfloat16), 'seq', pairs)  18.8 us
    ppermute x3, waiting for transfers between devices, decay_scan(): got = lax.ppermute(total, 'seq', [(i, i ^ span) for i in range(count)])  15 us
    ppermute x6, starting transfers between devices, entering_states(): lax.ppermute(totals[j].astype(jnp.bfloat16), 'seq', pairs)  14.9 us
    pallas_call x1, Pallas kernels, attention_core(): pl.pallas_call(attention_kernel, out_shape=jax.ShapeDtypeStruct(queries.s...  12 us
    pallas_call x1, Pallas kernels, mamba_base(): pl.pallas_call(mamba_base_kernel, out_shape=jax.ShapeDtypeStruct((slots,...  8.86 us
    convert_element_type x6, other arithmetic, entering_states(): lax.ppermute(totals[j].astype(jnp.bfloat16), 'seq', pairs)  6.96 us
    pallas_call x1, Pallas kernels, block_states(): pl.pallas_call(block_state_kernel, out_shape=jax.ShapeDtypeStruct((slots,...  6.51 us
    convert_element_type x6, other arithmetic, entering_states(): totals[j].astype(jnp.bfloat16)  6 us
  transfers between devices with their start and end apart: 10, of which 5 were waited for; matrix products, arithmetic and copies ran while one was open for 24% of the time, Pallas kernels for 19%

profile of v19, /device:TPU:0, one launch (start us, length us, event | category | flops | bytes accessed | tf_op | source)
XLA Modules:
  0.0 140.6 jit_solution(13417397020970873112)
XLA Ops:
  7.2 1.7 %pad_maximum_fusion = bf16[2,128,512]{2,1,0:T(8,128)(2,1)} fusion(bf16[2,128,256]{2,1,0:T(8,128)(2,1)} %bitcast.67, bf16[2,128,256]{2,1,0:T(8,128)(2,1)} %bitcast.68), kind=kLoop, calls=%fused_computation.23 | loop fusion | flops 524288 | bytes 524288 | tf_op jit(solution)/shard_map/concatenate | solution.py:246
  9.0 1.6 %copy.18 = bf16[2,128,128]{1,2,0:T(8,128)(2,1)} copy(bf16[2,128,128]{2,1,0:T(8,128)(2,1)} %bitcast.63) | data formatting | bytes 131072 | tf_op jit(solution)/shard_map/reshape | solution.py:255
  13.8 1.8 %copy.21.f_ref = f32[2,128,2048]{2,1,0:T(8,128)} copy(f32[2,128,2048]{1,2,0:T(8,128)S(1)} %bitcast.60) | data formatting | bytes 4194304 | tf_op jit(solution)/shard_map/reshape | solution.py:20
  15.6 6.5 %shard_map.104 = f32[2,128,2048]{2,1,0:T(8,128)} custom-call(bf16[2,128,128]{2,1,0:T(8,128)(2,1)} %bitcast.65, f32[2,128,2048]{2,1,0:T(8,128)} %copy.21.f_ref, bf16[256,2048]{1,0:T(8,128)(2,1)} %x_ref.2), custom_call_target="tpu_custom_call" | custom-call | flops 134217728 | bytes 5242880 | tf_op jit(solution)/shard_map/pallas_call | solution.py:152
  22.1 1.7 %fusion.11 = (f32[2,128,1024]{2,1,0:T(8,128)S(1)}, f32[2,128,1024]{2,1,0:T(8,128)S(1)}) fusion(f32[2,128,2048]{2,1,0:T(8,128)} %shard_map.104), kind=kLoop, calls=%fused_computation.43 | loop fusion | bytes 4194304 | tf_op jit(solution)/shard_map/slice | solution.py:42
  23.9 3.0 %collective-permute-start = (bf16[2,128,1024]{2,1,0:T(8,128)(2,1)S(1)}, bf16[2,128,1024]{2,1,0:T(8,128)(2,1)}, u32[]{:S(2)}, u32[]{:S(2)}) collective-permute-start(bf16[2,128,1024]{2,1,0:T(8,128)(2,1)S(1)} %convert_element_type.40), channel_id=1, source_target_pairs={{0,2},{2,0},{4,6},{6,4},{8,10},{10,8},{12,14},{14,12},{1,3},{3,1},... | collective-permute-start | bytes 1572872 | tf_op jit(solution)/shard_map/ppermute | solution.py:58
  28.0 10.9 %collective-permute-done.2 = f32[2,32]{1,0:T(2,128)S(1)} collective-permute-done((f32[2,32]{1,0:T(2,128)S(1)}, f32[2,32]{1,0:T(2,128)S(1)}, u32[]{:S(2)}, u32[]{:S(2)}) %collective-permute-start.2) | collective-permute-done | bytes 288 | tf_op jit(solution)/shard_map/ppermute | solution.py:30
  39.2 1.9 %collective-permute-start.3 = (f32[2,32]{1,0:T(2,128)S(1)}, f32[2,32]{1,0:T(2,128)S(1)}, u32[]{:S(2)}, u32[]{:S(2)}) collective-permute-start(f32[2,32]{1,0:T(2,128)S(1)} %exponential_multiply_fusion), channel_id=1, source_target_pairs={{0,4},{2,6},{4,0},{6,2},{8,12},{10,14},{12,8},{14,10},{1,5},{3,7},... | collective-permute-start | bytes 776 | tf_op jit(solution)/shard_map/ppermute | solution.py:30
  41.6 2.2 %collective-permute-done.3 = f32[2,32]{1,0:T(2,128)S(1)} collective-permute-done((f32[2,32]{1,0:T(2,128)S(1)}, f32[2,32]{1,0:T(2,128)S(1)}, u32[]{:S(2)}, u32[]{:S(2)}) %collective-permute-start.3) | collective-permute-done | bytes 288 | tf_op jit(solution)/shard_map/ppermute | solution.py:30
  43.8 1.9 %collective-permute-start.4 = (f32[2,32]{1,0:T(2,128)S(1)}, f32[2,32]{1,0:T(2,128)S(1)}, u32[]{:S(2)}, u32[]{:S(2)}) collective-permute-start(f32[2,32]{1,0:T(2,128)S(1)} %mul.280), channel_id=1, source_target_pairs={{0,8},{2,10},{4,12},{6,14},{8,0},{10,2},{12,4},{14,6},{1,9},{3,11}... | collective-permute-start | bytes 776 | tf_op jit(solution)/shard_map/ppermute | solution.py:30
  46.4 1.9 %collective-permute-done.4 = f32[2,32]{1,0:T(2,128)S(1)} collective-permute-done((f32[2,32]{1,0:T(2,128)S(1)}, f32[2,32]{1,0:T(2,128)S(1)}, u32[]{:S(2)}, u32[]{:S(2)}) %collective-permute-start.4) | collective-permute-done | bytes 288 | tf_op jit(solution)/shard_map/ppermute | solution.py:30
  48.5 1.1 convert_element_type.41
  50.5 1.5 %collective-permute-start.1 = (bf16[2,128,1024]{2,1,0:T(8,128)(2,1)}, bf16[2,128,1024]{2,1,0:T(8,128)(2,1)}, u32[]{:S(2)}, u32[]{:S(2)}) collective-permute-start(bf16[2,128,1024]{2,1,0:T(8,128)(2,1)} %convert_element_type.42), channel_id=1, source_target_pairs={{0,2},{2,0},{4,6},{6,4},{8,10},{10,8},{12,14},{14,12},{1,3},{3,1},... | collective-permute-start | bytes 1572872 | tf_op jit(solution)/shard_map/ppermute | solution.py:58
  56.7 8.9 %shard_map.105 = f32[2,128,2048]{2,1,0:T(8,128)} custom-call(bf16[256,2048]{1,0:T(8,128)(2,1)} %x_ref.2, f32[2,128,128]{2,1,0:T(8,128)} %fusion.20.inner_ref, f32[2,32,1,128]{3,2,1,0:T(1,128)} %bitcast.62, f32[2,32,1,128]{3,2,1,0:T(1,128)} %bitcast.66, f32[1,2048]{1,0:T(1,128)} %broadcast_in_dim_reshape.2.skip_ref), custom_call_target="tpu_custom_call" | custom-call | flops 140509184 | bytes 3145728 | tf_op jit(solution)/shard_map/pallas_call | solution.py:120
  65.6 1.1 convert_element_type.43
  66.8 1.5 %broadcast_in_dim.86 = f32[2,128,32,64]{1,3,2,0:T(8,128)} broadcast(f32[2,128,32]{1,2,0:T(8,128)S(1)} %exponential_bitcast_fusion), dimensions={0,1,2} | broadcast | bytes 2129920 | tf_op jit(solution)/shard_map/broadcast_in_dim | solution.py:20
  68.2 3.2 %collective-permute-done.5 = bf16[2,128,1024]{2,1,0:T(8,128)(2,1)} collective-permute-done((bf16[2,128,1024]{2,1,0:T(8,128)(2,1)}, bf16[2,128,1024]{2,1,0:T(8,128)(2,1)}, u32[]{:S(2)}, u32[]{:S(2)}) %collective-permute-start.5) | collective-permute-done | bytes 524320 | tf_op jit(solution)/shard_map/ppermute | solution.py:58
  71.4 1.1 convert_element_type.45
  72.6 1.2 add_select_fusion.7
  73.8 2.1 %convert_element_type.48 = bf16[2,128,1024]{2,1,0:T(8,128)(2,1)} convert(f32[2,128,1024]{2,1,0:T(8,128)} %add_select_fusion.7) | non-fusion elementwise | flops 262144 | bytes 1572864 | tf_op jit(solution)/shard_map/convert_element_type | solution.py:58
  77.3 1.5 %add_select_fusion.5 = f32[2,128,1024]{2,1,0:T(8,128)S(1)} fusion(f32[2,128,1024]{2,1,0:T(8,128)S(1)} %convert_element_type.45, f32[2,128,1024]{2,1,0:T(8,128)} %copy-done.3, f32[2,1024]{1,0:T(2,128)S(1)} %mul.304, f32[2,1024]{1,0:T(2,128)S(1)} %mul.289, pred[]{:T(512)S(6)} %eq.14), kind=kLoop, calls=%fused_computation.16 | loop fusion | flops 1310720 | bytes 3162113 | tf_op jit(solution)/shard_map/jit(_where)/select_n | solution.py:71
  80.6 2.5 %collective-permute-start.6 = (bf16[2,128,1024]{2,1,0:T(8,128)(2,1)}, bf16[2,128,1024]{2,1,0:T(8,128)(2,1)}, u32[]{:S(2)}, u32[]{:S(2)}) collective-permute-start(bf16[2,128,1024]{2,1,0:T(8,128)(2,1)} %convert_element_type.46), channel_id=1, source_target_pairs={{0,8},{2,10},{4,12},{6,14},{8,0},{10,2},{12,4},{14,6},{1,9},{3,11}... | collective-permute-start | bytes 1572872 | tf_op jit(solution)/shard_map/ppermute | solution.py:58
  83.1 12.0 %shard_map.106 = bf16[256,1024]{1,0:T(8,128)(2,1)} custom-call(bf16[256,1024]{1,0:T(8,128)(2,1)} %q_ref, bf16[2,1024,512]{2,1,0:T(8,128)(2,1)} %all-gather.2.cloned.1.call-done.k_ref.v_ref, bf16[2,1024,512]{2,1,0:T(8,128)(2,1)} %all-gather.2.cloned.1.call-done.k_ref.v_ref), custom_call_target="tpu_custom_call" | custom-call | flops 2147483648 | bytes 3145728 | tf_op jit(solution)/shard_map/pallas_call | solution.py:226
  95.1 1.2 convert_element_type.49
  97.9 6.5 %collective-permute-start.8 = (bf16[2,128,1024]{2,1,0:T(8,128)(2,1)}, bf16[2,128,1024]{2,1,0:T(8,128)(2,1)}, u32[]{:S(2)}, u32[]{:S(2)}) collective-permute-start(bf16[2,128,1024]{2,1,0:T(8,128)(2,1)} %convert_element_type.50), channel_id=1, source_target_pairs={{0,8},{2,10},{4,12},{6,14},{8,0},{10,2},{12,4},{14,6},{1,9},{3,11}... | collective-permute-start | bytes 1572872 | tf_op jit(solution)/shard_map/ppermute | solution.py:58
  105.6 2.9 %copy.26 = f32[2,128,2048]{2,1,0:T(8,128)} copy(f32[2,128,2048]{1,2,0:T(8,128)} %bitcast.59) | data formatting | bytes 4194304 | tf_op jit(solution)/shard_map/optimization_barrier | solution.py:61
  108.5 1.1 convert_element_type.47
  109.7 1.4 %add_select_fusion.2 = f32[2,128,1024]{2,1,0:T(8,128)S(1)} fusion(f32[2,128,1024]{2,1,0:T(8,128)S(1)} %convert_element_type.41, f32[2,128,1024]{2,1,0:T(8,128)S(1)} %convert_element_type.45, f32[2,1024]{1,0:T(2,128)S(1)} %mul.308, f32[2,1024]{1,0:T(2,128)S(1)} %mul.287, pred[]{:T(512)S(6)} %eq.15, pred[]{:T(512)S(6)} %eq.14, pred[]{:T(512)S(6)} %eq.13, ...), kind=kLoop, calls=%fused_computation.5 | loop fusion | flops 2097152 | bytes 3686403 | tf_op jit(solution)/shard_map/jit(_where)/select_n | solution.py:70
  111.1 15.6 %collective-permute-done.8 = bf16[2,128,1024]{2,1,0:T(8,128)(2,1)} collective-permute-done((bf16[2,128,1024]{2,1,0:T(8,128)(2,1)}, bf16[2,128,1024]{2,1,0:T(8,128)(2,1)}, u32[]{:S(2)}, u32[]{:S(2)}) %collective-permute-start.8) | collective-permute-done | bytes 524320 | tf_op jit(solution)/shard_map/ppermute | solution.py:58
  126.8 1.1 convert_element_type.51
  128.0 1.5 %add_select_fusion = f32[2,128,1024]{2,1,0:T(8,128)S(1)} fusion(f32[2,128,1024]{2,1,0:T(8,128)S(1)} %convert_element_type.43, f32[2,128,1024]{2,1,0:T(8,128)S(1)} %copy-done.2, f32[2,1024]{1,0:T(2,128)S(1)} %mul.338, f32[2,1024]{1,0:T(2,128)S(1)} %mul.329, pred[]{:T(512)S(6)} %eq.15, pred[]{:T(512)S(6)} %eq.14, pred[]{:T(512)S(6)} %eq.13, ...), kind=kLoop, calls=%fused_computation.3 | loop fusion | flops 2097152 | bytes 3686403 | tf_op jit(solution)/shard_map/jit(_where)/select_n | solution.py:70
  132.4 1.4 fusion.1
  (141 shorter events, 20.5 us)
Async XLA Ops:
  7.2 42.5 %copy-start = (bf16[256,128]{1,0:T(8,128)(2,1)S(1)}, bf16[256,128]{1,0:T(8,128)(2,1)}, u32[]{:S(2)}) copy-start(bf16[256,128]{1,0:T(8,128)(2,1)} %param.14) | copy-start | bytes 196612
  7.2 66.6 %all-gather.2.cloned.1.call-start = ((), (), s32[]{:S(2)}) async-start(), calls=%async_computation | async-start | bytes 2359296 | tf_op jit(solution)/shard_map/all_gather | solution.py:249
  12.6 3.0 %copy-start.13 = (f32[2,32,128]{2,1,0:T(8,128)}, f32[2,32,128]{2,1,0:T(8,128)S(1)}, u32[]{:S(2)}) copy-start(f32[2,32,128]{2,1,0:T(8,128)S(1)} %reduce_window_sum.11) | copy-start | bytes 98308
  22.1 5.1 %copy-start.15 = (f32[32,256]{1,0:T(8,128)S(1)}, f32[32,256]{1,0:T(8,128)}, u32[]{:S(2)}) copy-start(f32[32,256]{1,0:T(8,128)} %param.10) | copy-start | bytes 98308
  23.8 26.7 %copy-start.5 = (f32[2,128,1024]{2,1,0:T(8,128)}, f32[2,128,1024]{2,1,0:T(8,128)S(1)}, u32[]{:S(2)}) copy-start(f32[2,128,1024]{2,1,0:T(8,128)S(1)} %get-tuple-element.22) | copy-start | bytes 3145732
  23.9 24.6 %collective-permute-start = (bf16[2,128,1024]{2,1,0:T(8,128)(2,1)S(1)}, bf16[2,128,1024]{2,1,0:T(8,128)(2,1)}, u32[]{:S(2)}, u32[]{:S(2)}) collective-permute-start(bf16[2,128,1024]{2,1,0:T(8,128)(2,1)S(1)} %convert_element_type.40), channel_id=1, source_target_pairs={{0,2},{2,0},{4,6},{6,4},{8,10},{10,8},{12,14},{14,12},{1,3},{3,1},... | collective-permute-start | bytes 1572872 | tf_op jit(solution)/shard_map/ppermute | solution.py:58
  26.9 12.0 %collective-permute-start.2 = (f32[2,32]{1,0:T(2,128)S(1)}, f32[2,32]{1,0:T(2,128)S(1)}, u32[]{:S(2)}, u32[]{:S(2)}) collective-permute-start(f32[2,32]{1,0:T(2,128)S(1)} %exp.20), channel_id=1, source_target_pairs={{0,2},{2,0},{4,6},{6,4},{8,10},{10,8},{12,14},{14,12},{1,3},{3,1},... | collective-permute-start | bytes 776 | tf_op jit(solution)/shard_map/ppermute | solution.py:30
  39.2 4.6 %collective-permute-start.3 = (f32[2,32]{1,0:T(2,128)S(1)}, f32[2,32]{1,0:T(2,128)S(1)}, u32[]{:S(2)}, u32[]{:S(2)}) collective-permute-start(f32[2,32]{1,0:T(2,128)S(1)} %exponential_multiply_fusion), channel_id=1, source_target_pairs={{0,4},{2,6},{4,0},{6,2},{8,12},{10,14},{12,8},{14,10},{1,5},{3,7},... | collective-permute-start | bytes 776 | tf_op jit(solution)/shard_map/ppermute | solution.py:30
  43.8 4.5 %collective-permute-start.4 = (f32[2,32]{1,0:T(2,128)S(1)}, f32[2,32]{1,0:T(2,128)S(1)}, u32[]{:S(2)}, u32[]{:S(2)}) collective-permute-start(f32[2,32]{1,0:T(2,128)S(1)} %mul.280), channel_id=1, source_target_pairs={{0,8},{2,10},{4,12},{6,14},{8,0},{10,2},{12,4},{14,6},{1,9},{3,11}... | collective-permute-start | bytes 776 | tf_op jit(solution)/shard_map/ppermute | solution.py:30
  46.1 6.2 %copy-start.17 = (f32[2,1024]{1,0:T(2,128)}, f32[2,1024]{1,0:T(2,128)S(1)}, u32[]{:S(2)}) copy-start(f32[2,1024]{1,0:T(2,128)S(1)} %mul.347) | copy-start | bytes 24580
  46.4 5.9 %copy-start.18 = (f32[2,1024]{1,0:T(2,128)}, f32[2,1024]{1,0:T(2,128)S(1)}, u32[]{:S(2)}) copy-start(f32[2,1024]{1,0:T(2,128)S(1)} %mul.318) | copy-start | bytes 24580
  50.5 4.6 %copy-start.21 = (f32[32]{0:T(128)S(1)}, f32[32]{0:T(128)}, u32[]{:S(2)}) copy-start(f32[32]{0:T(128)} %param.12) | copy-start | bytes 388
  50.5 5.3 %copy-start.16 = (bf16[256,128]{1,0:T(8,128)(2,1)S(1)}, bf16[256,128]{1,0:T(8,128)(2,1)}, u32[]{:S(2)}) copy-start(bf16[256,128]{1,0:T(8,128)(2,1)} %param.13) | copy-start | bytes 196612
  50.5 15.0 %collective-permute-start.1 = (bf16[2,128,1024]{2,1,0:T(8,128)(2,1)}, bf16[2,128,1024]{2,1,0:T(8,128)(2,1)}, u32[]{:S(2)}, u32[]{:S(2)}) collective-permute-start(bf16[2,128,1024]{2,1,0:T(8,128)(2,1)} %convert_element_type.42), channel_id=1, source_target_pairs={{0,2},{2,0},{4,6},{6,4},{8,10},{10,8},{12,14},{14,12},{1,3},{3,1},... | collective-permute-start | bytes 1572872 | tf_op jit(solution)/shard_map/ppermute | solution.py:58
  54.2 11.3 %copy-start.14 = (f32[2,32,128]{2,1,0:T(8,128)S(1)}, f32[2,32,128]{2,1,0:T(8,128)}, u32[]{:S(2)}) copy-start(f32[2,32,128]{2,1,0:T(8,128)} %copy-done.13) | copy-start | bytes 98308
  54.2 17.2 %collective-permute-start.5 = (bf16[2,128,1024]{2,1,0:T(8,128)(2,1)}, bf16[2,128,1024]{2,1,0:T(8,128)(2,1)}, u32[]{:S(2)}, u32[]{:S(2)}) collective-permute-start(bf16[2,128,1024]{2,1,0:T(8,128)(2,1)} %convert_element_type.44), channel_id=1, source_target_pairs={{0,4},{2,6},{4,0},{6,2},{8,12},{10,14},{12,8},{14,10},{1,5},{3,7},... | collective-permute-start | bytes 1572872 | tf_op jit(solution)/shard_map/ppermute | solution.py:58
  66.7 5.9 %copy-start.6 = (f32[2,128,1024]{2,1,0:T(8,128)S(1)}, f32[2,128,1024]{2,1,0:T(8,128)}, u32[]{:S(2)}) copy-start(f32[2,128,1024]{2,1,0:T(8,128)} %copy-done.5) | copy-start | bytes 3145732
  75.9 19.1 %collective-permute-start.7 = (bf16[2,128,1024]{2,1,0:T(8,128)(2,1)}, bf16[2,128,1024]{2,1,0:T(8,128)(2,1)}, u32[]{:S(2)}, u32[]{:S(2)}) collective-permute-start(bf16[2,128,1024]{2,1,0:T(8,128)(2,1)} %convert_element_type.48), channel_id=1, source_target_pairs={{0,4},{2,6},{4,0},{6,2},{8,12},{10,14},{12,8},{14,10},{1,5},{3,7},... | collective-permute-start | bytes 1572872 | tf_op jit(solution)/shard_map/ppermute | solution.py:58
  77.3 3.3 %copy-start.19 = (f32[2,1024]{1,0:T(2,128)}, f32[2,1024]{1,0:T(2,128)S(1)}, u32[]{:S(2)}) copy-start(f32[2,1024]{1,0:T(2,128)S(1)} %mul.350) | copy-start | bytes 24580
  80.6 27.9 %collective-permute-start.6 = (bf16[2,128,1024]{2,1,0:T(8,128)(2,1)}, bf16[2,128,1024]{2,1,0:T(8,128)(2,1)}, u32[]{:S(2)}, u32[]{:S(2)}) collective-permute-start(bf16[2,128,1024]{2,1,0:T(8,128)(2,1)} %convert_element_type.46), channel_id=1, source_target_pairs={{0,8},{2,10},{4,12},{6,14},{8,0},{10,2},{12,4},{14,6},{1,9},{3,11}... | collective-permute-start | bytes 1572872 | tf_op jit(solution)/shard_map/ppermute | solution.py:58
  96.8 7.6 %copy-start.11 = (f32[2,128,1024]{2,1,0:T(8,128)}, f32[2,128,1024]{2,1,0:T(8,128)S(1)}, u32[]{:S(2)}) copy-start(f32[2,128,1024]{2,1,0:T(8,128)S(1)} %add_select_fusion.4) | copy-start | bytes 3145732
  97.9 28.9 %collective-permute-start.8 = (bf16[2,128,1024]{2,1,0:T(8,128)(2,1)}, bf16[2,128,1024]{2,1,0:T(8,128)(2,1)}, u32[]{:S(2)}, u32[]{:S(2)}) collective-permute-start(bf16[2,128,1024]{2,1,0:T(8,128)(2,1)} %convert_element_type.50), channel_id=1, source_target_pairs={{0,8},{2,10},{4,12},{6,14},{8,0},{10,2},{12,4},{14,6},{1,9},{3,11}... | collective-permute-start | bytes 1572872 | tf_op jit(solution)/shard_map/ppermute | solution.py:58
  105.2 3.3 %copy-start.20 = (f32[2,1024]{1,0:T(2,128)}, f32[2,1024]{1,0:T(2,128)S(1)}, u32[]{:S(2)}) copy-start(f32[2,1024]{1,0:T(2,128)S(1)} %mul.321) | copy-start | bytes 24580
  109.7 18.2 %copy-start.2 = (f32[2,128,1024]{2,1,0:T(8,128)S(1)}, f32[2,128,1024]{2,1,0:T(8,128)}, u32[]{:S(2)}) copy-start(f32[2,128,1024]{2,1,0:T(8,128)} %copy-done.1) | copy-start | bytes 3145732
  127.9 1.6 %copy-start.10 = (f32[2,128,1024]{2,1,0:T(8,128)S(1)}, f32[2,128,1024]{2,1,0:T(8,128)}, u32[]{:S(2)}) copy-start(f32[2,128,1024]{2,1,0:T(8,128)} %copy-done.9) | copy-start | bytes 3145732
  127.9 1.7 %copy-start.12 = (f32[2,128,1024]{2,1,0:T(8,128)S(1)}, f32[2,128,1024]{2,1,0:T(8,128)}, u32[]{:S(2)}) copy-start(f32[2,128,1024]{2,1,0:T(8,128)} %copy-done.11) | copy-start | bytes 3145732
  127.9 1.7 %slice-start = ((f32[2,1024]{1,0:T(2,128)}), f32[1,1024]{1,0:T(1,128)S(1)}, s32[]{:S(2)}) async-start(f32[2,1024]{1,0:T(2,128)} %copy-done.17), calls=%async_computation.1 | async-start | bytes 8192 | tf_op jit(solution)/shard_map/slice | solution.py:85
  127.9 1.7 %slice-start.1 = ((f32[2,1024]{1,0:T(2,128)}), f32[1,1024]{1,0:T(1,128)S(1)}, s32[]{:S(2)}) async-start(f32[2,1024]{1,0:T(2,128)} %copy-done.18), calls=%async_computation.2 | async-start | bytes 8192 | tf_op jit(solution)/shard_map/slice | solution.py:85
  128.0 1.7 %slice-start.2 = ((f32[2,1024]{1,0:T(2,128)}), f32[1,1024]{1,0:T(1,128)S(1)}, s32[]{:S(2)}) async-start(f32[2,1024]{1,0:T(2,128)} %copy-done.19), calls=%async_computation.3 | async-start | bytes 8192 | tf_op jit(solution)/shard_map/slice | solution.py:85
  128.0 1.7 %slice-start.3 = ((f32[2,1024]{1,0:T(2,128)}), f32[1,1024]{1,0:T(1,128)S(1)}, s32[]{:S(2)}) async-start(f32[2,1024]{1,0:T(2,128)} %copy-done.20), calls=%async_computation.4 | async-start | bytes 8192 | tf_op jit(solution)/shard_map/slice | solution.py:85
  130.1 1.6 %copy-start.7 = (f32[2,128,2048]{2,1,0:T(8,128)S(1)}, f32[2,128,2048]{2,1,0:T(8,128)}, u32[]{:S(2)}) copy-start(f32[2,128,2048]{2,1,0:T(8,128)} %shard_map.105) | copy-start | bytes 6291460
  130.1 2.2 %copy-start.8 = (f32[2,128,2048]{2,1,0:T(8,128)S(1)}, f32[2,128,2048]{2,1,0:T(8,128)}, u32[]{:S(2)}) copy-start(f32[2,128,2048]{2,1,0:T(8,128)} %copy.26) | copy-start | bytes 6291460
  (4 other events, 4.7 us)
Sparse Core Ops, SparseCore 0:
  10.2 56.6 all-gather.1
